TPU v7x, 32 devices: a whole 2x2x4 slice. The times are simulated.
32 devices in a mesh: row: 4 (over y, x), col: 8 (over z, core).
Axes of the slice: x: 2, y: 2, z: 4, core: 2. Of those that a mesh axis runs over, the one named last changes fastest.
Arguments:
- tokens: bfloat16 [256, 12288], P('col', 'row'), may hold values from -6 to 6
- weight: bfloat16 [12288, 24576], P('row', 'col'), may hold values from -0.0546875 to 0.0546875
- bias: float32 [24576], P('col'), may hold values from -4 to 4
- cotangent: bfloat16 [256, 24576], P(None, 'col'), may hold values from -6 to 6
Outputs:
- hidden: bfloat16 [256, 24576], P('row', 'col')
- grad_tokens: bfloat16 [256, 12288], P('col', 'row')
- grad_weight: bfloat16 [12288, 24576], P('row', 'col')
- grad_bias: float32 [24576], P('col')
All inputs are finite; a program needn't handle non-finite values.
Results may differ from a plain program's by a relative error of at most 0.0055.
Values may be sent and summed in bfloat16 or wider, within the bound.
No kernel may reach another device: no remote copies, remote signals or barrier semaphores. Data moves between devices by JAX's collectives and lax.ppermute only.
A program may use at most 192 MiB of HBM per device.

v0:
```python
import math

import jax
import jax.numpy as jnp
from jax import lax
from jax.sharding import PartitionSpec as P


def activate(preact, cotangent):
    normal_cdf = 0.5 * (1.0 + jax.scipy.special.erf(preact / math.sqrt(2.0)))
    normal_pdf = jnp.exp(-0.5 * preact * preact) / math.sqrt(2.0 * math.pi)
    hidden = (preact * normal_cdf).astype(jnp.bfloat16)
    grad_pre = (cotangent.astype(jnp.float32) * (normal_cdf + preact * normal_pdf)).astype(
        jnp.bfloat16
    )
    return (hidden, grad_pre)


def body(tokens, weight, bias, cotangent):
    local_x = lax.all_gather(tokens, "col", axis=0, tiled=True)
    total_rows = local_x.shape[0]
    my_rows = total_rows // lax.axis_size("row")
    first_row = lax.axis_index("row") * my_rows
    partial_value = jnp.dot(local_x, weight, preferred_element_type=jnp.float32)
    preact = lax.psum(partial_value, "row") + bias
    all_hidden, full_grad = activate(preact, cotangent)
    hidden = lax.dynamic_slice_in_dim(all_hidden, first_row, my_rows, 0)
    grad_tokens = lax.psum_scatter(
        lax.dot_general(
            full_grad, weight, (((1,), (1,)), ((), ())), preferred_element_type=jnp.float32
        ),
        "col",
        scatter_dimension=0,
        tiled=True,
    ).astype(jnp.bfloat16)
    grad_weight = lax.dot_general(
        local_x, full_grad, (((0,), (0,)), ((), ())), preferred_element_type=jnp.float32
    ).astype(jnp.bfloat16)
    grad_bias = jnp.sum(full_grad.astype(jnp.float32), axis=0)
    return (hidden, grad_tokens, grad_weight, grad_bias)


def solution(mesh):
    placed = (P("col", "row"), P("row", "col"), P("col"), P(None, "col"))
    return jax.shard_map(
        body,
        mesh=mesh,
        in_specs=placed,
        out_specs=(P("row", "col"), P("col", "row"), P("row", "col"), P("col")),
        check_vma=False,
    )
```

profile of v0, /device:TPU:0, one launch (start us, length us, event | category | flops | bytes accessed | tf_op | source)
XLA Modules:
  0.0 199.8 jit_solution(12277951146830679832)
XLA Ops:
  7.2 0.0 all-gather.2.cloned.1.call-start
  7.2 0.7 all-gather.2.cloned.1.call-update
  7.9 0.0 all-reduce.2.cloned.1.call-start
  7.9 29.5 %all-gather.2.cloned.1.call-done = bf16[256,3072]{1,0:T(8,128)(2,1)} async-done(((bf16[32,3072]{1,0:T(8,128)(2,1)}), bf16[256,3072]{1,0:T(8,128)(2,1)}) %all-gather.2.cloned.1.call-update) | async-done | bytes 1572880 | tf_op jit(solution)/shard_map/all_gather | solution.py:20
  37.4 10.6 %fusion.8 = f32[256,3072]{1,0:T(8,128)} fusion(bf16[256,3072]{1,0:T(8,128)(2,1)} %all-gather.2.cloned.1.call-done, bf16[3072,3072]{1,0:T(8,128)(2,1)} %param.5), kind=kOutput, calls=%fused_computation.13 | convolution fusion | flops 4831838208 | bytes 23592960 | tf_op jit(solution)/shard_map/dot_general | solution.py:24
  48.0 0.0 copy-start.1
  48.0 0.0 copy-start.2
  48.0 0.0 all-reduce.2.cloned.1.call-update
  48.0 0.0 reduce-scatter.2.cloned.1.call-start
  48.1 86.8 %all-reduce.2.cloned.1.call-done = f32[256,3072]{1,0:T(8,128)} async-done(((f32[256,3072]{1,0:T(8,128)}), f32[256,3072]{1,0:T(8,128)}) %all-reduce.2.cloned.1.call-update) | async-done | bytes 3145744 | tf_op jit(solution)/shard_map/psum | solution.py:25
  134.9 0.0 copy-done.1
  134.9 0.0 copy-done.2
  134.9 5.4 %convert_reduce_fusion = (f32[3072]{0:T(1024)}, bf16[256,3072]{1,0:T(8,128)(2,1)S(1)}, f32[256,3072]{1,0:T(8,128)}, f32[256,3072]{1,0:T(8,128)}) fusion(bf16[256,3072]{1,0:T(8,128)(2,1)S(1)} %copy-done.1, f32[256,3072]{1,0:T(8,128)} %all-reduce.2.cloned.1.call-done, f32[3072]{0:T(1024)S(1)} %copy-done.2), kind=kLoop, calls=%fused_computation.8 | loop fusion | flops 11006976 | bytes 12607488 | tf_op jit(solution)/shard_map/reduce_sum | solution.py:39
  140.3 10.7 %fusion.9 = f32[256,3072]{1,0:T(8,128)} fusion(bf16[256,3072]{1,0:T(8,128)(2,1)S(1)} %get-tuple-element.9, bf16[3072,3072]{1,0:T(8,128)(2,1)} %param.5), kind=kOutput, calls=%fused_computation.14 | convolution fusion | flops 4831838208 | bytes 23592960 | tf_op jit(solution)/shard_map/dot_general | solution.py:29
  151.1 0.0 copy-start
  151.1 0.0 reduce-scatter.2.cloned.1.call-update
  151.1 1.4 copy-done
  152.5 9.2 %convert_bitcast_fusion = bf16[3072,3072]{0,1:T(8,128)(2,1)} fusion(bf16[256,3072]{1,0:T(8,128)(2,1)S(1)} %get-tuple-element.9, bf16[256,3072]{1,0:T(8,128)(2,1)S(1)} %copy-done), kind=kOutput, calls=%fused_computation | convolution fusion | flops 4841275392 | bytes 22020096 | tf_op jit(solution)/shard_map/dot_general | solution.py:36
  161.6 24.7 %copy.8 = bf16[3072,3072]{1,0:T(8,128)(2,1)} copy(bf16[3072,3072]{0,1:T(8,128)(2,1)} %convert_bitcast_fusion) | data formatting | bytes 37748736
  186.3 2.2 %fusion.6 = bf16[64,3072]{1,0:T(8,128)(2,1)} fusion(f32[256,3072]{1,0:T(8,128)} %get-tuple-element.10, s32[]{:T(128)S(6)} %select_n.3, f32[256,3072]{1,0:T(8,128)} %get-tuple-element.11), kind=kLoop, calls=%fused_computation.12 | loop fusion | flops 393216 | bytes 1966084 | tf_op jit(solution)/shard_map/convert_element_type | solution.py:12
  188.5 3.1 %reduce-scatter.2.cloned.1.call-done = f32[32,3072]{1,0:T(8,128)} async-done(((f32[256,3072]{1,0:T(8,128)}), f32[32,3072]{1,0:T(8,128)}) %reduce-scatter.2.cloned.1.call-update) | async-done | bytes 393232 | tf_op jit(solution)/shard_map/reduce_scatter | solution.py:28
  191.6 1.7 convert_element_type.24
Async XLA Ops:
  7.2 30.3 %all-gather.2.cloned.1.call-start = ((), (), s32[]{:S(2)}) async-start(), calls=%async_computation.1 | async-start | bytes 1769472 | tf_op jit(solution)/shard_map/all_gather | solution.py:20
  7.9 127.0 %all-reduce.2.cloned.1.call-start = ((), (), s32[]{:S(2)}) async-start(), calls=%async_computation.2 | async-start | bytes 6291456 | tf_op jit(solution)/shard_map/psum | solution.py:25
  48.0 86.9 %copy-start.1 = (bf16[256,3072]{1,0:T(8,128)(2,1)S(1)}, bf16[256,3072]{1,0:T(8,128)(2,1)}, u32[]{:S(2)}) copy-start(bf16[256,3072]{1,0:T(8,128)(2,1)} %param.7) | copy-start | bytes 4718596
  48.0 86.9 %copy-start.2 = (f32[3072]{0:T(1024)S(1)}, f32[3072]{0:T(1024)}, u32[]{:S(2)}) copy-start(f32[3072]{0:T(1024)} %param.6) | copy-start | bytes 36868
  48.0 143.6 %reduce-scatter.2.cloned.1.call-start = ((), (), s32[]{:S(2)}) async-start(), calls=%async_computation.3 | async-start | bytes 3538944 | tf_op jit(solution)/shard_map/reduce_scatter | solution.py:28
  151.1 1.4 copy-start
Sparse Core Ops, SparseCore 0:
  9.6 27.7 all-gather.1
  48.1 86.7 all-reduce.1
  151.2 40.3 reduce-scatter.1
where the time goes:
time: 201 us; the launch traced here: 200 us
  waiting for transfers between devices  120 us (60%)
  matrix products  30.4 us (15%)
  local copies, waits for them, and re-layouts  26 us (13%)
  between operations  13.8 us (7%)
  other arithmetic  9.32 us (5%)
    psum x1, waiting for transfers between devices, body(): preact = lax.psum(partial_value, 'row') + bias  86.8 us
    all_gather x1, waiting for transfers between devices, body(): local_x = lax.all_gather(tokens, 'col', axis=0, tiled=True)  29.5 us
    unnamed x7, local copies, waits for them, and re-layouts  26 us
    dot_general x1, matrix products, body(): lax.dot_general(full_grad, weight, (((1,), (1,)), ((), ())), preferred_el...  10.7 us
    dot_general x1, matrix products, body(): partial_value = jnp.dot(local_x, weight, preferred_element_type=jnp.float32)  10.6 us
    dot_general x1, matrix products, body(): lax.dot_general(local_x, full_grad, (((0,), (0,)), ((), ())), preferred_e...  9.17 us
    reduce_sum x1, other arithmetic, body(): grad_bias = jnp.sum(full_grad.astype(jnp.float32), axis=0)  5.43 us
  transfers between devices with their start and end apart: 3, of which 3 were waited for; matrix products, arithmetic and copies ran while one was open for 18% of the time, Pallas kernels for 0%

commit v1 on v0

--- a/solution.py
+++ b/solution.py
@@ -3,6 +3,8 @@
 import jax
 import jax.numpy as jnp
 from jax import lax
+from jax.experimental import pallas as pl
+from jax.experimental.pallas import tpu as pltpu
 from jax.sharding import PartitionSpec as P
 
 
@@ -16,15 +18,41 @@
     return (hidden, grad_pre)
 
 
+def _outer_kernel(xt_ref, g_ref, o_ref):
+    o_ref[...] = jnp.dot(xt_ref[...], g_ref[...], preferred_element_type=jnp.float32).astype(
+        o_ref.dtype
+    )
+
+
+def outer_product_sum(xt, g, block_m=512, block_n=1536):
+    m, k = xt.shape
+    n = g.shape[1]
+    block_m = min(block_m, m)
+    block_n = min(block_n, n)
+    return pl.pallas_call(
+        _outer_kernel,
+        grid=(n // block_n, m // block_m),
+        in_specs=[
+            pl.BlockSpec((block_m, k), lambda j, i: (i, 0)),
+            pl.BlockSpec((k, block_n), lambda j, i: (0, j)),
+        ],
+        out_specs=pl.BlockSpec((block_m, block_n), lambda j, i: (i, j)),
+        out_shape=jax.ShapeDtypeStruct((m, n), jnp.bfloat16),
+        cost_estimate=pl.CostEstimate(
+            flops=2 * m * n * k, transcendentals=0, bytes_accessed=2 * (m * k + k * n + m * n)
+        ),
+    )(xt, g)
+
+
 def body(tokens, weight, bias, cotangent):
     local_x = lax.all_gather(tokens, "col", axis=0, tiled=True)
-    total_rows = local_x.shape[0]
-    my_rows = total_rows // lax.axis_size("row")
+    my_rows = local_x.shape[0] // lax.axis_size("row")
     first_row = lax.axis_index("row") * my_rows
     partial_value = jnp.dot(local_x, weight, preferred_element_type=jnp.float32)
-    preact = lax.psum(partial_value, "row") + bias
-    all_hidden, full_grad = activate(preact, cotangent)
-    hidden = lax.dynamic_slice_in_dim(all_hidden, first_row, my_rows, 0)
+    preact = lax.psum_scatter(partial_value, "row", scatter_dimension=0, tiled=True) + bias
+    my_cot = lax.dynamic_slice_in_dim(cotangent, first_row, my_rows, 0)
+    hidden, my_grad = activate(preact, my_cot)
+    full_grad = lax.all_gather(my_grad, "row", axis=0, tiled=True)
     grad_tokens = lax.psum_scatter(
         lax.dot_general(
             full_grad, weight, (((1,), (1,)), ((), ())), preferred_element_type=jnp.float32
@@ -33,9 +61,7 @@
         scatter_dimension=0,
         tiled=True,
     ).astype(jnp.bfloat16)
-    grad_weight = lax.dot_general(
-        local_x, full_grad, (((0,), (0,)), ((), ())), preferred_element_type=jnp.float32
-    ).astype(jnp.bfloat16)
+    grad_weight = outer_product_sum(local_x.T, full_grad)
     grad_bias = jnp.sum(full_grad.astype(jnp.float32), axis=0)
     return (hidden, grad_tokens, grad_weight, grad_bias)
 

time: 201 us -> 185 us (0.920)
  local copies, waits for them, and re-layouts: 26 us -> 2.96 us
  Pallas kernels: 0 us -> 13.4 us
  matrix products: 30.4 us -> 21.1 us
  waiting for transfers between devices: 120 us -> 128 us
  other arithmetic: 9.32 us -> 5.06 us
    psum x1 -> x0, waiting for transfers between devices: 86.8 us -> none  [body(): preact = lax.psum(partial_value, 'row') + bias]
    reduce_scatter x0 -> x1, waiting for transfers between devices: none -> 43.6 us  [body(): lax.psum_scatter(partial_value, 'row', scatter_dimension=0, tiled=True)]
    all_gather x0 -> x1, waiting for transfers between devices: none -> 31.1 us  [body(): full_grad = lax.all_gather(my_grad, 'row', axis=0, tiled=True)]
    unnamed x7 -> x6, local copies, waits for them, and re-layouts: 26 us -> 1.39 us
    reduce_scatter x1, waiting for transfers between devices: 3.08 us -> 23.3 us  [body(): lax.psum_scatter(lax.dot_general(full_grad, weight, (((1,), (1,)), ((), (...]
    pallas_call x0 -> x1, Pallas kernels: none -> 13.4 us  [outer_product_sum(): pl.pallas_call(_outer_kernel, grid=(n // block_n, m // block_m), in_specs...]
    dot_general x1 -> x0, matrix products: 9.17 us -> none  [body(): lax.dot_general(local_x, full_grad, (((0,), (0,)), ((), ())), preferred_e...]
    reduce_sum x1, other arithmetic: 5.43 us -> 0.85 us  [body(): grad_bias = jnp.sum(full_grad.astype(jnp.float32), axis=0)]
  transfers between devices with their start and end apart: 3 -> 4, of which waited for: 3 -> 4; matrix products, arithmetic and copies ran while one was open for 18% -> 1% of each run, Pallas kernels for 0% -> 7%
where the time goes in v1:
time: 185 us
  waiting for transfers between devices  128 us (69%)
  matrix products  21.1 us (11%)
  between operations  13.8 us (7%)
  Pallas kernels  13.4 us (7%)
  other arithmetic  5.06 us (3%)
  local copies, waits for them, and re-layouts  2.96 us (2%)
    reduce_scatter x1, waiting for transfers between devices, body(): lax.psum_scatter(partial_value, 'row', scatter_dimension=0, tiled=True)  43.6 us
    all_gather x1, waiting for transfers between devices, body(): full_grad = lax.all_gather(my_grad, 'row', axis=0, tiled=True)  31.1 us
    all_gather x1, waiting for transfers between devices, body(): local_x = lax.all_gather(tokens, 'col', axis=0, tiled=True)  29.5 us
    reduce_scatter x1, waiting for transfers between devices, body(): lax.psum_scatter(lax.dot_general(full_grad, weight, (((1,), (1,)), ((), (...  23.3 us
    pallas_call x1, Pallas kernels, outer_product_sum(): pl.pallas_call(_outer_kernel, grid=(n // block_n, m // block_m), in_specs...  13.4 us
    dot_general x1, matrix products, body(): lax.dot_general(full_grad, weight, (((1,), (1,)), ((), ())), preferred_el...  10.6 us
    dot_general x1, matrix products, body(): partial_value = jnp.dot(local_x, weight, preferred_element_type=jnp.float32)  10.6 us
  transfers between devices with their start and end apart: 4, of which 4 were waited for; matrix products, arithmetic and copies ran while one was open for 1% of the time, Pallas kernels for 7%

profile of v1, /device:TPU:0, one launch (start us, length us, event | category | flops | bytes accessed | tf_op | source)
XLA Modules:
  0.0 184.6 jit_solution(14059610110621439123)
XLA Ops:
  7.2 0.0 all-gather.3.cloned.1.call-start
  7.2 0.7 all-gather.3.cloned.1.call-update
  7.9 0.0 reduce-scatter.3.cloned.1.call-start
  7.9 29.5 %all-gather.3.cloned.1.call-done = bf16[256,3072]{1,0:T(8,128)(2,1)} async-done(((bf16[32,3072]{1,0:T(8,128)(2,1)}), bf16[256,3072]{1,0:T(8,128)(2,1)}) %all-gather.3.cloned.1.call-update) | async-done | bytes 1572880 | tf_op jit(solution)/shard_map/all_gather | solution.py:48
  37.4 10.6 %fusion.6 = f32[256,3072]{1,0:T(8,128)} fusion(bf16[256,3072]{1,0:T(8,128)(2,1)} %all-gather.3.cloned.1.call-done, bf16[3072,3072]{1,0:T(8,128)(2,1)} %param.5), kind=kOutput, calls=%fused_computation.10 | convolution fusion | flops 4831838208 | bytes 23592960 | tf_op jit(solution)/shard_map/dot_general | solution.py:51
  48.0 0.0 copy-start.2
  48.0 0.0 reduce-scatter.3.cloned.1.call-update
  48.0 0.0 all-gather.5.cloned.1.call-start
  48.1 43.6 %reduce-scatter.3.cloned.1.call-done = f32[64,3072]{1,0:T(8,128)} async-done(((f32[256,3072]{1,0:T(8,128)}), f32[64,3072]{1,0:T(8,128)}) %reduce-scatter.3.cloned.1.call-update) | async-done | bytes 786448 | tf_op jit(solution)/shard_map/reduce_scatter | solution.py:52
  91.6 0.0 copy-done.2
  91.7 2.5 %fusion.5 = (bf16[64,3072]{1,0:T(8,128)(2,1)}, bf16[64,3072]{1,0:T(8,128)(2,1)}) fusion(f32[64,3072]{1,0:T(8,128)} %reduce-scatter.3.cloned.1.call-done, bf16[256,3072]{1,0:T(8,128)(2,1)} %param.7, s32[]{:T(128)S(6)} %select_n.3, f32[3072]{0:T(1024)S(1)} %copy-done.2), kind=kLoop, calls=%fused_computation.7 | loop fusion | flops 2752512 | bytes 1978372 | tf_op jit(solution)/shard_map/convert_element_type | solution.py:15
  94.2 0.0 all-gather.5.cloned.1.call-update
  94.2 0.0 reduce-scatter.5.cloned.1.call-start
  94.2 31.1 %all-gather.5.cloned.1.call-done.g_ref = bf16[256,3072]{1,0:T(8,128)(2,1)} async-done(((bf16[64,3072]{1,0:T(8,128)(2,1)}), bf16[256,3072]{1,0:T(8,128)(2,1)}) %all-gather.5.cloned.1.call-update) | async-done | bytes 1572880 | tf_op jit(solution)/shard_map/all_gather | solution.py:55
  125.3 10.6 %fusion.7 = f32[256,3072]{1,0:T(8,128)} fusion(bf16[256,3072]{1,0:T(8,128)(2,1)} %all-gather.5.cloned.1.call-done.g_ref, bf16[3072,3072]{1,0:T(8,128)(2,1)} %param.5), kind=kOutput, calls=%fused_computation.11 | convolution fusion | flops 4831838208 | bytes 23592960 | tf_op jit(solution)/shard_map/dot_general | solution.py:57
  135.9 0.0 copy-start.1
  135.9 0.0 reduce-scatter.5.cloned.1.call-update
  135.9 1.4 copy-done.1
  137.3 1.6 copy.9
  138.9 0.0 copy-done
  138.9 0.9 convert_reduce_fusion
  139.7 13.4 %shard_map.75 = bf16[3072,3072]{1,0:T(8,128)(2,1)} custom-call(bf16[3072,256]{1,0:T(8,128)(2,1)} %bitcast.5, bf16[256,3072]{1,0:T(8,128)(2,1)} %all-gather.5.cloned.1.call-done.g_ref), custom_call_target="tpu_custom_call" | custom-call | flops 4831838208 | bytes 22020096 | tf_op jit(solution)/shard_map/pallas_call | solution.py:32
  153.1 23.3 %reduce-scatter.5.cloned.1.call-done = f32[32,3072]{1,0:T(8,128)} async-done(((f32[256,3072]{1,0:T(8,128)}), f32[32,3072]{1,0:T(8,128)}) %reduce-scatter.5.cloned.1.call-update) | async-done | bytes 393232 | tf_op jit(solution)/shard_map/reduce_scatter | solution.py:56
  176.4 1.7 convert_element_type.18
  (1 shorter events, 0.0 us)
Async XLA Ops:
  7.2 30.3 %all-gather.3.cloned.1.call-start = ((), (), s32[]{:S(2)}) async-start(), calls=%async_computation.2 | async-start | bytes 1769472 | tf_op jit(solution)/shard_map/all_gather | solution.py:48
  7.9 83.8 %reduce-scatter.3.cloned.1.call-start = ((), (), s32[]{:S(2)}) async-start(), calls=%async_computation.3 | async-start | bytes 3932160 | tf_op jit(solution)/shard_map/reduce_scatter | solution.py:52
  48.0 43.7 %copy-start.2 = (f32[3072]{0:T(1024)S(1)}, f32[3072]{0:T(1024)}, u32[]{:S(2)}) copy-start(f32[3072]{0:T(1024)} %param.6) | copy-start | bytes 36868
  48.0 77.3 %all-gather.5.cloned.1.call-start = ((), (), s32[]{:S(2)}) async-start(), calls=%async_computation.4 | async-start | bytes 1966080 | tf_op jit(solution)/shard_map/all_gather | solution.py:55
  94.2 82.2 %reduce-scatter.5.cloned.1.call-start = ((), (), s32[]{:S(2)}) async-start(), calls=%async_computation.5 | async-start | bytes 3538944 | tf_op jit(solution)/shard_map/reduce_scatter | solution.py:56
  135.9 1.4 copy-start.1
  135.9 3.0 %copy-start = (bf16[256,3072]{1,0:T(8,128)(2,1)S(1)}, bf16[256,3072]{1,0:T(8,128)(2,1)}, u32[]{:S(2)}) copy-start(bf16[256,3072]{1,0:T(8,128)(2,1)} %all-gather.5.cloned.1.call-done.g_ref) | copy-start | bytes 4718596
Sparse Core Ops, SparseCore 0:
  9.6 27.7 all-gather.2
  48.1 43.4 reduce-scatter.2
  94.3 30.9 all-gather.4
  136.0 40.3 reduce-scatter.4

commit v2 on v1

--- a/solution.py
+++ b/solution.py
@@ -44,15 +44,83 @@
     )(xt, g)
 
 
+def _swap(value, axis, flip):
+    size = lax.axis_size(axis)
+    return lax.ppermute(value, axis, [(i, i ^ flip) for i in range(size)])
+
+
+def _pick(index, blocks):
+    return lax.dynamic_index_in_dim(blocks, index, axis=0, keepdims=False)
+
+
+def _halves(value):
+    cols = value.shape[1]
+    if cols % 256:
+        return [value]
+    return [value[:, : cols // 2], value[:, cols // 2 :]]
+
+
+def _bit_orders(n):
+    order = list(range(n.bit_length() - 1))
+    return [order, order[::-1]]
+
+
+def row_reduce_scatter(partial, axis="row"):
+    n = lax.axis_size(axis)
+    if n & (n - 1):
+        return lax.psum_scatter(partial, axis, scatter_dimension=0, tiled=True)
+    levels = n.bit_length() - 1
+    r = lax.axis_index(axis)
+    m = partial.shape[0] // n
+    outs = []
+    for half, order in zip(_halves(partial), _bit_orders(n)):
+        cur = half.reshape([2] * levels + [m, half.shape[1]])
+        bits = list(range(levels))[::-1]
+        for bit in order:
+            mine = (r >> bit) & 1
+            t = jnp.moveaxis(cur, bits.index(bit), 0)
+            sent = _swap(_pick(1 - mine, t).astype(jnp.bfloat16), axis, 1 << bit)
+            cur = _pick(mine, t) + sent.astype(jnp.float32)
+            bits.remove(bit)
+        outs.append(cur.reshape(m, half.shape[1]))
+    return jnp.concatenate(outs, axis=1)
+
+
+def _pair(mine, theirs, bit):
+    first = jnp.where(bit == 0, mine, theirs)
+    second = jnp.where(bit == 0, theirs, mine)
+    return jnp.stack([first, second], axis=0)
+
+
+def row_all_gather(block, axis="row"):
+    n = lax.axis_size(axis)
+    if n & (n - 1):
+        return lax.all_gather(block, axis, axis=0, tiled=True)
+    levels = n.bit_length() - 1
+    r = lax.axis_index(axis)
+    m = block.shape[0]
+    outs = []
+    for half, order in zip(_halves(block), _bit_orders(n)):
+        cur = half
+        bits = []
+        for bit in order:
+            cur = _pair(cur, _swap(cur, axis, 1 << bit), (r >> bit) & 1)
+            bits.insert(0, bit)
+        perm = sorted(range(levels), key=lambda j: -bits[j])
+        cur = jnp.transpose(cur, perm + [levels, levels + 1])
+        outs.append(cur.reshape(n * m, half.shape[1]))
+    return jnp.concatenate(outs, axis=1)
+
+
 def body(tokens, weight, bias, cotangent):
     local_x = lax.all_gather(tokens, "col", axis=0, tiled=True)
     my_rows = local_x.shape[0] // lax.axis_size("row")
     first_row = lax.axis_index("row") * my_rows
     partial_value = jnp.dot(local_x, weight, preferred_element_type=jnp.float32)
-    preact = lax.psum_scatter(partial_value, "row", scatter_dimension=0, tiled=True) + bias
+    preact = row_reduce_scatter(partial_value) + bias
     my_cot = lax.dynamic_slice_in_dim(cotangent, first_row, my_rows, 0)
     hidden, my_grad = activate(preact, my_cot)
-    full_grad = lax.all_gather(my_grad, "row", axis=0, tiled=True)
+    full_grad = row_all_gather(my_grad)
     grad_tokens = lax.psum_scatter(
         lax.dot_general(
             full_grad, weight, (((1,), (1,)), ((), ())), preferred_element_type=jnp.float32

time: 185 us -> 144 us (0.78)
  waiting for transfers between devices: 128 us -> 75.6 us
  starting transfers between devices: 0.16 us -> 9.79 us
    reduce_scatter x1 -> x0, waiting for transfers between devices: 43.6 us -> none  [body(): lax.psum_scatter(partial_value, 'row', scatter_dimension=0, tiled=True)]
    all_gather x1 -> x0, waiting for transfers between devices: 31.1 us -> none  [body(): full_grad = lax.all_gather(my_grad, 'row', axis=0, tiled=True)]
    ppermute x0 -> x8, waiting for transfers between devices: none -> 24.9 us  [_swap(): return lax.ppermute(value, axis, [(i, i ^ flip) for i in range(size)])]
    ppermute x0 -> x8, starting transfers between devices: none -> 9.71 us  [_swap(): return lax.ppermute(value, axis, [(i, i ^ flip) for i in range(size)])]
    reduce_scatter x1, waiting for transfers between devices: 23.3 us -> 20.6 us  [body(): lax.psum_scatter(lax.dot_general(full_grad, weight, (((1,), (1,)), ((), (...]
  transfers between devices with their start and end apart: 4 -> 10, of which waited for: 4 -> 9; matrix products, arithmetic and copies ran while one was open for 1% -> 3% of each run, Pallas kernels for 7% -> 9%
where the time goes in v2:
time: 144 us
  waiting for transfers between devices  75.6 us (52%)
  matrix products  20.1 us (14%)
  between operations  14.2 us (10%)
  Pallas kernels  13.4 us (9%)
  starting transfers between devices  9.79 us (7%)
  other arithmetic  6.71 us (5%)
  local copies, waits for them, and re-layouts  4.16 us (3%)
    all_gather x1, waiting for transfers between devices, body(): local_x = lax.all_gather(tokens, 'col', axis=0, tiled=True)  29.5 us
    ppermute x8, waiting for transfers between devices, _swap(): return lax.ppermute(value, axis, [(i, i ^ flip) for i in range(size)])  24.9 us
    reduce_scatter x1, waiting for transfers between devices, body(): lax.psum_scatter(lax.dot_general(full_grad, weight, (((1,), (1,)), ((), (...  20.6 us
    pallas_call x1, Pallas kernels, outer_product_sum(): pl.pallas_call(_outer_kernel, grid=(n // block_n, m // block_m), in_specs...  13.4 us
    dot_general x1, matrix products, body(): lax.dot_general(full_grad, weight, (((1,), (1,)), ((), ())), preferred_el...  10.7 us
    ppermute x8, starting transfers between devices, _swap(): return lax.ppermute(value, axis, [(i, i ^ flip) for i in range(size)])  9.71 us
    dot_general x1, matrix products, body(): partial_value = jnp.dot(local_x, weight, preferred_element_type=jnp.float32)  9.42 us
  transfers between devices with their start and end apart: 10, of which 9 were waited for; matrix products, arithmetic and copies ran while one was open for 3% of the time, Pallas kernels for 9%

profile of v2, /device:TPU:0, one launch (start us, length us, event | category | flops | bytes accessed | tf_op | source)
XLA Modules:
  0.0 143.9 jit_solution(14827949376679117253)
XLA Ops:
  8.0 29.5 %all-gather.2.cloned.1.call-done = bf16[256,3072]{1,0:T(8,128)(2,1)} async-done(((bf16[32,3072]{1,0:T(8,128)(2,1)}), bf16[256,3072]{1,0:T(8,128)(2,1)}) %all-gather.2.cloned.1.call-update) | async-done | bytes 1572880 | tf_op jit(solution)/shard_map/all_gather | solution.py:116
  37.4 9.4 %fusion.13 = f32[256,3072]{1,0:T(8,128)S(1)} fusion(bf16[256,3072]{1,0:T(8,128)(2,1)} %all-gather.2.cloned.1.call-done, bf16[3072,3072]{1,0:T(8,128)(2,1)} %param.5), kind=kOutput, calls=%fused_computation.39 | convolution fusion | flops 4831838208 | bytes 23592960 | tf_op jit(solution)/shard_map/dot_general | solution.py:119
  47.1 0.8 fusion.7
  47.9 1.5 %collective-permute-start = (bf16[2,64,1536]{2,1,0:T(8,128)(2,1)}, bf16[2,64,1536]{2,1,0:T(8,128)(2,1)S(1)}, u32[]{:S(2)}, u32[]{:S(2)}) collective-permute-start(bf16[2,64,1536]{2,1,0:T(8,128)(2,1)} %fusion.7), channel_id=1, source_target_pairs={{0,8},{8,0},{16,24},{24,16},{1,9},{9,1},{17,25},{25,17},{2,10},{10... | collective-permute-start | bytes 1179656 | tf_op jit(solution)/shard_map/ppermute | solution.py:49
  49.4 1.5 %collective-permute-start.2 = (bf16[2,64,1536]{2,1,0:T(8,128)(2,1)S(1)}, bf16[2,64,1536]{2,1,0:T(8,128)(2,1)S(1)}, u32[]{:S(2)}, u32[]{:S(2)}) collective-permute-start(bf16[2,64,1536]{2,1,0:T(8,128)(2,1)S(1)} %fusion.6), channel_id=1, source_target_pairs={{0,16},{8,24},{16,0},{24,8},{1,17},{9,25},{17,1},{25,9},{2,18},{10... | collective-permute-start | bytes 1179656 | tf_op jit(solution)/shard_map/ppermute | solution.py:49
  50.9 8.4 %collective-permute-done = bf16[2,64,1536]{2,1,0:T(8,128)(2,1)S(1)} collective-permute-done((bf16[2,64,1536]{2,1,0:T(8,128)(2,1)}, bf16[2,64,1536]{2,1,0:T(8,128)(2,1)S(1)}, u32[]{:S(2)}, u32[]{:S(2)}) %collective-permute-start) | collective-permute-done | bytes 393248 | tf_op jit(solution)/shard_map/ppermute | solution.py:49
  59.5 1.5 %collective-permute-start.1 = (bf16[64,1536]{1,0:T(8,128)(2,1)S(1)}, bf16[64,1536]{1,0:T(8,128)(2,1)S(1)}, u32[]{:S(2)}, u32[]{:S(2)}) collective-permute-start(bf16[64,1536]{1,0:T(8,128)(2,1)S(1)} %fusion.8), channel_id=1, source_target_pairs={{0,16},{8,24},{16,0},{24,8},{1,17},{9,25},{17,1},{25,9},{2,18},{10... | collective-permute-start | bytes 589832 | tf_op jit(solution)/shard_map/ppermute | solution.py:49
  61.2 1.5 %collective-permute-start.3 = (bf16[64,1536]{1,0:T(8,128)(2,1)S(1)}, bf16[64,1536]{1,0:T(8,128)(2,1)S(1)}, u32[]{:S(2)}, u32[]{:S(2)}) collective-permute-start(bf16[64,1536]{1,0:T(8,128)(2,1)S(1)} %fusion.9), channel_id=1, source_target_pairs={{0,8},{8,0},{16,24},{24,16},{1,9},{9,1},{17,25},{25,17},{2,10},{10... | collective-permute-start | bytes 589832 | tf_op jit(solution)/shard_map/ppermute | solution.py:49
  62.7 3.1 %collective-permute-done.1 = bf16[64,1536]{1,0:T(8,128)(2,1)S(1)} collective-permute-done((bf16[64,1536]{1,0:T(8,128)(2,1)S(1)}, bf16[64,1536]{1,0:T(8,128)(2,1)S(1)}, u32[]{:S(2)}, u32[]{:S(2)}) %collective-permute-start.1) | collective-permute-done | bytes 196640 | tf_op jit(solution)/shard_map/ppermute | solution.py:49
  65.8 1.4 collective-permute-done.3
  67.2 2.2 %fusion.5 = (bf16[64,3072]{1,0:T(8,128)(2,1)S(1)}, bf16[64,3072]{1,0:T(8,128)(2,1)}) fusion(f32[64,1536]{1,0:T(8,128)S(1)} %bitcast_add_fusion.2, f32[64,1536]{1,0:T(8,128)S(1)} %bitcast_add_fusion.3, bf16[256,3072]{1,0:T(8,128)(2,1)} %param.7, s32[]{:T(128)S(6)} %select_n.71, f32[3072]{0:T(1024)S(1)} %copy-done.1), kind=kLoop, calls=%fused_computation.8 | loop fusion | flops 2949120 | bytes 1978372 | tf_op jit(solution)/shard_map/convert_element_type | solution.py:15
  69.4 1.5 %collective-permute-start.4 = (bf16[64,1536]{1,0:T(8,128)(2,1)S(1)}, bf16[64,1536]{1,0:T(8,128)(2,1)S(1)}, u32[]{:S(2)}, u32[]{:S(2)}) collective-permute-start(bf16[64,1536]{1,0:T(8,128)(2,1)S(1)} %get-tuple-element.18), channel_id=1, source_target_pairs={{0,8},{8,0},{16,24},{24,16},{1,9},{9,1},{17,25},{25,17},{2,10},{10... | collective-permute-start | bytes 589832 | tf_op jit(solution)/shard_map/ppermute | solution.py:49
  71.5 3.6 %collective-permute-done.4 = bf16[64,1536]{1,0:T(8,128)(2,1)S(1)} collective-permute-done((bf16[64,1536]{1,0:T(8,128)(2,1)S(1)}, bf16[64,1536]{1,0:T(8,128)(2,1)S(1)}, u32[]{:S(2)}, u32[]{:S(2)}) %collective-permute-start.4) | collective-permute-done | bytes 196640 | tf_op jit(solution)/shard_map/ppermute | solution.py:49
  75.1 1.5 %collective-permute-done.6 = bf16[64,1536]{1,0:T(8,128)(2,1)S(1)} collective-permute-done((bf16[64,1536]{1,0:T(8,128)(2,1)S(1)}, bf16[64,1536]{1,0:T(8,128)(2,1)S(1)}, u32[]{:S(2)}, u32[]{:S(2)}) %collective-permute-start.6) | collective-permute-done | bytes 196640 | tf_op jit(solution)/shard_map/ppermute | solution.py:49
  77.4 0.9 collective-permute-start.5
  78.3 6.6 %collective-permute-done.7 = bf16[2,64,1536]{2,1,0:T(8,128)(2,1)S(1)} collective-permute-done((bf16[2,64,1536]{2,1,0:T(8,128)(2,1)S(1)}, bf16[2,64,1536]{2,1,0:T(8,128)(2,1)S(1)}, u32[]{:S(2)}, u32[]{:S(2)}) %collective-permute-start.7) | collective-permute-done | bytes 393248 | tf_op jit(solution)/shard_map/ppermute | solution.py:49
  85.6 10.7 %fusion.10 = f32[256,3072]{1,0:T(8,128)} fusion(bf16[3072,3072]{1,0:T(8,128)(2,1)} %param.5, bf16[256,1536]{1,0:T(8,128)(2,1)S(1)} %bitcast.46, bf16[256,1536]{1,0:T(8,128)(2,1)S(1)} %bitcast.49), kind=kOutput, calls=%fused_computation.36 | convolution fusion | flops 4834983936 | bytes 23592960 | tf_op jit(solution)/shard_map/dot_general | solution.py:125
  96.2 1.4 copy-done
  97.6 1.6 %copy.13 = bf16[256,3072]{0,1:T(8,128)(2,1)} copy(bf16[256,3072]{1,0:T(8,128)(2,1)S(1)} %copy-done) | data formatting | bytes 3145728 | tf_op jit(solution)/shard_map/all_gather | solution.py:116
  99.2 0.9 convert_reduce_fusion
  100.0 1.4 pad_maximum_fusion.g_ref
  101.4 13.4 %shard_map.75 = bf16[3072,3072]{1,0:T(8,128)(2,1)} custom-call(bf16[3072,256]{1,0:T(8,128)(2,1)} %bitcast.52, bf16[256,3072]{1,0:T(8,128)(2,1)} %pad_maximum_fusion.g_ref), custom_call_target="tpu_custom_call" | custom-call | flops 4831838208 | bytes 22020096 | tf_op jit(solution)/shard_map/pallas_call | solution.py:32
  114.8 20.6 %reduce-scatter.2.cloned.1.call-done = f32[32,3072]{1,0:T(8,128)} async-done(((f32[256,3072]{1,0:T(8,128)}), f32[32,3072]{1,0:T(8,128)}) %reduce-scatter.2.cloned.1.call-update) | async-done | bytes 393232 | tf_op jit(solution)/shard_map/reduce_scatter | solution.py:124
  135.4 1.7 %convert_element_type.66 = bf16[32,3072]{1,0:T(8,128)(2,1)} convert(f32[32,3072]{1,0:T(8,128)} %reduce-scatter.2.cloned.1.call-done) | non-fusion elementwise | flops 98304 | bytes 589824 | tf_op jit(solution)/shard_map/convert_element_type | solution.py:131
  (27 shorter events, 3.3 us)
Async XLA Ops:
  7.2 30.3 %all-gather.2.cloned.1.call-start = ((), (), s32[]{:S(2)}) async-start(), calls=%async_computation.1 | async-start | bytes 1769472 | tf_op jit(solution)/shard_map/all_gather | solution.py:116
  7.9 127.5 %reduce-scatter.2.cloned.1.call-start = ((), (), s32[]{:S(2)}) async-start(), calls=%async_computation.2 | async-start | bytes 3538944 | tf_op jit(solution)/shard_map/reduce_scatter | solution.py:124
  47.9 11.5 %collective-permute-start = (bf16[2,64,1536]{2,1,0:T(8,128)(2,1)}, bf16[2,64,1536]{2,1,0:T(8,128)(2,1)S(1)}, u32[]{:S(2)}, u32[]{:S(2)}) collective-permute-start(bf16[2,64,1536]{2,1,0:T(8,128)(2,1)} %fusion.7), channel_id=1, source_target_pairs={{0,8},{8,0},{16,24},{24,16},{1,9},{9,1},{17,25},{25,17},{2,10},{10... | collective-permute-start | bytes 1179656 | tf_op jit(solution)/shard_map/ppermute | solution.py:49
  49.4 11.6 %collective-permute-start.2 = (bf16[2,64,1536]{2,1,0:T(8,128)(2,1)S(1)}, bf16[2,64,1536]{2,1,0:T(8,128)(2,1)S(1)}, u32[]{:S(2)}, u32[]{:S(2)}) collective-permute-start(bf16[2,64,1536]{2,1,0:T(8,128)(2,1)S(1)} %fusion.6), channel_id=1, source_target_pairs={{0,16},{8,24},{16,0},{24,8},{1,17},{9,25},{17,1},{25,9},{2,18},{10... | collective-permute-start | bytes 1179656 | tf_op jit(solution)/shard_map/ppermute | solution.py:49
  59.5 6.3 %collective-permute-start.1 = (bf16[64,1536]{1,0:T(8,128)(2,1)S(1)}, bf16[64,1536]{1,0:T(8,128)(2,1)S(1)}, u32[]{:S(2)}, u32[]{:S(2)}) collective-permute-start(bf16[64,1536]{1,0:T(8,128)(2,1)S(1)} %fusion.8), channel_id=1, source_target_pairs={{0,16},{8,24},{16,0},{24,8},{1,17},{9,25},{17,1},{25,9},{2,18},{10... | collective-permute-start | bytes 589832 | tf_op jit(solution)/shard_map/ppermute | solution.py:49
  61.1 6.1 %copy-start.1 = (f32[3072]{0:T(1024)S(1)}, f32[3072]{0:T(1024)}, u32[]{:S(2)}) copy-start(f32[3072]{0:T(1024)} %param.6) | copy-start | bytes 36868
  61.2 6.0 %collective-permute-start.3 = (bf16[64,1536]{1,0:T(8,128)(2,1)S(1)}, bf16[64,1536]{1,0:T(8,128)(2,1)S(1)}, u32[]{:S(2)}, u32[]{:S(2)}) collective-permute-start(bf16[64,1536]{1,0:T(8,128)(2,1)S(1)} %fusion.9), channel_id=1, source_target_pairs={{0,8},{8,0},{16,24},{24,16},{1,9},{9,1},{17,25},{25,17},{2,10},{10... | collective-permute-start | bytes 589832 | tf_op jit(solution)/shard_map/ppermute | solution.py:49
  69.4 5.7 %collective-permute-start.4 = (bf16[64,1536]{1,0:T(8,128)(2,1)S(1)}, bf16[64,1536]{1,0:T(8,128)(2,1)S(1)}, u32[]{:S(2)}, u32[]{:S(2)}) collective-permute-start(bf16[64,1536]{1,0:T(8,128)(2,1)S(1)} %get-tuple-element.18), channel_id=1, source_target_pairs={{0,8},{8,0},{16,24},{24,16},{1,9},{9,1},{17,25},{25,17},{2,10},{10... | collective-permute-start | bytes 589832 | tf_op jit(solution)/shard_map/ppermute | solution.py:49
  70.9 5.7 %collective-permute-start.6 = (bf16[64,1536]{1,0:T(8,128)(2,1)S(1)}, bf16[64,1536]{1,0:T(8,128)(2,1)S(1)}, u32[]{:S(2)}, u32[]{:S(2)}) collective-permute-start(bf16[64,1536]{1,0:T(8,128)(2,1)S(1)} %get-tuple-element.19), channel_id=1, source_target_pairs={{0,16},{8,24},{16,0},{24,8},{1,17},{9,25},{17,1},{25,9},{2,18},{10... | collective-permute-start | bytes 589832 | tf_op jit(solution)/shard_map/ppermute | solution.py:49
  76.7 8.2 %collective-permute-start.7 = (bf16[2,64,1536]{2,1,0:T(8,128)(2,1)S(1)}, bf16[2,64,1536]{2,1,0:T(8,128)(2,1)S(1)}, u32[]{:S(2)}, u32[]{:S(2)}) collective-permute-start(bf16[2,64,1536]{2,1,0:T(8,128)(2,1)S(1)} %pad_maximum_fusion.3), channel_id=1, source_target_pairs={{0,8},{8,0},{16,24},{24,16},{1,9},{9,1},{17,25},{25,17},{2,10},{10... | collective-permute-start | bytes 1179656 | tf_op jit(solution)/shard_map/ppermute | solution.py:49
  77.4 7.8 %collective-permute-start.5 = (bf16[2,64,1536]{2,1,0:T(8,128)(2,1)S(1)}, bf16[2,64,1536]{2,1,0:T(8,128)(2,1)S(1)}, u32[]{:S(2)}, u32[]{:S(2)}) collective-permute-start(bf16[2,64,1536]{2,1,0:T(8,128)(2,1)S(1)} %pad_maximum_fusion.2), channel_id=1, source_target_pairs={{0,16},{8,24},{16,0},{24,8},{1,17},{9,25},{17,1},{25,9},{2,18},{10... | collective-permute-start | bytes 1179656 | tf_op jit(solution)/shard_map/ppermute | solution.py:49
  96.2 1.4 copy-start
Sparse Core Ops, SparseCore 0:
  9.6 27.7 all-gather.1
  96.4 38.9 reduce-scatter.1

commit v3 on v2

--- a/solution.py
+++ b/solution.py
@@ -112,8 +112,62 @@
     return jnp.concatenate(outs, axis=1)
 
 
+def _chain_pairs(chips, step):
+    return [
+        (2 * z + k, 2 * (z + step) + k)
+        for z in range(chips)
+        if 0 <= z + step < chips
+        for k in range(2)
+    ]
+
+
+def col_all_gather(block, axis="col"):
+    n = lax.axis_size(axis)
+    if n % 2:
+        return lax.all_gather(block, axis, axis=0, tiled=True)
+    chips = n // 2
+    c = lax.axis_index(axis)
+    z, k = c // 2, c % 2
+    from_left, from_right = [], []
+    going_right = going_left = block
+    for _ in range(chips - 1):
+        going_right = lax.ppermute(going_right, axis, _chain_pairs(chips, 1))
+        going_left = lax.ppermute(going_left, axis, _chain_pairs(chips, -1))
+        from_left.append(going_right)
+        from_right.append(going_left)
+    held = jnp.stack([block] + from_left + from_right)
+    mine = []
+    for j in range(chips):
+        at = jnp.where(j == z, 0, jnp.where(j < z, z - j, chips - 1 + j - z))
+        mine.append(_pick(at, held))
+    mine = jnp.stack(mine)
+    both = _pair(mine, _swap(mine, axis, 1), k)
+    return jnp.swapaxes(both, 0, 1).reshape(n * block.shape[0], block.shape[1])
+
+
+def col_reduce_scatter(partial, axis="col"):
+    n = lax.axis_size(axis)
+    if n % 2:
+        return lax.psum_scatter(partial, axis, scatter_dimension=0, tiled=True)
+    chips = n // 2
+    m = partial.shape[0] // n
+    c = lax.axis_index(axis)
+    z, k = c // 2, c % 2
+    by_core = jnp.swapaxes(partial.reshape(chips, 2, m, partial.shape[1]), 0, 1)
+    chip = _pick(k, by_core) + _swap(_pick(1 - k, by_core), axis, 1)
+    to_right = to_left = jnp.zeros_like(chip[0])
+    for step in range(1, chips):
+        to_right = lax.ppermute(
+            _pick(z + chips - step, chip) + to_right, axis, _chain_pairs(chips, 1)
+        )
+        to_left = lax.ppermute(
+            _pick(z - chips + step, chip) + to_left, axis, _chain_pairs(chips, -1)
+        )
+    return _pick(z, chip) + to_right + to_left
+
+
 def body(tokens, weight, bias, cotangent):
-    local_x = lax.all_gather(tokens, "col", axis=0, tiled=True)
+    local_x = col_all_gather(tokens)
     my_rows = local_x.shape[0] // lax.axis_size("row")
     first_row = lax.axis_index("row") * my_rows
     partial_value = jnp.dot(local_x, weight, preferred_element_type=jnp.float32)
@@ -121,13 +175,10 @@
     my_cot = lax.dynamic_slice_in_dim(cotangent, first_row, my_rows, 0)
     hidden, my_grad = activate(preact, my_cot)
     full_grad = row_all_gather(my_grad)
-    grad_tokens = lax.psum_scatter(
+    grad_tokens = col_reduce_scatter(
         lax.dot_general(
             full_grad, weight, (((1,), (1,)), ((), ())), preferred_element_type=jnp.float32
-        ),
-        "col",
-        scatter_dimension=0,
-        tiled=True,
+        )
     ).astype(jnp.bfloat16)
     grad_weight = outer_product_sum(local_x.T, full_grad)
     grad_bias = jnp.sum(full_grad.astype(jnp.float32), axis=0)

time: 144 us -> 153 us (1.062)
  starting transfers between devices: 9.79 us -> 47.2 us
  waiting for transfers between devices: 75.6 us -> 53.2 us
  between operations: 14.2 us -> 1.09 us
  other arithmetic: 6.71 us -> 11.2 us
  local copies, waits for them, and re-layouts: 4.16 us -> 7.35 us
    ppermute x0 -> x12, starting transfers between devices: none -> 37.7 us  [the longest x3 15.3 us: col_reduce_scatter(): lax.ppermute(_pick(z + chips - step, chip) + to_right, axis, _chain_pairs...]
    all_gather x1 -> x0, waiting for transfers between devices: 29.5 us -> none  [body(): local_x = lax.all_gather(tokens, 'col', axis=0, tiled=True)]
    ppermute x0 -> x12, waiting for transfers between devices: none -> 22.6 us  [the longest x3 11.8 us: col_reduce_scatter(): lax.ppermute(_pick(z + chips - step, chip) + to_right, axis, _chain_pairs...]
    reduce_scatter x1 -> x0, waiting for transfers between devices: 20.6 us -> none  [body(): lax.psum_scatter(lax.dot_general(full_grad, weight, (((1,), (1,)), ((), (...]
    ppermute x8 -> x10, waiting for transfers between devices: 24.9 us -> 30.6 us  [_swap(): return lax.ppermute(value, axis, [(i, i ^ flip) for i in range(size)])]
    add x0 -> x4, other arithmetic: none -> 5.08 us  [the longest x2 2.98 us: col_reduce_scatter(): _pick(z + chips - step, chip) + to_right]
    reshape x0 -> x1, local copies, waits for them, and re-layouts: none -> 2.57 us  [col_all_gather(): return jnp.swapaxes(both, 0, 1).reshape(n * block.shape[0], block.shape[1])]
    dot_general x1, matrix products: 10.7 us -> 9.03 us  [body(): lax.dot_general(full_grad, weight, (((1,), (1,)), ((), ())), preferred_el...]
  transfers between devices with their start and end apart: 10 -> 22, of which waited for: 9 -> 15; matrix products, arithmetic and copies ran while one was open for 3% -> 5% of each run, Pallas kernels for 9% -> 9%
where the time goes in v3:
time: 153 us; the launch traced here: 152 us
  waiting for transfers between devices  53.2 us (35%)
  starting transfers between devices  47.2 us (31%)
  matrix products  18.6 us (12%)
  Pallas kernels  13.4 us (9%)
  other arithmetic  11.2 us (7%)
  local copies, waits for them, and re-layouts  7.35 us (5%)
    ppermute x10, waiting for transfers between devices, _swap(): return lax.ppermute(value, axis, [(i, i ^ flip) for i in range(size)])  30.6 us
    ppermute x3, starting transfers between devices, col_reduce_scatter(): lax.ppermute(_pick(z + chips - step, chip) + to_right, axis, _chain_pairs...  15.3 us
    ppermute x3, starting transfers between devices, col_all_gather(): going_right = lax.ppermute(going_right, axis, _chain_pairs(chips, 1))  14.7 us
    pallas_call x1, Pallas kernels, outer_product_sum(): pl.pallas_call(_outer_kernel, grid=(n // block_n, m // block_m), in_specs...  13.4 us
    ppermute x3, waiting for transfers between devices, col_reduce_scatter(): lax.ppermute(_pick(z + chips - step, chip) + to_right, axis, _chain_pairs...  11.8 us
    dot_general x1, matrix products, body(): partial_value = jnp.dot(local_x, weight, preferred_element_type=jnp.float32)  9.58 us
    ppermute x10, starting transfers between devices, _swap(): return lax.ppermute(value, axis, [(i, i ^ flip) for i in range(size)])  9.5 us
    dot_general x1, matrix products, body(): lax.dot_general(full_grad, weight, (((1,), (1,)), ((), ())), preferred_el...  9.03 us
  transfers between devices with their start and end apart: 22, of which 15 were waited for; matrix products, arithmetic and copies ran while one was open for 5% of the time, Pallas kernels for 9%

profile of v3, /device:TPU:0, one launch (start us, length us, event | category | flops | bytes accessed | tf_op | source)
XLA Modules:
  0.0 152.1 jit_solution(3992621887258137406)
XLA Ops:
  1.9 5.6 %collective-permute-start = (bf16[32,3072]{1,0:T(8,128)(2,1)}, bf16[32,3072]{1,0:T(8,128)(2,1)S(1)}, u32[]{:S(2)}, u32[]{:S(2)}) collective-permute-start(bf16[32,3072]{1,0:T(8,128)(2,1)} %param.4), channel_id=1, source_target_pairs={{0,2},{1,3},{2,4},{3,5},{4,6},{5,7},{8,10},{9,11},{10,12},{11,13},... | collective-permute-start | bytes 589832 | tf_op jit(solution)/shard_map/ppermute | solution.py:134
  8.5 2.1 %collective-permute-done.3 = bf16[32,3072]{1,0:T(8,128)(2,1)S(1)} collective-permute-done((bf16[32,3072]{1,0:T(8,128)(2,1)}, bf16[32,3072]{1,0:T(8,128)(2,1)S(1)}, u32[]{:S(2)}, u32[]{:S(2)}) %collective-permute-start.3) | collective-permute-done | bytes 196640 | tf_op jit(solution)/shard_map/ppermute | solution.py:135
  12.0 4.6 %collective-permute-start.1 = (bf16[32,3072]{1,0:T(8,128)(2,1)S(1)}, bf16[32,3072]{1,0:T(8,128)(2,1)S(1)}, u32[]{:S(2)}, u32[]{:S(2)}) collective-permute-start(bf16[32,3072]{1,0:T(8,128)(2,1)S(1)} %collective-permute-done), channel_id=1, source_target_pairs={{0,2},{1,3},{2,4},{3,5},{4,6},{5,7},{8,10},{9,11},{10,12},{11,13},... | collective-permute-start | bytes 589832 | tf_op jit(solution)/shard_map/ppermute | solution.py:134
  16.6 2.1 %collective-permute-done.4 = bf16[32,3072]{1,0:T(8,128)(2,1)S(1)} collective-permute-done((bf16[32,3072]{1,0:T(8,128)(2,1)S(1)}, bf16[32,3072]{1,0:T(8,128)(2,1)S(1)}, u32[]{:S(2)}, u32[]{:S(2)}) %collective-permute-start.4) | collective-permute-done | bytes 196640 | tf_op jit(solution)/shard_map/ppermute | solution.py:135
  19.9 4.6 %collective-permute-start.2 = (bf16[32,3072]{1,0:T(8,128)(2,1)S(1)}, bf16[32,3072]{1,0:T(8,128)(2,1)S(1)}, u32[]{:S(2)}, u32[]{:S(2)}) collective-permute-start(bf16[32,3072]{1,0:T(8,128)(2,1)S(1)} %collective-permute-done.1), channel_id=1, source_target_pairs={{0,2},{1,3},{2,4},{3,5},{4,6},{5,7},{8,10},{9,11},{10,12},{11,13},... | collective-permute-start | bytes 589832 | tf_op jit(solution)/shard_map/ppermute | solution.py:134
  24.5 3.1 %collective-permute-done.2 = bf16[32,3072]{1,0:T(8,128)(2,1)S(1)} collective-permute-done((bf16[32,3072]{1,0:T(8,128)(2,1)S(1)}, bf16[32,3072]{1,0:T(8,128)(2,1)S(1)}, u32[]{:S(2)}, u32[]{:S(2)}) %collective-permute-start.2) | collective-permute-done | bytes 196640 | tf_op jit(solution)/shard_map/ppermute | solution.py:134
  28.0 2.3 %collective-permute-done.6 = bf16[4,32,3072]{2,1,0:T(8,128)(2,1)S(1)} collective-permute-done((bf16[4,32,3072]{2,1,0:T(8,128)(2,1)S(1)}, bf16[4,32,3072]{2,1,0:T(8,128)(2,1)S(1)}, u32[]{:S(2)}, u32[]{:S(2)}) %collective-permute-start.6) | collective-permute-done | bytes 786464 | tf_op jit(solution)/shard_map/ppermute | solution.py:49
  30.6 9.6 %fusion.15 = f32[256,3072]{1,0:T(8,128)S(1)} fusion(bf16[256,3072]{1,0:T(8,128)(2,1)S(1)} %bitcast.98, bf16[3072,3072]{1,0:T(8,128)(2,1)} %param.5), kind=kOutput, calls=%fused_computation.65 | convolution fusion | flops 4831838208 | bytes 23592960 | tf_op jit(solution)/shard_map/dot_general | solution.py:173
  44.2 8.4 %collective-permute-done.7 = bf16[2,64,1536]{2,1,0:T(8,128)(2,1)S(1)} collective-permute-done((bf16[2,64,1536]{2,1,0:T(8,128)(2,1)}, bf16[2,64,1536]{2,1,0:T(8,128)(2,1)S(1)}, u32[]{:S(2)}, u32[]{:S(2)}) %collective-permute-start.7) | collective-permute-done | bytes 393248 | tf_op jit(solution)/shard_map/ppermute | solution.py:49
  55.8 3.1 %collective-permute-done.8 = bf16[64,1536]{1,0:T(8,128)(2,1)S(1)} collective-permute-done((bf16[64,1536]{1,0:T(8,128)(2,1)S(1)}, bf16[64,1536]{1,0:T(8,128)(2,1)S(1)}, u32[]{:S(2)}, u32[]{:S(2)}) %collective-permute-start.8) | collective-permute-done | bytes 196640 | tf_op jit(solution)/shard_map/ppermute | solution.py:49
  60.2 2.2 %fusion.5 = (bf16[64,3072]{1,0:T(8,128)(2,1)S(1)}, bf16[64,3072]{1,0:T(8,128)(2,1)}) fusion(f32[64,1536]{1,0:T(8,128)S(1)} %bitcast_add_fusion.8, f32[64,1536]{1,0:T(8,128)S(1)} %bitcast_add_fusion.9, bf16[256,3072]{1,0:T(8,128)(2,1)} %param.7, s32[]{:T(128)S(6)} %select_n.181, f32[3072]{0:T(1024)S(1)} %copy-done.2), kind=kLoop, calls=%fused_computation.11 | loop fusion | flops 2949120 | bytes 1978372 | tf_op jit(solution)/shard_map/convert_element_type | solution.py:15
  64.5 3.7 %collective-permute-done.11 = bf16[64,1536]{1,0:T(8,128)(2,1)S(1)} collective-permute-done((bf16[64,1536]{1,0:T(8,128)(2,1)S(1)}, bf16[64,1536]{1,0:T(8,128)(2,1)S(1)}, u32[]{:S(2)}, u32[]{:S(2)}) %collective-permute-start.11) | collective-permute-done | bytes 196640 | tf_op jit(solution)/shard_map/ppermute | solution.py:49
  71.3 6.5 %collective-permute-done.14 = bf16[2,64,1536]{2,1,0:T(8,128)(2,1)S(1)} collective-permute-done((bf16[2,64,1536]{2,1,0:T(8,128)(2,1)S(1)}, bf16[2,64,1536]{2,1,0:T(8,128)(2,1)S(1)}, u32[]{:S(2)}, u32[]{:S(2)}) %collective-permute-start.14) | collective-permute-done | bytes 393248 | tf_op jit(solution)/shard_map/ppermute | solution.py:49
  78.6 9.0 %fusion.12 = f32[256,3072]{1,0:T(8,128)S(1)} fusion(bf16[3072,3072]{1,0:T(8,128)(2,1)} %param.5, bf16[256,1536]{1,0:T(8,128)(2,1)S(1)} %bitcast.92, bf16[256,1536]{1,0:T(8,128)(2,1)S(1)} %bitcast.95), kind=kOutput, calls=%fused_computation.62 | convolution fusion | flops 4834983936 | bytes 23592960 | tf_op jit(solution)/shard_map/dot_general | solution.py:179
  89.3 3.5 %collective-permute-done.15 = f32[4,32,3072]{2,1,0:T(8,128)} collective-permute-done((f32[4,32,3072]{2,1,0:T(8,128)S(1)}, f32[4,32,3072]{2,1,0:T(8,128)}, u32[]{:S(2)}, u32[]{:S(2)}) %collective-permute-start.15) | collective-permute-done | bytes 1572896 | tf_op jit(solution)/shard_map/ppermute | solution.py:49
  92.8 2.0 %bitcast_add_fusion = f32[4,32,3072]{2,1,0:T(8,128)S(1)} fusion(f32[4,32,3072]{2,1,0:T(8,128)} %collective-permute-done.15, f32[4,2,32,3072]{3,2,1,0:T(8,128)} %bitcast.106, s32[]{:T(128)S(6)} %select_n.192), kind=kLoop, calls=%fused_computation.3 | loop fusion | flops 393216 | bytes 4718596 | tf_op jit(solution)/shard_map/add | solution.py:157
  95.7 5.2 %collective-permute-start.16 = (f32[32,3072]{1,0:T(8,128)}, f32[32,3072]{1,0:T(8,128)}, u32[]{:S(2)}, u32[]{:S(2)}) collective-permute-start(f32[32,3072]{1,0:T(8,128)} %get-tuple-element.8), channel_id=1, source_target_pairs={{0,2},{1,3},{2,4},{3,5},{4,6},{5,7},{8,10},{9,11},{10,12},{11,13},... | collective-permute-start | bytes 1179656 | tf_op jit(solution)/shard_map/ppermute | solution.py:160
  102.1 6.9 %collective-permute-done.16 = f32[32,3072]{1,0:T(8,128)} collective-permute-done((f32[32,3072]{1,0:T(8,128)}, f32[32,3072]{1,0:T(8,128)}, u32[]{:S(2)}, u32[]{:S(2)}) %collective-permute-start.16) | collective-permute-done | bytes 393248 | tf_op jit(solution)/shard_map/ppermute | solution.py:160
  110.8 5.1 %collective-permute-start.17 = (f32[32,3072]{1,0:T(8,128)}, f32[32,3072]{1,0:T(8,128)}, u32[]{:S(2)}, u32[]{:S(2)}) collective-permute-start(f32[32,3072]{1,0:T(8,128)} %bitcast_add_fusion.5), channel_id=1, source_target_pairs={{0,2},{1,3},{2,4},{3,5},{4,6},{5,7},{8,10},{9,11},{10,12},{11,13},... | collective-permute-start | bytes 1179656 | tf_op jit(solution)/shard_map/ppermute | solution.py:160
  116.0 2.6 %copy.14 = bf16[256,3072]{0,1:T(8,128)(2,1)} copy(bf16[256,3072]{1,0:T(8,128)(2,1)} %bitcast.99) | data formatting | bytes 3145728 | tf_op jit(solution)/shard_map/reshape | solution.py:145
  118.5 4.8 %collective-permute-done.17 = f32[32,3072]{1,0:T(8,128)} collective-permute-done((f32[32,3072]{1,0:T(8,128)}, f32[32,3072]{1,0:T(8,128)}, u32[]{:S(2)}, u32[]{:S(2)}) %collective-permute-start.17) | collective-permute-done | bytes 393248 | tf_op jit(solution)/shard_map/ppermute | solution.py:160
  128.1 5.0 %collective-permute-start.18 = (f32[32,3072]{1,0:T(8,128)S(1)}, f32[32,3072]{1,0:T(8,128)S(1)}, u32[]{:S(2)}, u32[]{:S(2)}) collective-permute-start(f32[32,3072]{1,0:T(8,128)S(1)} %get-tuple-element.6), channel_id=1, source_target_pairs={{0,2},{1,3},{2,4},{3,5},{4,6},{5,7},{8,10},{9,11},{10,12},{11,13},... | collective-permute-start | bytes 1179656 | tf_op jit(solution)/shard_map/ppermute | solution.py:160
  133.2 3.5 %collective-permute-done.20 = f32[32,3072]{1,0:T(8,128)S(1)} collective-permute-done((f32[32,3072]{1,0:T(8,128)S(1)}, f32[32,3072]{1,0:T(8,128)S(1)}, u32[]{:S(2)}, u32[]{:S(2)}) %collective-permute-start.20) | collective-permute-done | bytes 393248 | tf_op jit(solution)/shard_map/ppermute | solution.py:163
  138.0 13.4 %shard_map.75 = bf16[3072,3072]{1,0:T(8,128)(2,1)} custom-call(bf16[3072,256]{1,0:T(8,128)(2,1)} %bitcast.100, bf16[256,3072]{1,0:T(8,128)(2,1)} %pad_maximum_fusion.1.g_ref), custom_call_target="tpu_custom_call" | custom-call | flops 4831838208 | bytes 22020096 | tf_op jit(solution)/shard_map/pallas_call | solution.py:32
  (68 shorter events, 32.3 us)
Async XLA Ops:
  0.6 10.0 %collective-permute-start.3 = (bf16[32,3072]{1,0:T(8,128)(2,1)}, bf16[32,3072]{1,0:T(8,128)(2,1)S(1)}, u32[]{:S(2)}, u32[]{:S(2)}) collective-permute-start(bf16[32,3072]{1,0:T(8,128)(2,1)} %param.4), channel_id=1, source_target_pairs={{2,0},{3,1},{4,2},{5,3},{6,4},{7,5},{10,8},{11,9},{12,10},{13,11},... | collective-permute-start | bytes 589832 | tf_op jit(solution)/shard_map/ppermute | solution.py:135
  1.9 10.0 %collective-permute-start = (bf16[32,3072]{1,0:T(8,128)(2,1)}, bf16[32,3072]{1,0:T(8,128)(2,1)S(1)}, u32[]{:S(2)}, u32[]{:S(2)}) collective-permute-start(bf16[32,3072]{1,0:T(8,128)(2,1)} %param.4), channel_id=1, source_target_pairs={{0,2},{1,3},{2,4},{3,5},{4,6},{5,7},{8,10},{9,11},{10,12},{11,13},... | collective-permute-start | bytes 589832 | tf_op jit(solution)/shard_map/ppermute | solution.py:134
  10.7 8.0 %collective-permute-start.4 = (bf16[32,3072]{1,0:T(8,128)(2,1)S(1)}, bf16[32,3072]{1,0:T(8,128)(2,1)S(1)}, u32[]{:S(2)}, u32[]{:S(2)}) collective-permute-start(bf16[32,3072]{1,0:T(8,128)(2,1)S(1)} %collective-permute-done.3), channel_id=1, source_target_pairs={{2,0},{3,1},{4,2},{5,3},{6,4},{7,5},{10,8},{11,9},{12,10},{13,11},... | collective-permute-start | bytes 589832 | tf_op jit(solution)/shard_map/ppermute | solution.py:135
  12.0 8.0 %collective-permute-start.1 = (bf16[32,3072]{1,0:T(8,128)(2,1)S(1)}, bf16[32,3072]{1,0:T(8,128)(2,1)S(1)}, u32[]{:S(2)}, u32[]{:S(2)}) collective-permute-start(bf16[32,3072]{1,0:T(8,128)(2,1)S(1)} %collective-permute-done), channel_id=1, source_target_pairs={{0,2},{1,3},{2,4},{3,5},{4,6},{5,7},{8,10},{9,11},{10,12},{11,13},... | collective-permute-start | bytes 589832 | tf_op jit(solution)/shard_map/ppermute | solution.py:134
  18.6 9.1 %collective-permute-start.5 = (bf16[32,3072]{1,0:T(8,128)(2,1)S(1)}, bf16[32,3072]{1,0:T(8,128)(2,1)S(1)}, u32[]{:S(2)}, u32[]{:S(2)}) collective-permute-start(bf16[32,3072]{1,0:T(8,128)(2,1)S(1)} %collective-permute-done.4), channel_id=1, source_target_pairs={{2,0},{3,1},{4,2},{5,3},{6,4},{7,5},{10,8},{11,9},{12,10},{13,11},... | collective-permute-start | bytes 589832 | tf_op jit(solution)/shard_map/ppermute | solution.py:135
  19.9 7.7 %collective-permute-start.2 = (bf16[32,3072]{1,0:T(8,128)(2,1)S(1)}, bf16[32,3072]{1,0:T(8,128)(2,1)S(1)}, u32[]{:S(2)}, u32[]{:S(2)}) collective-permute-start(bf16[32,3072]{1,0:T(8,128)(2,1)S(1)} %collective-permute-done.1), channel_id=1, source_target_pairs={{0,2},{1,3},{2,4},{3,5},{4,6},{5,7},{8,10},{9,11},{10,12},{11,13},... | collective-permute-start | bytes 589832 | tf_op jit(solution)/shard_map/ppermute | solution.py:134
  27.9 2.4 %collective-permute-start.6 = (bf16[4,32,3072]{2,1,0:T(8,128)(2,1)S(1)}, bf16[4,32,3072]{2,1,0:T(8,128)(2,1)S(1)}, u32[]{:S(2)}, u32[]{:S(2)}) collective-permute-start(bf16[4,32,3072]{2,1,0:T(8,128)(2,1)S(1)} %pad_maximum_fusion.2), channel_id=1, source_target_pairs={{0,1},{1,0},{2,3},{3,2},{4,5},{5,4},{6,7},{7,6},{8,9},{9,8},{10,11... | collective-permute-start | bytes 2359304 | tf_op jit(solution)/shard_map/ppermute | solution.py:49
  30.6 9.6 %copy-start = (bf16[2,4,32,3072]{3,2,0,1:T(8,128)(2,1)}, bf16[2,4,32,3072]{3,2,0,1:T(8,128)(2,1)S(1)}, u32[]{:S(2)}) copy-start(bf16[2,4,32,3072]{3,2,0,1:T(8,128)(2,1)S(1)} %pad_maximum_fusion) | copy-start | bytes 4718596
  41.2 11.4 %collective-permute-start.7 = (bf16[2,64,1536]{2,1,0:T(8,128)(2,1)}, bf16[2,64,1536]{2,1,0:T(8,128)(2,1)S(1)}, u32[]{:S(2)}, u32[]{:S(2)}) collective-permute-start(bf16[2,64,1536]{2,1,0:T(8,128)(2,1)} %fusion.7), channel_id=1, source_target_pairs={{0,8},{8,0},{16,24},{24,16},{1,9},{9,1},{17,25},{25,17},{2,10},{10... | collective-permute-start | bytes 1179656 | tf_op jit(solution)/shard_map/ppermute | solution.py:49
  42.6 11.5 %collective-permute-start.9 = (bf16[2,64,1536]{2,1,0:T(8,128)(2,1)S(1)}, bf16[2,64,1536]{2,1,0:T(8,128)(2,1)S(1)}, u32[]{:S(2)}, u32[]{:S(2)}) collective-permute-start(bf16[2,64,1536]{2,1,0:T(8,128)(2,1)S(1)} %fusion.6), channel_id=1, source_target_pairs={{0,16},{8,24},{16,0},{24,8},{1,17},{9,25},{17,1},{25,9},{2,18},{10... | collective-permute-start | bytes 1179656 | tf_op jit(solution)/shard_map/ppermute | solution.py:49
  52.7 6.2 %collective-permute-start.8 = (bf16[64,1536]{1,0:T(8,128)(2,1)S(1)}, bf16[64,1536]{1,0:T(8,128)(2,1)S(1)}, u32[]{:S(2)}, u32[]{:S(2)}) collective-permute-start(bf16[64,1536]{1,0:T(8,128)(2,1)S(1)} %fusion.10), channel_id=1, source_target_pairs={{0,16},{8,24},{16,0},{24,8},{1,17},{9,25},{17,1},{25,9},{2,18},{10... | collective-permute-start | bytes 589832 | tf_op jit(solution)/shard_map/ppermute | solution.py:49
  54.2 6.0 %copy-start.2 = (f32[3072]{0:T(1024)S(1)}, f32[3072]{0:T(1024)}, u32[]{:S(2)}) copy-start(f32[3072]{0:T(1024)} %param.6) | copy-start | bytes 36868
  54.3 5.9 %collective-permute-start.10 = (bf16[64,1536]{1,0:T(8,128)(2,1)S(1)}, bf16[64,1536]{1,0:T(8,128)(2,1)S(1)}, u32[]{:S(2)}, u32[]{:S(2)}) collective-permute-start(bf16[64,1536]{1,0:T(8,128)(2,1)S(1)} %fusion.11), channel_id=1, source_target_pairs={{0,8},{8,0},{16,24},{24,16},{1,9},{9,1},{17,25},{25,17},{2,10},{10... | collective-permute-start | bytes 589832 | tf_op jit(solution)/shard_map/ppermute | solution.py:49
  62.4 5.7 %collective-permute-start.11 = (bf16[64,1536]{1,0:T(8,128)(2,1)S(1)}, bf16[64,1536]{1,0:T(8,128)(2,1)S(1)}, u32[]{:S(2)}, u32[]{:S(2)}) collective-permute-start(bf16[64,1536]{1,0:T(8,128)(2,1)S(1)} %get-tuple-element.28), channel_id=1, source_target_pairs={{0,8},{8,0},{16,24},{24,16},{1,9},{9,1},{17,25},{25,17},{2,10},{10... | collective-permute-start | bytes 589832 | tf_op jit(solution)/shard_map/ppermute | solution.py:49
  64.0 5.7 %collective-permute-start.13 = (bf16[64,1536]{1,0:T(8,128)(2,1)S(1)}, bf16[64,1536]{1,0:T(8,128)(2,1)S(1)}, u32[]{:S(2)}, u32[]{:S(2)}) collective-permute-start(bf16[64,1536]{1,0:T(8,128)(2,1)S(1)} %get-tuple-element.29), channel_id=1, source_target_pairs={{0,16},{8,24},{16,0},{24,8},{1,17},{9,25},{17,1},{25,9},{2,18},{10... | collective-permute-start | bytes 589832 | tf_op jit(solution)/shard_map/ppermute | solution.py:49
  69.8 8.0 %collective-permute-start.14 = (bf16[2,64,1536]{2,1,0:T(8,128)(2,1)S(1)}, bf16[2,64,1536]{2,1,0:T(8,128)(2,1)S(1)}, u32[]{:S(2)}, u32[]{:S(2)}) collective-permute-start(bf16[2,64,1536]{2,1,0:T(8,128)(2,1)S(1)} %pad_maximum_fusion.5), channel_id=1, source_target_pairs={{0,8},{8,0},{16,24},{24,16},{1,9},{9,1},{17,25},{25,17},{2,10},{10... | collective-permute-start | bytes 1179656 | tf_op jit(solution)/shard_map/ppermute | solution.py:49
  70.4 7.8 %collective-permute-start.12 = (bf16[2,64,1536]{2,1,0:T(8,128)(2,1)S(1)}, bf16[2,64,1536]{2,1,0:T(8,128)(2,1)S(1)}, u32[]{:S(2)}, u32[]{:S(2)}) collective-permute-start(bf16[2,64,1536]{2,1,0:T(8,128)(2,1)S(1)} %pad_maximum_fusion.4), channel_id=1, source_target_pairs={{0,16},{8,24},{16,0},{24,8},{1,17},{9,25},{17,1},{25,9},{2,18},{10... | collective-permute-start | bytes 1179656 | tf_op jit(solution)/shard_map/ppermute | solution.py:49
  89.3 3.5 %collective-permute-start.15 = (f32[4,32,3072]{2,1,0:T(8,128)S(1)}, f32[4,32,3072]{2,1,0:T(8,128)}, u32[]{:S(2)}, u32[]{:S(2)}) collective-permute-start(f32[4,32,3072]{2,1,0:T(8,128)S(1)} %dynamic-slice_bitcast_fusion), channel_id=1, source_target_pairs={{0,1},{1,0},{2,3},{3,2},{4,5},{5,4},{6,7},{7,6},{8,9},{9,8},{10,11... | collective-permute-start | bytes 4718600 | tf_op jit(solution)/shard_map/ppermute | solution.py:49
  95.7 13.4 %collective-permute-start.16 = (f32[32,3072]{1,0:T(8,128)}, f32[32,3072]{1,0:T(8,128)}, u32[]{:S(2)}, u32[]{:S(2)}) collective-permute-start(f32[32,3072]{1,0:T(8,128)} %get-tuple-element.8), channel_id=1, source_target_pairs={{0,2},{1,3},{2,4},{3,5},{4,6},{5,7},{8,10},{9,11},{10,12},{11,13},... | collective-permute-start | bytes 1179656 | tf_op jit(solution)/shard_map/ppermute | solution.py:160
  100.9 17.7 %collective-permute-start.19 = (f32[32,3072]{1,0:T(8,128)S(1)}, f32[32,3072]{1,0:T(8,128)}, u32[]{:S(2)}, u32[]{:S(2)}) collective-permute-start(f32[32,3072]{1,0:T(8,128)S(1)} %get-tuple-element.9), channel_id=1, source_target_pairs={{2,0},{3,1},{4,2},{5,3},{6,4},{7,5},{10,8},{11,9},{12,10},{13,11},... | collective-permute-start | bytes 1179656 | tf_op jit(solution)/shard_map/ppermute | solution.py:163
  110.8 12.5 %collective-permute-start.17 = (f32[32,3072]{1,0:T(8,128)}, f32[32,3072]{1,0:T(8,128)}, u32[]{:S(2)}, u32[]{:S(2)}) collective-permute-start(f32[32,3072]{1,0:T(8,128)} %bitcast_add_fusion.5), channel_id=1, source_target_pairs={{0,2},{1,3},{2,4},{3,5},{4,6},{5,7},{8,10},{9,11},{10,12},{11,13},... | collective-permute-start | bytes 1179656 | tf_op jit(solution)/shard_map/ppermute | solution.py:160
  124.6 12.0 %collective-permute-start.20 = (f32[32,3072]{1,0:T(8,128)S(1)}, f32[32,3072]{1,0:T(8,128)S(1)}, u32[]{:S(2)}, u32[]{:S(2)}) collective-permute-start(f32[32,3072]{1,0:T(8,128)S(1)} %get-tuple-element.7), channel_id=1, source_target_pairs={{2,0},{3,1},{4,2},{5,3},{6,4},{7,5},{10,8},{11,9},{12,10},{13,11},... | collective-permute-start | bytes 1179656 | tf_op jit(solution)/shard_map/ppermute | solution.py:163
  128.1 23.2 %collective-permute-start.18 = (f32[32,3072]{1,0:T(8,128)S(1)}, f32[32,3072]{1,0:T(8,128)S(1)}, u32[]{:S(2)}, u32[]{:S(2)}) collective-permute-start(f32[32,3072]{1,0:T(8,128)S(1)} %get-tuple-element.6), channel_id=1, source_target_pairs={{0,2},{1,3},{2,4},{3,5},{4,6},{5,7},{8,10},{9,11},{10,12},{11,13},... | collective-permute-start | bytes 1179656 | tf_op jit(solution)/shard_map/ppermute | solution.py:160
  136.7 14.7 %collective-permute-start.21 = (f32[32,3072]{1,0:T(8,128)S(1)}, f32[32,3072]{1,0:T(8,128)S(1)}, u32[]{:S(2)}, u32[]{:S(2)}) collective-permute-start(f32[32,3072]{1,0:T(8,128)S(1)} %bitcast_add_fusion.4), channel_id=1, source_target_pairs={{2,0},{3,1},{4,2},{5,3},{6,4},{7,5},{10,8},{11,9},{12,10},{13,11},... | collective-permute-start | bytes 1179656 | tf_op jit(solution)/shard_map/ppermute | solution.py:163
  (1 other events, 1.7 us)

commit v4 on v2

--- a/solution.py
+++ b/solution.py
@@ -112,8 +112,18 @@
     return jnp.concatenate(outs, axis=1)
 
 
+def col_all_gather(block, axis="col"):
+    n = lax.axis_size(axis)
+    if n % 2:
+        return lax.all_gather(block, axis, axis=0, tiled=True)
+    groups = [list(range(k, n, 2)) for k in range(2)]
+    mine = lax.all_gather(block, axis, axis_index_groups=groups)
+    both = _pair(mine, _swap(mine, axis, 1), lax.axis_index(axis) % 2)
+    return jnp.swapaxes(both, 0, 1).reshape(n * block.shape[0], block.shape[1])
+
+
 def body(tokens, weight, bias, cotangent):
-    local_x = lax.all_gather(tokens, "col", axis=0, tiled=True)
+    local_x = col_all_gather(tokens)
     my_rows = local_x.shape[0] // lax.axis_size("row")
     first_row = lax.axis_index("row") * my_rows
     partial_value = jnp.dot(local_x, weight, preferred_element_type=jnp.float32)

time: 144 us -> 140 us (0.972)
  waiting for transfers between devices: 75.6 us -> 49 us
  blocking collectives: 0 us -> 21.5 us
    all_gather x1 -> x0, waiting for transfers between devices: 29.5 us -> none  [body(): local_x = lax.all_gather(tokens, 'col', axis=0, tiled=True)]
    all_gather x0 -> x1, blocking collectives: none -> 21.5 us  [col_all_gather(): mine = lax.all_gather(block, axis, axis_index_groups=groups)]
    ppermute x8 -> x9, waiting for transfers between devices: 24.9 us -> 27.3 us  [_swap(): return lax.ppermute(value, axis, [(i, i ^ flip) for i in range(size)])]
    reshape x0 -> x1, local copies, waits for them, and re-layouts: none -> 1.57 us  [col_all_gather(): return jnp.swapaxes(both, 0, 1).reshape(n * block.shape[0], block.shape[1])]
    all_gather x1 -> x0, local copies, waits for them, and re-layouts: 1.56 us -> none  [body(): local_x = lax.all_gather(tokens, 'col', axis=0, tiled=True)]
    ppermute x8 -> x9, starting transfers between devices: 9.71 us -> 9.38 us  [_swap(): return lax.ppermute(value, axis, [(i, i ^ flip) for i in range(size)])]
  transfers between devices with their start and end apart: 10 -> 10, of which waited for: 9 -> 9; matrix products, arithmetic and copies ran while one was open for 3% -> 4% of each run, Pallas kernels for 9% -> 10%
where the time goes in v4:
time: 140 us; the launch traced here: 139 us
  waiting for transfers between devices  49 us (35%)
  blocking collectives  21.5 us (15%)
  matrix products  19.6 us (14%)
  between operations  14.2 us (10%)
  Pallas kernels  13.5 us (10%)
  starting transfers between devices  9.42 us (7%)
  other arithmetic  8.09 us (6%)
  local copies, waits for them, and re-layouts  4.04 us (3%)
    ppermute x9, waiting for transfers between devices, _swap(): return lax.ppermute(value, axis, [(i, i ^ flip) for i in range(size)])  27.3 us
    reduce_scatter x1, waiting for transfers between devices, body(): lax.psum_scatter(lax.dot_general(full_grad, weight, (((1,), (1,)), ((), (...  21.7 us
    all_gather x1, blocking collectives, col_all_gather(): mine = lax.all_gather(block, axis, axis_index_groups=groups)  21.5 us
    pallas_call x1, Pallas kernels, outer_product_sum(): pl.pallas_call(_outer_kernel, grid=(n // block_n, m // block_m), in_specs...  13.5 us
    dot_general x1, matrix products, body(): lax.dot_general(full_grad, weight, (((1,), (1,)), ((), ())), preferred_el...  10.7 us
    ppermute x9, starting transfers between devices, _swap(): return lax.ppermute(value, axis, [(i, i ^ flip) for i in range(size)])  9.38 us
    dot_general x1, matrix products, body(): partial_value = jnp.dot(local_x, weight, preferred_element_type=jnp.float32)  8.99 us
  transfers between devices with their start and end apart: 10, of which 9 were waited for; matrix products, arithmetic and copies ran while one was open for 4% of the time, Pallas kernels for 10%

profile of v4, /device:TPU:0, one launch (start us, length us, event | category | flops | bytes accessed | tf_op | source)
XLA Modules:
  0.0 139.4 jit_solution(17686403415086107555)
XLA Ops:
  7.2 21.5 %all-gather = bf16[128,3072]{1,0:T(8,128)(2,1)S(1)} all-gather(bf16[32,3072]{1,0:T(8,128)(2,1)} %param.4), channel_id=2, replica_groups={{0,2,4,6},{1,3,5,7},{8,10,12,14},{9,11,13,15},{16,18,20,22},{17,19,21,2..., dimensions={0}, use_global_device_ids=true | all-gather | bytes 983040 | tf_op jit(solution)/shard_map/all_gather | solution.py:120
  28.7 2.3 %collective-permute-done = bf16[4,32,3072]{2,1,0:T(8,128)(2,1)S(1)} collective-permute-done((bf16[4,32,3072]{2,1,0:T(8,128)(2,1)S(1)}, bf16[4,32,3072]{2,1,0:T(8,128)(2,1)S(1)}, u32[]{:S(2)}, u32[]{:S(2)}) %collective-permute-start) | collective-permute-done | bytes 786464 | tf_op jit(solution)/shard_map/ppermute | solution.py:49
  31.4 9.0 %fusion.13 = f32[256,3072]{1,0:T(8,128)S(1)} fusion(bf16[256,3072]{1,0:T(8,128)(2,1)S(1)} %bitcast.60, bf16[3072,3072]{1,0:T(8,128)(2,1)} %param.5), kind=kOutput, calls=%fused_computation.42 | convolution fusion | flops 4831838208 | bytes 23592960 | tf_op jit(solution)/shard_map/dot_general | solution.py:129
  40.6 1.1 copy-done
  42.6 1.5 %collective-permute-start.1 = (bf16[2,64,1536]{2,1,0:T(8,128)(2,1)}, bf16[2,64,1536]{2,1,0:T(8,128)(2,1)S(1)}, u32[]{:S(2)}, u32[]{:S(2)}) collective-permute-start(bf16[2,64,1536]{2,1,0:T(8,128)(2,1)} %fusion.7), channel_id=1, source_target_pairs={{0,8},{8,0},{16,24},{24,16},{1,9},{9,1},{17,25},{25,17},{2,10},{10... | collective-permute-start | bytes 1179656 | tf_op jit(solution)/shard_map/ppermute | solution.py:49
  44.1 1.6 %collective-permute-start.3 = (bf16[2,64,1536]{2,1,0:T(8,128)(2,1)S(1)}, bf16[2,64,1536]{2,1,0:T(8,128)(2,1)S(1)}, u32[]{:S(2)}, u32[]{:S(2)}) collective-permute-start(bf16[2,64,1536]{2,1,0:T(8,128)(2,1)S(1)} %fusion.6), channel_id=1, source_target_pairs={{0,16},{8,24},{16,0},{24,8},{1,17},{9,25},{17,1},{25,9},{2,18},{10... | collective-permute-start | bytes 1179656 | tf_op jit(solution)/shard_map/ppermute | solution.py:49
  45.7 8.2 %collective-permute-done.1 = bf16[2,64,1536]{2,1,0:T(8,128)(2,1)S(1)} collective-permute-done((bf16[2,64,1536]{2,1,0:T(8,128)(2,1)}, bf16[2,64,1536]{2,1,0:T(8,128)(2,1)S(1)}, u32[]{:S(2)}, u32[]{:S(2)}) %collective-permute-start.1) | collective-permute-done | bytes 393248 | tf_op jit(solution)/shard_map/ppermute | solution.py:49
  53.9 1.2 bitcast_add_fusion.1
  55.2 1.6 %collective-permute-start.2 = (bf16[64,1536]{1,0:T(8,128)(2,1)S(1)}, bf16[64,1536]{1,0:T(8,128)(2,1)S(1)}, u32[]{:S(2)}, u32[]{:S(2)}) collective-permute-start(bf16[64,1536]{1,0:T(8,128)(2,1)S(1)} %fusion.8), channel_id=1, source_target_pairs={{0,16},{8,24},{16,0},{24,8},{1,17},{9,25},{17,1},{25,9},{2,18},{10... | collective-permute-start | bytes 589832 | tf_op jit(solution)/shard_map/ppermute | solution.py:49
  56.9 1.6 %collective-permute-start.4 = (bf16[64,1536]{1,0:T(8,128)(2,1)S(1)}, bf16[64,1536]{1,0:T(8,128)(2,1)S(1)}, u32[]{:S(2)}, u32[]{:S(2)}) collective-permute-start(bf16[64,1536]{1,0:T(8,128)(2,1)S(1)} %fusion.9), channel_id=1, source_target_pairs={{0,8},{8,0},{16,24},{24,16},{1,9},{9,1},{17,25},{25,17},{2,10},{10... | collective-permute-start | bytes 589832 | tf_op jit(solution)/shard_map/ppermute | solution.py:49
  58.5 2.9 %collective-permute-done.2 = bf16[64,1536]{1,0:T(8,128)(2,1)S(1)} collective-permute-done((bf16[64,1536]{1,0:T(8,128)(2,1)S(1)}, bf16[64,1536]{1,0:T(8,128)(2,1)S(1)}, u32[]{:S(2)}, u32[]{:S(2)}) %collective-permute-start.2) | collective-permute-done | bytes 196640 | tf_op jit(solution)/shard_map/ppermute | solution.py:49
  61.4 1.4 %collective-permute-done.4 = bf16[64,1536]{1,0:T(8,128)(2,1)S(1)} collective-permute-done((bf16[64,1536]{1,0:T(8,128)(2,1)S(1)}, bf16[64,1536]{1,0:T(8,128)(2,1)S(1)}, u32[]{:S(2)}, u32[]{:S(2)}) %collective-permute-start.4) | collective-permute-done | bytes 196640 | tf_op jit(solution)/shard_map/ppermute | solution.py:49
  62.9 2.2 %fusion.5 = (bf16[64,3072]{1,0:T(8,128)(2,1)S(1)}, bf16[64,3072]{1,0:T(8,128)(2,1)}) fusion(f32[64,1536]{1,0:T(8,128)S(1)} %bitcast_add_fusion.2, f32[64,1536]{1,0:T(8,128)S(1)} %bitcast_add_fusion.3, bf16[256,3072]{1,0:T(8,128)(2,1)} %param.7, s32[]{:T(128)S(6)} %select_n.94, f32[3072]{0:T(1024)S(1)} %copy-done.1), kind=kLoop, calls=%fused_computation.9 | loop fusion | flops 2949120 | bytes 1978372 | tf_op jit(solution)/shard_map/convert_element_type | solution.py:15
  65.1 1.6 %collective-permute-start.5 = (bf16[64,1536]{1,0:T(8,128)(2,1)S(1)}, bf16[64,1536]{1,0:T(8,128)(2,1)S(1)}, u32[]{:S(2)}, u32[]{:S(2)}) collective-permute-start(bf16[64,1536]{1,0:T(8,128)(2,1)S(1)} %get-tuple-element.20), channel_id=1, source_target_pairs={{0,8},{8,0},{16,24},{24,16},{1,9},{9,1},{17,25},{25,17},{2,10},{10... | collective-permute-start | bytes 589832 | tf_op jit(solution)/shard_map/ppermute | solution.py:49
  67.1 3.7 %collective-permute-done.5 = bf16[64,1536]{1,0:T(8,128)(2,1)S(1)} collective-permute-done((bf16[64,1536]{1,0:T(8,128)(2,1)S(1)}, bf16[64,1536]{1,0:T(8,128)(2,1)S(1)}, u32[]{:S(2)}, u32[]{:S(2)}) %collective-permute-start.5) | collective-permute-done | bytes 196640 | tf_op jit(solution)/shard_map/ppermute | solution.py:49
  70.8 1.6 %collective-permute-done.7 = bf16[64,1536]{1,0:T(8,128)(2,1)S(1)} collective-permute-done((bf16[64,1536]{1,0:T(8,128)(2,1)S(1)}, bf16[64,1536]{1,0:T(8,128)(2,1)S(1)}, u32[]{:S(2)}, u32[]{:S(2)}) %collective-permute-start.7) | collective-permute-done | bytes 196640 | tf_op jit(solution)/shard_map/ppermute | solution.py:49
  73.6 6.9 %collective-permute-done.8 = bf16[2,64,1536]{2,1,0:T(8,128)(2,1)S(1)} collective-permute-done((bf16[2,64,1536]{2,1,0:T(8,128)(2,1)S(1)}, bf16[2,64,1536]{2,1,0:T(8,128)(2,1)S(1)}, u32[]{:S(2)}, u32[]{:S(2)}) %collective-permute-start.8) | collective-permute-done | bytes 393248 | tf_op jit(solution)/shard_map/ppermute | solution.py:49
  81.2 10.7 %fusion.10 = f32[256,3072]{1,0:T(8,128)} fusion(bf16[3072,3072]{1,0:T(8,128)(2,1)} %param.5, bf16[256,1536]{1,0:T(8,128)(2,1)S(1)} %bitcast.54, bf16[256,1536]{1,0:T(8,128)(2,1)S(1)} %bitcast.57), kind=kOutput, calls=%fused_computation.39 | convolution fusion | flops 4834983936 | bytes 23592960 | tf_op jit(solution)/shard_map/dot_general | solution.py:135
  91.9 1.6 %copy.17 = bf16[256,3072]{0,1:T(8,128)(2,1)} copy(bf16[256,3072]{1,0:T(8,128)(2,1)S(1)} %bitcast.61) | data formatting | bytes 3145728 | tf_op jit(solution)/shard_map/reshape | solution.py:122
  93.5 0.9 convert_reduce_fusion
  94.3 1.4 pad_maximum_fusion.g_ref
  95.7 13.5 %shard_map.75 = bf16[3072,3072]{1,0:T(8,128)(2,1)} custom-call(bf16[3072,256]{1,0:T(8,128)(2,1)} %bitcast.62, bf16[256,3072]{1,0:T(8,128)(2,1)} %pad_maximum_fusion.g_ref), custom_call_target="tpu_custom_call" | custom-call | flops 4831838208 | bytes 22020096 | tf_op jit(solution)/shard_map/pallas_call | solution.py:32
  109.2 21.7 %reduce-scatter.2.cloned.1.call-done = f32[32,3072]{1,0:T(8,128)} async-done(((f32[256,3072]{1,0:T(8,128)}), f32[32,3072]{1,0:T(8,128)}) %reduce-scatter.2.cloned.1.call-update) | async-done | bytes 393232 | tf_op jit(solution)/shard_map/reduce_scatter | solution.py:134
  130.8 1.7 %convert_element_type.66 = bf16[32,3072]{1,0:T(8,128)(2,1)} convert(f32[32,3072]{1,0:T(8,128)} %reduce-scatter.2.cloned.1.call-done) | non-fusion elementwise | flops 98304 | bytes 589824 | tf_op jit(solution)/shard_map/convert_element_type | solution.py:141
  (30 shorter events, 4.2 us)
Async XLA Ops:
  7.2 123.7 %reduce-scatter.2.cloned.1.call-start = ((), (), s32[]{:S(2)}) async-start(), calls=%async_computation.1 | async-start | bytes 3538944 | tf_op jit(solution)/shard_map/reduce_scatter | solution.py:134
  28.7 2.3 %collective-permute-start = (bf16[4,32,3072]{2,1,0:T(8,128)(2,1)S(1)}, bf16[4,32,3072]{2,1,0:T(8,128)(2,1)S(1)}, u32[]{:S(2)}, u32[]{:S(2)}) collective-permute-start(bf16[4,32,3072]{2,1,0:T(8,128)(2,1)S(1)} %bitcast.67), channel_id=1, source_target_pairs={{0,1},{1,0},{2,3},{3,2},{4,5},{5,4},{6,7},{7,6},{8,9},{9,8},{10,11... | collective-permute-start | bytes 2359304 | tf_op jit(solution)/shard_map/ppermute | solution.py:49
  40.6 1.1 copy-start
  42.6 11.4 %collective-permute-start.1 = (bf16[2,64,1536]{2,1,0:T(8,128)(2,1)}, bf16[2,64,1536]{2,1,0:T(8,128)(2,1)S(1)}, u32[]{:S(2)}, u32[]{:S(2)}) collective-permute-start(bf16[2,64,1536]{2,1,0:T(8,128)(2,1)} %fusion.7), channel_id=1, source_target_pairs={{0,8},{8,0},{16,24},{24,16},{1,9},{9,1},{17,25},{25,17},{2,10},{10... | collective-permute-start | bytes 1179656 | tf_op jit(solution)/shard_map/ppermute | solution.py:49
  44.1 12.7 %collective-permute-start.3 = (bf16[2,64,1536]{2,1,0:T(8,128)(2,1)S(1)}, bf16[2,64,1536]{2,1,0:T(8,128)(2,1)S(1)}, u32[]{:S(2)}, u32[]{:S(2)}) collective-permute-start(bf16[2,64,1536]{2,1,0:T(8,128)(2,1)S(1)} %fusion.6), channel_id=1, source_target_pairs={{0,16},{8,24},{16,0},{24,8},{1,17},{9,25},{17,1},{25,9},{2,18},{10... | collective-permute-start | bytes 1179656 | tf_op jit(solution)/shard_map/ppermute | solution.py:49
  55.2 6.2 %collective-permute-start.2 = (bf16[64,1536]{1,0:T(8,128)(2,1)S(1)}, bf16[64,1536]{1,0:T(8,128)(2,1)S(1)}, u32[]{:S(2)}, u32[]{:S(2)}) collective-permute-start(bf16[64,1536]{1,0:T(8,128)(2,1)S(1)} %fusion.8), channel_id=1, source_target_pairs={{0,16},{8,24},{16,0},{24,8},{1,17},{9,25},{17,1},{25,9},{2,18},{10... | collective-permute-start | bytes 589832 | tf_op jit(solution)/shard_map/ppermute | solution.py:49
  56.9 6.0 %copy-start.1 = (f32[3072]{0:T(1024)S(1)}, f32[3072]{0:T(1024)}, u32[]{:S(2)}) copy-start(f32[3072]{0:T(1024)} %param.6) | copy-start | bytes 36868
  56.9 5.9 %collective-permute-start.4 = (bf16[64,1536]{1,0:T(8,128)(2,1)S(1)}, bf16[64,1536]{1,0:T(8,128)(2,1)S(1)}, u32[]{:S(2)}, u32[]{:S(2)}) collective-permute-start(bf16[64,1536]{1,0:T(8,128)(2,1)S(1)} %fusion.9), channel_id=1, source_target_pairs={{0,8},{8,0},{16,24},{24,16},{1,9},{9,1},{17,25},{25,17},{2,10},{10... | collective-permute-start | bytes 589832 | tf_op jit(solution)/shard_map/ppermute | solution.py:49
  65.1 5.7 %collective-permute-start.5 = (bf16[64,1536]{1,0:T(8,128)(2,1)S(1)}, bf16[64,1536]{1,0:T(8,128)(2,1)S(1)}, u32[]{:S(2)}, u32[]{:S(2)}) collective-permute-start(bf16[64,1536]{1,0:T(8,128)(2,1)S(1)} %get-tuple-element.20), channel_id=1, source_target_pairs={{0,8},{8,0},{16,24},{24,16},{1,9},{9,1},{17,25},{25,17},{2,10},{10... | collective-permute-start | bytes 589832 | tf_op jit(solution)/shard_map/ppermute | solution.py:49
  66.6 5.7 %collective-permute-start.7 = (bf16[64,1536]{1,0:T(8,128)(2,1)S(1)}, bf16[64,1536]{1,0:T(8,128)(2,1)S(1)}, u32[]{:S(2)}, u32[]{:S(2)}) collective-permute-start(bf16[64,1536]{1,0:T(8,128)(2,1)S(1)} %get-tuple-element.21), channel_id=1, source_target_pairs={{0,16},{8,24},{16,0},{24,8},{1,17},{9,25},{17,1},{25,9},{2,18},{10... | collective-permute-start | bytes 589832 | tf_op jit(solution)/shard_map/ppermute | solution.py:49
  72.5 8.0 %collective-permute-start.8 = (bf16[2,64,1536]{2,1,0:T(8,128)(2,1)S(1)}, bf16[2,64,1536]{2,1,0:T(8,128)(2,1)S(1)}, u32[]{:S(2)}, u32[]{:S(2)}) collective-permute-start(bf16[2,64,1536]{2,1,0:T(8,128)(2,1)S(1)} %pad_maximum_fusion.3), channel_id=1, source_target_pairs={{0,8},{8,0},{16,24},{24,16},{1,9},{9,1},{17,25},{25,17},{2,10},{10... | collective-permute-start | bytes 1179656 | tf_op jit(solution)/shard_map/ppermute | solution.py:49
  73.0 7.8 %collective-permute-start.6 = (bf16[2,64,1536]{2,1,0:T(8,128)(2,1)S(1)}, bf16[2,64,1536]{2,1,0:T(8,128)(2,1)S(1)}, u32[]{:S(2)}, u32[]{:S(2)}) collective-permute-start(bf16[2,64,1536]{2,1,0:T(8,128)(2,1)S(1)} %pad_maximum_fusion.2), channel_id=1, source_target_pairs={{0,16},{8,24},{16,0},{24,8},{1,17},{9,25},{17,1},{25,9},{2,18},{10... | collective-permute-start | bytes 1179656 | tf_op jit(solution)/shard_map/ppermute | solution.py:49
Sparse Core Ops, SparseCore 0:
  92.0 38.7 reduce-scatter.1

commit v5 on v4

--- a/solution.py
+++ b/solution.py
@@ -24,7 +24,7 @@
     )
 
 
-def outer_product_sum(xt, g, block_m=512, block_n=1536):
+def outer_product_sum(xt, g, block_m=768, block_n=3072):
     m, k = xt.shape
     n = g.shape[1]
     block_m = min(block_m, m)

time: 140 us -> 140 us (level)
  waiting for transfers between devices: 49 us -> 52.1 us
  Pallas kernels: 13.5 us -> 10.4 us
    pallas_call x1, Pallas kernels: 13.5 us -> 10.4 us  [outer_product_sum(): pl.pallas_call(_outer_kernel, grid=(n // block_n, m // block_m), in_specs...]
    reduce_scatter x1, waiting for transfers between devices: 21.7 us -> 24.7 us  [body(): lax.psum_scatter(lax.dot_general(full_grad, weight, (((1,), (1,)), ((), (...]
  transfers between devices with their start and end apart: 10 -> 10, of which waited for: 9 -> 9; matrix products, arithmetic and copies ran while one was open for 4% -> 4% of each run, Pallas kernels for 10% -> 7%
where the time goes in v5:
time: 140 us; the launch traced here: 139 us
  waiting for transfers between devices  52.1 us (37%)
  blocking collectives  21.5 us (15%)
  matrix products  19.6 us (14%)
  between operations  14.2 us (10%)
  Pallas kernels  10.4 us (7%)
  starting transfers between devices  9.42 us (7%)
  other arithmetic  8.09 us (6%)
  local copies, waits for them, and re-layouts  4.04 us (3%)
    ppermute x9, waiting for transfers between devices, _swap(): return lax.ppermute(value, axis, [(i, i ^ flip) for i in range(size)])  27.3 us
    reduce_scatter x1, waiting for transfers between devices, body(): lax.psum_scatter(lax.dot_general(full_grad, weight, (((1,), (1,)), ((), (...  24.7 us
    all_gather x1, blocking collectives, col_all_gather(): mine = lax.all_gather(block, axis, axis_index_groups=groups)  21.5 us
    dot_general x1, matrix products, body(): lax.dot_general(full_grad, weight, (((1,), (1,)), ((), ())), preferred_el...  10.7 us
    pallas_call x1, Pallas kernels, outer_product_sum(): pl.pallas_call(_outer_kernel, grid=(n // block_n, m // block_m), in_specs...  10.4 us
    ppermute x9, starting transfers between devices, _swap(): return lax.ppermute(value, axis, [(i, i ^ flip) for i in range(size)])  9.38 us
    dot_general x1, matrix products, body(): partial_value = jnp.dot(local_x, weight, preferred_element_type=jnp.float32)  8.99 us
  transfers between devices with their start and end apart: 10, of which 9 were waited for; matrix products, arithmetic and copies ran while one was open for 4% of the time, Pallas kernels for 7%

profile of v5, /device:TPU:0, one launch (start us, length us, event | category | flops | bytes accessed | tf_op | source)
XLA Modules:
  0.0 139.4 jit_solution(683842275057332546)
XLA Ops:
  7.2 21.5 %all-gather = bf16[128,3072]{1,0:T(8,128)(2,1)S(1)} all-gather(bf16[32,3072]{1,0:T(8,128)(2,1)} %param.4), channel_id=2, replica_groups={{0,2,4,6},{1,3,5,7},{8,10,12,14},{9,11,13,15},{16,18,20,22},{17,19,21,2..., dimensions={0}, use_global_device_ids=true | all-gather | bytes 983040 | tf_op jit(solution)/shard_map/all_gather | solution.py:120
  28.7 2.3 %collective-permute-done = bf16[4,32,3072]{2,1,0:T(8,128)(2,1)S(1)} collective-permute-done((bf16[4,32,3072]{2,1,0:T(8,128)(2,1)S(1)}, bf16[4,32,3072]{2,1,0:T(8,128)(2,1)S(1)}, u32[]{:S(2)}, u32[]{:S(2)}) %collective-permute-start) | collective-permute-done | bytes 786464 | tf_op jit(solution)/shard_map/ppermute | solution.py:49
  31.4 9.0 %fusion.13 = f32[256,3072]{1,0:T(8,128)S(1)} fusion(bf16[256,3072]{1,0:T(8,128)(2,1)S(1)} %bitcast.60, bf16[3072,3072]{1,0:T(8,128)(2,1)} %param.5), kind=kOutput, calls=%fused_computation.42 | convolution fusion | flops 4831838208 | bytes 23592960 | tf_op jit(solution)/shard_map/dot_general | solution.py:129
  40.6 1.1 copy-done
  42.6 1.5 %collective-permute-start.1 = (bf16[2,64,1536]{2,1,0:T(8,128)(2,1)}, bf16[2,64,1536]{2,1,0:T(8,128)(2,1)S(1)}, u32[]{:S(2)}, u32[]{:S(2)}) collective-permute-start(bf16[2,64,1536]{2,1,0:T(8,128)(2,1)} %fusion.7), channel_id=1, source_target_pairs={{0,8},{8,0},{16,24},{24,16},{1,9},{9,1},{17,25},{25,17},{2,10},{10... | collective-permute-start | bytes 1179656 | tf_op jit(solution)/shard_map/ppermute | solution.py:49
  44.1 1.6 %collective-permute-start.3 = (bf16[2,64,1536]{2,1,0:T(8,128)(2,1)S(1)}, bf16[2,64,1536]{2,1,0:T(8,128)(2,1)S(1)}, u32[]{:S(2)}, u32[]{:S(2)}) collective-permute-start(bf16[2,64,1536]{2,1,0:T(8,128)(2,1)S(1)} %fusion.6), channel_id=1, source_target_pairs={{0,16},{8,24},{16,0},{24,8},{1,17},{9,25},{17,1},{25,9},{2,18},{10... | collective-permute-start | bytes 1179656 | tf_op jit(solution)/shard_map/ppermute | solution.py:49
  45.7 8.2 %collective-permute-done.1 = bf16[2,64,1536]{2,1,0:T(8,128)(2,1)S(1)} collective-permute-done((bf16[2,64,1536]{2,1,0:T(8,128)(2,1)}, bf16[2,64,1536]{2,1,0:T(8,128)(2,1)S(1)}, u32[]{:S(2)}, u32[]{:S(2)}) %collective-permute-start.1) | collective-permute-done | bytes 393248 | tf_op jit(solution)/shard_map/ppermute | solution.py:49
  53.9 1.2 bitcast_add_fusion.1
  55.2 1.6 %collective-permute-start.2 = (bf16[64,1536]{1,0:T(8,128)(2,1)S(1)}, bf16[64,1536]{1,0:T(8,128)(2,1)S(1)}, u32[]{:S(2)}, u32[]{:S(2)}) collective-permute-start(bf16[64,1536]{1,0:T(8,128)(2,1)S(1)} %fusion.8), channel_id=1, source_target_pairs={{0,16},{8,24},{16,0},{24,8},{1,17},{9,25},{17,1},{25,9},{2,18},{10... | collective-permute-start | bytes 589832 | tf_op jit(solution)/shard_map/ppermute | solution.py:49
  56.9 1.6 %collective-permute-start.4 = (bf16[64,1536]{1,0:T(8,128)(2,1)S(1)}, bf16[64,1536]{1,0:T(8,128)(2,1)S(1)}, u32[]{:S(2)}, u32[]{:S(2)}) collective-permute-start(bf16[64,1536]{1,0:T(8,128)(2,1)S(1)} %fusion.9), channel_id=1, source_target_pairs={{0,8},{8,0},{16,24},{24,16},{1,9},{9,1},{17,25},{25,17},{2,10},{10... | collective-permute-start | bytes 589832 | tf_op jit(solution)/shard_map/ppermute | solution.py:49
  58.5 2.9 %collective-permute-done.2 = bf16[64,1536]{1,0:T(8,128)(2,1)S(1)} collective-permute-done((bf16[64,1536]{1,0:T(8,128)(2,1)S(1)}, bf16[64,1536]{1,0:T(8,128)(2,1)S(1)}, u32[]{:S(2)}, u32[]{:S(2)}) %collective-permute-start.2) | collective-permute-done | bytes 196640 | tf_op jit(solution)/shard_map/ppermute | solution.py:49
  61.4 1.4 %collective-permute-done.4 = bf16[64,1536]{1,0:T(8,128)(2,1)S(1)} collective-permute-done((bf16[64,1536]{1,0:T(8,128)(2,1)S(1)}, bf16[64,1536]{1,0:T(8,128)(2,1)S(1)}, u32[]{:S(2)}, u32[]{:S(2)}) %collective-permute-start.4) | collective-permute-done | bytes 196640 | tf_op jit(solution)/shard_map/ppermute | solution.py:49
  62.9 2.2 %fusion.5 = (bf16[64,3072]{1,0:T(8,128)(2,1)S(1)}, bf16[64,3072]{1,0:T(8,128)(2,1)}) fusion(f32[64,1536]{1,0:T(8,128)S(1)} %bitcast_add_fusion.2, f32[64,1536]{1,0:T(8,128)S(1)} %bitcast_add_fusion.3, bf16[256,3072]{1,0:T(8,128)(2,1)} %param.7, s32[]{:T(128)S(6)} %select_n.94, f32[3072]{0:T(1024)S(1)} %copy-done.1), kind=kLoop, calls=%fused_computation.9 | loop fusion | flops 2949120 | bytes 1978372 | tf_op jit(solution)/shard_map/convert_element_type | solution.py:15
  65.1 1.6 %collective-permute-start.5 = (bf16[64,1536]{1,0:T(8,128)(2,1)S(1)}, bf16[64,1536]{1,0:T(8,128)(2,1)S(1)}, u32[]{:S(2)}, u32[]{:S(2)}) collective-permute-start(bf16[64,1536]{1,0:T(8,128)(2,1)S(1)} %get-tuple-element.20), channel_id=1, source_target_pairs={{0,8},{8,0},{16,24},{24,16},{1,9},{9,1},{17,25},{25,17},{2,10},{10... | collective-permute-start | bytes 589832 | tf_op jit(solution)/shard_map/ppermute | solution.py:49
  67.1 3.7 %collective-permute-done.5 = bf16[64,1536]{1,0:T(8,128)(2,1)S(1)} collective-permute-done((bf16[64,1536]{1,0:T(8,128)(2,1)S(1)}, bf16[64,1536]{1,0:T(8,128)(2,1)S(1)}, u32[]{:S(2)}, u32[]{:S(2)}) %collective-permute-start.5) | collective-permute-done | bytes 196640 | tf_op jit(solution)/shard_map/ppermute | solution.py:49
  70.8 1.6 %collective-permute-done.7 = bf16[64,1536]{1,0:T(8,128)(2,1)S(1)} collective-permute-done((bf16[64,1536]{1,0:T(8,128)(2,1)S(1)}, bf16[64,1536]{1,0:T(8,128)(2,1)S(1)}, u32[]{:S(2)}, u32[]{:S(2)}) %collective-permute-start.7) | collective-permute-done | bytes 196640 | tf_op jit(solution)/shard_map/ppermute | solution.py:49
  73.6 6.9 %collective-permute-done.8 = bf16[2,64,1536]{2,1,0:T(8,128)(2,1)S(1)} collective-permute-done((bf16[2,64,1536]{2,1,0:T(8,128)(2,1)S(1)}, bf16[2,64,1536]{2,1,0:T(8,128)(2,1)S(1)}, u32[]{:S(2)}, u32[]{:S(2)}) %collective-permute-start.8) | collective-permute-done | bytes 393248 | tf_op jit(solution)/shard_map/ppermute | solution.py:49
  81.2 10.7 %fusion.10 = f32[256,3072]{1,0:T(8,128)} fusion(bf16[3072,3072]{1,0:T(8,128)(2,1)} %param.5, bf16[256,1536]{1,0:T(8,128)(2,1)S(1)} %bitcast.54, bf16[256,1536]{1,0:T(8,128)(2,1)S(1)} %bitcast.57), kind=kOutput, calls=%fused_computation.39 | convolution fusion | flops 4834983936 | bytes 23592960 | tf_op jit(solution)/shard_map/dot_general | solution.py:135
  91.9 1.6 %copy.17 = bf16[256,3072]{0,1:T(8,128)(2,1)} copy(bf16[256,3072]{1,0:T(8,128)(2,1)S(1)} %bitcast.61) | data formatting | bytes 3145728 | tf_op jit(solution)/shard_map/reshape | solution.py:122
  93.5 0.9 convert_reduce_fusion
  94.3 1.4 pad_maximum_fusion.g_ref
  95.7 10.4 %shard_map.75 = bf16[3072,3072]{1,0:T(8,128)(2,1)} custom-call(bf16[3072,256]{1,0:T(8,128)(2,1)} %bitcast.62, bf16[256,3072]{1,0:T(8,128)(2,1)} %pad_maximum_fusion.g_ref), custom_call_target="tpu_custom_call" | custom-call | flops 4831838208 | bytes 22020096 | tf_op jit(solution)/shard_map/pallas_call | solution.py:32
  106.1 24.7 %reduce-scatter.2.cloned.1.call-done = f32[32,3072]{1,0:T(8,128)} async-done(((f32[256,3072]{1,0:T(8,128)}), f32[32,3072]{1,0:T(8,128)}) %reduce-scatter.2.cloned.1.call-update) | async-done | bytes 393232 | tf_op jit(solution)/shard_map/reduce_scatter | solution.py:134
  130.8 1.7 %convert_element_type.66 = bf16[32,3072]{1,0:T(8,128)(2,1)} convert(f32[32,3072]{1,0:T(8,128)} %reduce-scatter.2.cloned.1.call-done) | non-fusion elementwise | flops 98304 | bytes 589824 | tf_op jit(solution)/shard_map/convert_element_type | solution.py:141
  (30 shorter events, 4.2 us)
Async XLA Ops:
  7.2 123.7 %reduce-scatter.2.cloned.1.call-start = ((), (), s32[]{:S(2)}) async-start(), calls=%async_computation.1 | async-start | bytes 3538944 | tf_op jit(solution)/shard_map/reduce_scatter | solution.py:134
  28.7 2.3 %collective-permute-start = (bf16[4,32,3072]{2,1,0:T(8,128)(2,1)S(1)}, bf16[4,32,3072]{2,1,0:T(8,128)(2,1)S(1)}, u32[]{:S(2)}, u32[]{:S(2)}) collective-permute-start(bf16[4,32,3072]{2,1,0:T(8,128)(2,1)S(1)} %bitcast.67), channel_id=1, source_target_pairs={{0,1},{1,0},{2,3},{3,2},{4,5},{5,4},{6,7},{7,6},{8,9},{9,8},{10,11... | collective-permute-start | bytes 2359304 | tf_op jit(solution)/shard_map/ppermute | solution.py:49
  40.6 1.1 copy-start
  42.6 11.4 %collective-permute-start.1 = (bf16[2,64,1536]{2,1,0:T(8,128)(2,1)}, bf16[2,64,1536]{2,1,0:T(8,128)(2,1)S(1)}, u32[]{:S(2)}, u32[]{:S(2)}) collective-permute-start(bf16[2,64,1536]{2,1,0:T(8,128)(2,1)} %fusion.7), channel_id=1, source_target_pairs={{0,8},{8,0},{16,24},{24,16},{1,9},{9,1},{17,25},{25,17},{2,10},{10... | collective-permute-start | bytes 1179656 | tf_op jit(solution)/shard_map/ppermute | solution.py:49
  44.1 12.7 %collective-permute-start.3 = (bf16[2,64,1536]{2,1,0:T(8,128)(2,1)S(1)}, bf16[2,64,1536]{2,1,0:T(8,128)(2,1)S(1)}, u32[]{:S(2)}, u32[]{:S(2)}) collective-permute-start(bf16[2,64,1536]{2,1,0:T(8,128)(2,1)S(1)} %fusion.6), channel_id=1, source_target_pairs={{0,16},{8,24},{16,0},{24,8},{1,17},{9,25},{17,1},{25,9},{2,18},{10... | collective-permute-start | bytes 1179656 | tf_op jit(solution)/shard_map/ppermute | solution.py:49
  55.2 6.2 %collective-permute-start.2 = (bf16[64,1536]{1,0:T(8,128)(2,1)S(1)}, bf16[64,1536]{1,0:T(8,128)(2,1)S(1)}, u32[]{:S(2)}, u32[]{:S(2)}) collective-permute-start(bf16[64,1536]{1,0:T(8,128)(2,1)S(1)} %fusion.8), channel_id=1, source_target_pairs={{0,16},{8,24},{16,0},{24,8},{1,17},{9,25},{17,1},{25,9},{2,18},{10... | collective-permute-start | bytes 589832 | tf_op jit(solution)/shard_map/ppermute | solution.py:49
  56.9 6.0 %copy-start.1 = (f32[3072]{0:T(1024)S(1)}, f32[3072]{0:T(1024)}, u32[]{:S(2)}) copy-start(f32[3072]{0:T(1024)} %param.6) | copy-start | bytes 36868
  56.9 5.9 %collective-permute-start.4 = (bf16[64,1536]{1,0:T(8,128)(2,1)S(1)}, bf16[64,1536]{1,0:T(8,128)(2,1)S(1)}, u32[]{:S(2)}, u32[]{:S(2)}) collective-permute-start(bf16[64,1536]{1,0:T(8,128)(2,1)S(1)} %fusion.9), channel_id=1, source_target_pairs={{0,8},{8,0},{16,24},{24,16},{1,9},{9,1},{17,25},{25,17},{2,10},{10... | collective-permute-start | bytes 589832 | tf_op jit(solution)/shard_map/ppermute | solution.py:49
  65.1 5.7 %collective-permute-start.5 = (bf16[64,1536]{1,0:T(8,128)(2,1)S(1)}, bf16[64,1536]{1,0:T(8,128)(2,1)S(1)}, u32[]{:S(2)}, u32[]{:S(2)}) collective-permute-start(bf16[64,1536]{1,0:T(8,128)(2,1)S(1)} %get-tuple-element.20), channel_id=1, source_target_pairs={{0,8},{8,0},{16,24},{24,16},{1,9},{9,1},{17,25},{25,17},{2,10},{10... | collective-permute-start | bytes 589832 | tf_op jit(solution)/shard_map/ppermute | solution.py:49
  66.6 5.7 %collective-permute-start.7 = (bf16[64,1536]{1,0:T(8,128)(2,1)S(1)}, bf16[64,1536]{1,0:T(8,128)(2,1)S(1)}, u32[]{:S(2)}, u32[]{:S(2)}) collective-permute-start(bf16[64,1536]{1,0:T(8,128)(2,1)S(1)} %get-tuple-element.21), channel_id=1, source_target_pairs={{0,16},{8,24},{16,0},{24,8},{1,17},{9,25},{17,1},{25,9},{2,18},{10... | collective-permute-start | bytes 589832 | tf_op jit(solution)/shard_map/ppermute | solution.py:49
  72.5 8.0 %collective-permute-start.8 = (bf16[2,64,1536]{2,1,0:T(8,128)(2,1)S(1)}, bf16[2,64,1536]{2,1,0:T(8,128)(2,1)S(1)}, u32[]{:S(2)}, u32[]{:S(2)}) collective-permute-start(bf16[2,64,1536]{2,1,0:T(8,128)(2,1)S(1)} %pad_maximum_fusion.3), channel_id=1, source_target_pairs={{0,8},{8,0},{16,24},{24,16},{1,9},{9,1},{17,25},{25,17},{2,10},{10... | collective-permute-start | bytes 1179656 | tf_op jit(solution)/shard_map/ppermute | solution.py:49
  73.0 7.8 %collective-permute-start.6 = (bf16[2,64,1536]{2,1,0:T(8,128)(2,1)S(1)}, bf16[2,64,1536]{2,1,0:T(8,128)(2,1)S(1)}, u32[]{:S(2)}, u32[]{:S(2)}) collective-permute-start(bf16[2,64,1536]{2,1,0:T(8,128)(2,1)S(1)} %pad_maximum_fusion.2), channel_id=1, source_target_pairs={{0,16},{8,24},{16,0},{24,8},{1,17},{9,25},{17,1},{25,9},{2,18},{10... | collective-permute-start | bytes 1179656 | tf_op jit(solution)/shard_map/ppermute | solution.py:49
Sparse Core Ops, SparseCore 0:
  92.0 38.7 reduce-scatter.1

commit v6 on v5

--- a/solution.py
+++ b/solution.py
@@ -122,6 +122,24 @@
     return jnp.swapaxes(both, 0, 1).reshape(n * block.shape[0], block.shape[1])
 
 
+def col_reduce_scatter(partial, axis="col"):
+    n = lax.axis_size(axis)
+    if n % 2:
+        return lax.psum_scatter(partial, axis, scatter_dimension=0, tiled=True)
+    m = partial.shape[0] // n
+    k = lax.axis_index(axis) % 2
+    by_core = jnp.swapaxes(partial.reshape(n // 2, 2, m, partial.shape[1]), 0, 1)
+    chip = _pick(k, by_core) + _swap(_pick(1 - k, by_core), axis, 1)
+    groups = [list(range(j, n, 2)) for j in range(2)]
+    return lax.psum_scatter(
+        chip.reshape(n // 2 * m, partial.shape[1]),
+        axis,
+        scatter_dimension=0,
+        tiled=True,
+        axis_index_groups=groups,
+    )
+
+
 def body(tokens, weight, bias, cotangent):
     local_x = col_all_gather(tokens)
     my_rows = local_x.shape[0] // lax.axis_size("row")
@@ -131,13 +149,10 @@
     my_cot = lax.dynamic_slice_in_dim(cotangent, first_row, my_rows, 0)
     hidden, my_grad = activate(preact, my_cot)
     full_grad = row_all_gather(my_grad)
-    grad_tokens = lax.psum_scatter(
+    grad_tokens = col_reduce_scatter(
         lax.dot_general(
             full_grad, weight, (((1,), (1,)), ((), ())), preferred_element_type=jnp.float32
-        ),
-        "col",
-        scatter_dimension=0,
-        tiled=True,
+        )
     ).astype(jnp.bfloat16)
     grad_weight = outer_product_sum(local_x.T, full_grad)
     grad_bias = jnp.sum(full_grad.astype(jnp.float32), axis=0)

time: 140 us -> 143 us (1.021)
  other arithmetic: 8.09 us -> 12.3 us
  local copies, waits for them, and re-layouts: 4.04 us -> 6.22 us
  matrix products: 19.6 us -> 18 us
    reduce_scatter x1, waiting for transfers between devices: 24.7 us -> 19.6 us  [col_reduce_scatter(): lax.psum_scatter(chip.reshape(n // 2 * m, partial.shape[1]), axis, scatte...]
    ppermute x9 -> x10, waiting for transfers between devices: 27.3 us -> 31.2 us  [_swap(): return lax.ppermute(value, axis, [(i, i ^ flip) for i in range(size)])]
    add x0 -> x1, other arithmetic: none -> 3.25 us  [col_reduce_scatter(): chip = _pick(k, by_core) + _swap(_pick(1 - k, by_core), axis, 1)]
    dot_general x1, matrix products: 10.7 us -> 9.03 us  [body(): lax.dot_general(full_grad, weight, (((1,), (1,)), ((), ())), preferred_el...]
    ppermute x9 -> x10, starting transfers between devices: 9.38 us -> 9.38 us  [_swap(): return lax.ppermute(value, axis, [(i, i ^ flip) for i in range(size)])]
  transfers between devices with their start and end apart: 10 -> 11, of which waited for: 9 -> 10; matrix products, arithmetic and copies ran while one was open for 4% -> 4% of each run, Pallas kernels for 7% -> 7%
where the time goes in v6:
time: 143 us
  waiting for transfers between devices  50.8 us (36%)
  blocking collectives  21.5 us (15%)
  matrix products  18 us (13%)
  between operations  14.2 us (10%)
  other arithmetic  12.3 us (9%)
  Pallas kernels  10.5 us (7%)
  starting transfers between devices  9.42 us (7%)
  local copies, waits for them, and re-layouts  6.22 us (4%)
    ppermute x10, waiting for transfers between devices, _swap(): return lax.ppermute(value, axis, [(i, i ^ flip) for i in range(size)])  31.2 us
    all_gather x1, blocking collectives, col_all_gather(): mine = lax.all_gather(block, axis, axis_index_groups=groups)  21.5 us
    reduce_scatter x1, waiting for transfers between devices, col_reduce_scatter(): lax.psum_scatter(chip.reshape(n // 2 * m, partial.shape[1]), axis, scatte...  19.6 us
    pallas_call x1, Pallas kernels, outer_product_sum(): pl.pallas_call(_outer_kernel, grid=(n // block_n, m // block_m), in_specs...  10.5 us
    ppermute x10, starting transfers between devices, _swap(): return lax.ppermute(value, axis, [(i, i ^ flip) for i in range(size)])  9.38 us
    dot_general x1, matrix products, body(): lax.dot_general(full_grad, weight, (((1,), (1,)), ((), ())), preferred_el...  9.03 us
    dot_general x1, matrix products, body(): partial_value = jnp.dot(local_x, weight, preferred_element_type=jnp.float32)  8.99 us
    add x1, other arithmetic, col_reduce_scatter(): chip = _pick(k, by_core) + _swap(_pick(1 - k, by_core), axis, 1)  3.25 us
  transfers between devices with their start and end apart: 11, of which 10 were waited for; matrix products, arithmetic and copies ran while one was open for 4% of the time, Pallas kernels for 7%

profile of v6, /device:TPU:0, one launch (start us, length us, event | category | flops | bytes accessed | tf_op | source)
XLA Modules:
  0.0 143.0 jit_solution(2338238895994984887)
XLA Ops:
  7.2 21.5 %all-gather = bf16[128,3072]{1,0:T(8,128)(2,1)S(1)} all-gather(bf16[32,3072]{1,0:T(8,128)(2,1)} %param.4), channel_id=2, replica_groups={{0,2,4,6},{1,3,5,7},{8,10,12,14},{9,11,13,15},{16,18,20,22},{17,19,21,2..., dimensions={0}, use_global_device_ids=true | all-gather | bytes 983040 | tf_op jit(solution)/shard_map/all_gather | solution.py:120
  28.7 2.3 %collective-permute-done = bf16[4,32,3072]{2,1,0:T(8,128)(2,1)S(1)} collective-permute-done((bf16[4,32,3072]{2,1,0:T(8,128)(2,1)S(1)}, bf16[4,32,3072]{2,1,0:T(8,128)(2,1)S(1)}, u32[]{:S(2)}, u32[]{:S(2)}) %collective-permute-start) | collective-permute-done | bytes 786464 | tf_op jit(solution)/shard_map/ppermute | solution.py:49
  31.4 9.0 %fusion.13 = f32[256,3072]{1,0:T(8,128)S(1)} fusion(bf16[256,3072]{1,0:T(8,128)(2,1)S(1)} %bitcast.66, bf16[3072,3072]{1,0:T(8,128)(2,1)} %param.5), kind=kOutput, calls=%fused_computation.44 | convolution fusion | flops 4831838208 | bytes 23592960 | tf_op jit(solution)/shard_map/dot_general | solution.py:147
  42.6 1.5 %collective-permute-start.1 = (bf16[2,64,1536]{2,1,0:T(8,128)(2,1)}, bf16[2,64,1536]{2,1,0:T(8,128)(2,1)S(1)}, u32[]{:S(2)}, u32[]{:S(2)}) collective-permute-start(bf16[2,64,1536]{2,1,0:T(8,128)(2,1)} %fusion.7), channel_id=1, source_target_pairs={{0,8},{8,0},{16,24},{24,16},{1,9},{9,1},{17,25},{25,17},{2,10},{10... | collective-permute-start | bytes 1179656 | tf_op jit(solution)/shard_map/ppermute | solution.py:49
  44.1 1.6 %collective-permute-start.3 = (bf16[2,64,1536]{2,1,0:T(8,128)(2,1)S(1)}, bf16[2,64,1536]{2,1,0:T(8,128)(2,1)S(1)}, u32[]{:S(2)}, u32[]{:S(2)}) collective-permute-start(bf16[2,64,1536]{2,1,0:T(8,128)(2,1)S(1)} %fusion.6), channel_id=1, source_target_pairs={{0,16},{8,24},{16,0},{24,8},{1,17},{9,25},{17,1},{25,9},{2,18},{10... | collective-permute-start | bytes 1179656 | tf_op jit(solution)/shard_map/ppermute | solution.py:49
  45.7 8.2 %collective-permute-done.1 = bf16[2,64,1536]{2,1,0:T(8,128)(2,1)S(1)} collective-permute-done((bf16[2,64,1536]{2,1,0:T(8,128)(2,1)}, bf16[2,64,1536]{2,1,0:T(8,128)(2,1)S(1)}, u32[]{:S(2)}, u32[]{:S(2)}) %collective-permute-start.1) | collective-permute-done | bytes 393248 | tf_op jit(solution)/shard_map/ppermute | solution.py:49
  55.2 1.6 %collective-permute-start.2 = (bf16[64,1536]{1,0:T(8,128)(2,1)S(1)}, bf16[64,1536]{1,0:T(8,128)(2,1)S(1)}, u32[]{:S(2)}, u32[]{:S(2)}) collective-permute-start(bf16[64,1536]{1,0:T(8,128)(2,1)S(1)} %fusion.8), channel_id=1, source_target_pairs={{0,16},{8,24},{16,0},{24,8},{1,17},{9,25},{17,1},{25,9},{2,18},{10... | collective-permute-start | bytes 589832 | tf_op jit(solution)/shard_map/ppermute | solution.py:49
  56.9 1.6 %collective-permute-start.4 = (bf16[64,1536]{1,0:T(8,128)(2,1)S(1)}, bf16[64,1536]{1,0:T(8,128)(2,1)S(1)}, u32[]{:S(2)}, u32[]{:S(2)}) collective-permute-start(bf16[64,1536]{1,0:T(8,128)(2,1)S(1)} %fusion.9), channel_id=1, source_target_pairs={{0,8},{8,0},{16,24},{24,16},{1,9},{9,1},{17,25},{25,17},{2,10},{10... | collective-permute-start | bytes 589832 | tf_op jit(solution)/shard_map/ppermute | solution.py:49
  58.5 2.9 %collective-permute-done.2 = bf16[64,1536]{1,0:T(8,128)(2,1)S(1)} collective-permute-done((bf16[64,1536]{1,0:T(8,128)(2,1)S(1)}, bf16[64,1536]{1,0:T(8,128)(2,1)S(1)}, u32[]{:S(2)}, u32[]{:S(2)}) %collective-permute-start.2) | collective-permute-done | bytes 196640 | tf_op jit(solution)/shard_map/ppermute | solution.py:49
  61.4 1.4 collective-permute-done.4
  62.9 2.2 %fusion.5 = (bf16[64,3072]{1,0:T(8,128)(2,1)S(1)}, bf16[64,3072]{1,0:T(8,128)(2,1)}) fusion(f32[64,1536]{1,0:T(8,128)S(1)} %bitcast_add_fusion.3, f32[64,1536]{1,0:T(8,128)S(1)} %bitcast_add_fusion.4, bf16[256,3072]{1,0:T(8,128)(2,1)} %param.7, s32[]{:T(128)S(6)} %select_n.103, f32[3072]{0:T(1024)S(1)} %copy-done.2), kind=kLoop, calls=%fused_computation.11 | loop fusion | flops 2949120 | bytes 1978372 | tf_op jit(solution)/shard_map/convert_element_type | solution.py:15
  65.1 1.6 %collective-permute-start.5 = (bf16[64,1536]{1,0:T(8,128)(2,1)S(1)}, bf16[64,1536]{1,0:T(8,128)(2,1)S(1)}, u32[]{:S(2)}, u32[]{:S(2)}) collective-permute-start(bf16[64,1536]{1,0:T(8,128)(2,1)S(1)} %get-tuple-element.20), channel_id=1, source_target_pairs={{0,8},{8,0},{16,24},{24,16},{1,9},{9,1},{17,25},{25,17},{2,10},{10... | collective-permute-start | bytes 589832 | tf_op jit(solution)/shard_map/ppermute | solution.py:49
  67.1 3.7 %collective-permute-done.5 = bf16[64,1536]{1,0:T(8,128)(2,1)S(1)} collective-permute-done((bf16[64,1536]{1,0:T(8,128)(2,1)S(1)}, bf16[64,1536]{1,0:T(8,128)(2,1)S(1)}, u32[]{:S(2)}, u32[]{:S(2)}) %collective-permute-start.5) | collective-permute-done | bytes 196640 | tf_op jit(solution)/shard_map/ppermute | solution.py:49
  70.8 1.6 %collective-permute-done.7 = bf16[64,1536]{1,0:T(8,128)(2,1)S(1)} collective-permute-done((bf16[64,1536]{1,0:T(8,128)(2,1)S(1)}, bf16[64,1536]{1,0:T(8,128)(2,1)S(1)}, u32[]{:S(2)}, u32[]{:S(2)}) %collective-permute-start.7) | collective-permute-done | bytes 196640 | tf_op jit(solution)/shard_map/ppermute | solution.py:49
  73.6 6.9 %collective-permute-done.8 = bf16[2,64,1536]{2,1,0:T(8,128)(2,1)S(1)} collective-permute-done((bf16[2,64,1536]{2,1,0:T(8,128)(2,1)S(1)}, bf16[2,64,1536]{2,1,0:T(8,128)(2,1)S(1)}, u32[]{:S(2)}, u32[]{:S(2)}) %collective-permute-start.8) | collective-permute-done | bytes 393248 | tf_op jit(solution)/shard_map/ppermute | solution.py:49
  82.3 9.0 %fusion.10 = f32[256,3072]{1,0:T(8,128)S(1)} fusion(bf16[3072,3072]{1,0:T(8,128)(2,1)} %param.5, bf16[256,1536]{1,0:T(8,128)(2,1)S(1)} %bitcast.60, bf16[256,1536]{1,0:T(8,128)(2,1)S(1)} %bitcast.63), kind=kOutput, calls=%fused_computation.41 | convolution fusion | flops 4834983936 | bytes 23592960 | tf_op jit(solution)/shard_map/dot_general | solution.py:153
  91.4 1.4 dynamic-slice_bitcast_fusion
  93.5 3.7 %collective-permute-done.9 = f32[4,32,3072]{2,1,0:T(8,128)} collective-permute-done((f32[4,32,3072]{2,1,0:T(8,128)}, f32[4,32,3072]{2,1,0:T(8,128)}, u32[]{:S(2)}, u32[]{:S(2)}) %collective-permute-start.9) | collective-permute-done | bytes 1572896 | tf_op jit(solution)/shard_map/ppermute | solution.py:49
  97.3 3.3 %bitcast_add_fusion = f32[4,32,3072]{2,1,0:T(8,128)} fusion(f32[4,32,3072]{2,1,0:T(8,128)} %collective-permute-done.9, f32[4,2,32,3072]{3,2,1,0:T(8,128)} %bitcast.75, s32[]{:T(128)S(6)} %select_n.114), kind=kLoop, calls=%fused_computation.3 | loop fusion | flops 393216 | bytes 4718596 | tf_op jit(solution)/shard_map/add | solution.py:132
  100.6 1.6 %copy.17 = bf16[256,3072]{0,1:T(8,128)(2,1)} copy(bf16[256,3072]{1,0:T(8,128)(2,1)S(1)} %bitcast.67) | data formatting | bytes 3145728 | tf_op jit(solution)/shard_map/reshape | solution.py:122
  103.0 1.4 pad_maximum_fusion.g_ref
  104.4 10.5 %shard_map.75 = bf16[3072,3072]{1,0:T(8,128)(2,1)} custom-call(bf16[3072,256]{1,0:T(8,128)(2,1)} %bitcast.69, bf16[256,3072]{1,0:T(8,128)(2,1)} %pad_maximum_fusion.g_ref), custom_call_target="tpu_custom_call" | custom-call | flops 4831838208 | bytes 22020096 | tf_op jit(solution)/shard_map/pallas_call | solution.py:32
  114.8 19.6 %reduce-scatter.2.cloned.1.call-done = f32[32,3072]{1,0:T(8,128)} async-done(((f32[128,3072]{1,0:T(8,128)}), f32[32,3072]{1,0:T(8,128)}) %reduce-scatter.2.cloned.1.call-update) | async-done | bytes 393232 | tf_op jit(solution)/shard_map/reduce_scatter | solution.py:134
  134.5 1.7 %convert_element_type.66 = bf16[32,3072]{1,0:T(8,128)(2,1)} convert(f32[32,3072]{1,0:T(8,128)} %reduce-scatter.2.cloned.1.call-done) | non-fusion elementwise | flops 98304 | bytes 589824 | tf_op jit(solution)/shard_map/convert_element_type | solution.py:156
  (36 shorter events, 9.3 us)
Async XLA Ops:
  7.2 127.3 %reduce-scatter.2.cloned.1.call-start = ((), (), s32[]{:S(2)}) async-start(), calls=%async_computation.1 | async-start | bytes 1966080 | tf_op jit(solution)/shard_map/reduce_scatter | solution.py:134
  28.7 2.3 %collective-permute-start = (bf16[4,32,3072]{2,1,0:T(8,128)(2,1)S(1)}, bf16[4,32,3072]{2,1,0:T(8,128)(2,1)S(1)}, u32[]{:S(2)}, u32[]{:S(2)}) collective-permute-start(bf16[4,32,3072]{2,1,0:T(8,128)(2,1)S(1)} %bitcast.76), channel_id=1, source_target_pairs={{0,1},{1,0},{2,3},{3,2},{4,5},{5,4},{6,7},{7,6},{8,9},{9,8},{10,11... | collective-permute-start | bytes 2359304 | tf_op jit(solution)/shard_map/ppermute | solution.py:49
  40.6 1.1 copy-start
  42.6 11.4 %collective-permute-start.1 = (bf16[2,64,1536]{2,1,0:T(8,128)(2,1)}, bf16[2,64,1536]{2,1,0:T(8,128)(2,1)S(1)}, u32[]{:S(2)}, u32[]{:S(2)}) collective-permute-start(bf16[2,64,1536]{2,1,0:T(8,128)(2,1)} %fusion.7), channel_id=1, source_target_pairs={{0,8},{8,0},{16,24},{24,16},{1,9},{9,1},{17,25},{25,17},{2,10},{10... | collective-permute-start | bytes 1179656 | tf_op jit(solution)/shard_map/ppermute | solution.py:49
  44.1 12.7 %collective-permute-start.3 = (bf16[2,64,1536]{2,1,0:T(8,128)(2,1)S(1)}, bf16[2,64,1536]{2,1,0:T(8,128)(2,1)S(1)}, u32[]{:S(2)}, u32[]{:S(2)}) collective-permute-start(bf16[2,64,1536]{2,1,0:T(8,128)(2,1)S(1)} %fusion.6), channel_id=1, source_target_pairs={{0,16},{8,24},{16,0},{24,8},{1,17},{9,25},{17,1},{25,9},{2,18},{10... | collective-permute-start | bytes 1179656 | tf_op jit(solution)/shard_map/ppermute | solution.py:49
  55.2 6.2 %collective-permute-start.2 = (bf16[64,1536]{1,0:T(8,128)(2,1)S(1)}, bf16[64,1536]{1,0:T(8,128)(2,1)S(1)}, u32[]{:S(2)}, u32[]{:S(2)}) collective-permute-start(bf16[64,1536]{1,0:T(8,128)(2,1)S(1)} %fusion.8), channel_id=1, source_target_pairs={{0,16},{8,24},{16,0},{24,8},{1,17},{9,25},{17,1},{25,9},{2,18},{10... | collective-permute-start | bytes 589832 | tf_op jit(solution)/shard_map/ppermute | solution.py:49
  56.9 6.0 %copy-start.2 = (f32[3072]{0:T(1024)S(1)}, f32[3072]{0:T(1024)}, u32[]{:S(2)}) copy-start(f32[3072]{0:T(1024)} %param.6) | copy-start | bytes 36868
  56.9 5.9 %collective-permute-start.4 = (bf16[64,1536]{1,0:T(8,128)(2,1)S(1)}, bf16[64,1536]{1,0:T(8,128)(2,1)S(1)}, u32[]{:S(2)}, u32[]{:S(2)}) collective-permute-start(bf16[64,1536]{1,0:T(8,128)(2,1)S(1)} %fusion.9), channel_id=1, source_target_pairs={{0,8},{8,0},{16,24},{24,16},{1,9},{9,1},{17,25},{25,17},{2,10},{10... | collective-permute-start | bytes 589832 | tf_op jit(solution)/shard_map/ppermute | solution.py:49
  65.1 5.7 %collective-permute-start.5 = (bf16[64,1536]{1,0:T(8,128)(2,1)S(1)}, bf16[64,1536]{1,0:T(8,128)(2,1)S(1)}, u32[]{:S(2)}, u32[]{:S(2)}) collective-permute-start(bf16[64,1536]{1,0:T(8,128)(2,1)S(1)} %get-tuple-element.20), channel_id=1, source_target_pairs={{0,8},{8,0},{16,24},{24,16},{1,9},{9,1},{17,25},{25,17},{2,10},{10... | collective-permute-start | bytes 589832 | tf_op jit(solution)/shard_map/ppermute | solution.py:49
  66.6 5.7 %collective-permute-start.7 = (bf16[64,1536]{1,0:T(8,128)(2,1)S(1)}, bf16[64,1536]{1,0:T(8,128)(2,1)S(1)}, u32[]{:S(2)}, u32[]{:S(2)}) collective-permute-start(bf16[64,1536]{1,0:T(8,128)(2,1)S(1)} %get-tuple-element.21), channel_id=1, source_target_pairs={{0,16},{8,24},{16,0},{24,8},{1,17},{9,25},{17,1},{25,9},{2,18},{10... | collective-permute-start | bytes 589832 | tf_op jit(solution)/shard_map/ppermute | solution.py:49
  72.5 8.0 %collective-permute-start.8 = (bf16[2,64,1536]{2,1,0:T(8,128)(2,1)S(1)}, bf16[2,64,1536]{2,1,0:T(8,128)(2,1)S(1)}, u32[]{:S(2)}, u32[]{:S(2)}) collective-permute-start(bf16[2,64,1536]{2,1,0:T(8,128)(2,1)S(1)} %pad_maximum_fusion.3), channel_id=1, source_target_pairs={{0,8},{8,0},{16,24},{24,16},{1,9},{9,1},{17,25},{25,17},{2,10},{10... | collective-permute-start | bytes 1179656 | tf_op jit(solution)/shard_map/ppermute | solution.py:49
  73.0 7.9 %collective-permute-start.6 = (bf16[2,64,1536]{2,1,0:T(8,128)(2,1)S(1)}, bf16[2,64,1536]{2,1,0:T(8,128)(2,1)}, u32[]{:S(2)}, u32[]{:S(2)}) collective-permute-start(bf16[2,64,1536]{2,1,0:T(8,128)(2,1)S(1)} %pad_maximum_fusion.2), channel_id=1, source_target_pairs={{0,16},{8,24},{16,0},{24,8},{1,17},{9,25},{17,1},{25,9},{2,18},{10... | collective-permute-start | bytes 1179656 | tf_op jit(solution)/shard_map/ppermute | solution.py:49
  91.3 2.2 %copy-start.1 = (f32[256,3072]{1,0:T(8,128)}, f32[256,3072]{1,0:T(8,128)S(1)}, u32[]{:S(2)}) copy-start(f32[256,3072]{1,0:T(8,128)S(1)} %fusion.10) | copy-start | bytes 9437188
  93.5 3.8 %collective-permute-start.9 = (f32[4,32,3072]{2,1,0:T(8,128)}, f32[4,32,3072]{2,1,0:T(8,128)}, u32[]{:S(2)}, u32[]{:S(2)}) collective-permute-start(f32[4,32,3072]{2,1,0:T(8,128)} %dynamic-slice_bitcast_fusion), channel_id=1, source_target_pairs={{0,1},{1,0},{2,3},{3,2},{4,5},{5,4},{6,7},{7,6},{8,9},{9,8},{10,11... | collective-permute-start | bytes 4718600 | tf_op jit(solution)/shard_map/ppermute | solution.py:49
Sparse Core Ops, SparseCore 0:
  100.7 33.7 reduce-scatter.1

commit v7 on v6

--- a/solution.py
+++ b/solution.py
@@ -130,14 +130,13 @@
     k = lax.axis_index(axis) % 2
     by_core = jnp.swapaxes(partial.reshape(n // 2, 2, m, partial.shape[1]), 0, 1)
     chip = _pick(k, by_core) + _swap(_pick(1 - k, by_core), axis, 1)
-    groups = [list(range(j, n, 2)) for j in range(2)]
-    return lax.psum_scatter(
-        chip.reshape(n // 2 * m, partial.shape[1]),
-        axis,
-        scatter_dimension=0,
-        tiled=True,
-        axis_index_groups=groups,
-    )
+    chips = n // 2
+    z = lax.axis_index(axis) // 2
+    total = _pick(z, chip)
+    for d in range(1, chips):
+        pairs = [(2 * i + j, 2 * ((i + d) % chips) + j) for i in range(chips) for j in range(2)]
+        total = total + lax.ppermute(_pick((z + d) % chips, chip), axis, pairs)
+    return total
 
 
 def body(tokens, weight, bias, cotangent):

time: 143 us -> 133 us (0.930)
  between operations: 14.2 us -> 0.83 us
  starting transfers between devices: 9.42 us -> 13.3 us
  other arithmetic: 12.3 us -> 10.7 us
    ppermute x0 -> x3, waiting for transfers between devices: none -> 23.4 us  [col_reduce_scatter(): total = total + lax.ppermute(_pick((z + d) % chips, chip), axis, pairs)]
    reduce_scatter x1 -> x0, waiting for transfers between devices: 19.6 us -> none  [col_reduce_scatter(): lax.psum_scatter(chip.reshape(n // 2 * m, partial.shape[1]), axis, scatte...]
    ppermute x0 -> x3, starting transfers between devices: none -> 3.87 us  [col_reduce_scatter(): total = total + lax.ppermute(_pick((z + d) % chips, chip), axis, pairs)]
    ppermute x10, waiting for transfers between devices: 31.2 us -> 27.4 us  [_swap(): return lax.ppermute(value, axis, [(i, i ^ flip) for i in range(size)])]
    add x1, other arithmetic: 3.25 us -> 1.61 us  [col_reduce_scatter(): chip = _pick(k, by_core) + _swap(_pick(1 - k, by_core), axis, 1)]
    unnamed x6 -> x8, local copies, waits for them, and re-layouts: 1.93 us -> 3.03 us
  transfers between devices with their start and end apart: 11 -> 13, of which waited for: 10 -> 10; matrix products, arithmetic and copies ran while one was open for 4% -> 4% of each run, Pallas kernels for 7% -> 8%
where the time goes in v7:
time: 133 us
  waiting for transfers between devices  50.8 us (38%)
  blocking collectives  21.5 us (16%)
  matrix products  18 us (14%)
  starting transfers between devices  13.3 us (10%)
  other arithmetic  10.7 us (8%)
  Pallas kernels  10.2 us (8%)
  local copies, waits for them, and re-layouts  7.45 us (6%)
    ppermute x10, waiting for transfers between devices, _swap(): return lax.ppermute(value, axis, [(i, i ^ flip) for i in range(size)])  27.4 us
    ppermute x3, waiting for transfers between devices, col_reduce_scatter(): total = total + lax.ppermute(_pick((z + d) % chips, chip), axis, pairs)  23.4 us
    all_gather x1, blocking collectives, col_all_gather(): mine = lax.all_gather(block, axis, axis_index_groups=groups)  21.5 us
    pallas_call x1, Pallas kernels, outer_product_sum(): pl.pallas_call(_outer_kernel, grid=(n // block_n, m // block_m), in_specs...  10.2 us
    ppermute x10, starting transfers between devices, _swap(): return lax.ppermute(value, axis, [(i, i ^ flip) for i in range(size)])  9.39 us
    dot_general x1, matrix products, body(): lax.dot_general(full_grad, weight, (((1,), (1,)), ((), ())), preferred_el...  9.04 us
    dot_general x1, matrix products, body(): partial_value = jnp.dot(local_x, weight, preferred_element_type=jnp.float32)  8.99 us
    ppermute x3, starting transfers between devices, col_reduce_scatter(): total = total + lax.ppermute(_pick((z + d) % chips, chip), axis, pairs)  3.87 us
  transfers between devices with their start and end apart: 13, of which 10 were waited for; matrix products, arithmetic and copies ran while one was open for 4% of the time, Pallas kernels for 8%

profile of v7, /device:TPU:0, one launch (start us, length us, event | category | flops | bytes accessed | tf_op | source)
XLA Modules:
  0.0 132.8 jit_solution(8960195732322718500)
XLA Ops:
  0.6 21.5 %all-gather = bf16[128,3072]{1,0:T(8,128)(2,1)S(1)} all-gather(bf16[32,3072]{1,0:T(8,128)(2,1)} %param.4), channel_id=2, replica_groups={{0,2,4,6},{1,3,5,7},{8,10,12,14},{9,11,13,15},{16,18,20,22},{17,19,21,2..., dimensions={0}, use_global_device_ids=true | all-gather | bytes 983040 | tf_op jit(solution)/shard_map/all_gather | solution.py:120
  22.1 2.3 %collective-permute-done = bf16[4,32,3072]{2,1,0:T(8,128)(2,1)S(1)} collective-permute-done((bf16[4,32,3072]{2,1,0:T(8,128)(2,1)S(1)}, bf16[4,32,3072]{2,1,0:T(8,128)(2,1)S(1)}, u32[]{:S(2)}, u32[]{:S(2)}) %collective-permute-start) | collective-permute-done | bytes 786464 | tf_op jit(solution)/shard_map/ppermute | solution.py:49
  24.8 9.0 %fusion.16 = f32[256,3072]{1,0:T(8,128)S(1)} fusion(bf16[256,3072]{1,0:T(8,128)(2,1)S(1)} %bitcast.79, bf16[3072,3072]{1,0:T(8,128)(2,1)} %param.5), kind=kOutput, calls=%fused_computation.51 | convolution fusion | flops 4831838208 | bytes 23592960 | tf_op jit(solution)/shard_map/dot_general | solution.py:146
  36.0 1.5 %collective-permute-start.1 = (bf16[2,64,1536]{2,1,0:T(8,128)(2,1)}, bf16[2,64,1536]{2,1,0:T(8,128)(2,1)S(1)}, u32[]{:S(2)}, u32[]{:S(2)}) collective-permute-start(bf16[2,64,1536]{2,1,0:T(8,128)(2,1)} %fusion.7), channel_id=1, source_target_pairs={{0,8},{8,0},{16,24},{24,16},{1,9},{9,1},{17,25},{25,17},{2,10},{10... | collective-permute-start | bytes 1179656 | tf_op jit(solution)/shard_map/ppermute | solution.py:49
  37.5 1.6 %collective-permute-start.3 = (bf16[2,64,1536]{2,1,0:T(8,128)(2,1)S(1)}, bf16[2,64,1536]{2,1,0:T(8,128)(2,1)S(1)}, u32[]{:S(2)}, u32[]{:S(2)}) collective-permute-start(bf16[2,64,1536]{2,1,0:T(8,128)(2,1)S(1)} %fusion.6), channel_id=1, source_target_pairs={{0,16},{8,24},{16,0},{24,8},{1,17},{9,25},{17,1},{25,9},{2,18},{10... | collective-permute-start | bytes 1179656 | tf_op jit(solution)/shard_map/ppermute | solution.py:49
  39.1 8.2 %collective-permute-done.1 = bf16[2,64,1536]{2,1,0:T(8,128)(2,1)S(1)} collective-permute-done((bf16[2,64,1536]{2,1,0:T(8,128)(2,1)}, bf16[2,64,1536]{2,1,0:T(8,128)(2,1)S(1)}, u32[]{:S(2)}, u32[]{:S(2)}) %collective-permute-start.1) | collective-permute-done | bytes 393248 | tf_op jit(solution)/shard_map/ppermute | solution.py:49
  48.6 1.6 %collective-permute-start.2 = (bf16[64,1536]{1,0:T(8,128)(2,1)S(1)}, bf16[64,1536]{1,0:T(8,128)(2,1)S(1)}, u32[]{:S(2)}, u32[]{:S(2)}) collective-permute-start(bf16[64,1536]{1,0:T(8,128)(2,1)S(1)} %fusion.11), channel_id=1, source_target_pairs={{0,16},{8,24},{16,0},{24,8},{1,17},{9,25},{17,1},{25,9},{2,18},{10... | collective-permute-start | bytes 589832 | tf_op jit(solution)/shard_map/ppermute | solution.py:49
  50.3 1.6 %collective-permute-start.4 = (bf16[64,1536]{1,0:T(8,128)(2,1)S(1)}, bf16[64,1536]{1,0:T(8,128)(2,1)S(1)}, u32[]{:S(2)}, u32[]{:S(2)}) collective-permute-start(bf16[64,1536]{1,0:T(8,128)(2,1)S(1)} %fusion.12), channel_id=1, source_target_pairs={{0,8},{8,0},{16,24},{24,16},{1,9},{9,1},{17,25},{25,17},{2,10},{10... | collective-permute-start | bytes 589832 | tf_op jit(solution)/shard_map/ppermute | solution.py:49
  51.9 2.9 %collective-permute-done.2 = bf16[64,1536]{1,0:T(8,128)(2,1)S(1)} collective-permute-done((bf16[64,1536]{1,0:T(8,128)(2,1)S(1)}, bf16[64,1536]{1,0:T(8,128)(2,1)S(1)}, u32[]{:S(2)}, u32[]{:S(2)}) %collective-permute-start.2) | collective-permute-done | bytes 196640 | tf_op jit(solution)/shard_map/ppermute | solution.py:49
  54.8 1.4 %collective-permute-done.4 = bf16[64,1536]{1,0:T(8,128)(2,1)S(1)} collective-permute-done((bf16[64,1536]{1,0:T(8,128)(2,1)S(1)}, bf16[64,1536]{1,0:T(8,128)(2,1)S(1)}, u32[]{:S(2)}, u32[]{:S(2)}) %collective-permute-start.4) | collective-permute-done | bytes 196640 | tf_op jit(solution)/shard_map/ppermute | solution.py:49
  56.3 2.2 %fusion.5 = (bf16[64,3072]{1,0:T(8,128)(2,1)S(1)}, bf16[64,3072]{1,0:T(8,128)(2,1)}) fusion(f32[64,1536]{1,0:T(8,128)S(1)} %bitcast_add_fusion.4, f32[64,1536]{1,0:T(8,128)S(1)} %bitcast_add_fusion.5, bf16[256,3072]{1,0:T(8,128)(2,1)} %param.7, s32[]{:T(128)S(6)} %select_n.132, f32[3072]{0:T(1024)S(1)} %copy-done.3), kind=kLoop, calls=%fused_computation.11 | loop fusion | flops 2949120 | bytes 1978372 | tf_op jit(solution)/shard_map/convert_element_type | solution.py:15
  58.5 1.6 %collective-permute-start.5 = (bf16[64,1536]{1,0:T(8,128)(2,1)S(1)}, bf16[64,1536]{1,0:T(8,128)(2,1)S(1)}, u32[]{:S(2)}, u32[]{:S(2)}) collective-permute-start(bf16[64,1536]{1,0:T(8,128)(2,1)S(1)} %get-tuple-element.23), channel_id=1, source_target_pairs={{0,8},{8,0},{16,24},{24,16},{1,9},{9,1},{17,25},{25,17},{2,10},{10... | collective-permute-start | bytes 589832 | tf_op jit(solution)/shard_map/ppermute | solution.py:49
  60.5 3.7 %collective-permute-done.5 = bf16[64,1536]{1,0:T(8,128)(2,1)S(1)} collective-permute-done((bf16[64,1536]{1,0:T(8,128)(2,1)S(1)}, bf16[64,1536]{1,0:T(8,128)(2,1)S(1)}, u32[]{:S(2)}, u32[]{:S(2)}) %collective-permute-start.5) | collective-permute-done | bytes 196640 | tf_op jit(solution)/shard_map/ppermute | solution.py:49
  64.2 1.6 %collective-permute-done.7 = bf16[64,1536]{1,0:T(8,128)(2,1)S(1)} collective-permute-done((bf16[64,1536]{1,0:T(8,128)(2,1)S(1)}, bf16[64,1536]{1,0:T(8,128)(2,1)S(1)}, u32[]{:S(2)}, u32[]{:S(2)}) %collective-permute-start.7) | collective-permute-done | bytes 196640 | tf_op jit(solution)/shard_map/ppermute | solution.py:49
  67.0 6.8 %collective-permute-done.8 = bf16[2,64,1536]{2,1,0:T(8,128)(2,1)S(1)} collective-permute-done((bf16[2,64,1536]{2,1,0:T(8,128)(2,1)S(1)}, bf16[2,64,1536]{2,1,0:T(8,128)(2,1)S(1)}, u32[]{:S(2)}, u32[]{:S(2)}) %collective-permute-start.8) | collective-permute-done | bytes 393248 | tf_op jit(solution)/shard_map/ppermute | solution.py:49
  75.7 9.0 %fusion.13 = f32[256,3072]{1,0:T(8,128)S(1)} fusion(bf16[3072,3072]{1,0:T(8,128)(2,1)} %param.5, bf16[256,1536]{1,0:T(8,128)(2,1)S(1)} %bitcast.73, bf16[256,1536]{1,0:T(8,128)(2,1)S(1)} %bitcast.76), kind=kOutput, calls=%fused_computation.48 | convolution fusion | flops 4834983936 | bytes 23592960 | tf_op jit(solution)/shard_map/dot_general | solution.py:152
  84.8 1.4 %dynamic-slice_bitcast_fusion = f32[4,32,3072]{2,1,0:T(8,128)} fusion(f32[4,2,32,3072]{3,2,1,0:T(8,128)S(1)} %bitcast.86, s32[]{:T(128)S(6)} %select_n.144), kind=kLoop, calls=%fused_computation.4 | loop fusion | bytes 3145732 | tf_op jit(solution)/shard_map/jit(dynamic_index_in_dim)/squeeze | solution.py:53
  87.0 1.6 %copy.17 = bf16[256,3072]{0,1:T(8,128)(2,1)} copy(bf16[256,3072]{1,0:T(8,128)(2,1)S(1)} %bitcast.80) | data formatting | bytes 3145728 | tf_op jit(solution)/shard_map/reshape | solution.py:122
  91.9 1.6 %bitcast_add_fusion = f32[4,32,3072]{2,1,0:T(8,128)S(1)} fusion(f32[4,32,3072]{2,1,0:T(8,128)} %collective-permute-done.9, f32[4,2,32,3072]{3,2,1,0:T(8,128)S(1)} %bitcast.87, s32[]{:T(128)S(6)} %select_n.143), kind=kLoop, calls=%fused_computation.3 | loop fusion | flops 393216 | bytes 4718596 | tf_op jit(solution)/shard_map/add | solution.py:132
  93.7 3.8 %collective-permute-start.12 = (f32[32,3072]{1,0:T(8,128)S(1)}, f32[32,3072]{1,0:T(8,128)S(1)}, u32[]{:S(2)}, u32[]{:S(2)}) collective-permute-start(f32[32,3072]{1,0:T(8,128)S(1)} %get-tuple-element.7), channel_id=1, source_target_pairs={{0,6},{1,7},{2,0},{3,1},{4,2},{5,3},{6,4},{7,5},{8,14},{9,15},{10,... | collective-permute-start | bytes 1179656 | tf_op jit(solution)/shard_map/ppermute | solution.py:138
  97.5 10.2 %shard_map.75 = bf16[3072,3072]{1,0:T(8,128)(2,1)} custom-call(bf16[3072,256]{1,0:T(8,128)(2,1)} %bitcast.81, bf16[256,3072]{1,0:T(8,128)(2,1)} %pad_maximum_fusion.g_ref), custom_call_target="tpu_custom_call" | custom-call | flops 4831838208 | bytes 22020096 | tf_op jit(solution)/shard_map/pallas_call | solution.py:32
  107.7 6.2 %collective-permute-done.12 = f32[32,3072]{1,0:T(8,128)S(1)} collective-permute-done((f32[32,3072]{1,0:T(8,128)S(1)}, f32[32,3072]{1,0:T(8,128)S(1)}, u32[]{:S(2)}, u32[]{:S(2)}) %collective-permute-start.12) | collective-permute-done | bytes 393248 | tf_op jit(solution)/shard_map/ppermute | solution.py:138
  113.9 17.2 %collective-permute-done.11 = f32[32,3072]{1,0:T(8,128)} collective-permute-done((f32[32,3072]{1,0:T(8,128)S(1)}, f32[32,3072]{1,0:T(8,128)}, u32[]{:S(2)}, u32[]{:S(2)}) %collective-permute-start.11) | collective-permute-done | bytes 393248 | tf_op jit(solution)/shard_map/ppermute | solution.py:138
  131.1 1.7 %fusion.10 = bf16[32,3072]{1,0:T(8,128)(2,1)} fusion(f32[32,3072]{1,0:T(8,128)S(1)} %collective-permute-done.12, f32[32,3072]{1,0:T(8,128)} %collective-permute-done.11, f32[32,3072]{1,0:T(8,128)S(1)} %collective-permute-done.10, f32[4,32,3072]{2,1,0:T(8,128)S(1)} %bitcast_add_fusion, s32[]{:T(128)S(6)} %select_n.146), kind=kLoop, calls=%fused_computation.30 | loop fusion | flops 393216 | bytes 1769476 | tf_op jit(solution)/shard_map/convert_element_type | solution.py:155
  (42 shorter events, 11.9 us)
Async XLA Ops:
  22.1 2.3 %collective-permute-start = (bf16[4,32,3072]{2,1,0:T(8,128)(2,1)S(1)}, bf16[4,32,3072]{2,1,0:T(8,128)(2,1)S(1)}, u32[]{:S(2)}, u32[]{:S(2)}) collective-permute-start(bf16[4,32,3072]{2,1,0:T(8,128)(2,1)S(1)} %bitcast.88), channel_id=1, source_target_pairs={{0,1},{1,0},{2,3},{3,2},{4,5},{5,4},{6,7},{7,6},{8,9},{9,8},{10,11... | collective-permute-start | bytes 2359304 | tf_op jit(solution)/shard_map/ppermute | solution.py:49
  34.1 1.1 copy-start
  36.0 11.4 %collective-permute-start.1 = (bf16[2,64,1536]{2,1,0:T(8,128)(2,1)}, bf16[2,64,1536]{2,1,0:T(8,128)(2,1)S(1)}, u32[]{:S(2)}, u32[]{:S(2)}) collective-permute-start(bf16[2,64,1536]{2,1,0:T(8,128)(2,1)} %fusion.7), channel_id=1, source_target_pairs={{0,8},{8,0},{16,24},{24,16},{1,9},{9,1},{17,25},{25,17},{2,10},{10... | collective-permute-start | bytes 1179656 | tf_op jit(solution)/shard_map/ppermute | solution.py:49
  37.5 12.7 %collective-permute-start.3 = (bf16[2,64,1536]{2,1,0:T(8,128)(2,1)S(1)}, bf16[2,64,1536]{2,1,0:T(8,128)(2,1)S(1)}, u32[]{:S(2)}, u32[]{:S(2)}) collective-permute-start(bf16[2,64,1536]{2,1,0:T(8,128)(2,1)S(1)} %fusion.6), channel_id=1, source_target_pairs={{0,16},{8,24},{16,0},{24,8},{1,17},{9,25},{17,1},{25,9},{2,18},{10... | collective-permute-start | bytes 1179656 | tf_op jit(solution)/shard_map/ppermute | solution.py:49
  48.6 6.2 %collective-permute-start.2 = (bf16[64,1536]{1,0:T(8,128)(2,1)S(1)}, bf16[64,1536]{1,0:T(8,128)(2,1)S(1)}, u32[]{:S(2)}, u32[]{:S(2)}) collective-permute-start(bf16[64,1536]{1,0:T(8,128)(2,1)S(1)} %fusion.11), channel_id=1, source_target_pairs={{0,16},{8,24},{16,0},{24,8},{1,17},{9,25},{17,1},{25,9},{2,18},{10... | collective-permute-start | bytes 589832 | tf_op jit(solution)/shard_map/ppermute | solution.py:49
  50.3 6.0 %copy-start.3 = (f32[3072]{0:T(1024)S(1)}, f32[3072]{0:T(1024)}, u32[]{:S(2)}) copy-start(f32[3072]{0:T(1024)} %param.6) | copy-start | bytes 36868
  50.3 5.9 %collective-permute-start.4 = (bf16[64,1536]{1,0:T(8,128)(2,1)S(1)}, bf16[64,1536]{1,0:T(8,128)(2,1)S(1)}, u32[]{:S(2)}, u32[]{:S(2)}) collective-permute-start(bf16[64,1536]{1,0:T(8,128)(2,1)S(1)} %fusion.12), channel_id=1, source_target_pairs={{0,8},{8,0},{16,24},{24,16},{1,9},{9,1},{17,25},{25,17},{2,10},{10... | collective-permute-start | bytes 589832 | tf_op jit(solution)/shard_map/ppermute | solution.py:49
  58.5 5.7 %collective-permute-start.5 = (bf16[64,1536]{1,0:T(8,128)(2,1)S(1)}, bf16[64,1536]{1,0:T(8,128)(2,1)S(1)}, u32[]{:S(2)}, u32[]{:S(2)}) collective-permute-start(bf16[64,1536]{1,0:T(8,128)(2,1)S(1)} %get-tuple-element.23), channel_id=1, source_target_pairs={{0,8},{8,0},{16,24},{24,16},{1,9},{9,1},{17,25},{25,17},{2,10},{10... | collective-permute-start | bytes 589832 | tf_op jit(solution)/shard_map/ppermute | solution.py:49
  60.0 5.7 %collective-permute-start.7 = (bf16[64,1536]{1,0:T(8,128)(2,1)S(1)}, bf16[64,1536]{1,0:T(8,128)(2,1)S(1)}, u32[]{:S(2)}, u32[]{:S(2)}) collective-permute-start(bf16[64,1536]{1,0:T(8,128)(2,1)S(1)} %get-tuple-element.24), channel_id=1, source_target_pairs={{0,16},{8,24},{16,0},{24,8},{1,17},{9,25},{17,1},{25,9},{2,18},{10... | collective-permute-start | bytes 589832 | tf_op jit(solution)/shard_map/ppermute | solution.py:49
  65.9 8.0 %collective-permute-start.8 = (bf16[2,64,1536]{2,1,0:T(8,128)(2,1)S(1)}, bf16[2,64,1536]{2,1,0:T(8,128)(2,1)S(1)}, u32[]{:S(2)}, u32[]{:S(2)}) collective-permute-start(bf16[2,64,1536]{2,1,0:T(8,128)(2,1)S(1)} %pad_maximum_fusion.3), channel_id=1, source_target_pairs={{0,8},{8,0},{16,24},{24,16},{1,9},{9,1},{17,25},{25,17},{2,10},{10... | collective-permute-start | bytes 1179656 | tf_op jit(solution)/shard_map/ppermute | solution.py:49
  66.4 7.9 %collective-permute-start.6 = (bf16[2,64,1536]{2,1,0:T(8,128)(2,1)S(1)}, bf16[2,64,1536]{2,1,0:T(8,128)(2,1)}, u32[]{:S(2)}, u32[]{:S(2)}) collective-permute-start(bf16[2,64,1536]{2,1,0:T(8,128)(2,1)S(1)} %pad_maximum_fusion.2), channel_id=1, source_target_pairs={{0,16},{8,24},{16,0},{24,8},{1,17},{9,25},{17,1},{25,9},{2,18},{10... | collective-permute-start | bytes 1179656 | tf_op jit(solution)/shard_map/ppermute | solution.py:49
  84.8 2.2 %copy-start.1 = (f32[256,3072]{1,0:T(8,128)}, f32[256,3072]{1,0:T(8,128)S(1)}, u32[]{:S(2)}) copy-start(f32[256,3072]{1,0:T(8,128)S(1)} %fusion.13) | copy-start | bytes 9437188
  87.0 3.8 %collective-permute-start.9 = (f32[4,32,3072]{2,1,0:T(8,128)}, f32[4,32,3072]{2,1,0:T(8,128)}, u32[]{:S(2)}, u32[]{:S(2)}) collective-permute-start(f32[4,32,3072]{2,1,0:T(8,128)} %dynamic-slice_bitcast_fusion), channel_id=1, source_target_pairs={{0,1},{1,0},{2,3},{3,2},{4,5},{5,4},{6,7},{7,6},{8,9},{9,8},{10,11... | collective-permute-start | bytes 4718600 | tf_op jit(solution)/shard_map/ppermute | solution.py:49
  89.4 2.5 %copy-start.2 = (f32[256,3072]{1,0:T(8,128)S(1)}, f32[256,3072]{1,0:T(8,128)}, u32[]{:S(2)}) copy-start(f32[256,3072]{1,0:T(8,128)} %copy-done.1) | copy-start | bytes 9437188
  93.6 14.1 %collective-permute-start.10 = (f32[32,3072]{1,0:T(8,128)S(1)}, f32[32,3072]{1,0:T(8,128)S(1)}, u32[]{:S(2)}, u32[]{:S(2)}) collective-permute-start(f32[32,3072]{1,0:T(8,128)S(1)} %get-tuple-element.6), channel_id=1, source_target_pairs={{0,2},{1,3},{2,4},{3,5},{4,6},{5,7},{6,0},{7,1},{8,10},{9,11},{10,... | collective-permute-start | bytes 1179656 | tf_op jit(solution)/shard_map/ppermute | solution.py:138
  93.7 20.2 %collective-permute-start.12 = (f32[32,3072]{1,0:T(8,128)S(1)}, f32[32,3072]{1,0:T(8,128)S(1)}, u32[]{:S(2)}, u32[]{:S(2)}) collective-permute-start(f32[32,3072]{1,0:T(8,128)S(1)} %get-tuple-element.7), channel_id=1, source_target_pairs={{0,6},{1,7},{2,0},{3,1},{4,2},{5,3},{6,4},{7,5},{8,14},{9,15},{10,... | collective-permute-start | bytes 1179656 | tf_op jit(solution)/shard_map/ppermute | solution.py:138
  97.5 33.6 %collective-permute-start.11 = (f32[32,3072]{1,0:T(8,128)S(1)}, f32[32,3072]{1,0:T(8,128)}, u32[]{:S(2)}, u32[]{:S(2)}) collective-permute-start(f32[32,3072]{1,0:T(8,128)S(1)} %get-tuple-element.8), channel_id=1, source_target_pairs={{0,4},{1,5},{2,6},{3,7},{4,0},{5,1},{6,2},{7,3},{8,12},{9,13},{10,... | collective-permute-start | bytes 1179656 | tf_op jit(solution)/shard_map/ppermute | solution.py:138

commit v8 on v7

--- a/solution.py
+++ b/solution.py
@@ -132,11 +132,21 @@
     chip = _pick(k, by_core) + _swap(_pick(1 - k, by_core), axis, 1)
     chips = n // 2
     z = lax.axis_index(axis) // 2
-    total = _pick(z, chip)
-    for d in range(1, chips):
-        pairs = [(2 * i + j, 2 * ((i + d) % chips) + j) for i in range(chips) for j in range(2)]
-        total = total + lax.ppermute(_pick((z + d) % chips, chip), axis, pairs)
-    return total
+    if chips & (chips - 1):
+        total = _pick(z, chip)
+        for d in range(1, chips):
+            pairs = [(2 * i + j, 2 * ((i + d) % chips) + j) for i in range(chips) for j in range(2)]
+            total = total + lax.ppermute(_pick((z + d) % chips, chip), axis, pairs)
+        return total
+    levels = chips.bit_length() - 1
+    cur = chip.reshape([2] * levels + [m, partial.shape[1]])
+    bits = list(range(levels))[::-1]
+    for bit in range(levels):
+        mine = (z >> bit) & 1
+        t = jnp.moveaxis(cur, bits.index(bit), 0)
+        cur = _pick(mine, t) + _swap(_pick(1 - mine, t), axis, 2 << bit)
+        bits.remove(bit)
+    return cur.reshape(m, partial.shape[1])
 
 
 def body(tokens, weight, bias, cotangent):

time: 133 us -> 132 us (level)
  waiting for transfers between devices: 50.8 us -> 54.2 us
  starting transfers between devices: 13.3 us -> 10.6 us
  other arithmetic: 10.7 us -> 9.23 us
    ppermute x10 -> x12, waiting for transfers between devices: 27.4 us -> 54.2 us  [_swap(): return lax.ppermute(value, axis, [(i, i ^ flip) for i in range(size)])]
    ppermute x3 -> x0, waiting for transfers between devices: 23.4 us -> none  [col_reduce_scatter(): total = total + lax.ppermute(_pick((z + d) % chips, chip), axis, pairs)]
    ppermute x3 -> x0, starting transfers between devices: 3.87 us -> none  [col_reduce_scatter(): total = total + lax.ppermute(_pick((z + d) % chips, chip), axis, pairs)]
    unnamed x8 -> x6, local copies, waits for them, and re-layouts: 3.03 us -> 1.52 us
    ppermute x10 -> x12, starting transfers between devices: 9.39 us -> 10.6 us  [_swap(): return lax.ppermute(value, axis, [(i, i ^ flip) for i in range(size)])]
  transfers between devices with their start and end apart: 13 -> 12, of which waited for: 10 -> 11; matrix products, arithmetic and copies ran while one was open for 4% -> 4% of each run, Pallas kernels for 8% -> 8%
where the time goes in v8:
time: 132 us
  waiting for transfers between devices  54.2 us (41%)
  blocking collectives  21.5 us (16%)
  matrix products  18.6 us (14%)
  starting transfers between devices  10.6 us (8%)
  Pallas kernels  10.3 us (8%)
  other arithmetic  9.23 us (7%)
  local copies, waits for them, and re-layouts  6.53 us (5%)
    ppermute x12, waiting for transfers between devices, _swap(): return lax.ppermute(value, axis, [(i, i ^ flip) for i in range(size)])  54.2 us
    all_gather x1, blocking collectives, col_all_gather(): mine = lax.all_gather(block, axis, axis_index_groups=groups)  21.5 us
    ppermute x12, starting transfers between devices, _swap(): return lax.ppermute(value, axis, [(i, i ^ flip) for i in range(size)])  10.6 us
    pallas_call x1, Pallas kernels, outer_product_sum(): pl.pallas_call(_outer_kernel, grid=(n // block_n, m // block_m), in_specs...  10.3 us
    dot_general x1, matrix products, body(): partial_value = jnp.dot(local_x, weight, preferred_element_type=jnp.float32)  9.58 us
    dot_general x1, matrix products, body(): lax.dot_general(full_grad, weight, (((1,), (1,)), ((), ())), preferred_el...  9.04 us
  transfers between devices with their start and end apart: 12, of which 11 were waited for; matrix products, arithmetic and copies ran while one was open for 4% of the time, Pallas kernels for 8%

profile of v8, /device:TPU:0, one launch (start us, length us, event | category | flops | bytes accessed | tf_op | source)
XLA Modules:
  0.0 131.8 jit_solution(9903517791624891781)
XLA Ops:
  0.6 21.5 %all-gather = bf16[128,3072]{1,0:T(8,128)(2,1)S(1)} all-gather(bf16[32,3072]{1,0:T(8,128)(2,1)} %param.4), channel_id=2, replica_groups={{0,2,4,6},{1,3,5,7},{8,10,12,14},{9,11,13,15},{16,18,20,22},{17,19,21,2..., dimensions={0}, use_global_device_ids=true | all-gather | bytes 983040 | tf_op jit(solution)/shard_map/all_gather | solution.py:120
  22.1 2.3 %collective-permute-done = bf16[4,32,3072]{2,1,0:T(8,128)(2,1)S(1)} collective-permute-done((bf16[4,32,3072]{2,1,0:T(8,128)(2,1)S(1)}, bf16[4,32,3072]{2,1,0:T(8,128)(2,1)S(1)}, u32[]{:S(2)}, u32[]{:S(2)}) %collective-permute-start) | collective-permute-done | bytes 786464 | tf_op jit(solution)/shard_map/ppermute | solution.py:49
  24.8 9.6 %fusion.14 = f32[256,3072]{1,0:T(8,128)S(1)} fusion(bf16[256,3072]{1,0:T(8,128)(2,1)S(1)} %bitcast.78, bf16[3072,3072]{1,0:T(8,128)(2,1)} %param.5), kind=kOutput, calls=%fused_computation.49 | convolution fusion | flops 4831838208 | bytes 23592960 | tf_op jit(solution)/shard_map/dot_general | solution.py:156
  35.4 1.5 %collective-permute-start.1 = (bf16[2,64,1536]{2,1,0:T(8,128)(2,1)}, bf16[2,64,1536]{2,1,0:T(8,128)(2,1)S(1)}, u32[]{:S(2)}, u32[]{:S(2)}) collective-permute-start(bf16[2,64,1536]{2,1,0:T(8,128)(2,1)} %fusion.7), channel_id=1, source_target_pairs={{0,8},{8,0},{16,24},{24,16},{1,9},{9,1},{17,25},{25,17},{2,10},{10... | collective-permute-start | bytes 1179656 | tf_op jit(solution)/shard_map/ppermute | solution.py:49
  37.0 1.6 %collective-permute-start.3 = (bf16[2,64,1536]{2,1,0:T(8,128)(2,1)S(1)}, bf16[2,64,1536]{2,1,0:T(8,128)(2,1)S(1)}, u32[]{:S(2)}, u32[]{:S(2)}) collective-permute-start(bf16[2,64,1536]{2,1,0:T(8,128)(2,1)S(1)} %fusion.6), channel_id=1, source_target_pairs={{0,16},{8,24},{16,0},{24,8},{1,17},{9,25},{17,1},{25,9},{2,18},{10... | collective-permute-start | bytes 1179656 | tf_op jit(solution)/shard_map/ppermute | solution.py:49
  38.6 8.2 %collective-permute-done.1 = bf16[2,64,1536]{2,1,0:T(8,128)(2,1)S(1)} collective-permute-done((bf16[2,64,1536]{2,1,0:T(8,128)(2,1)}, bf16[2,64,1536]{2,1,0:T(8,128)(2,1)S(1)}, u32[]{:S(2)}, u32[]{:S(2)}) %collective-permute-start.1) | collective-permute-done | bytes 393248 | tf_op jit(solution)/shard_map/ppermute | solution.py:49
  46.9 1.6 %collective-permute-start.2 = (bf16[64,1536]{1,0:T(8,128)(2,1)S(1)}, bf16[64,1536]{1,0:T(8,128)(2,1)S(1)}, u32[]{:S(2)}, u32[]{:S(2)}) collective-permute-start(bf16[64,1536]{1,0:T(8,128)(2,1)S(1)} %fusion.9), channel_id=1, source_target_pairs={{0,16},{8,24},{16,0},{24,8},{1,17},{9,25},{17,1},{25,9},{2,18},{10... | collective-permute-start | bytes 589832 | tf_op jit(solution)/shard_map/ppermute | solution.py:49
  48.7 1.6 %collective-permute-start.4 = (bf16[64,1536]{1,0:T(8,128)(2,1)S(1)}, bf16[64,1536]{1,0:T(8,128)(2,1)S(1)}, u32[]{:S(2)}, u32[]{:S(2)}) collective-permute-start(bf16[64,1536]{1,0:T(8,128)(2,1)S(1)} %fusion.10), channel_id=1, source_target_pairs={{0,8},{8,0},{16,24},{24,16},{1,9},{9,1},{17,25},{25,17},{2,10},{10... | collective-permute-start | bytes 589832 | tf_op jit(solution)/shard_map/ppermute | solution.py:49
  50.2 2.9 %collective-permute-done.2 = bf16[64,1536]{1,0:T(8,128)(2,1)S(1)} collective-permute-done((bf16[64,1536]{1,0:T(8,128)(2,1)S(1)}, bf16[64,1536]{1,0:T(8,128)(2,1)S(1)}, u32[]{:S(2)}, u32[]{:S(2)}) %collective-permute-start.2) | collective-permute-done | bytes 196640 | tf_op jit(solution)/shard_map/ppermute | solution.py:49
  53.2 1.4 %collective-permute-done.4 = bf16[64,1536]{1,0:T(8,128)(2,1)S(1)} collective-permute-done((bf16[64,1536]{1,0:T(8,128)(2,1)S(1)}, bf16[64,1536]{1,0:T(8,128)(2,1)S(1)}, u32[]{:S(2)}, u32[]{:S(2)}) %collective-permute-start.4) | collective-permute-done | bytes 196640 | tf_op jit(solution)/shard_map/ppermute | solution.py:49
  54.6 2.2 %fusion.5 = (bf16[64,3072]{1,0:T(8,128)(2,1)S(1)}, bf16[64,3072]{1,0:T(8,128)(2,1)}) fusion(f32[64,1536]{1,0:T(8,128)S(1)} %bitcast_add_fusion.5, f32[64,1536]{1,0:T(8,128)S(1)} %bitcast_add_fusion.6, bf16[256,3072]{1,0:T(8,128)(2,1)} %param.7, s32[]{:T(128)S(6)} %select_n.121, f32[3072]{0:T(1024)S(1)} %copy-done.2), kind=kLoop, calls=%fused_computation.11 | loop fusion | flops 2949120 | bytes 1978372 | tf_op jit(solution)/shard_map/convert_element_type | solution.py:15
  56.8 1.6 %collective-permute-start.5 = (bf16[64,1536]{1,0:T(8,128)(2,1)S(1)}, bf16[64,1536]{1,0:T(8,128)(2,1)S(1)}, u32[]{:S(2)}, u32[]{:S(2)}) collective-permute-start(bf16[64,1536]{1,0:T(8,128)(2,1)S(1)} %get-tuple-element.20), channel_id=1, source_target_pairs={{0,8},{8,0},{16,24},{24,16},{1,9},{9,1},{17,25},{25,17},{2,10},{10... | collective-permute-start | bytes 589832 | tf_op jit(solution)/shard_map/ppermute | solution.py:49
  58.9 3.7 %collective-permute-done.5 = bf16[64,1536]{1,0:T(8,128)(2,1)S(1)} collective-permute-done((bf16[64,1536]{1,0:T(8,128)(2,1)S(1)}, bf16[64,1536]{1,0:T(8,128)(2,1)S(1)}, u32[]{:S(2)}, u32[]{:S(2)}) %collective-permute-start.5) | collective-permute-done | bytes 196640 | tf_op jit(solution)/shard_map/ppermute | solution.py:49
  62.5 1.6 %collective-permute-done.7 = bf16[64,1536]{1,0:T(8,128)(2,1)S(1)} collective-permute-done((bf16[64,1536]{1,0:T(8,128)(2,1)S(1)}, bf16[64,1536]{1,0:T(8,128)(2,1)S(1)}, u32[]{:S(2)}, u32[]{:S(2)}) %collective-permute-start.7) | collective-permute-done | bytes 196640 | tf_op jit(solution)/shard_map/ppermute | solution.py:49
  65.7 6.5 %collective-permute-done.8 = bf16[2,64,1536]{2,1,0:T(8,128)(2,1)S(1)} collective-permute-done((bf16[2,64,1536]{2,1,0:T(8,128)(2,1)S(1)}, bf16[2,64,1536]{2,1,0:T(8,128)(2,1)S(1)}, u32[]{:S(2)}, u32[]{:S(2)}) %collective-permute-start.8) | collective-permute-done | bytes 393248 | tf_op jit(solution)/shard_map/ppermute | solution.py:49
  72.9 9.0 %fusion.11 = f32[256,3072]{1,0:T(8,128)S(1)} fusion(bf16[3072,3072]{1,0:T(8,128)(2,1)} %param.5, bf16[256,1536]{1,0:T(8,128)(2,1)S(1)} %bitcast.70, bf16[256,1536]{1,0:T(8,128)(2,1)S(1)} %bitcast.73), kind=kOutput, calls=%fused_computation.46 | convolution fusion | flops 4834983936 | bytes 23592960 | tf_op jit(solution)/shard_map/dot_general | solution.py:162
  82.2 1.5 %copy-done.1 = f32[256,3072]{1,0:T(8,128)} copy-done((f32[256,3072]{1,0:T(8,128)}, f32[256,3072]{1,0:T(8,128)S(1)}, u32[]{:S(2)}) %copy-start.1) | copy-done | bytes 3145752
  83.7 3.5 %collective-permute-done.9 = f32[4,32,3072]{2,1,0:T(8,128)} collective-permute-done((f32[4,32,3072]{2,1,0:T(8,128)S(1)}, f32[4,32,3072]{2,1,0:T(8,128)}, u32[]{:S(2)}, u32[]{:S(2)}) %collective-permute-start.9) | collective-permute-done | bytes 1572896 | tf_op jit(solution)/shard_map/ppermute | solution.py:49
  87.2 2.0 %bitcast_add_fusion = f32[4,32,3072]{2,1,0:T(8,128)S(1)} fusion(f32[4,32,3072]{2,1,0:T(8,128)} %collective-permute-done.9, f32[4,2,32,3072]{3,2,1,0:T(8,128)} %bitcast.86, s32[]{:T(128)S(6)} %select_n.132), kind=kLoop, calls=%fused_computation.3 | loop fusion | flops 393216 | bytes 4718596 | tf_op jit(solution)/shard_map/add | solution.py:132
  90.2 2.6 %copy.17 = bf16[256,3072]{0,1:T(8,128)(2,1)} copy(bf16[256,3072]{1,0:T(8,128)(2,1)} %bitcast.79) | data formatting | bytes 3145728 | tf_op jit(solution)/shard_map/reshape | solution.py:122
  93.6 1.4 %pad_maximum_fusion.g_ref = bf16[256,3072]{1,0:T(8,128)(2,1)} fusion(bf16[256,1536]{1,0:T(8,128)(2,1)S(1)} %bitcast.72, bf16[256,1536]{1,0:T(8,128)(2,1)S(1)} %bitcast.75), kind=kLoop, calls=%fused_computation.2 | loop fusion | flops 3145728 | bytes 3145728 | tf_op jit(solution)/shard_map/concatenate | solution.py:112
  95.0 15.1 %collective-permute-done.10 = f32[2,32,3072]{2,1,0:T(8,128)} collective-permute-done((f32[2,32,3072]{2,1,0:T(8,128)}, f32[2,32,3072]{2,1,0:T(8,128)}, u32[]{:S(2)}, u32[]{:S(2)}) %collective-permute-start.10) | collective-permute-done | bytes 786464 | tf_op jit(solution)/shard_map/ppermute | solution.py:49
  112.3 10.3 %shard_map.75 = bf16[3072,3072]{1,0:T(8,128)(2,1)} custom-call(bf16[3072,256]{1,0:T(8,128)(2,1)} %bitcast.80, bf16[256,3072]{1,0:T(8,128)(2,1)} %pad_maximum_fusion.g_ref), custom_call_target="tpu_custom_call" | custom-call | flops 4831838208 | bytes 22020096 | tf_op jit(solution)/shard_map/pallas_call | solution.py:32
  122.5 8.6 %collective-permute-done.11 = f32[32,3072]{1,0:T(8,128)S(1)} collective-permute-done((f32[32,3072]{1,0:T(8,128)S(1)}, f32[32,3072]{1,0:T(8,128)S(1)}, u32[]{:S(2)}, u32[]{:S(2)}) %collective-permute-start.11) | collective-permute-done | bytes 393248 | tf_op jit(solution)/shard_map/ppermute | solution.py:49
  (40 shorter events, 9.4 us)
Async XLA Ops:
  22.1 2.3 %collective-permute-start = (bf16[4,32,3072]{2,1,0:T(8,128)(2,1)S(1)}, bf16[4,32,3072]{2,1,0:T(8,128)(2,1)S(1)}, u32[]{:S(2)}, u32[]{:S(2)}) collective-permute-start(bf16[4,32,3072]{2,1,0:T(8,128)(2,1)S(1)} %bitcast.87), channel_id=1, source_target_pairs={{0,1},{1,0},{2,3},{3,2},{4,5},{5,4},{6,7},{7,6},{8,9},{9,8},{10,11... | collective-permute-start | bytes 2359304 | tf_op jit(solution)/shard_map/ppermute | solution.py:49
  24.8 9.6 %copy-start = (bf16[4,2,32,3072]{3,2,1,0:T(8,128)(2,1)}, bf16[4,2,32,3072]{3,2,1,0:T(8,128)(2,1)S(1)}, u32[]{:S(2)}) copy-start(bf16[4,2,32,3072]{3,2,1,0:T(8,128)(2,1)S(1)} %copy.14) | copy-start | bytes 4718596
  35.4 11.4 %collective-permute-start.1 = (bf16[2,64,1536]{2,1,0:T(8,128)(2,1)}, bf16[2,64,1536]{2,1,0:T(8,128)(2,1)S(1)}, u32[]{:S(2)}, u32[]{:S(2)}) collective-permute-start(bf16[2,64,1536]{2,1,0:T(8,128)(2,1)} %fusion.7), channel_id=1, source_target_pairs={{0,8},{8,0},{16,24},{24,16},{1,9},{9,1},{17,25},{25,17},{2,10},{10... | collective-permute-start | bytes 1179656 | tf_op jit(solution)/shard_map/ppermute | solution.py:49
  37.0 11.5 %collective-permute-start.3 = (bf16[2,64,1536]{2,1,0:T(8,128)(2,1)S(1)}, bf16[2,64,1536]{2,1,0:T(8,128)(2,1)S(1)}, u32[]{:S(2)}, u32[]{:S(2)}) collective-permute-start(bf16[2,64,1536]{2,1,0:T(8,128)(2,1)S(1)} %fusion.6), channel_id=1, source_target_pairs={{0,16},{8,24},{16,0},{24,8},{1,17},{9,25},{17,1},{25,9},{2,18},{10... | collective-permute-start | bytes 1179656 | tf_op jit(solution)/shard_map/ppermute | solution.py:49
  46.9 6.2 %collective-permute-start.2 = (bf16[64,1536]{1,0:T(8,128)(2,1)S(1)}, bf16[64,1536]{1,0:T(8,128)(2,1)S(1)}, u32[]{:S(2)}, u32[]{:S(2)}) collective-permute-start(bf16[64,1536]{1,0:T(8,128)(2,1)S(1)} %fusion.9), channel_id=1, source_target_pairs={{0,16},{8,24},{16,0},{24,8},{1,17},{9,25},{17,1},{25,9},{2,18},{10... | collective-permute-start | bytes 589832 | tf_op jit(solution)/shard_map/ppermute | solution.py:49
  48.6 6.0 %copy-start.2 = (f32[3072]{0:T(1024)S(1)}, f32[3072]{0:T(1024)}, u32[]{:S(2)}) copy-start(f32[3072]{0:T(1024)} %param.6) | copy-start | bytes 36868
  48.7 5.9 %collective-permute-start.4 = (bf16[64,1536]{1,0:T(8,128)(2,1)S(1)}, bf16[64,1536]{1,0:T(8,128)(2,1)S(1)}, u32[]{:S(2)}, u32[]{:S(2)}) collective-permute-start(bf16[64,1536]{1,0:T(8,128)(2,1)S(1)} %fusion.10), channel_id=1, source_target_pairs={{0,8},{8,0},{16,24},{24,16},{1,9},{9,1},{17,25},{25,17},{2,10},{10... | collective-permute-start | bytes 589832 | tf_op jit(solution)/shard_map/ppermute | solution.py:49
  56.8 5.7 %collective-permute-start.5 = (bf16[64,1536]{1,0:T(8,128)(2,1)S(1)}, bf16[64,1536]{1,0:T(8,128)(2,1)S(1)}, u32[]{:S(2)}, u32[]{:S(2)}) collective-permute-start(bf16[64,1536]{1,0:T(8,128)(2,1)S(1)} %get-tuple-element.20), channel_id=1, source_target_pairs={{0,8},{8,0},{16,24},{24,16},{1,9},{9,1},{17,25},{25,17},{2,10},{10... | collective-permute-start | bytes 589832 | tf_op jit(solution)/shard_map/ppermute | solution.py:49
  58.3 5.7 %collective-permute-start.7 = (bf16[64,1536]{1,0:T(8,128)(2,1)S(1)}, bf16[64,1536]{1,0:T(8,128)(2,1)S(1)}, u32[]{:S(2)}, u32[]{:S(2)}) collective-permute-start(bf16[64,1536]{1,0:T(8,128)(2,1)S(1)} %get-tuple-element.21), channel_id=1, source_target_pairs={{0,16},{8,24},{16,0},{24,8},{1,17},{9,25},{17,1},{25,9},{2,18},{10... | collective-permute-start | bytes 589832 | tf_op jit(solution)/shard_map/ppermute | solution.py:49
  64.2 8.0 %collective-permute-start.8 = (bf16[2,64,1536]{2,1,0:T(8,128)(2,1)S(1)}, bf16[2,64,1536]{2,1,0:T(8,128)(2,1)S(1)}, u32[]{:S(2)}, u32[]{:S(2)}) collective-permute-start(bf16[2,64,1536]{2,1,0:T(8,128)(2,1)S(1)} %pad_maximum_fusion.3), channel_id=1, source_target_pairs={{0,8},{8,0},{16,24},{24,16},{1,9},{9,1},{17,25},{25,17},{2,10},{10... | collective-permute-start | bytes 1179656 | tf_op jit(solution)/shard_map/ppermute | solution.py:49
  64.8 7.8 %collective-permute-start.6 = (bf16[2,64,1536]{2,1,0:T(8,128)(2,1)S(1)}, bf16[2,64,1536]{2,1,0:T(8,128)(2,1)S(1)}, u32[]{:S(2)}, u32[]{:S(2)}) collective-permute-start(bf16[2,64,1536]{2,1,0:T(8,128)(2,1)S(1)} %pad_maximum_fusion.2), channel_id=1, source_target_pairs={{0,16},{8,24},{16,0},{24,8},{1,17},{9,25},{17,1},{25,9},{2,18},{10... | collective-permute-start | bytes 1179656 | tf_op jit(solution)/shard_map/ppermute | solution.py:49
  82.0 1.7 %copy-start.1 = (f32[256,3072]{1,0:T(8,128)}, f32[256,3072]{1,0:T(8,128)S(1)}, u32[]{:S(2)}) copy-start(f32[256,3072]{1,0:T(8,128)S(1)} %fusion.11) | copy-start | bytes 9437188
  83.7 3.5 %collective-permute-start.9 = (f32[4,32,3072]{2,1,0:T(8,128)S(1)}, f32[4,32,3072]{2,1,0:T(8,128)}, u32[]{:S(2)}, u32[]{:S(2)}) collective-permute-start(f32[4,32,3072]{2,1,0:T(8,128)S(1)} %dynamic-slice_bitcast_fusion), channel_id=1, source_target_pairs={{0,1},{1,0},{2,3},{3,2},{4,5},{5,4},{6,7},{7,6},{8,9},{9,8},{10,11... | collective-permute-start | bytes 4718600 | tf_op jit(solution)/shard_map/ppermute | solution.py:49
  90.2 19.9 %collective-permute-start.10 = (f32[2,32,3072]{2,1,0:T(8,128)}, f32[2,32,3072]{2,1,0:T(8,128)}, u32[]{:S(2)}, u32[]{:S(2)}) collective-permute-start(f32[2,32,3072]{2,1,0:T(8,128)} %dynamic-slice_bitcast_fusion.1), channel_id=1, source_target_pairs={{0,2},{1,3},{2,0},{3,1},{4,6},{5,7},{6,4},{7,5},{8,10},{9,11},{10,... | collective-permute-start | bytes 2359304 | tf_op jit(solution)/shard_map/ppermute | solution.py:49
  111.4 19.7 %collective-permute-start.11 = (f32[32,3072]{1,0:T(8,128)S(1)}, f32[32,3072]{1,0:T(8,128)S(1)}, u32[]{:S(2)}, u32[]{:S(2)}) collective-permute-start(f32[32,3072]{1,0:T(8,128)S(1)} %dynamic-slice_bitcast_fusion.2), channel_id=1, source_target_pairs={{0,4},{1,5},{2,6},{3,7},{4,0},{5,1},{6,2},{7,3},{8,12},{9,13},{10,... | collective-permute-start | bytes 1179656 | tf_op jit(solution)/shard_map/ppermute | solution.py:49

commit v9 on v8

--- a/solution.py
+++ b/solution.py
@@ -122,10 +122,10 @@
     return jnp.swapaxes(both, 0, 1).reshape(n * block.shape[0], block.shape[1])
 
 
-def col_reduce_scatter(partial, axis="col"):
+def col_reduce_scatter(partial, hold, axis="col"):
     n = lax.axis_size(axis)
     if n % 2:
-        return lax.psum_scatter(partial, axis, scatter_dimension=0, tiled=True)
+        return lax.psum_scatter(partial, axis, scatter_dimension=0, tiled=True), hold
     m = partial.shape[0] // n
     k = lax.axis_index(axis) % 2
     by_core = jnp.swapaxes(partial.reshape(n // 2, 2, m, partial.shape[1]), 0, 1)
@@ -137,7 +137,7 @@
         for d in range(1, chips):
             pairs = [(2 * i + j, 2 * ((i + d) % chips) + j) for i in range(chips) for j in range(2)]
             total = total + lax.ppermute(_pick((z + d) % chips, chip), axis, pairs)
-        return total
+        return total, hold
     levels = chips.bit_length() - 1
     cur = chip.reshape([2] * levels + [m, partial.shape[1]])
     bits = list(range(levels))[::-1]
@@ -146,7 +146,9 @@
         t = jnp.moveaxis(cur, bits.index(bit), 0)
         cur = _pick(mine, t) + _swap(_pick(1 - mine, t), axis, 2 << bit)
         bits.remove(bit)
-    return cur.reshape(m, partial.shape[1])
+        if bit == 0:
+            cur, hold = lax.optimization_barrier((cur, hold))
+    return cur.reshape(m, partial.shape[1]), hold
 
 
 def body(tokens, weight, bias, cotangent):
@@ -158,12 +160,14 @@
     my_cot = lax.dynamic_slice_in_dim(cotangent, first_row, my_rows, 0)
     hidden, my_grad = activate(preact, my_cot)
     full_grad = row_all_gather(my_grad)
-    grad_tokens = col_reduce_scatter(
+    grad_weight = outer_product_sum(local_x.T, full_grad)
+    grad_tokens, grad_weight = col_reduce_scatter(
         lax.dot_general(
             full_grad, weight, (((1,), (1,)), ((), ())), preferred_element_type=jnp.float32
-        )
-    ).astype(jnp.bfloat16)
-    grad_weight = outer_product_sum(local_x.T, full_grad)
+        ),
+        grad_weight,
+    )
+    grad_tokens = grad_tokens.astype(jnp.bfloat16)
     grad_bias = jnp.sum(full_grad.astype(jnp.float32), axis=0)
     return (hidden, grad_tokens, grad_weight, grad_bias)
 

time: 132 us -> 137 us (1.038)
  other arithmetic: 9.23 us -> 11.4 us
  waiting for transfers between devices: 54.2 us -> 55.9 us
  local copies, waits for them, and re-layouts: 6.53 us -> 8.11 us
    ppermute x12, waiting for transfers between devices: 54.2 us -> 55.9 us  [_swap(): return lax.ppermute(value, axis, [(i, i ^ flip) for i in range(size)])]
    unnamed x6 -> x10, local copies, waits for them, and re-layouts: 1.52 us -> 2.78 us
where the time goes in v9:
time: 137 us; the launch traced here: 136 us
  waiting for transfers between devices  55.9 us (41%)
  blocking collectives  21.5 us (16%)
  matrix products  18 us (13%)
  other arithmetic  11.4 us (8%)
  starting transfers between devices  10.3 us (8%)
  Pallas kernels  10.3 us (8%)
  local copies, waits for them, and re-layouts  8.11 us (6%)
    ppermute x12, waiting for transfers between devices, _swap(): return lax.ppermute(value, axis, [(i, i ^ flip) for i in range(size)])  55.9 us
    all_gather x1, blocking collectives, col_all_gather(): mine = lax.all_gather(block, axis, axis_index_groups=groups)  21.5 us
    ppermute x12, starting transfers between devices, _swap(): return lax.ppermute(value, axis, [(i, i ^ flip) for i in range(size)])  10.3 us
    pallas_call x1, Pallas kernels, outer_product_sum(): pl.pallas_call(_outer_kernel, grid=(n // block_n, m // block_m), in_specs...  10.3 us
    dot_general x1, matrix products, body(): lax.dot_general(full_grad, weight, (((1,), (1,)), ((), ())), preferred_el...  9.04 us
    dot_general x1, matrix products, body(): partial_value = jnp.dot(local_x, weight, preferred_element_type=jnp.float32)  8.99 us
    unnamed x10, local copies, waits for them, and re-layouts  2.78 us
  transfers between devices with their start and end apart: 12, of which 11 were waited for; matrix products, arithmetic and copies ran while one was open for 4% of the time, Pallas kernels for 8%

profile of v9, /device:TPU:0, one launch (start us, length us, event | category | flops | bytes accessed | tf_op | source)
XLA Modules:
  0.0 136.2 jit_solution(2538267132223260628)
XLA Ops:
  0.6 21.5 %all-gather = bf16[128,3072]{1,0:T(8,128)(2,1)S(1)} all-gather(bf16[32,3072]{1,0:T(8,128)(2,1)} %param.4), channel_id=2, replica_groups={{0,2,4,6},{1,3,5,7},{8,10,12,14},{9,11,13,15},{16,18,20,22},{17,19,21,2..., dimensions={0}, use_global_device_ids=true | all-gather | bytes 983040 | tf_op jit(solution)/shard_map/all_gather | solution.py:120
  22.1 2.3 %collective-permute-done = bf16[4,32,3072]{2,1,0:T(8,128)(2,1)S(1)} collective-permute-done((bf16[4,32,3072]{2,1,0:T(8,128)(2,1)S(1)}, bf16[4,32,3072]{2,1,0:T(8,128)(2,1)S(1)}, u32[]{:S(2)}, u32[]{:S(2)}) %collective-permute-start) | collective-permute-done | bytes 786464 | tf_op jit(solution)/shard_map/ppermute | solution.py:49
  24.8 9.0 %fusion.14 = f32[256,3072]{1,0:T(8,128)S(1)} fusion(bf16[256,3072]{1,0:T(8,128)(2,1)S(1)} %bitcast.78, bf16[3072,3072]{1,0:T(8,128)(2,1)} %param.5), kind=kOutput, calls=%fused_computation.49 | convolution fusion | flops 4831838208 | bytes 23592960 | tf_op jit(solution)/shard_map/dot_general | solution.py:158
  36.0 1.5 %collective-permute-start.1 = (bf16[2,64,1536]{2,1,0:T(8,128)(2,1)}, bf16[2,64,1536]{2,1,0:T(8,128)(2,1)S(1)}, u32[]{:S(2)}, u32[]{:S(2)}) collective-permute-start(bf16[2,64,1536]{2,1,0:T(8,128)(2,1)} %fusion.7), channel_id=1, source_target_pairs={{0,8},{8,0},{16,24},{24,16},{1,9},{9,1},{17,25},{25,17},{2,10},{10... | collective-permute-start | bytes 1179656 | tf_op jit(solution)/shard_map/ppermute | solution.py:49
  37.5 1.6 %collective-permute-start.3 = (bf16[2,64,1536]{2,1,0:T(8,128)(2,1)S(1)}, bf16[2,64,1536]{2,1,0:T(8,128)(2,1)S(1)}, u32[]{:S(2)}, u32[]{:S(2)}) collective-permute-start(bf16[2,64,1536]{2,1,0:T(8,128)(2,1)S(1)} %fusion.6), channel_id=1, source_target_pairs={{0,16},{8,24},{16,0},{24,8},{1,17},{9,25},{17,1},{25,9},{2,18},{10... | collective-permute-start | bytes 1179656 | tf_op jit(solution)/shard_map/ppermute | solution.py:49
  39.1 8.2 %collective-permute-done.1 = bf16[2,64,1536]{2,1,0:T(8,128)(2,1)S(1)} collective-permute-done((bf16[2,64,1536]{2,1,0:T(8,128)(2,1)}, bf16[2,64,1536]{2,1,0:T(8,128)(2,1)S(1)}, u32[]{:S(2)}, u32[]{:S(2)}) %collective-permute-start.1) | collective-permute-done | bytes 393248 | tf_op jit(solution)/shard_map/ppermute | solution.py:49
  48.6 1.6 %collective-permute-start.2 = (bf16[64,1536]{1,0:T(8,128)(2,1)S(1)}, bf16[64,1536]{1,0:T(8,128)(2,1)S(1)}, u32[]{:S(2)}, u32[]{:S(2)}) collective-permute-start(bf16[64,1536]{1,0:T(8,128)(2,1)S(1)} %fusion.9), channel_id=1, source_target_pairs={{0,16},{8,24},{16,0},{24,8},{1,17},{9,25},{17,1},{25,9},{2,18},{10... | collective-permute-start | bytes 589832 | tf_op jit(solution)/shard_map/ppermute | solution.py:49
  50.3 1.6 %collective-permute-start.4 = (bf16[64,1536]{1,0:T(8,128)(2,1)S(1)}, bf16[64,1536]{1,0:T(8,128)(2,1)S(1)}, u32[]{:S(2)}, u32[]{:S(2)}) collective-permute-start(bf16[64,1536]{1,0:T(8,128)(2,1)S(1)} %fusion.10), channel_id=1, source_target_pairs={{0,8},{8,0},{16,24},{24,16},{1,9},{9,1},{17,25},{25,17},{2,10},{10... | collective-permute-start | bytes 589832 | tf_op jit(solution)/shard_map/ppermute | solution.py:49
  51.9 2.9 %collective-permute-done.2 = bf16[64,1536]{1,0:T(8,128)(2,1)S(1)} collective-permute-done((bf16[64,1536]{1,0:T(8,128)(2,1)S(1)}, bf16[64,1536]{1,0:T(8,128)(2,1)S(1)}, u32[]{:S(2)}, u32[]{:S(2)}) %collective-permute-start.2) | collective-permute-done | bytes 196640 | tf_op jit(solution)/shard_map/ppermute | solution.py:49
  54.8 1.4 %collective-permute-done.4 = bf16[64,1536]{1,0:T(8,128)(2,1)S(1)} collective-permute-done((bf16[64,1536]{1,0:T(8,128)(2,1)S(1)}, bf16[64,1536]{1,0:T(8,128)(2,1)S(1)}, u32[]{:S(2)}, u32[]{:S(2)}) %collective-permute-start.4) | collective-permute-done | bytes 196640 | tf_op jit(solution)/shard_map/ppermute | solution.py:49
  56.3 2.2 %fusion.5 = (bf16[64,3072]{1,0:T(8,128)(2,1)S(1)}, bf16[64,3072]{1,0:T(8,128)(2,1)}) fusion(f32[64,1536]{1,0:T(8,128)S(1)} %bitcast_add_fusion.5, f32[64,1536]{1,0:T(8,128)S(1)} %bitcast_add_fusion.6, bf16[256,3072]{1,0:T(8,128)(2,1)} %param.7, s32[]{:T(128)S(6)} %select_n.121, f32[3072]{0:T(1024)S(1)} %copy-done.4), kind=kLoop, calls=%fused_computation.11 | loop fusion | flops 2949120 | bytes 1978372 | tf_op jit(solution)/shard_map/convert_element_type | solution.py:15
  58.5 1.6 %collective-permute-start.5 = (bf16[64,1536]{1,0:T(8,128)(2,1)S(1)}, bf16[64,1536]{1,0:T(8,128)(2,1)S(1)}, u32[]{:S(2)}, u32[]{:S(2)}) collective-permute-start(bf16[64,1536]{1,0:T(8,128)(2,1)S(1)} %get-tuple-element.24), channel_id=1, source_target_pairs={{0,8},{8,0},{16,24},{24,16},{1,9},{9,1},{17,25},{25,17},{2,10},{10... | collective-permute-start | bytes 589832 | tf_op jit(solution)/shard_map/ppermute | solution.py:49
  60.5 3.7 %collective-permute-done.5 = bf16[64,1536]{1,0:T(8,128)(2,1)S(1)} collective-permute-done((bf16[64,1536]{1,0:T(8,128)(2,1)S(1)}, bf16[64,1536]{1,0:T(8,128)(2,1)S(1)}, u32[]{:S(2)}, u32[]{:S(2)}) %collective-permute-start.5) | collective-permute-done | bytes 196640 | tf_op jit(solution)/shard_map/ppermute | solution.py:49
  64.2 1.6 %collective-permute-done.7 = bf16[64,1536]{1,0:T(8,128)(2,1)S(1)} collective-permute-done((bf16[64,1536]{1,0:T(8,128)(2,1)S(1)}, bf16[64,1536]{1,0:T(8,128)(2,1)S(1)}, u32[]{:S(2)}, u32[]{:S(2)}) %collective-permute-start.7) | collective-permute-done | bytes 196640 | tf_op jit(solution)/shard_map/ppermute | solution.py:49
  67.0 6.8 %collective-permute-done.8 = bf16[2,64,1536]{2,1,0:T(8,128)(2,1)S(1)} collective-permute-done((bf16[2,64,1536]{2,1,0:T(8,128)(2,1)S(1)}, bf16[2,64,1536]{2,1,0:T(8,128)(2,1)S(1)}, u32[]{:S(2)}, u32[]{:S(2)}) %collective-permute-start.8) | collective-permute-done | bytes 393248 | tf_op jit(solution)/shard_map/ppermute | solution.py:49
  75.7 9.0 %fusion.11 = f32[256,3072]{1,0:T(8,128)S(1)} fusion(bf16[3072,3072]{1,0:T(8,128)(2,1)} %param.5, bf16[256,1536]{1,0:T(8,128)(2,1)S(1)} %bitcast.70, bf16[256,1536]{1,0:T(8,128)(2,1)S(1)} %bitcast.73), kind=kOutput, calls=%fused_computation.46 | convolution fusion | flops 4834983936 | bytes 23592960 | tf_op jit(solution)/shard_map/dot_general | solution.py:165
  84.8 1.4 %dynamic-slice_bitcast_fusion = f32[4,32,3072]{2,1,0:T(8,128)} fusion(f32[4,2,32,3072]{3,2,1,0:T(8,128)S(1)} %bitcast.85, s32[]{:T(128)S(6)} %select_n.133), kind=kLoop, calls=%fused_computation.4 | loop fusion | bytes 3145732 | tf_op jit(solution)/shard_map/jit(dynamic_index_in_dim)/squeeze | solution.py:53
  87.0 1.6 %copy.17 = bf16[256,3072]{0,1:T(8,128)(2,1)} copy(bf16[256,3072]{1,0:T(8,128)(2,1)S(1)} %bitcast.79) | data formatting | bytes 3145728 | tf_op jit(solution)/shard_map/reshape | solution.py:122
  88.6 2.2 %collective-permute-done.9 = f32[4,32,3072]{2,1,0:T(8,128)} collective-permute-done((f32[4,32,3072]{2,1,0:T(8,128)}, f32[4,32,3072]{2,1,0:T(8,128)}, u32[]{:S(2)}, u32[]{:S(2)}) %collective-permute-start.9) | collective-permute-done | bytes 1572896 | tf_op jit(solution)/shard_map/ppermute | solution.py:49
  90.7 2.1 %bitcast_add_fusion = f32[4,32,3072]{2,1,0:T(8,128)S(1)} fusion(f32[4,32,3072]{2,1,0:T(8,128)} %collective-permute-done.9, f32[4,2,32,3072]{3,2,1,0:T(8,128)} %bitcast.86, s32[]{:T(128)S(6)} %select_n.132), kind=kLoop, calls=%fused_computation.3 | loop fusion | flops 393216 | bytes 4718596 | tf_op jit(solution)/shard_map/add | solution.py:132
  93.8 1.3 pad_maximum_fusion.g_ref
  95.1 10.3 %shard_map.75 = bf16[3072,3072]{1,0:T(8,128)(2,1)} custom-call(bf16[3072,256]{1,0:T(8,128)(2,1)} %bitcast.80, bf16[256,3072]{1,0:T(8,128)(2,1)} %pad_maximum_fusion.g_ref), custom_call_target="tpu_custom_call" | custom-call | flops 4831838208 | bytes 22020096 | tf_op jit(solution)/shard_map/pallas_call | solution.py:32
  105.4 8.3 %collective-permute-done.10 = f32[2,32,3072]{2,1,0:T(8,128)} collective-permute-done((f32[2,32,3072]{2,1,0:T(8,128)}, f32[2,32,3072]{2,1,0:T(8,128)}, u32[]{:S(2)}, u32[]{:S(2)}) %collective-permute-start.10) | collective-permute-done | bytes 786464 | tf_op jit(solution)/shard_map/ppermute | solution.py:49
  117.5 18.0 %collective-permute-done.11 = f32[32,3072]{1,0:T(8,128)S(1)} collective-permute-done((f32[32,3072]{1,0:T(8,128)S(1)}, f32[32,3072]{1,0:T(8,128)S(1)}, u32[]{:S(2)}, u32[]{:S(2)}) %collective-permute-start.11) | collective-permute-done | bytes 393248 | tf_op jit(solution)/shard_map/ppermute | solution.py:49
  (44 shorter events, 13.9 us)
Async XLA Ops:
  22.1 2.3 %collective-permute-start = (bf16[4,32,3072]{2,1,0:T(8,128)(2,1)S(1)}, bf16[4,32,3072]{2,1,0:T(8,128)(2,1)S(1)}, u32[]{:S(2)}, u32[]{:S(2)}) collective-permute-start(bf16[4,32,3072]{2,1,0:T(8,128)(2,1)S(1)} %bitcast.87), channel_id=1, source_target_pairs={{0,1},{1,0},{2,3},{3,2},{4,5},{5,4},{6,7},{7,6},{8,9},{9,8},{10,11... | collective-permute-start | bytes 2359304 | tf_op jit(solution)/shard_map/ppermute | solution.py:49
  34.1 1.1 copy-start
  36.0 11.4 %collective-permute-start.1 = (bf16[2,64,1536]{2,1,0:T(8,128)(2,1)}, bf16[2,64,1536]{2,1,0:T(8,128)(2,1)S(1)}, u32[]{:S(2)}, u32[]{:S(2)}) collective-permute-start(bf16[2,64,1536]{2,1,0:T(8,128)(2,1)} %fusion.7), channel_id=1, source_target_pairs={{0,8},{8,0},{16,24},{24,16},{1,9},{9,1},{17,25},{25,17},{2,10},{10... | collective-permute-start | bytes 1179656 | tf_op jit(solution)/shard_map/ppermute | solution.py:49
  37.5 12.7 %collective-permute-start.3 = (bf16[2,64,1536]{2,1,0:T(8,128)(2,1)S(1)}, bf16[2,64,1536]{2,1,0:T(8,128)(2,1)S(1)}, u32[]{:S(2)}, u32[]{:S(2)}) collective-permute-start(bf16[2,64,1536]{2,1,0:T(8,128)(2,1)S(1)} %fusion.6), channel_id=1, source_target_pairs={{0,16},{8,24},{16,0},{24,8},{1,17},{9,25},{17,1},{25,9},{2,18},{10... | collective-permute-start | bytes 1179656 | tf_op jit(solution)/shard_map/ppermute | solution.py:49
  48.6 6.2 %collective-permute-start.2 = (bf16[64,1536]{1,0:T(8,128)(2,1)S(1)}, bf16[64,1536]{1,0:T(8,128)(2,1)S(1)}, u32[]{:S(2)}, u32[]{:S(2)}) collective-permute-start(bf16[64,1536]{1,0:T(8,128)(2,1)S(1)} %fusion.9), channel_id=1, source_target_pairs={{0,16},{8,24},{16,0},{24,8},{1,17},{9,25},{17,1},{25,9},{2,18},{10... | collective-permute-start | bytes 589832 | tf_op jit(solution)/shard_map/ppermute | solution.py:49
  50.3 6.0 %copy-start.4 = (f32[3072]{0:T(1024)S(1)}, f32[3072]{0:T(1024)}, u32[]{:S(2)}) copy-start(f32[3072]{0:T(1024)} %param.6) | copy-start | bytes 36868
  50.3 5.9 %collective-permute-start.4 = (bf16[64,1536]{1,0:T(8,128)(2,1)S(1)}, bf16[64,1536]{1,0:T(8,128)(2,1)S(1)}, u32[]{:S(2)}, u32[]{:S(2)}) collective-permute-start(bf16[64,1536]{1,0:T(8,128)(2,1)S(1)} %fusion.10), channel_id=1, source_target_pairs={{0,8},{8,0},{16,24},{24,16},{1,9},{9,1},{17,25},{25,17},{2,10},{10... | collective-permute-start | bytes 589832 | tf_op jit(solution)/shard_map/ppermute | solution.py:49
  58.5 5.7 %collective-permute-start.5 = (bf16[64,1536]{1,0:T(8,128)(2,1)S(1)}, bf16[64,1536]{1,0:T(8,128)(2,1)S(1)}, u32[]{:S(2)}, u32[]{:S(2)}) collective-permute-start(bf16[64,1536]{1,0:T(8,128)(2,1)S(1)} %get-tuple-element.24), channel_id=1, source_target_pairs={{0,8},{8,0},{16,24},{24,16},{1,9},{9,1},{17,25},{25,17},{2,10},{10... | collective-permute-start | bytes 589832 | tf_op jit(solution)/shard_map/ppermute | solution.py:49
  60.0 5.7 %collective-permute-start.7 = (bf16[64,1536]{1,0:T(8,128)(2,1)S(1)}, bf16[64,1536]{1,0:T(8,128)(2,1)S(1)}, u32[]{:S(2)}, u32[]{:S(2)}) collective-permute-start(bf16[64,1536]{1,0:T(8,128)(2,1)S(1)} %get-tuple-element.25), channel_id=1, source_target_pairs={{0,16},{8,24},{16,0},{24,8},{1,17},{9,25},{17,1},{25,9},{2,18},{10... | collective-permute-start | bytes 589832 | tf_op jit(solution)/shard_map/ppermute | solution.py:49
  65.9 8.0 %collective-permute-start.8 = (bf16[2,64,1536]{2,1,0:T(8,128)(2,1)S(1)}, bf16[2,64,1536]{2,1,0:T(8,128)(2,1)S(1)}, u32[]{:S(2)}, u32[]{:S(2)}) collective-permute-start(bf16[2,64,1536]{2,1,0:T(8,128)(2,1)S(1)} %pad_maximum_fusion.3), channel_id=1, source_target_pairs={{0,8},{8,0},{16,24},{24,16},{1,9},{9,1},{17,25},{25,17},{2,10},{10... | collective-permute-start | bytes 1179656 | tf_op jit(solution)/shard_map/ppermute | solution.py:49
  66.4 7.9 %collective-permute-start.6 = (bf16[2,64,1536]{2,1,0:T(8,128)(2,1)S(1)}, bf16[2,64,1536]{2,1,0:T(8,128)(2,1)}, u32[]{:S(2)}, u32[]{:S(2)}) collective-permute-start(bf16[2,64,1536]{2,1,0:T(8,128)(2,1)S(1)} %pad_maximum_fusion.2), channel_id=1, source_target_pairs={{0,16},{8,24},{16,0},{24,8},{1,17},{9,25},{17,1},{25,9},{2,18},{10... | collective-permute-start | bytes 1179656 | tf_op jit(solution)/shard_map/ppermute | solution.py:49
  84.8 2.2 %copy-start.3 = (f32[256,3072]{1,0:T(8,128)}, f32[256,3072]{1,0:T(8,128)S(1)}, u32[]{:S(2)}) copy-start(f32[256,3072]{1,0:T(8,128)S(1)} %fusion.11) | copy-start | bytes 9437188
  87.0 3.8 %collective-permute-start.9 = (f32[4,32,3072]{2,1,0:T(8,128)}, f32[4,32,3072]{2,1,0:T(8,128)}, u32[]{:S(2)}, u32[]{:S(2)}) collective-permute-start(f32[4,32,3072]{2,1,0:T(8,128)} %dynamic-slice_bitcast_fusion), channel_id=1, source_target_pairs={{0,1},{1,0},{2,3},{3,2},{4,5},{5,4},{6,7},{7,6},{8,9},{9,8},{10,11... | collective-permute-start | bytes 4718600 | tf_op jit(solution)/shard_map/ppermute | solution.py:49
  93.8 19.9 %collective-permute-start.10 = (f32[2,32,3072]{2,1,0:T(8,128)}, f32[2,32,3072]{2,1,0:T(8,128)}, u32[]{:S(2)}, u32[]{:S(2)}) collective-permute-start(f32[2,32,3072]{2,1,0:T(8,128)} %dynamic-slice_bitcast_fusion.1), channel_id=1, source_target_pairs={{0,2},{1,3},{2,0},{3,1},{4,6},{5,7},{6,4},{7,5},{8,10},{9,11},{10,... | collective-permute-start | bytes 2359304 | tf_op jit(solution)/shard_map/ppermute | solution.py:49
  114.9 0.9 copy-start.1
  115.8 19.7 %copy-start.2 = (f32[2,32,3072]{2,1,0:T(8,128)S(1)}, f32[2,32,3072]{2,1,0:T(8,128)}, u32[]{:S(2)}) copy-start(f32[2,32,3072]{2,1,0:T(8,128)} %copy-done.1) | copy-start | bytes 2359300
  115.8 19.7 %collective-permute-start.11 = (f32[32,3072]{1,0:T(8,128)S(1)}, f32[32,3072]{1,0:T(8,128)S(1)}, u32[]{:S(2)}, u32[]{:S(2)}) collective-permute-start(f32[32,3072]{1,0:T(8,128)S(1)} %dynamic-slice_bitcast_fusion.2), channel_id=1, source_target_pairs={{0,4},{1,5},{2,6},{3,7},{4,0},{5,1},{6,2},{7,3},{8,12},{9,13},{10,... | collective-permute-start | bytes 1179656 | tf_op jit(solution)/shard_map/ppermute | solution.py:49

commit v10 on v8

--- a/solution.py
+++ b/solution.py
@@ -144,7 +144,8 @@
     for bit in range(levels):
         mine = (z >> bit) & 1
         t = jnp.moveaxis(cur, bits.index(bit), 0)
-        cur = _pick(mine, t) + _swap(_pick(1 - mine, t), axis, 2 << bit)
+        sent = _swap(_pick(1 - mine, t).astype(jnp.bfloat16), axis, 2 << bit)
+        cur = _pick(mine, t) + sent.astype(jnp.float32)
         bits.remove(bit)
     return cur.reshape(m, partial.shape[1])
 

time: 132 us -> 120 us (0.909)
  waiting for transfers between devices: 54.2 us -> 39.6 us
  local copies, waits for them, and re-layouts: 6.53 us -> 9.37 us
    ppermute x12, waiting for transfers between devices: 54.2 us -> 39.6 us  [_swap(): return lax.ppermute(value, axis, [(i, i ^ flip) for i in range(size)])]
    unnamed x6 -> x14, local copies, waits for them, and re-layouts: 1.52 us -> 4.24 us
  transfers between devices with their start and end apart: 12 -> 12, of which waited for: 11 -> 10; matrix products, arithmetic and copies ran while one was open for 4% -> 4% of each run, Pallas kernels for 8% -> 9%
where the time goes in v10:
time: 120 us
  waiting for transfers between devices  39.6 us (33%)
  blocking collectives  21.5 us (18%)
  matrix products  18 us (15%)
  starting transfers between devices  10.3 us (9%)
  Pallas kernels  10.3 us (9%)
  other arithmetic  10.2 us (8%)
  local copies, waits for them, and re-layouts  9.37 us (8%)
    ppermute x12, waiting for transfers between devices, _swap(): return lax.ppermute(value, axis, [(i, i ^ flip) for i in range(size)])  39.6 us
    all_gather x1, blocking collectives, col_all_gather(): mine = lax.all_gather(block, axis, axis_index_groups=groups)  21.5 us
    ppermute x12, starting transfers between devices, _swap(): return lax.ppermute(value, axis, [(i, i ^ flip) for i in range(size)])  10.3 us
    pallas_call x1, Pallas kernels, outer_product_sum(): pl.pallas_call(_outer_kernel, grid=(n // block_n, m // block_m), in_specs...  10.3 us
    dot_general x1, matrix products, body(): lax.dot_general(full_grad, weight, (((1,), (1,)), ((), ())), preferred_el...  9.04 us
    dot_general x1, matrix products, body(): partial_value = jnp.dot(local_x, weight, preferred_element_type=jnp.float32)  8.99 us
    unnamed x14, local copies, waits for them, and re-layouts  4.24 us
  transfers between devices with their start and end apart: 12, of which 10 were waited for; matrix products, arithmetic and copies ran while one was open for 4% of the time, Pallas kernels for 9%

profile of v10, /device:TPU:0, one launch (start us, length us, event | category | flops | bytes accessed | tf_op | source)
XLA Modules:
  0.0 120.1 jit_solution(6519028378491184679)
XLA Ops:
  0.6 21.5 %all-gather = bf16[128,3072]{1,0:T(8,128)(2,1)S(1)} all-gather(bf16[32,3072]{1,0:T(8,128)(2,1)} %param.4), channel_id=2, replica_groups={{0,2,4,6},{1,3,5,7},{8,10,12,14},{9,11,13,15},{16,18,20,22},{17,19,21,2..., dimensions={0}, use_global_device_ids=true | all-gather | bytes 983040 | tf_op jit(solution)/shard_map/all_gather | solution.py:120
  22.1 2.3 %collective-permute-done = bf16[4,32,3072]{2,1,0:T(8,128)(2,1)S(1)} collective-permute-done((bf16[4,32,3072]{2,1,0:T(8,128)(2,1)S(1)}, bf16[4,32,3072]{2,1,0:T(8,128)(2,1)S(1)}, u32[]{:S(2)}, u32[]{:S(2)}) %collective-permute-start) | collective-permute-done | bytes 786464 | tf_op jit(solution)/shard_map/ppermute | solution.py:49
  24.8 9.0 %fusion.16 = f32[256,3072]{1,0:T(8,128)S(1)} fusion(bf16[256,3072]{1,0:T(8,128)(2,1)S(1)} %bitcast.76, bf16[3072,3072]{1,0:T(8,128)(2,1)} %param.5), kind=kOutput, calls=%fused_computation.51 | convolution fusion | flops 4831838208 | bytes 23592960 | tf_op jit(solution)/shard_map/dot_general | solution.py:157
  36.0 1.5 %collective-permute-start.1 = (bf16[2,64,1536]{2,1,0:T(8,128)(2,1)}, bf16[2,64,1536]{2,1,0:T(8,128)(2,1)S(1)}, u32[]{:S(2)}, u32[]{:S(2)}) collective-permute-start(bf16[2,64,1536]{2,1,0:T(8,128)(2,1)} %fusion.8), channel_id=1, source_target_pairs={{0,8},{8,0},{16,24},{24,16},{1,9},{9,1},{17,25},{25,17},{2,10},{10... | collective-permute-start | bytes 1179656 | tf_op jit(solution)/shard_map/ppermute | solution.py:49
  37.5 1.6 %collective-permute-start.3 = (bf16[2,64,1536]{2,1,0:T(8,128)(2,1)S(1)}, bf16[2,64,1536]{2,1,0:T(8,128)(2,1)S(1)}, u32[]{:S(2)}, u32[]{:S(2)}) collective-permute-start(bf16[2,64,1536]{2,1,0:T(8,128)(2,1)S(1)} %fusion.6), channel_id=1, source_target_pairs={{0,16},{8,24},{16,0},{24,8},{1,17},{9,25},{17,1},{25,9},{2,18},{10... | collective-permute-start | bytes 1179656 | tf_op jit(solution)/shard_map/ppermute | solution.py:49
  39.1 8.2 %collective-permute-done.1 = bf16[2,64,1536]{2,1,0:T(8,128)(2,1)S(1)} collective-permute-done((bf16[2,64,1536]{2,1,0:T(8,128)(2,1)}, bf16[2,64,1536]{2,1,0:T(8,128)(2,1)S(1)}, u32[]{:S(2)}, u32[]{:S(2)}) %collective-permute-start.1) | collective-permute-done | bytes 393248 | tf_op jit(solution)/shard_map/ppermute | solution.py:49
  47.4 1.2 %bitcast_add_fusion.3 = f32[2,64,1536]{2,1,0:T(8,128)S(1)} fusion(bf16[2,64,1536]{2,1,0:T(8,128)(2,1)S(1)} %collective-permute-done.1, f32[2,2,64,1536]{3,2,1,0:T(8,128)} %bitcast.84, s32[]{:T(128)S(6)} %select_n.115), kind=kLoop, calls=%fused_computation.18 | loop fusion | flops 393216 | bytes 1966084 | tf_op jit(solution)/shard_map/add | solution.py:83
  48.6 1.6 %collective-permute-start.2 = (bf16[64,1536]{1,0:T(8,128)(2,1)S(1)}, bf16[64,1536]{1,0:T(8,128)(2,1)S(1)}, u32[]{:S(2)}, u32[]{:S(2)}) collective-permute-start(bf16[64,1536]{1,0:T(8,128)(2,1)S(1)} %fusion.10), channel_id=1, source_target_pairs={{0,16},{8,24},{16,0},{24,8},{1,17},{9,25},{17,1},{25,9},{2,18},{10... | collective-permute-start | bytes 589832 | tf_op jit(solution)/shard_map/ppermute | solution.py:49
  50.3 1.6 %collective-permute-start.4 = (bf16[64,1536]{1,0:T(8,128)(2,1)S(1)}, bf16[64,1536]{1,0:T(8,128)(2,1)S(1)}, u32[]{:S(2)}, u32[]{:S(2)}) collective-permute-start(bf16[64,1536]{1,0:T(8,128)(2,1)S(1)} %fusion.11), channel_id=1, source_target_pairs={{0,8},{8,0},{16,24},{24,16},{1,9},{9,1},{17,25},{25,17},{2,10},{10... | collective-permute-start | bytes 589832 | tf_op jit(solution)/shard_map/ppermute | solution.py:49
  51.9 2.9 %collective-permute-done.2 = bf16[64,1536]{1,0:T(8,128)(2,1)S(1)} collective-permute-done((bf16[64,1536]{1,0:T(8,128)(2,1)S(1)}, bf16[64,1536]{1,0:T(8,128)(2,1)S(1)}, u32[]{:S(2)}, u32[]{:S(2)}) %collective-permute-start.2) | collective-permute-done | bytes 196640 | tf_op jit(solution)/shard_map/ppermute | solution.py:49
  54.8 1.4 %collective-permute-done.4 = bf16[64,1536]{1,0:T(8,128)(2,1)S(1)} collective-permute-done((bf16[64,1536]{1,0:T(8,128)(2,1)S(1)}, bf16[64,1536]{1,0:T(8,128)(2,1)S(1)}, u32[]{:S(2)}, u32[]{:S(2)}) %collective-permute-start.4) | collective-permute-done | bytes 196640 | tf_op jit(solution)/shard_map/ppermute | solution.py:49
  56.3 2.2 %fusion.5 = (bf16[64,3072]{1,0:T(8,128)(2,1)S(1)}, bf16[64,3072]{1,0:T(8,128)(2,1)}) fusion(f32[64,1536]{1,0:T(8,128)S(1)} %bitcast_add_fusion.5, f32[64,1536]{1,0:T(8,128)S(1)} %bitcast_add_fusion.6, bf16[256,3072]{1,0:T(8,128)(2,1)} %param.7, s32[]{:T(128)S(6)} %select_n.121, f32[3072]{0:T(1024)S(1)} %copy-done.6), kind=kLoop, calls=%fused_computation.11 | loop fusion | flops 2949120 | bytes 1978372 | tf_op jit(solution)/shard_map/convert_element_type | solution.py:15
  58.5 1.6 %collective-permute-start.5 = (bf16[64,1536]{1,0:T(8,128)(2,1)S(1)}, bf16[64,1536]{1,0:T(8,128)(2,1)S(1)}, u32[]{:S(2)}, u32[]{:S(2)}) collective-permute-start(bf16[64,1536]{1,0:T(8,128)(2,1)S(1)} %get-tuple-element.20), channel_id=1, source_target_pairs={{0,8},{8,0},{16,24},{24,16},{1,9},{9,1},{17,25},{25,17},{2,10},{10... | collective-permute-start | bytes 589832 | tf_op jit(solution)/shard_map/ppermute | solution.py:49
  60.5 3.7 %collective-permute-done.5 = bf16[64,1536]{1,0:T(8,128)(2,1)S(1)} collective-permute-done((bf16[64,1536]{1,0:T(8,128)(2,1)S(1)}, bf16[64,1536]{1,0:T(8,128)(2,1)S(1)}, u32[]{:S(2)}, u32[]{:S(2)}) %collective-permute-start.5) | collective-permute-done | bytes 196640 | tf_op jit(solution)/shard_map/ppermute | solution.py:49
  64.2 1.6 %collective-permute-done.7 = bf16[64,1536]{1,0:T(8,128)(2,1)S(1)} collective-permute-done((bf16[64,1536]{1,0:T(8,128)(2,1)S(1)}, bf16[64,1536]{1,0:T(8,128)(2,1)S(1)}, u32[]{:S(2)}, u32[]{:S(2)}) %collective-permute-start.7) | collective-permute-done | bytes 196640 | tf_op jit(solution)/shard_map/ppermute | solution.py:49
  67.0 6.8 %collective-permute-done.8 = bf16[2,64,1536]{2,1,0:T(8,128)(2,1)S(1)} collective-permute-done((bf16[2,64,1536]{2,1,0:T(8,128)(2,1)S(1)}, bf16[2,64,1536]{2,1,0:T(8,128)(2,1)S(1)}, u32[]{:S(2)}, u32[]{:S(2)}) %collective-permute-start.8) | collective-permute-done | bytes 393248 | tf_op jit(solution)/shard_map/ppermute | solution.py:49
  75.7 9.0 %fusion.13 = f32[256,3072]{1,0:T(8,128)S(1)} fusion(bf16[3072,3072]{1,0:T(8,128)(2,1)} %param.5, bf16[256,1536]{1,0:T(8,128)(2,1)S(1)} %bitcast.70, bf16[256,1536]{1,0:T(8,128)(2,1)S(1)} %bitcast.73), kind=kOutput, calls=%fused_computation.48 | convolution fusion | flops 4834983936 | bytes 23592960 | tf_op jit(solution)/shard_map/dot_general | solution.py:163
  84.8 1.4 %dynamic-slice_bitcast_fusion = f32[4,32,3072]{2,1,0:T(8,128)} fusion(f32[4,2,32,3072]{3,2,1,0:T(8,128)S(1)} %bitcast.85, s32[]{:T(128)S(6)} %select_n.133), kind=kLoop, calls=%fused_computation.4 | loop fusion | bytes 3145732 | tf_op jit(solution)/shard_map/jit(dynamic_index_in_dim)/squeeze | solution.py:53
  87.0 3.7 %collective-permute-done.9 = f32[4,32,3072]{2,1,0:T(8,128)} collective-permute-done((f32[4,32,3072]{2,1,0:T(8,128)}, f32[4,32,3072]{2,1,0:T(8,128)}, u32[]{:S(2)}, u32[]{:S(2)}) %collective-permute-start.9) | collective-permute-done | bytes 1572896 | tf_op jit(solution)/shard_map/ppermute | solution.py:49
  90.7 2.1 %bitcast_add_fusion = f32[4,32,3072]{2,1,0:T(8,128)S(1)} fusion(f32[4,32,3072]{2,1,0:T(8,128)} %collective-permute-done.9, f32[4,2,32,3072]{3,2,1,0:T(8,128)} %bitcast.86, s32[]{:T(128)S(6)} %select_n.132), kind=kLoop, calls=%fused_computation.3 | loop fusion | flops 393216 | bytes 4718596 | tf_op jit(solution)/shard_map/add | solution.py:132
  94.7 1.6 %copy.17 = bf16[256,3072]{0,1:T(8,128)(2,1)} copy(bf16[256,3072]{1,0:T(8,128)(2,1)S(1)} %bitcast.77) | data formatting | bytes 3145728 | tf_op jit(solution)/shard_map/reshape | solution.py:122
  96.3 1.3 %pad_maximum_fusion.g_ref = bf16[256,3072]{1,0:T(8,128)(2,1)} fusion(bf16[256,1536]{1,0:T(8,128)(2,1)S(1)} %bitcast.71, bf16[256,1536]{1,0:T(8,128)(2,1)S(1)} %bitcast.74), kind=kLoop, calls=%fused_computation.2 | loop fusion | flops 3145728 | bytes 3145728 | tf_op jit(solution)/shard_map/concatenate | solution.py:112
  97.7 8.4 %collective-permute-done.10 = bf16[2,32,3072]{2,1,0:T(8,128)(2,1)S(1)} collective-permute-done((bf16[2,32,3072]{2,1,0:T(8,128)(2,1)}, bf16[2,32,3072]{2,1,0:T(8,128)(2,1)S(1)}, u32[]{:S(2)}, u32[]{:S(2)}) %collective-permute-start.10) | collective-permute-done | bytes 393248 | tf_op jit(solution)/shard_map/ppermute | solution.py:49
  108.0 10.3 %shard_map.75 = bf16[3072,3072]{1,0:T(8,128)(2,1)} custom-call(bf16[3072,256]{1,0:T(8,128)(2,1)} %bitcast.78, bf16[256,3072]{1,0:T(8,128)(2,1)} %pad_maximum_fusion.g_ref), custom_call_target="tpu_custom_call" | custom-call | flops 4831838208 | bytes 22020096 | tf_op jit(solution)/shard_map/pallas_call | solution.py:32
  (48 shorter events, 12.9 us)
Async XLA Ops:
  22.1 2.3 %collective-permute-start = (bf16[4,32,3072]{2,1,0:T(8,128)(2,1)S(1)}, bf16[4,32,3072]{2,1,0:T(8,128)(2,1)S(1)}, u32[]{:S(2)}, u32[]{:S(2)}) collective-permute-start(bf16[4,32,3072]{2,1,0:T(8,128)(2,1)S(1)} %bitcast.87), channel_id=1, source_target_pairs={{0,1},{1,0},{2,3},{3,2},{4,5},{5,4},{6,7},{7,6},{8,9},{9,8},{10,11... | collective-permute-start | bytes 2359304 | tf_op jit(solution)/shard_map/ppermute | solution.py:49
  34.1 1.1 copy-start.2
  36.0 11.4 %collective-permute-start.1 = (bf16[2,64,1536]{2,1,0:T(8,128)(2,1)}, bf16[2,64,1536]{2,1,0:T(8,128)(2,1)S(1)}, u32[]{:S(2)}, u32[]{:S(2)}) collective-permute-start(bf16[2,64,1536]{2,1,0:T(8,128)(2,1)} %fusion.8), channel_id=1, source_target_pairs={{0,8},{8,0},{16,24},{24,16},{1,9},{9,1},{17,25},{25,17},{2,10},{10... | collective-permute-start | bytes 1179656 | tf_op jit(solution)/shard_map/ppermute | solution.py:49
  37.5 12.7 %collective-permute-start.3 = (bf16[2,64,1536]{2,1,0:T(8,128)(2,1)S(1)}, bf16[2,64,1536]{2,1,0:T(8,128)(2,1)S(1)}, u32[]{:S(2)}, u32[]{:S(2)}) collective-permute-start(bf16[2,64,1536]{2,1,0:T(8,128)(2,1)S(1)} %fusion.6), channel_id=1, source_target_pairs={{0,16},{8,24},{16,0},{24,8},{1,17},{9,25},{17,1},{25,9},{2,18},{10... | collective-permute-start | bytes 1179656 | tf_op jit(solution)/shard_map/ppermute | solution.py:49
  48.6 6.2 %collective-permute-start.2 = (bf16[64,1536]{1,0:T(8,128)(2,1)S(1)}, bf16[64,1536]{1,0:T(8,128)(2,1)S(1)}, u32[]{:S(2)}, u32[]{:S(2)}) collective-permute-start(bf16[64,1536]{1,0:T(8,128)(2,1)S(1)} %fusion.10), channel_id=1, source_target_pairs={{0,16},{8,24},{16,0},{24,8},{1,17},{9,25},{17,1},{25,9},{2,18},{10... | collective-permute-start | bytes 589832 | tf_op jit(solution)/shard_map/ppermute | solution.py:49
  50.3 6.0 %copy-start.6 = (f32[3072]{0:T(1024)S(1)}, f32[3072]{0:T(1024)}, u32[]{:S(2)}) copy-start(f32[3072]{0:T(1024)} %param.6) | copy-start | bytes 36868
  50.3 5.9 %collective-permute-start.4 = (bf16[64,1536]{1,0:T(8,128)(2,1)S(1)}, bf16[64,1536]{1,0:T(8,128)(2,1)S(1)}, u32[]{:S(2)}, u32[]{:S(2)}) collective-permute-start(bf16[64,1536]{1,0:T(8,128)(2,1)S(1)} %fusion.11), channel_id=1, source_target_pairs={{0,8},{8,0},{16,24},{24,16},{1,9},{9,1},{17,25},{25,17},{2,10},{10... | collective-permute-start | bytes 589832 | tf_op jit(solution)/shard_map/ppermute | solution.py:49
  58.5 5.7 %collective-permute-start.5 = (bf16[64,1536]{1,0:T(8,128)(2,1)S(1)}, bf16[64,1536]{1,0:T(8,128)(2,1)S(1)}, u32[]{:S(2)}, u32[]{:S(2)}) collective-permute-start(bf16[64,1536]{1,0:T(8,128)(2,1)S(1)} %get-tuple-element.20), channel_id=1, source_target_pairs={{0,8},{8,0},{16,24},{24,16},{1,9},{9,1},{17,25},{25,17},{2,10},{10... | collective-permute-start | bytes 589832 | tf_op jit(solution)/shard_map/ppermute | solution.py:49
  60.0 5.7 %collective-permute-start.7 = (bf16[64,1536]{1,0:T(8,128)(2,1)S(1)}, bf16[64,1536]{1,0:T(8,128)(2,1)S(1)}, u32[]{:S(2)}, u32[]{:S(2)}) collective-permute-start(bf16[64,1536]{1,0:T(8,128)(2,1)S(1)} %get-tuple-element.21), channel_id=1, source_target_pairs={{0,16},{8,24},{16,0},{24,8},{1,17},{9,25},{17,1},{25,9},{2,18},{10... | collective-permute-start | bytes 589832 | tf_op jit(solution)/shard_map/ppermute | solution.py:49
  65.9 8.0 %collective-permute-start.8 = (bf16[2,64,1536]{2,1,0:T(8,128)(2,1)S(1)}, bf16[2,64,1536]{2,1,0:T(8,128)(2,1)S(1)}, u32[]{:S(2)}, u32[]{:S(2)}) collective-permute-start(bf16[2,64,1536]{2,1,0:T(8,128)(2,1)S(1)} %pad_maximum_fusion.3), channel_id=1, source_target_pairs={{0,8},{8,0},{16,24},{24,16},{1,9},{9,1},{17,25},{25,17},{2,10},{10... | collective-permute-start | bytes 1179656 | tf_op jit(solution)/shard_map/ppermute | solution.py:49
  66.4 7.9 %collective-permute-start.6 = (bf16[2,64,1536]{2,1,0:T(8,128)(2,1)S(1)}, bf16[2,64,1536]{2,1,0:T(8,128)(2,1)}, u32[]{:S(2)}, u32[]{:S(2)}) collective-permute-start(bf16[2,64,1536]{2,1,0:T(8,128)(2,1)S(1)} %pad_maximum_fusion.2), channel_id=1, source_target_pairs={{0,16},{8,24},{16,0},{24,8},{1,17},{9,25},{17,1},{25,9},{2,18},{10... | collective-permute-start | bytes 1179656 | tf_op jit(solution)/shard_map/ppermute | solution.py:49
  84.8 2.2 %copy-start.3 = (f32[256,3072]{1,0:T(8,128)}, f32[256,3072]{1,0:T(8,128)S(1)}, u32[]{:S(2)}) copy-start(f32[256,3072]{1,0:T(8,128)S(1)} %fusion.13) | copy-start | bytes 9437188
  87.0 3.8 %collective-permute-start.9 = (f32[4,32,3072]{2,1,0:T(8,128)}, f32[4,32,3072]{2,1,0:T(8,128)}, u32[]{:S(2)}, u32[]{:S(2)}) collective-permute-start(f32[4,32,3072]{2,1,0:T(8,128)} %dynamic-slice_bitcast_fusion), channel_id=1, source_target_pairs={{0,1},{1,0},{2,3},{3,2},{4,5},{5,4},{6,7},{7,6},{8,9},{9,8},{10,11... | collective-permute-start | bytes 4718600 | tf_op jit(solution)/shard_map/ppermute | solution.py:49
  92.8 1.1 copy-start
  94.7 11.4 %collective-permute-start.10 = (bf16[2,32,3072]{2,1,0:T(8,128)(2,1)}, bf16[2,32,3072]{2,1,0:T(8,128)(2,1)S(1)}, u32[]{:S(2)}, u32[]{:S(2)}) collective-permute-start(bf16[2,32,3072]{2,1,0:T(8,128)(2,1)} %fusion.7), channel_id=1, source_target_pairs={{0,2},{1,3},{2,0},{3,1},{4,6},{5,7},{6,4},{7,5},{8,10},{9,11},{10,... | collective-permute-start | bytes 1179656 | tf_op jit(solution)/shard_map/ppermute | solution.py:49
  96.3 9.8 %copy-start.1 = (f32[4,32,3072]{2,1,0:T(8,128)S(1)}, f32[4,32,3072]{2,1,0:T(8,128)}, u32[]{:S(2)}) copy-start(f32[4,32,3072]{2,1,0:T(8,128)} %copy-done) | copy-start | bytes 4718596
  106.2 0.9 copy-start.4
  107.1 12.0 %collective-permute-start.11 = (bf16[32,3072]{1,0:T(8,128)(2,1)S(1)}, bf16[32,3072]{1,0:T(8,128)(2,1)S(1)}, u32[]{:S(2)}, u32[]{:S(2)}) collective-permute-start(bf16[32,3072]{1,0:T(8,128)(2,1)S(1)} %fusion.12), channel_id=1, source_target_pairs={{0,4},{1,5},{2,6},{3,7},{4,0},{5,1},{6,2},{7,3},{8,12},{9,13},{10,... | collective-permute-start | bytes 589832 | tf_op jit(solution)/shard_map/ppermute | solution.py:49
  118.2 1.1 copy-start.5

commit v11 on v8

--- a/solution.py
+++ b/solution.py
@@ -122,14 +122,13 @@
     return jnp.swapaxes(both, 0, 1).reshape(n * block.shape[0], block.shape[1])
 
 
-def col_reduce_scatter(partial, axis="col"):
+def col_reduce_scatter(rows_of, axis="col"):
     n = lax.axis_size(axis)
-    if n % 2:
-        return lax.psum_scatter(partial, axis, scatter_dimension=0, tiled=True)
-    m = partial.shape[0] // n
     k = lax.axis_index(axis) % 2
-    by_core = jnp.swapaxes(partial.reshape(n // 2, 2, m, partial.shape[1]), 0, 1)
-    chip = _pick(k, by_core) + _swap(_pick(1 - k, by_core), axis, 1)
+    sent = rows_of(1 - k)
+    m = sent.shape[0] * 2 // n
+    kept = lax.optimization_barrier(rows_of(k))
+    chip = (kept + _swap(sent, axis, 1)).reshape(n // 2, m, sent.shape[1])
     chips = n // 2
     z = lax.axis_index(axis) // 2
     if chips & (chips - 1):
@@ -139,14 +138,15 @@
             total = total + lax.ppermute(_pick((z + d) % chips, chip), axis, pairs)
         return total
     levels = chips.bit_length() - 1
-    cur = chip.reshape([2] * levels + [m, partial.shape[1]])
+    cur = chip.reshape([2] * levels + [m, sent.shape[1]])
     bits = list(range(levels))[::-1]
     for bit in range(levels):
         mine = (z >> bit) & 1
         t = jnp.moveaxis(cur, bits.index(bit), 0)
-        cur = _pick(mine, t) + _swap(_pick(1 - mine, t), axis, 2 << bit)
+        moved = _swap(_pick(1 - mine, t).astype(jnp.bfloat16), axis, 2 << bit)
+        cur = _pick(mine, t) + moved.astype(jnp.float32)
         bits.remove(bit)
-    return cur.reshape(m, partial.shape[1])
+    return cur.reshape(m, sent.shape[1])
 
 
 def body(tokens, weight, bias, cotangent):
@@ -158,11 +158,27 @@
     my_cot = lax.dynamic_slice_in_dim(cotangent, first_row, my_rows, 0)
     hidden, my_grad = activate(preact, my_cot)
     full_grad = row_all_gather(my_grad)
-    grad_tokens = col_reduce_scatter(
-        lax.dot_general(
-            full_grad, weight, (((1,), (1,)), ((), ())), preferred_element_type=jnp.float32
+    cols = lax.axis_size("col")
+    if cols % 2:
+        grad_tokens = lax.psum_scatter(
+            lax.dot_general(
+                full_grad, weight, (((1,), (1,)), ((), ())), preferred_element_type=jnp.float32
+            ),
+            "col",
+            scatter_dimension=0,
+            tiled=True,
         )
-    ).astype(jnp.bfloat16)
+    else:
+        by_core = jnp.swapaxes(full_grad.reshape(cols // 2, 2, -1, full_grad.shape[1]), 0, 1)
+
+        def rows_of(j):
+            g = _pick(j, by_core).reshape(-1, full_grad.shape[1])
+            return lax.dot_general(
+                g, weight, (((1,), (1,)), ((), ())), preferred_element_type=jnp.float32
+            )
+
+        grad_tokens = col_reduce_scatter(rows_of)
+    grad_tokens = grad_tokens.astype(jnp.bfloat16)
     grad_weight = outer_product_sum(local_x.T, full_grad)
     grad_bias = jnp.sum(full_grad.astype(jnp.float32), axis=0)
     return (hidden, grad_tokens, grad_weight, grad_bias)

time: 132 us -> 134 us (1.015)
  waiting for transfers between devices: 54.2 us -> 34 us
  matrix products: 18.6 us -> 37.2 us
  starting transfers between devices: 10.6 us -> 12.4 us
    ppermute x12, waiting for transfers between devices: 54.2 us -> 34 us  [_swap(): return lax.ppermute(value, axis, [(i, i ^ flip) for i in range(size)])]
    dot_general x1 -> x2, matrix products: 9.04 us -> 28.2 us  [rows_of(): lax.dot_general(g, weight, (((1,), (1,)), ((), ())), preferred_element_ty...]
    unnamed x6 -> x12, local copies, waits for them, and re-layouts: 1.52 us -> 3.44 us
    ppermute x12, starting transfers between devices: 10.6 us -> 12.4 us  [_swap(): return lax.ppermute(value, axis, [(i, i ^ flip) for i in range(size)])]
    concatenate x1 -> x2, other arithmetic: 1.38 us -> 2.7 us  [row_all_gather(): return jnp.concatenate(outs, axis=1)]
  transfers between devices with their start and end apart: 12 -> 12, of which waited for: 11 -> 9; matrix products, arithmetic and copies ran while one was open for 4% -> 15% of each run, Pallas kernels for 8% -> 8%
where the time goes in v11:
time: 134 us
  matrix products  37.2 us (28%)
  waiting for transfers between devices  34 us (25%)
  blocking collectives  21.5 us (16%)
  starting transfers between devices  12.4 us (9%)
  other arithmetic  10.5 us (8%)
  Pallas kernels  10.3 us (8%)
  local copies, waits for them, and re-layouts  7.11 us (5%)
    ppermute x12, waiting for transfers between devices, _swap(): return lax.ppermute(value, axis, [(i, i ^ flip) for i in range(size)])  34 us
    dot_general x2, matrix products, rows_of(): lax.dot_general(g, weight, (((1,), (1,)), ((), ())), preferred_element_ty...  28.2 us
    all_gather x1, blocking collectives, col_all_gather(): mine = lax.all_gather(block, axis, axis_index_groups=groups)  21.5 us
    ppermute x12, starting transfers between devices, _swap(): return lax.ppermute(value, axis, [(i, i ^ flip) for i in range(size)])  12.4 us
    pallas_call x1, Pallas kernels, outer_product_sum(): pl.pallas_call(_outer_kernel, grid=(n // block_n, m // block_m), in_specs...  10.3 us
    dot_general x1, matrix products, body(): partial_value = jnp.dot(local_x, weight, preferred_element_type=jnp.float32)  8.99 us
    unnamed x12, local copies, waits for them, and re-layouts  3.44 us
    concatenate x2, other arithmetic, row_all_gather(): return jnp.concatenate(outs, axis=1)  2.7 us
  transfers between devices with their start and end apart: 12, of which 9 were waited for; matrix products, arithmetic and copies ran while one was open for 15% of the time, Pallas kernels for 8%

profile of v11, /device:TPU:0, one launch (start us, length us, event | category | flops | bytes accessed | tf_op | source)
XLA Modules:
  0.0 133.8 jit_solution(2603825793926922533)
XLA Ops:
  0.6 21.5 %all-gather = bf16[128,3072]{1,0:T(8,128)(2,1)S(1)} all-gather(bf16[32,3072]{1,0:T(8,128)(2,1)} %param.4), channel_id=2, replica_groups={{0,2,4,6},{1,3,5,7},{8,10,12,14},{9,11,13,15},{16,18,20,22},{17,19,21,2..., dimensions={0}, use_global_device_ids=true | all-gather | bytes 983040 | tf_op jit(solution)/shard_map/all_gather | solution.py:120
  22.1 2.3 %collective-permute-done = bf16[4,32,3072]{2,1,0:T(8,128)(2,1)S(1)} collective-permute-done((bf16[4,32,3072]{2,1,0:T(8,128)(2,1)S(1)}, bf16[4,32,3072]{2,1,0:T(8,128)(2,1)S(1)}, u32[]{:S(2)}, u32[]{:S(2)}) %collective-permute-start) | collective-permute-done | bytes 786464 | tf_op jit(solution)/shard_map/ppermute | solution.py:49
  24.8 9.0 %fusion.17 = f32[256,3072]{1,0:T(8,128)S(1)} fusion(bf16[256,3072]{1,0:T(8,128)(2,1)S(1)} %bitcast.85, bf16[3072,3072]{1,0:T(8,128)(2,1)} %param.5), kind=kOutput, calls=%fused_computation.54 | convolution fusion | flops 4831838208 | bytes 23592960 | tf_op jit(solution)/shard_map/dot_general | solution.py:156
  36.0 1.5 %collective-permute-start.1 = (bf16[2,64,1536]{2,1,0:T(8,128)(2,1)}, bf16[2,64,1536]{2,1,0:T(8,128)(2,1)S(1)}, u32[]{:S(2)}, u32[]{:S(2)}) collective-permute-start(bf16[2,64,1536]{2,1,0:T(8,128)(2,1)} %fusion.9), channel_id=1, source_target_pairs={{0,8},{8,0},{16,24},{24,16},{1,9},{9,1},{17,25},{25,17},{2,10},{10... | collective-permute-start | bytes 1179656 | tf_op jit(solution)/shard_map/ppermute | solution.py:49
  37.5 1.6 %collective-permute-start.3 = (bf16[2,64,1536]{2,1,0:T(8,128)(2,1)S(1)}, bf16[2,64,1536]{2,1,0:T(8,128)(2,1)S(1)}, u32[]{:S(2)}, u32[]{:S(2)}) collective-permute-start(bf16[2,64,1536]{2,1,0:T(8,128)(2,1)S(1)} %fusion.8), channel_id=1, source_target_pairs={{0,16},{8,24},{16,0},{24,8},{1,17},{9,25},{17,1},{25,9},{2,18},{10... | collective-permute-start | bytes 1179656 | tf_op jit(solution)/shard_map/ppermute | solution.py:49
  39.1 8.2 %collective-permute-done.1 = bf16[2,64,1536]{2,1,0:T(8,128)(2,1)S(1)} collective-permute-done((bf16[2,64,1536]{2,1,0:T(8,128)(2,1)}, bf16[2,64,1536]{2,1,0:T(8,128)(2,1)S(1)}, u32[]{:S(2)}, u32[]{:S(2)}) %collective-permute-start.1) | collective-permute-done | bytes 393248 | tf_op jit(solution)/shard_map/ppermute | solution.py:49
  48.6 1.6 %collective-permute-start.2 = (bf16[64,1536]{1,0:T(8,128)(2,1)S(1)}, bf16[64,1536]{1,0:T(8,128)(2,1)S(1)}, u32[]{:S(2)}, u32[]{:S(2)}) collective-permute-start(bf16[64,1536]{1,0:T(8,128)(2,1)S(1)} %fusion.12), channel_id=1, source_target_pairs={{0,16},{8,24},{16,0},{24,8},{1,17},{9,25},{17,1},{25,9},{2,18},{10... | collective-permute-start | bytes 589832 | tf_op jit(solution)/shard_map/ppermute | solution.py:49
  50.3 1.6 %collective-permute-start.4 = (bf16[64,1536]{1,0:T(8,128)(2,1)S(1)}, bf16[64,1536]{1,0:T(8,128)(2,1)S(1)}, u32[]{:S(2)}, u32[]{:S(2)}) collective-permute-start(bf16[64,1536]{1,0:T(8,128)(2,1)S(1)} %fusion.13), channel_id=1, source_target_pairs={{0,8},{8,0},{16,24},{24,16},{1,9},{9,1},{17,25},{25,17},{2,10},{10... | collective-permute-start | bytes 589832 | tf_op jit(solution)/shard_map/ppermute | solution.py:49
  51.9 2.9 %collective-permute-done.2 = bf16[64,1536]{1,0:T(8,128)(2,1)S(1)} collective-permute-done((bf16[64,1536]{1,0:T(8,128)(2,1)S(1)}, bf16[64,1536]{1,0:T(8,128)(2,1)S(1)}, u32[]{:S(2)}, u32[]{:S(2)}) %collective-permute-start.2) | collective-permute-done | bytes 196640 | tf_op jit(solution)/shard_map/ppermute | solution.py:49
  54.8 1.4 %collective-permute-done.4 = bf16[64,1536]{1,0:T(8,128)(2,1)S(1)} collective-permute-done((bf16[64,1536]{1,0:T(8,128)(2,1)S(1)}, bf16[64,1536]{1,0:T(8,128)(2,1)S(1)}, u32[]{:S(2)}, u32[]{:S(2)}) %collective-permute-start.4) | collective-permute-done | bytes 196640 | tf_op jit(solution)/shard_map/ppermute | solution.py:49
  56.3 2.2 %fusion.5 = (bf16[64,3072]{1,0:T(8,128)(2,1)S(1)}, bf16[64,3072]{1,0:T(8,128)(2,1)}) fusion(f32[64,1536]{1,0:T(8,128)S(1)} %bitcast_add_fusion.4, f32[64,1536]{1,0:T(8,128)S(1)} %bitcast_add_fusion.5, bf16[256,3072]{1,0:T(8,128)(2,1)} %param.7, s32[]{:T(128)S(6)} %select_n.121, f32[3072]{0:T(1024)S(1)} %copy-done.5), kind=kLoop, calls=%fused_computation.13 | loop fusion | flops 2949120 | bytes 1978372 | tf_op jit(solution)/shard_map/convert_element_type | solution.py:15
  59.0 1.5 %collective-permute-start.5 = (bf16[64,1536]{1,0:T(8,128)(2,1)S(1)}, bf16[64,1536]{1,0:T(8,128)(2,1)S(1)}, u32[]{:S(2)}, u32[]{:S(2)}) collective-permute-start(bf16[64,1536]{1,0:T(8,128)(2,1)S(1)} %get-tuple-element.23), channel_id=1, source_target_pairs={{0,8},{8,0},{16,24},{24,16},{1,9},{9,1},{17,25},{25,17},{2,10},{10... | collective-permute-start | bytes 589832 | tf_op jit(solution)/shard_map/ppermute | solution.py:49
  60.5 3.7 %collective-permute-done.7 = bf16[64,1536]{1,0:T(8,128)(2,1)S(1)} collective-permute-done((bf16[64,1536]{1,0:T(8,128)(2,1)S(1)}, bf16[64,1536]{1,0:T(8,128)(2,1)S(1)}, u32[]{:S(2)}, u32[]{:S(2)}) %collective-permute-start.7) | collective-permute-done | bytes 196640 | tf_op jit(solution)/shard_map/ppermute | solution.py:49
  64.8 1.6 %collective-permute-start.6 = (bf16[2,64,1536]{2,1,0:T(8,128)(2,1)S(1)}, bf16[2,64,1536]{2,1,0:T(8,128)(2,1)S(1)}, u32[]{:S(2)}, u32[]{:S(2)}) collective-permute-start(bf16[2,64,1536]{2,1,0:T(8,128)(2,1)S(1)} %pad_maximum_fusion.3), channel_id=1, source_target_pairs={{0,16},{8,24},{16,0},{24,8},{1,17},{9,25},{17,1},{25,9},{2,18},{10... | collective-permute-start | bytes 1179656 | tf_op jit(solution)/shard_map/ppermute | solution.py:49
  66.5 1.6 %collective-permute-start.8 = (bf16[2,64,1536]{2,1,0:T(8,128)(2,1)S(1)}, bf16[2,64,1536]{2,1,0:T(8,128)(2,1)S(1)}, u32[]{:S(2)}, u32[]{:S(2)}) collective-permute-start(bf16[2,64,1536]{2,1,0:T(8,128)(2,1)S(1)} %pad_maximum_fusion.4), channel_id=1, source_target_pairs={{0,8},{8,0},{16,24},{24,16},{1,9},{9,1},{17,25},{25,17},{2,10},{10... | collective-permute-start | bytes 1179656 | tf_op jit(solution)/shard_map/ppermute | solution.py:49
  68.1 4.6 %collective-permute-done.6 = bf16[2,64,1536]{2,1,0:T(8,128)(2,1)S(1)} collective-permute-done((bf16[2,64,1536]{2,1,0:T(8,128)(2,1)S(1)}, bf16[2,64,1536]{2,1,0:T(8,128)(2,1)S(1)}, u32[]{:S(2)}, u32[]{:S(2)}) %collective-permute-start.6) | collective-permute-done | bytes 393248 | tf_op jit(solution)/shard_map/ppermute | solution.py:49
  72.8 1.5 %collective-permute-done.8 = bf16[2,64,1536]{2,1,0:T(8,128)(2,1)S(1)} collective-permute-done((bf16[2,64,1536]{2,1,0:T(8,128)(2,1)S(1)}, bf16[2,64,1536]{2,1,0:T(8,128)(2,1)S(1)}, u32[]{:S(2)}, u32[]{:S(2)}) %collective-permute-start.8) | collective-permute-done | bytes 393248 | tf_op jit(solution)/shard_map/ppermute | solution.py:49
  74.5 1.4 %fusion.6 = (bf16[4,1,32,3072]{3,2,1,0:T(8,128)(2,1)}, bf16[4,1,32,3072]{3,2,1,0:T(8,128)(2,1)}) fusion(s32[]{:T(128)S(6)} %select_n.133, bf16[4,2,32,1536]{3,2,1,0:T(8,128)(2,1)S(1)} %bitcast.79, bf16[4,2,32,1536]{3,2,1,0:T(8,128)(2,1)S(1)} %bitcast.82, s32[]{:T(128)S(6)} %select_n.132), kind=kLoop, calls=%fused_computation.14 | loop fusion | flops 3145728 | bytes 3145736 | tf_op jit(solution)/shard_map/concatenate | solution.py:112
  75.8 14.1 %fusion.19 = f32[128,3072]{1,0:T(8,128)} fusion(bf16[128,3072]{1,0:T(8,128)(2,1)} %bitcast.97, bf16[3072,3072]{1,0:T(8,128)(2,1)} %param.5), kind=kOutput, calls=%fused_computation.56 | convolution fusion | flops 2415919104 | bytes 21233664 | tf_op jit(solution)/shard_map/dot_general | solution.py:176
  90.0 14.1 %fusion.18 = f32[128,3072]{1,0:T(8,128)} fusion(bf16[128,3072]{1,0:T(8,128)(2,1)} %bitcast.96, bf16[3072,3072]{1,0:T(8,128)(2,1)} %param.5), kind=kOutput, calls=%fused_computation.55 | convolution fusion | flops 2415919104 | bytes 21233664 | tf_op jit(solution)/shard_map/dot_general | solution.py:176
  104.1 2.1 %add.108 = f32[128,3072]{1,0:T(8,128)S(1)} add(f32[128,3072]{1,0:T(8,128)} %fusion.18, f32[128,3072]{1,0:T(8,128)} %collective-permute-done.9) | non-fusion elementwise | flops 393216 | bytes 4718592 | tf_op jit(solution)/shard_map/add | solution.py:131
  108.0 1.6 %copy.19 = bf16[256,3072]{0,1:T(8,128)(2,1)} copy(bf16[256,3072]{1,0:T(8,128)(2,1)S(1)} %bitcast.86) | data formatting | bytes 3145728 | tf_op jit(solution)/shard_map/reshape | solution.py:122
  111.0 8.8 %collective-permute-done.10 = bf16[2,32,3072]{2,1,0:T(8,128)(2,1)S(1)} collective-permute-done((bf16[2,32,3072]{2,1,0:T(8,128)(2,1)}, bf16[2,32,3072]{2,1,0:T(8,128)(2,1)S(1)}, u32[]{:S(2)}, u32[]{:S(2)}) %collective-permute-start.10) | collective-permute-done | bytes 393248 | tf_op jit(solution)/shard_map/ppermute | solution.py:49
  121.7 10.3 %shard_map.75 = bf16[3072,3072]{1,0:T(8,128)(2,1)} custom-call(bf16[3072,256]{1,0:T(8,128)(2,1)} %bitcast.87, bf16[256,3072]{1,0:T(8,128)(2,1)} %pad_maximum_fusion.g_ref), custom_call_target="tpu_custom_call" | custom-call | flops 4831838208 | bytes 22020096 | tf_op jit(solution)/shard_map/pallas_call | solution.py:32
  (47 shorter events, 12.5 us)
Async XLA Ops:
  22.1 2.3 %collective-permute-start = (bf16[4,32,3072]{2,1,0:T(8,128)(2,1)S(1)}, bf16[4,32,3072]{2,1,0:T(8,128)(2,1)S(1)}, u32[]{:S(2)}, u32[]{:S(2)}) collective-permute-start(bf16[4,32,3072]{2,1,0:T(8,128)(2,1)S(1)} %bitcast.94), channel_id=1, source_target_pairs={{0,1},{1,0},{2,3},{3,2},{4,5},{5,4},{6,7},{7,6},{8,9},{9,8},{10,11... | collective-permute-start | bytes 2359304 | tf_op jit(solution)/shard_map/ppermute | solution.py:49
  34.1 1.1 copy-start
  36.0 11.4 %collective-permute-start.1 = (bf16[2,64,1536]{2,1,0:T(8,128)(2,1)}, bf16[2,64,1536]{2,1,0:T(8,128)(2,1)S(1)}, u32[]{:S(2)}, u32[]{:S(2)}) collective-permute-start(bf16[2,64,1536]{2,1,0:T(8,128)(2,1)} %fusion.9), channel_id=1, source_target_pairs={{0,8},{8,0},{16,24},{24,16},{1,9},{9,1},{17,25},{25,17},{2,10},{10... | collective-permute-start | bytes 1179656 | tf_op jit(solution)/shard_map/ppermute | solution.py:49
  37.5 12.7 %collective-permute-start.3 = (bf16[2,64,1536]{2,1,0:T(8,128)(2,1)S(1)}, bf16[2,64,1536]{2,1,0:T(8,128)(2,1)S(1)}, u32[]{:S(2)}, u32[]{:S(2)}) collective-permute-start(bf16[2,64,1536]{2,1,0:T(8,128)(2,1)S(1)} %fusion.8), channel_id=1, source_target_pairs={{0,16},{8,24},{16,0},{24,8},{1,17},{9,25},{17,1},{25,9},{2,18},{10... | collective-permute-start | bytes 1179656 | tf_op jit(solution)/shard_map/ppermute | solution.py:49
  48.6 6.2 %collective-permute-start.2 = (bf16[64,1536]{1,0:T(8,128)(2,1)S(1)}, bf16[64,1536]{1,0:T(8,128)(2,1)S(1)}, u32[]{:S(2)}, u32[]{:S(2)}) collective-permute-start(bf16[64,1536]{1,0:T(8,128)(2,1)S(1)} %fusion.12), channel_id=1, source_target_pairs={{0,16},{8,24},{16,0},{24,8},{1,17},{9,25},{17,1},{25,9},{2,18},{10... | collective-permute-start | bytes 589832 | tf_op jit(solution)/shard_map/ppermute | solution.py:49
  50.3 6.0 %copy-start.5 = (f32[3072]{0:T(1024)S(1)}, f32[3072]{0:T(1024)}, u32[]{:S(2)}) copy-start(f32[3072]{0:T(1024)} %param.6) | copy-start | bytes 36868
  50.3 5.9 %collective-permute-start.4 = (bf16[64,1536]{1,0:T(8,128)(2,1)S(1)}, bf16[64,1536]{1,0:T(8,128)(2,1)S(1)}, u32[]{:S(2)}, u32[]{:S(2)}) collective-permute-start(bf16[64,1536]{1,0:T(8,128)(2,1)S(1)} %fusion.13), channel_id=1, source_target_pairs={{0,8},{8,0},{16,24},{24,16},{1,9},{9,1},{17,25},{25,17},{2,10},{10... | collective-permute-start | bytes 589832 | tf_op jit(solution)/shard_map/ppermute | solution.py:49
  58.5 5.7 %collective-permute-start.7 = (bf16[64,1536]{1,0:T(8,128)(2,1)S(1)}, bf16[64,1536]{1,0:T(8,128)(2,1)S(1)}, u32[]{:S(2)}, u32[]{:S(2)}) collective-permute-start(bf16[64,1536]{1,0:T(8,128)(2,1)S(1)} %get-tuple-element.22), channel_id=1, source_target_pairs={{0,16},{8,24},{16,0},{24,8},{1,17},{9,25},{17,1},{25,9},{2,18},{10... | collective-permute-start | bytes 589832 | tf_op jit(solution)/shard_map/ppermute | solution.py:49
  59.0 5.7 %collective-permute-start.5 = (bf16[64,1536]{1,0:T(8,128)(2,1)S(1)}, bf16[64,1536]{1,0:T(8,128)(2,1)S(1)}, u32[]{:S(2)}, u32[]{:S(2)}) collective-permute-start(bf16[64,1536]{1,0:T(8,128)(2,1)S(1)} %get-tuple-element.23), channel_id=1, source_target_pairs={{0,8},{8,0},{16,24},{24,16},{1,9},{9,1},{17,25},{25,17},{2,10},{10... | collective-permute-start | bytes 589832 | tf_op jit(solution)/shard_map/ppermute | solution.py:49
  64.8 7.8 %collective-permute-start.6 = (bf16[2,64,1536]{2,1,0:T(8,128)(2,1)S(1)}, bf16[2,64,1536]{2,1,0:T(8,128)(2,1)S(1)}, u32[]{:S(2)}, u32[]{:S(2)}) collective-permute-start(bf16[2,64,1536]{2,1,0:T(8,128)(2,1)S(1)} %pad_maximum_fusion.3), channel_id=1, source_target_pairs={{0,16},{8,24},{16,0},{24,8},{1,17},{9,25},{17,1},{25,9},{2,18},{10... | collective-permute-start | bytes 1179656 | tf_op jit(solution)/shard_map/ppermute | solution.py:49
  66.5 7.8 %collective-permute-start.8 = (bf16[2,64,1536]{2,1,0:T(8,128)(2,1)S(1)}, bf16[2,64,1536]{2,1,0:T(8,128)(2,1)S(1)}, u32[]{:S(2)}, u32[]{:S(2)}) collective-permute-start(bf16[2,64,1536]{2,1,0:T(8,128)(2,1)S(1)} %pad_maximum_fusion.4), channel_id=1, source_target_pairs={{0,8},{8,0},{16,24},{24,16},{1,9},{9,1},{17,25},{25,17},{2,10},{10... | collective-permute-start | bytes 1179656 | tf_op jit(solution)/shard_map/ppermute | solution.py:49
  90.0 14.1 %collective-permute-start.9 = (f32[128,3072]{1,0:T(8,128)}, f32[128,3072]{1,0:T(8,128)}, u32[]{:S(2)}, u32[]{:S(2)}) collective-permute-start(f32[128,3072]{1,0:T(8,128)} %fusion.19), channel_id=1, source_target_pairs={{0,1},{1,0},{2,3},{3,2},{4,5},{5,4},{6,7},{7,6},{8,9},{9,8},{10,11... | collective-permute-start | bytes 4718600 | tf_op jit(solution)/shard_map/ppermute | solution.py:49
  106.1 1.1 copy-start.1
  108.0 11.7 %collective-permute-start.10 = (bf16[2,32,3072]{2,1,0:T(8,128)(2,1)}, bf16[2,32,3072]{2,1,0:T(8,128)(2,1)S(1)}, u32[]{:S(2)}, u32[]{:S(2)}) collective-permute-start(bf16[2,32,3072]{2,1,0:T(8,128)(2,1)} %fusion.10), channel_id=1, source_target_pairs={{0,2},{1,3},{2,0},{3,1},{4,6},{5,7},{6,4},{7,5},{8,10},{9,11},{10,... | collective-permute-start | bytes 1179656 | tf_op jit(solution)/shard_map/ppermute | solution.py:49
  109.6 10.1 %copy-start.2 = (f32[128,3072]{1,0:T(8,128)S(1)}, f32[128,3072]{1,0:T(8,128)}, u32[]{:S(2)}) copy-start(f32[128,3072]{1,0:T(8,128)} %copy-done.1) | copy-start | bytes 4718596
  119.9 0.9 copy-start.3
  120.8 12.0 %collective-permute-start.11 = (bf16[32,3072]{1,0:T(8,128)(2,1)S(1)}, bf16[32,3072]{1,0:T(8,128)(2,1)S(1)}, u32[]{:S(2)}, u32[]{:S(2)}) collective-permute-start(bf16[32,3072]{1,0:T(8,128)(2,1)S(1)} %fusion.14), channel_id=1, source_target_pairs={{0,4},{1,5},{2,6},{3,7},{4,0},{5,1},{6,2},{7,3},{8,12},{9,13},{10,... | collective-permute-start | bytes 589832 | tf_op jit(solution)/shard_map/ppermute | solution.py:49
  131.9 1.1 copy-start.4

commit v12 on v10

--- a/solution.py
+++ b/solution.py
@@ -150,19 +150,72 @@
     return cur.reshape(m, partial.shape[1])
 
 
+def _block(size, preferred):
+    for b in (preferred, 256, 128):
+        if size % b == 0:
+            return min(b, size)
+    return size
+
+
+def _mm_kernel(x_ref, w_ref, o_ref):
+    o_ref[...] = jnp.dot(x_ref[...], w_ref[...], preferred_element_type=jnp.float32)
+
+
+def matmul(x, w):
+    m, k = x.shape
+    n = w.shape[1]
+    bn = _block(n, 512)
+    return pl.pallas_call(
+        _mm_kernel,
+        grid=(n // bn,),
+        in_specs=[
+            pl.BlockSpec((m, k), lambda j: (0, 0)),
+            pl.BlockSpec((k, bn), lambda j: (0, j)),
+        ],
+        out_specs=pl.BlockSpec((m, bn), lambda j: (0, j)),
+        out_shape=jax.ShapeDtypeStruct((m, n), jnp.float32),
+        cost_estimate=pl.CostEstimate(
+            flops=2 * m * n * k, transcendentals=0, bytes_accessed=2 * (m * k + k * n) + 4 * m * n
+        ),
+    )(x, w)
+
+
+def _mm_nt_kernel(g_ref, w_ref, o_ref):
+    o_ref[...] = lax.dot_general(
+        g_ref[...], w_ref[...], (((1,), (1,)), ((), ())), preferred_element_type=jnp.float32
+    )
+
+
+def matmul_nt(g, w):
+    m, k = g.shape
+    n = w.shape[0]
+    bn = _block(n, 512)
+    return pl.pallas_call(
+        _mm_nt_kernel,
+        grid=(n // bn,),
+        in_specs=[
+            pl.BlockSpec((m, k), lambda i: (0, 0)),
+            pl.BlockSpec((bn, k), lambda i: (i, 0)),
+        ],
+        out_specs=pl.BlockSpec((m, bn), lambda i: (0, i)),
+        out_shape=jax.ShapeDtypeStruct((m, n), jnp.float32),
+        cost_estimate=pl.CostEstimate(
+            flops=2 * m * n * k, transcendentals=0, bytes_accessed=2 * (m * k + k * n) + 4 * m * n
+        ),
+    )(g, w)
+
+
 def body(tokens, weight, bias, cotangent):
     local_x = col_all_gather(tokens)
     my_rows = local_x.shape[0] // lax.axis_size("row")
     first_row = lax.axis_index("row") * my_rows
-    partial_value = jnp.dot(local_x, weight, preferred_element_type=jnp.float32)
+    partial_value = matmul(local_x, weight)
     preact = row_reduce_scatter(partial_value) + bias
     my_cot = lax.dynamic_slice_in_dim(cotangent, first_row, my_rows, 0)
     hidden, my_grad = activate(preact, my_cot)
     full_grad = row_all_gather(my_grad)
     grad_tokens = col_reduce_scatter(
-        lax.dot_general(
-            full_grad, weight, (((1,), (1,)), ((), ())), preferred_element_type=jnp.float32
-        )
+        matmul_nt(full_grad, weight)
     ).astype(jnp.bfloat16)
     grad_weight = outer_product_sum(local_x.T, full_grad)
     grad_bias = jnp.sum(full_grad.astype(jnp.float32), axis=0)

time: 120 us -> 127 us (1.058)
  Pallas kernels: 10.3 us -> 34.1 us
  matrix products: 18 us -> 0 us
    pallas_call x0 -> x2, Pallas kernels: none -> 23.8 us  [the longest x1 11.9 us: matmul(): pl.pallas_call(_mm_kernel, grid=(n // bn,), in_specs=[pl.BlockSpec((m, k)...]
    dot_general x2 -> x0, matrix products: 18 us -> none  [the longest x1 9.04 us: body(): lax.dot_general(full_grad, weight, (((1,), (1,)), ((), ())), preferred_el...]
    unnamed x14 -> x6, local copies, waits for them, and re-layouts: 4.24 us -> 1.15 us
    slice x2, local copies, waits for them, and re-layouts: 0.23 us -> 2.11 us  [_halves(): return [value[:, :cols // 2], value[:, cols // 2:]]]
  transfers between devices with their start and end apart: 12 -> 12, of which waited for: 10 -> 10; matrix products, arithmetic and copies ran while one was open for 4% -> 2% of each run, Pallas kernels for 9% -> 8%
where the time goes in v12:
time: 127 us; the launch traced here: 126 us
  waiting for transfers between devices  40.3 us (32%)
  Pallas kernels  34.1 us (27%)
  blocking collectives  21.5 us (17%)
  starting transfers between devices  10.7 us (8%)
  local copies, waits for them, and re-layouts  9.37 us (7%)
  other arithmetic  9.34 us (7%)
    ppermute x12, waiting for transfers between devices, _swap(): return lax.ppermute(value, axis, [(i, i ^ flip) for i in range(size)])  40.3 us
    all_gather x1, blocking collectives, col_all_gather(): mine = lax.all_gather(block, axis, axis_index_groups=groups)  21.5 us
    pallas_call x1, Pallas kernels, matmul(): pl.pallas_call(_mm_kernel, grid=(n // bn,), in_specs=[pl.BlockSpec((m, k)...  11.9 us
    pallas_call x1, Pallas kernels, matmul_nt(): pl.pallas_call(_mm_nt_kernel, grid=(n // bn,), in_specs=[pl.BlockSpec((m,...  11.9 us
    ppermute x12, starting transfers between devices, _swap(): return lax.ppermute(value, axis, [(i, i ^ flip) for i in range(size)])  10.7 us
    pallas_call x1, Pallas kernels, outer_product_sum(): pl.pallas_call(_outer_kernel, grid=(n // block_n, m // block_m), in_specs...  10.3 us
  transfers between devices with their start and end apart: 12, of which 10 were waited for; matrix products, arithmetic and copies ran while one was open for 2% of the time, Pallas kernels for 8%

profile of v12, /device:TPU:0, one launch (start us, length us, event | category | flops | bytes accessed | tf_op | source)
XLA Modules:
  0.0 126.1 jit_solution(17615476587722213182)
XLA Ops:
  0.6 21.5 %all-gather = bf16[128,3072]{1,0:T(8,128)(2,1)S(1)} all-gather(bf16[32,3072]{1,0:T(8,128)(2,1)} %param.4), channel_id=2, replica_groups={{0,2,4,6},{1,3,5,7},{8,10,12,14},{9,11,13,15},{16,18,20,22},{17,19,21,2..., dimensions={0}, use_global_device_ids=true | all-gather | bytes 983040 | tf_op jit(solution)/shard_map/all_gather | solution.py:120
  22.1 2.3 %collective-permute-done = bf16[4,32,3072]{2,1,0:T(8,128)(2,1)S(1)} collective-permute-done((bf16[4,32,3072]{2,1,0:T(8,128)(2,1)S(1)}, bf16[4,32,3072]{2,1,0:T(8,128)(2,1)S(1)}, u32[]{:S(2)}, u32[]{:S(2)}) %collective-permute-start) | collective-permute-done | bytes 786464 | tf_op jit(solution)/shard_map/ppermute | solution.py:49
  25.9 11.9 %shard_map.75 = f32[256,3072]{1,0:T(8,128)} custom-call(bf16[256,3072]{1,0:T(8,128)(2,1)} %bitcast.67, bf16[3072,3072]{1,0:T(8,128)(2,1)} %w_ref.3), custom_call_target="tpu_custom_call" | custom-call | flops 4831838208 | bytes 23592960 | tf_op jit(solution)/shard_map/pallas_call | solution.py:168
  37.9 2.1 %fusion.13 = (f32[256,1536]{1,0:T(8,128)S(1)}, f32[256,1536]{1,0:T(8,128)S(1)}) fusion(f32[256,3072]{1,0:T(8,128)} %shard_map.75), kind=kLoop, calls=%fused_computation.48 | loop fusion | bytes 6291456 | tf_op jit(solution)/shard_map/slice | solution.py:60
  40.7 1.5 %collective-permute-start.1 = (bf16[2,64,1536]{2,1,0:T(8,128)(2,1)}, bf16[2,64,1536]{2,1,0:T(8,128)(2,1)S(1)}, u32[]{:S(2)}, u32[]{:S(2)}) collective-permute-start(bf16[2,64,1536]{2,1,0:T(8,128)(2,1)} %fusion.8), channel_id=1, source_target_pairs={{0,8},{8,0},{16,24},{24,16},{1,9},{9,1},{17,25},{25,17},{2,10},{10... | collective-permute-start | bytes 1179656 | tf_op jit(solution)/shard_map/ppermute | solution.py:49
  42.3 1.6 %collective-permute-start.3 = (bf16[2,64,1536]{2,1,0:T(8,128)(2,1)S(1)}, bf16[2,64,1536]{2,1,0:T(8,128)(2,1)S(1)}, u32[]{:S(2)}, u32[]{:S(2)}) collective-permute-start(bf16[2,64,1536]{2,1,0:T(8,128)(2,1)S(1)} %fusion.6), channel_id=1, source_target_pairs={{0,16},{8,24},{16,0},{24,8},{1,17},{9,25},{17,1},{25,9},{2,18},{10... | collective-permute-start | bytes 1179656 | tf_op jit(solution)/shard_map/ppermute | solution.py:49
  43.9 8.2 %collective-permute-done.1 = bf16[2,64,1536]{2,1,0:T(8,128)(2,1)S(1)} collective-permute-done((bf16[2,64,1536]{2,1,0:T(8,128)(2,1)}, bf16[2,64,1536]{2,1,0:T(8,128)(2,1)S(1)}, u32[]{:S(2)}, u32[]{:S(2)}) %collective-permute-start.1) | collective-permute-done | bytes 393248 | tf_op jit(solution)/shard_map/ppermute | solution.py:49
  52.2 1.6 %collective-permute-start.2 = (bf16[64,1536]{1,0:T(8,128)(2,1)S(1)}, bf16[64,1536]{1,0:T(8,128)(2,1)S(1)}, u32[]{:S(2)}, u32[]{:S(2)}) collective-permute-start(bf16[64,1536]{1,0:T(8,128)(2,1)S(1)} %fusion.10), channel_id=1, source_target_pairs={{0,16},{8,24},{16,0},{24,8},{1,17},{9,25},{17,1},{25,9},{2,18},{10... | collective-permute-start | bytes 589832 | tf_op jit(solution)/shard_map/ppermute | solution.py:49
  53.9 1.6 %collective-permute-start.4 = (bf16[64,1536]{1,0:T(8,128)(2,1)S(1)}, bf16[64,1536]{1,0:T(8,128)(2,1)S(1)}, u32[]{:S(2)}, u32[]{:S(2)}) collective-permute-start(bf16[64,1536]{1,0:T(8,128)(2,1)S(1)} %fusion.11), channel_id=1, source_target_pairs={{0,8},{8,0},{16,24},{24,16},{1,9},{9,1},{17,25},{25,17},{2,10},{10... | collective-permute-start | bytes 589832 | tf_op jit(solution)/shard_map/ppermute | solution.py:49
  55.5 2.9 %collective-permute-done.2 = bf16[64,1536]{1,0:T(8,128)(2,1)S(1)} collective-permute-done((bf16[64,1536]{1,0:T(8,128)(2,1)S(1)}, bf16[64,1536]{1,0:T(8,128)(2,1)S(1)}, u32[]{:S(2)}, u32[]{:S(2)}) %collective-permute-start.2) | collective-permute-done | bytes 196640 | tf_op jit(solution)/shard_map/ppermute | solution.py:49
  58.4 1.4 %collective-permute-done.4 = bf16[64,1536]{1,0:T(8,128)(2,1)S(1)} collective-permute-done((bf16[64,1536]{1,0:T(8,128)(2,1)S(1)}, bf16[64,1536]{1,0:T(8,128)(2,1)S(1)}, u32[]{:S(2)}, u32[]{:S(2)}) %collective-permute-start.4) | collective-permute-done | bytes 196640 | tf_op jit(solution)/shard_map/ppermute | solution.py:49
  59.9 2.2 %fusion.5 = (bf16[64,3072]{1,0:T(8,128)(2,1)S(1)}, bf16[64,3072]{1,0:T(8,128)(2,1)}) fusion(f32[64,1536]{1,0:T(8,128)S(1)} %bitcast_add_fusion.5, f32[64,1536]{1,0:T(8,128)S(1)} %bitcast_add_fusion.6, bf16[256,3072]{1,0:T(8,128)(2,1)} %param.7, s32[]{:T(128)S(6)} %select_n.121, f32[3072]{0:T(1024)S(1)} %copy-done.2), kind=kLoop, calls=%fused_computation.11 | loop fusion | flops 2949120 | bytes 1978372 | tf_op jit(solution)/shard_map/convert_element_type | solution.py:15
  62.1 1.6 %collective-permute-start.5 = (bf16[64,1536]{1,0:T(8,128)(2,1)S(1)}, bf16[64,1536]{1,0:T(8,128)(2,1)S(1)}, u32[]{:S(2)}, u32[]{:S(2)}) collective-permute-start(bf16[64,1536]{1,0:T(8,128)(2,1)S(1)} %get-tuple-element.20), channel_id=1, source_target_pairs={{0,8},{8,0},{16,24},{24,16},{1,9},{9,1},{17,25},{25,17},{2,10},{10... | collective-permute-start | bytes 589832 | tf_op jit(solution)/shard_map/ppermute | solution.py:49
  64.1 3.7 %collective-permute-done.5 = bf16[64,1536]{1,0:T(8,128)(2,1)S(1)} collective-permute-done((bf16[64,1536]{1,0:T(8,128)(2,1)S(1)}, bf16[64,1536]{1,0:T(8,128)(2,1)S(1)}, u32[]{:S(2)}, u32[]{:S(2)}) %collective-permute-start.5) | collective-permute-done | bytes 196640 | tf_op jit(solution)/shard_map/ppermute | solution.py:49
  67.8 1.6 %collective-permute-done.7 = bf16[64,1536]{1,0:T(8,128)(2,1)S(1)} collective-permute-done((bf16[64,1536]{1,0:T(8,128)(2,1)S(1)}, bf16[64,1536]{1,0:T(8,128)(2,1)S(1)}, u32[]{:S(2)}, u32[]{:S(2)}) %collective-permute-start.7) | collective-permute-done | bytes 196640 | tf_op jit(solution)/shard_map/ppermute | solution.py:49
  71.0 6.5 %collective-permute-done.8 = bf16[2,64,1536]{2,1,0:T(8,128)(2,1)S(1)} collective-permute-done((bf16[2,64,1536]{2,1,0:T(8,128)(2,1)S(1)}, bf16[2,64,1536]{2,1,0:T(8,128)(2,1)S(1)}, u32[]{:S(2)}, u32[]{:S(2)}) %collective-permute-start.8) | collective-permute-done | bytes 393248 | tf_op jit(solution)/shard_map/ppermute | solution.py:49
  78.2 1.4 %pad_maximum_fusion.g_ref = bf16[256,3072]{1,0:T(8,128)(2,1)} fusion(bf16[256,1536]{1,0:T(8,128)(2,1)S(1)} %bitcast.71, bf16[256,1536]{1,0:T(8,128)(2,1)S(1)} %bitcast.73), kind=kLoop, calls=%fused_computation.2 | loop fusion | flops 3145728 | bytes 3145728 | tf_op jit(solution)/shard_map/concatenate | solution.py:112
  79.6 11.9 %shard_map.76 = f32[256,3072]{1,0:T(8,128)} custom-call(bf16[256,3072]{1,0:T(8,128)(2,1)} %pad_maximum_fusion.g_ref, bf16[3072,3072]{1,0:T(8,128)(2,1)} %w_ref.3), custom_call_target="tpu_custom_call" | custom-call | flops 4831838208 | bytes 23592960 | tf_op jit(solution)/shard_map/pallas_call | solution.py:193
  91.5 1.5 %dynamic-slice_bitcast_fusion = f32[4,32,3072]{2,1,0:T(8,128)S(1)} fusion(f32[4,2,32,3072]{3,2,1,0:T(8,128)} %bitcast.69, s32[]{:T(128)S(6)} %select_n.133), kind=kLoop, calls=%fused_computation.4 | loop fusion | bytes 3145732 | tf_op jit(solution)/shard_map/jit(dynamic_index_in_dim)/squeeze | solution.py:53
  93.1 3.5 %collective-permute-done.9 = f32[4,32,3072]{2,1,0:T(8,128)} collective-permute-done((f32[4,32,3072]{2,1,0:T(8,128)S(1)}, f32[4,32,3072]{2,1,0:T(8,128)}, u32[]{:S(2)}, u32[]{:S(2)}) %collective-permute-start.9) | collective-permute-done | bytes 1572896 | tf_op jit(solution)/shard_map/ppermute | solution.py:49
  96.6 2.2 %bitcast_add_fusion = f32[4,32,3072]{2,1,0:T(8,128)S(1)} fusion(f32[4,32,3072]{2,1,0:T(8,128)} %collective-permute-done.9, f32[4,2,32,3072]{3,2,1,0:T(8,128)} %bitcast.70, s32[]{:T(128)S(6)} %select_n.132), kind=kLoop, calls=%fused_computation.3 | loop fusion | flops 393216 | bytes 4718596 | tf_op jit(solution)/shard_map/add | solution.py:132
  100.8 1.6 %copy.18 = bf16[256,3072]{0,1:T(8,128)(2,1)} copy(bf16[256,3072]{1,0:T(8,128)(2,1)S(1)} %bitcast.68) | data formatting | bytes 3145728 | tf_op jit(solution)/shard_map/reshape | solution.py:122
  102.3 9.8 %collective-permute-done.10 = bf16[2,32,3072]{2,1,0:T(8,128)(2,1)S(1)} collective-permute-done((bf16[2,32,3072]{2,1,0:T(8,128)(2,1)}, bf16[2,32,3072]{2,1,0:T(8,128)(2,1)S(1)}, u32[]{:S(2)}, u32[]{:S(2)}) %collective-permute-start.10) | collective-permute-done | bytes 393248 | tf_op jit(solution)/shard_map/ppermute | solution.py:49
  114.3 10.3 %shard_map.77 = bf16[3072,3072]{1,0:T(8,128)(2,1)} custom-call(bf16[3072,256]{1,0:T(8,128)(2,1)} %bitcast.75, bf16[256,3072]{1,0:T(8,128)(2,1)} %pad_maximum_fusion.g_ref), custom_call_target="tpu_custom_call" | custom-call | flops 4831838208 | bytes 22020096 | tf_op jit(solution)/shard_map/pallas_call | solution.py:32
  (40 shorter events, 11.2 us)
Async XLA Ops:
  22.1 2.3 %collective-permute-start = (bf16[4,32,3072]{2,1,0:T(8,128)(2,1)S(1)}, bf16[4,32,3072]{2,1,0:T(8,128)(2,1)S(1)}, u32[]{:S(2)}, u32[]{:S(2)}) collective-permute-start(bf16[4,32,3072]{2,1,0:T(8,128)(2,1)S(1)} %bitcast.82), channel_id=1, source_target_pairs={{0,1},{1,0},{2,3},{3,2},{4,5},{5,4},{6,7},{7,6},{8,9},{9,8},{10,11... | collective-permute-start | bytes 2359304 | tf_op jit(solution)/shard_map/ppermute | solution.py:49
  40.7 11.4 %collective-permute-start.1 = (bf16[2,64,1536]{2,1,0:T(8,128)(2,1)}, bf16[2,64,1536]{2,1,0:T(8,128)(2,1)S(1)}, u32[]{:S(2)}, u32[]{:S(2)}) collective-permute-start(bf16[2,64,1536]{2,1,0:T(8,128)(2,1)} %fusion.8), channel_id=1, source_target_pairs={{0,8},{8,0},{16,24},{24,16},{1,9},{9,1},{17,25},{25,17},{2,10},{10... | collective-permute-start | bytes 1179656 | tf_op jit(solution)/shard_map/ppermute | solution.py:49
  42.3 11.5 %collective-permute-start.3 = (bf16[2,64,1536]{2,1,0:T(8,128)(2,1)S(1)}, bf16[2,64,1536]{2,1,0:T(8,128)(2,1)S(1)}, u32[]{:S(2)}, u32[]{:S(2)}) collective-permute-start(bf16[2,64,1536]{2,1,0:T(8,128)(2,1)S(1)} %fusion.6), channel_id=1, source_target_pairs={{0,16},{8,24},{16,0},{24,8},{1,17},{9,25},{17,1},{25,9},{2,18},{10... | collective-permute-start | bytes 1179656 | tf_op jit(solution)/shard_map/ppermute | solution.py:49
  52.2 6.2 %collective-permute-start.2 = (bf16[64,1536]{1,0:T(8,128)(2,1)S(1)}, bf16[64,1536]{1,0:T(8,128)(2,1)S(1)}, u32[]{:S(2)}, u32[]{:S(2)}) collective-permute-start(bf16[64,1536]{1,0:T(8,128)(2,1)S(1)} %fusion.10), channel_id=1, source_target_pairs={{0,16},{8,24},{16,0},{24,8},{1,17},{9,25},{17,1},{25,9},{2,18},{10... | collective-permute-start | bytes 589832 | tf_op jit(solution)/shard_map/ppermute | solution.py:49
  53.9 6.0 %copy-start.2 = (f32[3072]{0:T(1024)S(1)}, f32[3072]{0:T(1024)}, u32[]{:S(2)}) copy-start(f32[3072]{0:T(1024)} %param.6) | copy-start | bytes 36868
  53.9 5.9 %collective-permute-start.4 = (bf16[64,1536]{1,0:T(8,128)(2,1)S(1)}, bf16[64,1536]{1,0:T(8,128)(2,1)S(1)}, u32[]{:S(2)}, u32[]{:S(2)}) collective-permute-start(bf16[64,1536]{1,0:T(8,128)(2,1)S(1)} %fusion.11), channel_id=1, source_target_pairs={{0,8},{8,0},{16,24},{24,16},{1,9},{9,1},{17,25},{25,17},{2,10},{10... | collective-permute-start | bytes 589832 | tf_op jit(solution)/shard_map/ppermute | solution.py:49
  62.1 5.7 %collective-permute-start.5 = (bf16[64,1536]{1,0:T(8,128)(2,1)S(1)}, bf16[64,1536]{1,0:T(8,128)(2,1)S(1)}, u32[]{:S(2)}, u32[]{:S(2)}) collective-permute-start(bf16[64,1536]{1,0:T(8,128)(2,1)S(1)} %get-tuple-element.20), channel_id=1, source_target_pairs={{0,8},{8,0},{16,24},{24,16},{1,9},{9,1},{17,25},{25,17},{2,10},{10... | collective-permute-start | bytes 589832 | tf_op jit(solution)/shard_map/ppermute | solution.py:49
  63.6 5.7 %collective-permute-start.7 = (bf16[64,1536]{1,0:T(8,128)(2,1)S(1)}, bf16[64,1536]{1,0:T(8,128)(2,1)S(1)}, u32[]{:S(2)}, u32[]{:S(2)}) collective-permute-start(bf16[64,1536]{1,0:T(8,128)(2,1)S(1)} %get-tuple-element.21), channel_id=1, source_target_pairs={{0,16},{8,24},{16,0},{24,8},{1,17},{9,25},{17,1},{25,9},{2,18},{10... | collective-permute-start | bytes 589832 | tf_op jit(solution)/shard_map/ppermute | solution.py:49
  69.5 8.0 %collective-permute-start.8 = (bf16[2,64,1536]{2,1,0:T(8,128)(2,1)S(1)}, bf16[2,64,1536]{2,1,0:T(8,128)(2,1)S(1)}, u32[]{:S(2)}, u32[]{:S(2)}) collective-permute-start(bf16[2,64,1536]{2,1,0:T(8,128)(2,1)S(1)} %pad_maximum_fusion.3), channel_id=1, source_target_pairs={{0,8},{8,0},{16,24},{24,16},{1,9},{9,1},{17,25},{25,17},{2,10},{10... | collective-permute-start | bytes 1179656 | tf_op jit(solution)/shard_map/ppermute | solution.py:49
  70.1 7.8 %collective-permute-start.6 = (bf16[2,64,1536]{2,1,0:T(8,128)(2,1)S(1)}, bf16[2,64,1536]{2,1,0:T(8,128)(2,1)S(1)}, u32[]{:S(2)}, u32[]{:S(2)}) collective-permute-start(bf16[2,64,1536]{2,1,0:T(8,128)(2,1)S(1)} %pad_maximum_fusion.2), channel_id=1, source_target_pairs={{0,16},{8,24},{16,0},{24,8},{1,17},{9,25},{17,1},{25,9},{2,18},{10... | collective-permute-start | bytes 1179656 | tf_op jit(solution)/shard_map/ppermute | solution.py:49
  93.0 3.6 %collective-permute-start.9 = (f32[4,32,3072]{2,1,0:T(8,128)S(1)}, f32[4,32,3072]{2,1,0:T(8,128)}, u32[]{:S(2)}, u32[]{:S(2)}) collective-permute-start(f32[4,32,3072]{2,1,0:T(8,128)S(1)} %dynamic-slice_bitcast_fusion), channel_id=1, source_target_pairs={{0,1},{1,0},{2,3},{3,2},{4,5},{5,4},{6,7},{7,6},{8,9},{9,8},{10,11... | collective-permute-start | bytes 4718600 | tf_op jit(solution)/shard_map/ppermute | solution.py:49
  96.6 4.1 %copy-start = (bf16[4,2,32,3072]{3,2,1,0:T(8,128)(2,1)S(1)}, bf16[4,2,32,3072]{3,2,1,0:T(8,128)(2,1)}, u32[]{:S(2)}) copy-start(bf16[4,2,32,3072]{3,2,1,0:T(8,128)(2,1)} %copy.15) | copy-start | bytes 4718596
  98.8 1.1 copy-start.1
  100.8 11.4 %collective-permute-start.10 = (bf16[2,32,3072]{2,1,0:T(8,128)(2,1)}, bf16[2,32,3072]{2,1,0:T(8,128)(2,1)S(1)}, u32[]{:S(2)}, u32[]{:S(2)}) collective-permute-start(bf16[2,32,3072]{2,1,0:T(8,128)(2,1)} %fusion.7), channel_id=1, source_target_pairs={{0,2},{1,3},{2,0},{3,1},{4,6},{5,7},{6,4},{7,5},{8,10},{9,11},{10,... | collective-permute-start | bytes 1179656 | tf_op jit(solution)/shard_map/ppermute | solution.py:49
  113.4 12.0 %collective-permute-start.11 = (bf16[32,3072]{1,0:T(8,128)(2,1)S(1)}, bf16[32,3072]{1,0:T(8,128)(2,1)S(1)}, u32[]{:S(2)}, u32[]{:S(2)}) collective-permute-start(bf16[32,3072]{1,0:T(8,128)(2,1)S(1)} %fusion.12), channel_id=1, source_target_pairs={{0,4},{1,5},{2,6},{3,7},{4,0},{5,1},{6,2},{7,3},{8,12},{9,13},{10,... | collective-permute-start | bytes 589832 | tf_op jit(solution)/shard_map/ppermute | solution.py:49

commit v13 on v10

--- a/solution.py
+++ b/solution.py
@@ -129,7 +129,8 @@
     m = partial.shape[0] // n
     k = lax.axis_index(axis) % 2
     by_core = jnp.swapaxes(partial.reshape(n // 2, 2, m, partial.shape[1]), 0, 1)
-    chip = _pick(k, by_core) + _swap(_pick(1 - k, by_core), axis, 1)
+    moved = _swap(_pick(1 - k, by_core).astype(jnp.bfloat16), axis, 1)
+    chip = _pick(k, by_core) + moved.astype(jnp.float32)
     chips = n // 2
     z = lax.axis_index(axis) // 2
     if chips & (chips - 1):

time: 120 us -> 120 us (level)
    squeeze x1 -> x0, local copies, waits for them, and re-layouts: 1.39 us -> none  [_pick(): return lax.dynamic_index_in_dim(blocks, index, axis=0, keepdims=False)]
where the time goes in v13:
time: 120 us; the launch traced here: 119 us
  waiting for transfers between devices  38.5 us (32%)
  blocking collectives  21.5 us (18%)
  matrix products  18 us (15%)
  starting transfers between devices  10.3 us (9%)
  Pallas kernels  10.2 us (8%)
  other arithmetic  9.94 us (8%)
  local copies, waits for them, and re-layouts  9.83 us (8%)
    ppermute x12, waiting for transfers between devices, _swap(): return lax.ppermute(value, axis, [(i, i ^ flip) for i in range(size)])  38.5 us
    all_gather x1, blocking collectives, col_all_gather(): mine = lax.all_gather(block, axis, axis_index_groups=groups)  21.5 us
    ppermute x12, starting transfers between devices, _swap(): return lax.ppermute(value, axis, [(i, i ^ flip) for i in range(size)])  10.3 us
    pallas_call x1, Pallas kernels, outer_product_sum(): pl.pallas_call(_outer_kernel, grid=(n // block_n, m // block_m), in_specs...  10.2 us
    dot_general x1, matrix products, body(): lax.dot_general(full_grad, weight, (((1,), (1,)), ((), ())), preferred_el...  9.04 us
    dot_general x1, matrix products, body(): partial_value = jnp.dot(local_x, weight, preferred_element_type=jnp.float32)  8.99 us
    unnamed x14, local copies, waits for them, and re-layouts  5.11 us
  transfers between devices with their start and end apart: 12, of which 10 were waited for; matrix products, arithmetic and copies ran while one was open for 4% of the time, Pallas kernels for 9%

profile of v13, /device:TPU:0, one launch (start us, length us, event | category | flops | bytes accessed | tf_op | source)
XLA Modules:
  0.0 119.2 jit_solution(2101304772264787294)
XLA Ops:
  0.6 21.5 %all-gather = bf16[128,3072]{1,0:T(8,128)(2,1)S(1)} all-gather(bf16[32,3072]{1,0:T(8,128)(2,1)} %param.4), channel_id=2, replica_groups={{0,2,4,6},{1,3,5,7},{8,10,12,14},{9,11,13,15},{16,18,20,22},{17,19,21,2..., dimensions={0}, use_global_device_ids=true | all-gather | bytes 983040 | tf_op jit(solution)/shard_map/all_gather | solution.py:120
  22.1 2.3 %collective-permute-done = bf16[4,32,3072]{2,1,0:T(8,128)(2,1)S(1)} collective-permute-done((bf16[4,32,3072]{2,1,0:T(8,128)(2,1)S(1)}, bf16[4,32,3072]{2,1,0:T(8,128)(2,1)S(1)}, u32[]{:S(2)}, u32[]{:S(2)}) %collective-permute-start) | collective-permute-done | bytes 786464 | tf_op jit(solution)/shard_map/ppermute | solution.py:49
  24.8 9.0 %fusion.17 = f32[256,3072]{1,0:T(8,128)S(1)} fusion(bf16[256,3072]{1,0:T(8,128)(2,1)S(1)} %bitcast.80, bf16[3072,3072]{1,0:T(8,128)(2,1)} %param.5), kind=kOutput, calls=%fused_computation.52 | convolution fusion | flops 4831838208 | bytes 23592960 | tf_op jit(solution)/shard_map/dot_general | solution.py:158
  36.0 1.5 %collective-permute-start.1 = (bf16[2,64,1536]{2,1,0:T(8,128)(2,1)}, bf16[2,64,1536]{2,1,0:T(8,128)(2,1)S(1)}, u32[]{:S(2)}, u32[]{:S(2)}) collective-permute-start(bf16[2,64,1536]{2,1,0:T(8,128)(2,1)} %fusion.9), channel_id=1, source_target_pairs={{0,8},{8,0},{16,24},{24,16},{1,9},{9,1},{17,25},{25,17},{2,10},{10... | collective-permute-start | bytes 1179656 | tf_op jit(solution)/shard_map/ppermute | solution.py:49
  37.5 1.6 %collective-permute-start.3 = (bf16[2,64,1536]{2,1,0:T(8,128)(2,1)S(1)}, bf16[2,64,1536]{2,1,0:T(8,128)(2,1)S(1)}, u32[]{:S(2)}, u32[]{:S(2)}) collective-permute-start(bf16[2,64,1536]{2,1,0:T(8,128)(2,1)S(1)} %fusion.7), channel_id=1, source_target_pairs={{0,16},{8,24},{16,0},{24,8},{1,17},{9,25},{17,1},{25,9},{2,18},{10... | collective-permute-start | bytes 1179656 | tf_op jit(solution)/shard_map/ppermute | solution.py:49
  39.1 8.2 %collective-permute-done.1 = bf16[2,64,1536]{2,1,0:T(8,128)(2,1)S(1)} collective-permute-done((bf16[2,64,1536]{2,1,0:T(8,128)(2,1)}, bf16[2,64,1536]{2,1,0:T(8,128)(2,1)S(1)}, u32[]{:S(2)}, u32[]{:S(2)}) %collective-permute-start.1) | collective-permute-done | bytes 393248 | tf_op jit(solution)/shard_map/ppermute | solution.py:49
  47.4 1.2 %bitcast_add_fusion.3 = f32[2,64,1536]{2,1,0:T(8,128)S(1)} fusion(bf16[2,64,1536]{2,1,0:T(8,128)(2,1)S(1)} %collective-permute-done.1, f32[2,2,64,1536]{3,2,1,0:T(8,128)} %bitcast.86, s32[]{:T(128)S(6)} %select_n.115), kind=kLoop, calls=%fused_computation.19 | loop fusion | flops 393216 | bytes 1966084 | tf_op jit(solution)/shard_map/add | solution.py:83
  48.6 1.6 %collective-permute-start.2 = (bf16[64,1536]{1,0:T(8,128)(2,1)S(1)}, bf16[64,1536]{1,0:T(8,128)(2,1)S(1)}, u32[]{:S(2)}, u32[]{:S(2)}) collective-permute-start(bf16[64,1536]{1,0:T(8,128)(2,1)S(1)} %fusion.11), channel_id=1, source_target_pairs={{0,16},{8,24},{16,0},{24,8},{1,17},{9,25},{17,1},{25,9},{2,18},{10... | collective-permute-start | bytes 589832 | tf_op jit(solution)/shard_map/ppermute | solution.py:49
  50.3 1.6 %collective-permute-start.4 = (bf16[64,1536]{1,0:T(8,128)(2,1)S(1)}, bf16[64,1536]{1,0:T(8,128)(2,1)S(1)}, u32[]{:S(2)}, u32[]{:S(2)}) collective-permute-start(bf16[64,1536]{1,0:T(8,128)(2,1)S(1)} %fusion.12), channel_id=1, source_target_pairs={{0,8},{8,0},{16,24},{24,16},{1,9},{9,1},{17,25},{25,17},{2,10},{10... | collective-permute-start | bytes 589832 | tf_op jit(solution)/shard_map/ppermute | solution.py:49
  51.9 2.9 %collective-permute-done.2 = bf16[64,1536]{1,0:T(8,128)(2,1)S(1)} collective-permute-done((bf16[64,1536]{1,0:T(8,128)(2,1)S(1)}, bf16[64,1536]{1,0:T(8,128)(2,1)S(1)}, u32[]{:S(2)}, u32[]{:S(2)}) %collective-permute-start.2) | collective-permute-done | bytes 196640 | tf_op jit(solution)/shard_map/ppermute | solution.py:49
  54.8 1.4 %collective-permute-done.4 = bf16[64,1536]{1,0:T(8,128)(2,1)S(1)} collective-permute-done((bf16[64,1536]{1,0:T(8,128)(2,1)S(1)}, bf16[64,1536]{1,0:T(8,128)(2,1)S(1)}, u32[]{:S(2)}, u32[]{:S(2)}) %collective-permute-start.4) | collective-permute-done | bytes 196640 | tf_op jit(solution)/shard_map/ppermute | solution.py:49
  56.3 2.2 %fusion.5 = (bf16[64,3072]{1,0:T(8,128)(2,1)S(1)}, bf16[64,3072]{1,0:T(8,128)(2,1)}) fusion(f32[64,1536]{1,0:T(8,128)S(1)} %bitcast_add_fusion.5, f32[64,1536]{1,0:T(8,128)S(1)} %bitcast_add_fusion.6, bf16[256,3072]{1,0:T(8,128)(2,1)} %param.7, s32[]{:T(128)S(6)} %select_n.121, f32[3072]{0:T(1024)S(1)} %copy-done.6), kind=kLoop, calls=%fused_computation.11 | loop fusion | flops 2949120 | bytes 1978372 | tf_op jit(solution)/shard_map/convert_element_type | solution.py:15
  58.5 1.6 %collective-permute-start.5 = (bf16[64,1536]{1,0:T(8,128)(2,1)S(1)}, bf16[64,1536]{1,0:T(8,128)(2,1)S(1)}, u32[]{:S(2)}, u32[]{:S(2)}) collective-permute-start(bf16[64,1536]{1,0:T(8,128)(2,1)S(1)} %get-tuple-element.20), channel_id=1, source_target_pairs={{0,8},{8,0},{16,24},{24,16},{1,9},{9,1},{17,25},{25,17},{2,10},{10... | collective-permute-start | bytes 589832 | tf_op jit(solution)/shard_map/ppermute | solution.py:49
  60.5 3.7 %collective-permute-done.5 = bf16[64,1536]{1,0:T(8,128)(2,1)S(1)} collective-permute-done((bf16[64,1536]{1,0:T(8,128)(2,1)S(1)}, bf16[64,1536]{1,0:T(8,128)(2,1)S(1)}, u32[]{:S(2)}, u32[]{:S(2)}) %collective-permute-start.5) | collective-permute-done | bytes 196640 | tf_op jit(solution)/shard_map/ppermute | solution.py:49
  64.2 1.6 %collective-permute-done.7 = bf16[64,1536]{1,0:T(8,128)(2,1)S(1)} collective-permute-done((bf16[64,1536]{1,0:T(8,128)(2,1)S(1)}, bf16[64,1536]{1,0:T(8,128)(2,1)S(1)}, u32[]{:S(2)}, u32[]{:S(2)}) %collective-permute-start.7) | collective-permute-done | bytes 196640 | tf_op jit(solution)/shard_map/ppermute | solution.py:49
  67.0 6.8 %collective-permute-done.8 = bf16[2,64,1536]{2,1,0:T(8,128)(2,1)S(1)} collective-permute-done((bf16[2,64,1536]{2,1,0:T(8,128)(2,1)S(1)}, bf16[2,64,1536]{2,1,0:T(8,128)(2,1)S(1)}, u32[]{:S(2)}, u32[]{:S(2)}) %collective-permute-start.8) | collective-permute-done | bytes 393248 | tf_op jit(solution)/shard_map/ppermute | solution.py:49
  75.7 9.0 %fusion.14 = f32[256,3072]{1,0:T(8,128)S(1)} fusion(bf16[3072,3072]{1,0:T(8,128)(2,1)} %param.5, bf16[256,1536]{1,0:T(8,128)(2,1)S(1)} %bitcast.74, bf16[256,1536]{1,0:T(8,128)(2,1)S(1)} %bitcast.77), kind=kOutput, calls=%fused_computation.49 | convolution fusion | flops 4834983936 | bytes 23592960 | tf_op jit(solution)/shard_map/dot_general | solution.py:164
  84.8 1.7 %copy-done.5 = f32[256,3072]{1,0:T(8,128)} copy-done((f32[256,3072]{1,0:T(8,128)}, f32[256,3072]{1,0:T(8,128)S(1)}, u32[]{:S(2)}) %copy-start.5) | copy-done | bytes 3145752
  87.4 2.6 %collective-permute-done.9 = bf16[4,32,3072]{2,1,0:T(8,128)(2,1)} collective-permute-done((bf16[4,32,3072]{2,1,0:T(8,128)(2,1)}, bf16[4,32,3072]{2,1,0:T(8,128)(2,1)}, u32[]{:S(2)}, u32[]{:S(2)}) %collective-permute-start.9) | collective-permute-done | bytes 786464 | tf_op jit(solution)/shard_map/ppermute | solution.py:49
  90.1 1.8 %bitcast_add_fusion = f32[4,32,3072]{2,1,0:T(8,128)S(1)} fusion(bf16[4,32,3072]{2,1,0:T(8,128)(2,1)} %collective-permute-done.9, f32[4,2,32,3072]{3,2,1,0:T(8,128)} %bitcast.92, s32[]{:T(128)S(6)} %select_n.132), kind=kLoop, calls=%fused_computation.4 | loop fusion | flops 786432 | bytes 3932164 | tf_op jit(solution)/shard_map/add | solution.py:133
  93.8 1.6 %copy.18 = bf16[256,3072]{0,1:T(8,128)(2,1)} copy(bf16[256,3072]{1,0:T(8,128)(2,1)S(1)} %bitcast.81) | data formatting | bytes 3145728 | tf_op jit(solution)/shard_map/reshape | solution.py:122
  95.4 1.3 %pad_maximum_fusion.g_ref = bf16[256,3072]{1,0:T(8,128)(2,1)} fusion(bf16[256,1536]{1,0:T(8,128)(2,1)S(1)} %bitcast.75, bf16[256,1536]{1,0:T(8,128)(2,1)S(1)} %bitcast.78), kind=kLoop, calls=%fused_computation.2 | loop fusion | flops 3145728 | bytes 3145728 | tf_op jit(solution)/shard_map/concatenate | solution.py:112
  96.8 8.4 %collective-permute-done.10 = bf16[2,32,3072]{2,1,0:T(8,128)(2,1)S(1)} collective-permute-done((bf16[2,32,3072]{2,1,0:T(8,128)(2,1)}, bf16[2,32,3072]{2,1,0:T(8,128)(2,1)S(1)}, u32[]{:S(2)}, u32[]{:S(2)}) %collective-permute-start.10) | collective-permute-done | bytes 393248 | tf_op jit(solution)/shard_map/ppermute | solution.py:49
  107.1 10.2 %shard_map.75 = bf16[3072,3072]{1,0:T(8,128)(2,1)} custom-call(bf16[3072,256]{1,0:T(8,128)(2,1)} %bitcast.82, bf16[256,3072]{1,0:T(8,128)(2,1)} %pad_maximum_fusion.g_ref), custom_call_target="tpu_custom_call" | custom-call | flops 4831838208 | bytes 22020096 | tf_op jit(solution)/shard_map/pallas_call | solution.py:32
  (48 shorter events, 13.1 us)
Async XLA Ops:
  22.1 2.3 %collective-permute-start = (bf16[4,32,3072]{2,1,0:T(8,128)(2,1)S(1)}, bf16[4,32,3072]{2,1,0:T(8,128)(2,1)S(1)}, u32[]{:S(2)}, u32[]{:S(2)}) collective-permute-start(bf16[4,32,3072]{2,1,0:T(8,128)(2,1)S(1)} %bitcast.89), channel_id=1, source_target_pairs={{0,1},{1,0},{2,3},{3,2},{4,5},{5,4},{6,7},{7,6},{8,9},{9,8},{10,11... | collective-permute-start | bytes 2359304 | tf_op jit(solution)/shard_map/ppermute | solution.py:49
  34.1 1.1 copy-start
  36.0 11.4 %collective-permute-start.1 = (bf16[2,64,1536]{2,1,0:T(8,128)(2,1)}, bf16[2,64,1536]{2,1,0:T(8,128)(2,1)S(1)}, u32[]{:S(2)}, u32[]{:S(2)}) collective-permute-start(bf16[2,64,1536]{2,1,0:T(8,128)(2,1)} %fusion.9), channel_id=1, source_target_pairs={{0,8},{8,0},{16,24},{24,16},{1,9},{9,1},{17,25},{25,17},{2,10},{10... | collective-permute-start | bytes 1179656 | tf_op jit(solution)/shard_map/ppermute | solution.py:49
  37.5 12.7 %collective-permute-start.3 = (bf16[2,64,1536]{2,1,0:T(8,128)(2,1)S(1)}, bf16[2,64,1536]{2,1,0:T(8,128)(2,1)S(1)}, u32[]{:S(2)}, u32[]{:S(2)}) collective-permute-start(bf16[2,64,1536]{2,1,0:T(8,128)(2,1)S(1)} %fusion.7), channel_id=1, source_target_pairs={{0,16},{8,24},{16,0},{24,8},{1,17},{9,25},{17,1},{25,9},{2,18},{10... | collective-permute-start | bytes 1179656 | tf_op jit(solution)/shard_map/ppermute | solution.py:49
  48.6 6.2 %collective-permute-start.2 = (bf16[64,1536]{1,0:T(8,128)(2,1)S(1)}, bf16[64,1536]{1,0:T(8,128)(2,1)S(1)}, u32[]{:S(2)}, u32[]{:S(2)}) collective-permute-start(bf16[64,1536]{1,0:T(8,128)(2,1)S(1)} %fusion.11), channel_id=1, source_target_pairs={{0,16},{8,24},{16,0},{24,8},{1,17},{9,25},{17,1},{25,9},{2,18},{10... | collective-permute-start | bytes 589832 | tf_op jit(solution)/shard_map/ppermute | solution.py:49
  50.3 6.0 %copy-start.6 = (f32[3072]{0:T(1024)S(1)}, f32[3072]{0:T(1024)}, u32[]{:S(2)}) copy-start(f32[3072]{0:T(1024)} %param.6) | copy-start | bytes 36868
  50.3 5.9 %collective-permute-start.4 = (bf16[64,1536]{1,0:T(8,128)(2,1)S(1)}, bf16[64,1536]{1,0:T(8,128)(2,1)S(1)}, u32[]{:S(2)}, u32[]{:S(2)}) collective-permute-start(bf16[64,1536]{1,0:T(8,128)(2,1)S(1)} %fusion.12), channel_id=1, source_target_pairs={{0,8},{8,0},{16,24},{24,16},{1,9},{9,1},{17,25},{25,17},{2,10},{10... | collective-permute-start | bytes 589832 | tf_op jit(solution)/shard_map/ppermute | solution.py:49
  58.5 5.7 %collective-permute-start.5 = (bf16[64,1536]{1,0:T(8,128)(2,1)S(1)}, bf16[64,1536]{1,0:T(8,128)(2,1)S(1)}, u32[]{:S(2)}, u32[]{:S(2)}) collective-permute-start(bf16[64,1536]{1,0:T(8,128)(2,1)S(1)} %get-tuple-element.20), channel_id=1, source_target_pairs={{0,8},{8,0},{16,24},{24,16},{1,9},{9,1},{17,25},{25,17},{2,10},{10... | collective-permute-start | bytes 589832 | tf_op jit(solution)/shard_map/ppermute | solution.py:49
  60.0 5.7 %collective-permute-start.7 = (bf16[64,1536]{1,0:T(8,128)(2,1)S(1)}, bf16[64,1536]{1,0:T(8,128)(2,1)S(1)}, u32[]{:S(2)}, u32[]{:S(2)}) collective-permute-start(bf16[64,1536]{1,0:T(8,128)(2,1)S(1)} %get-tuple-element.21), channel_id=1, source_target_pairs={{0,16},{8,24},{16,0},{24,8},{1,17},{9,25},{17,1},{25,9},{2,18},{10... | collective-permute-start | bytes 589832 | tf_op jit(solution)/shard_map/ppermute | solution.py:49
  65.9 8.0 %collective-permute-start.8 = (bf16[2,64,1536]{2,1,0:T(8,128)(2,1)S(1)}, bf16[2,64,1536]{2,1,0:T(8,128)(2,1)S(1)}, u32[]{:S(2)}, u32[]{:S(2)}) collective-permute-start(bf16[2,64,1536]{2,1,0:T(8,128)(2,1)S(1)} %pad_maximum_fusion.3), channel_id=1, source_target_pairs={{0,8},{8,0},{16,24},{24,16},{1,9},{9,1},{17,25},{25,17},{2,10},{10... | collective-permute-start | bytes 1179656 | tf_op jit(solution)/shard_map/ppermute | solution.py:49
  66.4 7.9 %collective-permute-start.6 = (bf16[2,64,1536]{2,1,0:T(8,128)(2,1)S(1)}, bf16[2,64,1536]{2,1,0:T(8,128)(2,1)}, u32[]{:S(2)}, u32[]{:S(2)}) collective-permute-start(bf16[2,64,1536]{2,1,0:T(8,128)(2,1)S(1)} %pad_maximum_fusion.2), channel_id=1, source_target_pairs={{0,16},{8,24},{16,0},{24,8},{1,17},{9,25},{17,1},{25,9},{2,18},{10... | collective-permute-start | bytes 1179656 | tf_op jit(solution)/shard_map/ppermute | solution.py:49
  84.8 1.7 %copy-start.5 = (f32[256,3072]{1,0:T(8,128)}, f32[256,3072]{1,0:T(8,128)S(1)}, u32[]{:S(2)}) copy-start(f32[256,3072]{1,0:T(8,128)S(1)} %fusion.14) | copy-start | bytes 9437188
  87.4 2.6 %collective-permute-start.9 = (bf16[4,32,3072]{2,1,0:T(8,128)(2,1)}, bf16[4,32,3072]{2,1,0:T(8,128)(2,1)}, u32[]{:S(2)}, u32[]{:S(2)}) collective-permute-start(bf16[4,32,3072]{2,1,0:T(8,128)(2,1)} %fusion.6), channel_id=1, source_target_pairs={{0,1},{1,0},{2,3},{3,2},{4,5},{5,4},{6,7},{7,6},{8,9},{9,8},{10,11... | collective-permute-start | bytes 2359304 | tf_op jit(solution)/shard_map/ppermute | solution.py:49
  91.9 1.1 copy-start.1
  93.8 11.4 %collective-permute-start.10 = (bf16[2,32,3072]{2,1,0:T(8,128)(2,1)}, bf16[2,32,3072]{2,1,0:T(8,128)(2,1)S(1)}, u32[]{:S(2)}, u32[]{:S(2)}) collective-permute-start(bf16[2,32,3072]{2,1,0:T(8,128)(2,1)} %fusion.8), channel_id=1, source_target_pairs={{0,2},{1,3},{2,0},{3,1},{4,6},{5,7},{6,4},{7,5},{8,10},{9,11},{10,... | collective-permute-start | bytes 1179656 | tf_op jit(solution)/shard_map/ppermute | solution.py:49
  95.4 9.8 %copy-start.2 = (f32[4,32,3072]{2,1,0:T(8,128)S(1)}, f32[4,32,3072]{2,1,0:T(8,128)}, u32[]{:S(2)}) copy-start(f32[4,32,3072]{2,1,0:T(8,128)} %copy-done.1) | copy-start | bytes 4718596
  105.3 0.9 copy-start.3
  106.2 12.0 %collective-permute-start.11 = (bf16[32,3072]{1,0:T(8,128)(2,1)S(1)}, bf16[32,3072]{1,0:T(8,128)(2,1)S(1)}, u32[]{:S(2)}, u32[]{:S(2)}) collective-permute-start(bf16[32,3072]{1,0:T(8,128)(2,1)S(1)} %fusion.13), channel_id=1, source_target_pairs={{0,4},{1,5},{2,6},{3,7},{4,0},{5,1},{6,2},{7,3},{8,12},{9,13},{10,... | collective-permute-start | bytes 589832 | tf_op jit(solution)/shard_map/ppermute | solution.py:49
  117.3 1.1 copy-start.4

commit v14 on v9

--- a/solution.py
+++ b/solution.py
@@ -24,24 +24,39 @@
     )
 
 
-def outer_product_sum(xt, g, block_m=768, block_n=3072):
+def _outer_into_kernel(xt_ref, g_ref, _, o_ref):
+    _outer_kernel(xt_ref, g_ref, o_ref)
+
+
+def outer_product_sum(xt, g, first=0, count=None, into=None, block_m=768, block_n=3072):
     m, k = xt.shape
     n = g.shape[1]
     block_m = min(block_m, m)
     block_n = min(block_n, n)
+    if count is None:
+        count = m // block_m - first
+    in_specs = [
+        pl.BlockSpec((block_m, k), lambda j, i: (i + first, 0)),
+        pl.BlockSpec((k, block_n), lambda j, i: (0, j)),
+    ]
+    operands = [xt, g]
+    kernel, aliases = _outer_kernel, {}
+    if into is not None:
+        in_specs.append(pl.BlockSpec(memory_space=pl.ANY))
+        operands.append(into)
+        kernel, aliases = _outer_into_kernel, {2: 0}
+    rows = count * block_m
     return pl.pallas_call(
-        _outer_kernel,
-        grid=(n // block_n, m // block_m),
-        in_specs=[
-            pl.BlockSpec((block_m, k), lambda j, i: (i, 0)),
-            pl.BlockSpec((k, block_n), lambda j, i: (0, j)),
-        ],
-        out_specs=pl.BlockSpec((block_m, block_n), lambda j, i: (i, j)),
+        kernel,
+        grid=(n // block_n, count),
+        in_specs=in_specs,
+        out_specs=pl.BlockSpec((block_m, block_n), lambda j, i: (i + first, j)),
         out_shape=jax.ShapeDtypeStruct((m, n), jnp.bfloat16),
+        input_output_aliases=aliases,
         cost_estimate=pl.CostEstimate(
-            flops=2 * m * n * k, transcendentals=0, bytes_accessed=2 * (m * k + k * n + m * n)
+            flops=2 * rows * n * k, transcendentals=0, bytes_accessed=2 * (rows * k + k * n + rows * n)
         ),
-    )(xt, g)
+    )(*operands)
 
 
 def _swap(value, axis, flip):
@@ -144,7 +159,8 @@
     for bit in range(levels):
         mine = (z >> bit) & 1
         t = jnp.moveaxis(cur, bits.index(bit), 0)
-        cur = _pick(mine, t) + _swap(_pick(1 - mine, t), axis, 2 << bit)
+        sent = _swap(_pick(1 - mine, t).astype(jnp.bfloat16), axis, 2 << bit)
+        cur = _pick(mine, t) + sent.astype(jnp.float32)
         bits.remove(bit)
         if bit == 0:
             cur, hold = lax.optimization_barrier((cur, hold))
@@ -160,14 +176,20 @@
     my_cot = lax.dynamic_slice_in_dim(cotangent, first_row, my_rows, 0)
     hidden, my_grad = activate(preact, my_cot)
     full_grad = row_all_gather(my_grad)
-    grad_weight = outer_product_sum(local_x.T, full_grad)
-    grad_tokens, grad_weight = col_reduce_scatter(
+    local_xt = local_x.T
+    blocks = local_xt.shape[0] // min(768, local_xt.shape[0])
+    first_half = outer_product_sum(local_xt, full_grad, 0, blocks // 2)
+    grad_tokens, first_half = col_reduce_scatter(
         lax.dot_general(
             full_grad, weight, (((1,), (1,)), ((), ())), preferred_element_type=jnp.float32
         ),
-        grad_weight,
+        first_half,
     )
     grad_tokens = grad_tokens.astype(jnp.bfloat16)
+    if blocks // 2:
+        grad_weight = outer_product_sum(local_xt, full_grad, blocks // 2, into=first_half)
+    else:
+        grad_weight = outer_product_sum(local_xt, full_grad)
     grad_bias = jnp.sum(full_grad.astype(jnp.float32), axis=0)
     return (hidden, grad_tokens, grad_weight, grad_bias)
 

time: 137 us -> 117 us (0.85)
  waiting for transfers between devices: 55.9 us -> 35.8 us
  Pallas kernels: 10.3 us -> 13.3 us
    ppermute x12, waiting for transfers between devices: 55.9 us -> 35.8 us  [_swap(): return lax.ppermute(value, axis, [(i, i ^ flip) for i in range(size)])]
    pallas_call x1 -> x2, Pallas kernels: 10.3 us -> 13.3 us  [outer_product_sum(): pl.pallas_call(kernel, grid=(n // block_n, count), in_specs=in_specs, out...]
    unnamed x10 -> x6, local copies, waits for them, and re-layouts: 2.78 us -> 1.9 us
  transfers between devices with their start and end apart: 12 -> 12, of which waited for: 11 -> 11; matrix products, arithmetic and copies ran while one was open for 4% -> 4% of each run, Pallas kernels for 8% -> 11%
where the time goes in v14:
time: 117 us
  waiting for transfers between devices  35.8 us (31%)
  blocking collectives  21.5 us (18%)
  matrix products  18 us (15%)
  Pallas kernels  13.3 us (11%)
  starting transfers between devices  10.3 us (9%)
  other arithmetic  10.2 us (9%)
  local copies, waits for them, and re-layouts  7.09 us (6%)
    ppermute x12, waiting for transfers between devices, _swap(): return lax.ppermute(value, axis, [(i, i ^ flip) for i in range(size)])  35.8 us
    all_gather x1, blocking collectives, col_all_gather(): mine = lax.all_gather(block, axis, axis_index_groups=groups)  21.5 us
    pallas_call x2, Pallas kernels, outer_product_sum(): pl.pallas_call(kernel, grid=(n // block_n, count), in_specs=in_specs, out...  13.3 us
    ppermute x12, starting transfers between devices, _swap(): return lax.ppermute(value, axis, [(i, i ^ flip) for i in range(size)])  10.3 us
    dot_general x1, matrix products, body(): lax.dot_general(full_grad, weight, (((1,), (1,)), ((), ())), preferred_el...  9.04 us
    dot_general x1, matrix products, body(): partial_value = jnp.dot(local_x, weight, preferred_element_type=jnp.float32)  8.99 us
  transfers between devices with their start and end apart: 12, of which 11 were waited for; matrix products, arithmetic and copies ran while one was open for 4% of the time, Pallas kernels for 11%

profile of v14, /device:TPU:0, one launch (start us, length us, event | category | flops | bytes accessed | tf_op | source)
XLA Modules:
  0.0 117.1 jit_solution(13496574593202304291)
XLA Ops:
  0.6 21.5 %all-gather = bf16[128,3072]{1,0:T(8,128)(2,1)S(1)} all-gather(bf16[32,3072]{1,0:T(8,128)(2,1)} %param.4), channel_id=2, replica_groups={{0,2,4,6},{1,3,5,7},{8,10,12,14},{9,11,13,15},{16,18,20,22},{17,19,21,2..., dimensions={0}, use_global_device_ids=true | all-gather | bytes 983040 | tf_op jit(solution)/shard_map/all_gather | solution.py:135
  22.1 2.3 %collective-permute-done = bf16[4,32,3072]{2,1,0:T(8,128)(2,1)S(1)} collective-permute-done((bf16[4,32,3072]{2,1,0:T(8,128)(2,1)S(1)}, bf16[4,32,3072]{2,1,0:T(8,128)(2,1)S(1)}, u32[]{:S(2)}, u32[]{:S(2)}) %collective-permute-start) | collective-permute-done | bytes 786464 | tf_op jit(solution)/shard_map/ppermute | solution.py:64
  24.8 9.0 %fusion.16 = f32[256,3072]{1,0:T(8,128)S(1)} fusion(bf16[256,3072]{1,0:T(8,128)(2,1)S(1)} %bitcast.78, bf16[3072,3072]{1,0:T(8,128)(2,1)} %param.5), kind=kOutput, calls=%fused_computation.51 | convolution fusion | flops 4831838208 | bytes 23592960 | tf_op jit(solution)/shard_map/dot_general | solution.py:174
  36.0 1.5 %collective-permute-start.1 = (bf16[2,64,1536]{2,1,0:T(8,128)(2,1)}, bf16[2,64,1536]{2,1,0:T(8,128)(2,1)S(1)}, u32[]{:S(2)}, u32[]{:S(2)}) collective-permute-start(bf16[2,64,1536]{2,1,0:T(8,128)(2,1)} %fusion.8), channel_id=1, source_target_pairs={{0,8},{8,0},{16,24},{24,16},{1,9},{9,1},{17,25},{25,17},{2,10},{10... | collective-permute-start | bytes 1179656 | tf_op jit(solution)/shard_map/ppermute | solution.py:64
  37.5 1.6 %collective-permute-start.3 = (bf16[2,64,1536]{2,1,0:T(8,128)(2,1)S(1)}, bf16[2,64,1536]{2,1,0:T(8,128)(2,1)S(1)}, u32[]{:S(2)}, u32[]{:S(2)}) collective-permute-start(bf16[2,64,1536]{2,1,0:T(8,128)(2,1)S(1)} %fusion.6), channel_id=1, source_target_pairs={{0,16},{8,24},{16,0},{24,8},{1,17},{9,25},{17,1},{25,9},{2,18},{10... | collective-permute-start | bytes 1179656 | tf_op jit(solution)/shard_map/ppermute | solution.py:64
  39.1 8.2 %collective-permute-done.1 = bf16[2,64,1536]{2,1,0:T(8,128)(2,1)S(1)} collective-permute-done((bf16[2,64,1536]{2,1,0:T(8,128)(2,1)}, bf16[2,64,1536]{2,1,0:T(8,128)(2,1)S(1)}, u32[]{:S(2)}, u32[]{:S(2)}) %collective-permute-start.1) | collective-permute-done | bytes 393248 | tf_op jit(solution)/shard_map/ppermute | solution.py:64
  48.6 1.6 %collective-permute-start.2 = (bf16[64,1536]{1,0:T(8,128)(2,1)S(1)}, bf16[64,1536]{1,0:T(8,128)(2,1)S(1)}, u32[]{:S(2)}, u32[]{:S(2)}) collective-permute-start(bf16[64,1536]{1,0:T(8,128)(2,1)S(1)} %fusion.10), channel_id=1, source_target_pairs={{0,16},{8,24},{16,0},{24,8},{1,17},{9,25},{17,1},{25,9},{2,18},{10... | collective-permute-start | bytes 589832 | tf_op jit(solution)/shard_map/ppermute | solution.py:64
  50.3 1.6 %collective-permute-start.4 = (bf16[64,1536]{1,0:T(8,128)(2,1)S(1)}, bf16[64,1536]{1,0:T(8,128)(2,1)S(1)}, u32[]{:S(2)}, u32[]{:S(2)}) collective-permute-start(bf16[64,1536]{1,0:T(8,128)(2,1)S(1)} %fusion.11), channel_id=1, source_target_pairs={{0,8},{8,0},{16,24},{24,16},{1,9},{9,1},{17,25},{25,17},{2,10},{10... | collective-permute-start | bytes 589832 | tf_op jit(solution)/shard_map/ppermute | solution.py:64
  51.9 2.9 %collective-permute-done.2 = bf16[64,1536]{1,0:T(8,128)(2,1)S(1)} collective-permute-done((bf16[64,1536]{1,0:T(8,128)(2,1)S(1)}, bf16[64,1536]{1,0:T(8,128)(2,1)S(1)}, u32[]{:S(2)}, u32[]{:S(2)}) %collective-permute-start.2) | collective-permute-done | bytes 196640 | tf_op jit(solution)/shard_map/ppermute | solution.py:64
  54.8 1.4 %collective-permute-done.4 = bf16[64,1536]{1,0:T(8,128)(2,1)S(1)} collective-permute-done((bf16[64,1536]{1,0:T(8,128)(2,1)S(1)}, bf16[64,1536]{1,0:T(8,128)(2,1)S(1)}, u32[]{:S(2)}, u32[]{:S(2)}) %collective-permute-start.4) | collective-permute-done | bytes 196640 | tf_op jit(solution)/shard_map/ppermute | solution.py:64
  56.3 2.2 %fusion.5 = (bf16[64,3072]{1,0:T(8,128)(2,1)S(1)}, bf16[64,3072]{1,0:T(8,128)(2,1)}) fusion(f32[64,1536]{1,0:T(8,128)S(1)} %bitcast_add_fusion.5, f32[64,1536]{1,0:T(8,128)S(1)} %bitcast_add_fusion.6, bf16[256,3072]{1,0:T(8,128)(2,1)} %param.7, s32[]{:T(128)S(6)} %select_n.121, f32[3072]{0:T(1024)S(1)} %copy-done.2), kind=kLoop, calls=%fused_computation.11 | loop fusion | flops 2949120 | bytes 1978372 | tf_op jit(solution)/shard_map/convert_element_type | solution.py:15
  58.5 1.6 %collective-permute-start.5 = (bf16[64,1536]{1,0:T(8,128)(2,1)S(1)}, bf16[64,1536]{1,0:T(8,128)(2,1)S(1)}, u32[]{:S(2)}, u32[]{:S(2)}) collective-permute-start(bf16[64,1536]{1,0:T(8,128)(2,1)S(1)} %get-tuple-element.24), channel_id=1, source_target_pairs={{0,8},{8,0},{16,24},{24,16},{1,9},{9,1},{17,25},{25,17},{2,10},{10... | collective-permute-start | bytes 589832 | tf_op jit(solution)/shard_map/ppermute | solution.py:64
  60.5 3.7 %collective-permute-done.5 = bf16[64,1536]{1,0:T(8,128)(2,1)S(1)} collective-permute-done((bf16[64,1536]{1,0:T(8,128)(2,1)S(1)}, bf16[64,1536]{1,0:T(8,128)(2,1)S(1)}, u32[]{:S(2)}, u32[]{:S(2)}) %collective-permute-start.5) | collective-permute-done | bytes 196640 | tf_op jit(solution)/shard_map/ppermute | solution.py:64
  64.2 1.6 %collective-permute-done.7 = bf16[64,1536]{1,0:T(8,128)(2,1)S(1)} collective-permute-done((bf16[64,1536]{1,0:T(8,128)(2,1)S(1)}, bf16[64,1536]{1,0:T(8,128)(2,1)S(1)}, u32[]{:S(2)}, u32[]{:S(2)}) %collective-permute-start.7) | collective-permute-done | bytes 196640 | tf_op jit(solution)/shard_map/ppermute | solution.py:64
  67.0 6.8 %collective-permute-done.8 = bf16[2,64,1536]{2,1,0:T(8,128)(2,1)S(1)} collective-permute-done((bf16[2,64,1536]{2,1,0:T(8,128)(2,1)S(1)}, bf16[2,64,1536]{2,1,0:T(8,128)(2,1)S(1)}, u32[]{:S(2)}, u32[]{:S(2)}) %collective-permute-start.8) | collective-permute-done | bytes 393248 | tf_op jit(solution)/shard_map/ppermute | solution.py:64
  75.7 9.0 %fusion.13 = f32[256,3072]{1,0:T(8,128)S(1)} fusion(bf16[3072,3072]{1,0:T(8,128)(2,1)} %param.5, bf16[256,1536]{1,0:T(8,128)(2,1)S(1)} %bitcast.72, bf16[256,1536]{1,0:T(8,128)(2,1)S(1)} %bitcast.75), kind=kOutput, calls=%fused_computation.48 | convolution fusion | flops 4834983936 | bytes 23592960 | tf_op jit(solution)/shard_map/dot_general | solution.py:183
  84.8 1.4 %dynamic-slice_bitcast_fusion = f32[4,32,3072]{2,1,0:T(8,128)} fusion(f32[4,2,32,3072]{3,2,1,0:T(8,128)S(1)} %bitcast.86, s32[]{:T(128)S(6)} %select_n.133), kind=kLoop, calls=%fused_computation.4 | loop fusion | bytes 3145732 | tf_op jit(solution)/shard_map/jit(dynamic_index_in_dim)/squeeze | solution.py:68
  87.0 1.6 %copy.18 = bf16[256,3072]{0,1:T(8,128)(2,1)} copy(bf16[256,3072]{1,0:T(8,128)(2,1)S(1)} %bitcast.79) | data formatting | bytes 3145728 | tf_op jit(solution)/shard_map/reshape | solution.py:137
  88.6 2.2 %collective-permute-done.9 = f32[4,32,3072]{2,1,0:T(8,128)} collective-permute-done((f32[4,32,3072]{2,1,0:T(8,128)}, f32[4,32,3072]{2,1,0:T(8,128)}, u32[]{:S(2)}, u32[]{:S(2)}) %collective-permute-start.9) | collective-permute-done | bytes 1572896 | tf_op jit(solution)/shard_map/ppermute | solution.py:64
  90.7 2.1 %bitcast_add_fusion = f32[4,32,3072]{2,1,0:T(8,128)S(1)} fusion(f32[4,32,3072]{2,1,0:T(8,128)} %collective-permute-done.9, f32[4,2,32,3072]{3,2,1,0:T(8,128)} %bitcast.87, s32[]{:T(128)S(6)} %select_n.132), kind=kLoop, calls=%fused_computation.3 | loop fusion | flops 393216 | bytes 4718596 | tf_op jit(solution)/shard_map/add | solution.py:147
  95.8 6.7 %shard_map.75._ = bf16[3072,3072]{1,0:T(8,128)(2,1)} custom-call(bf16[3072,256]{1,0:T(8,128)(2,1)} %bitcast.70, bf16[256,3072]{1,0:T(8,128)(2,1)} %pad_maximum_fusion.g_ref), custom_call_target="tpu_custom_call" | custom-call | flops 2415919104 | bytes 11796480 | tf_op jit(solution)/shard_map/pallas_call | solution.py:49
  102.5 2.5 %collective-permute-done.10 = bf16[2,32,3072]{2,1,0:T(8,128)(2,1)S(1)} collective-permute-done((bf16[2,32,3072]{2,1,0:T(8,128)(2,1)}, bf16[2,32,3072]{2,1,0:T(8,128)(2,1)S(1)}, u32[]{:S(2)}, u32[]{:S(2)}) %collective-permute-start.10) | collective-permute-done | bytes 393248 | tf_op jit(solution)/shard_map/ppermute | solution.py:64
  106.0 6.7 %shard_map.76 = bf16[3072,3072]{1,0:T(8,128)(2,1)} custom-call(bf16[3072,256]{1,0:T(8,128)(2,1)} %bitcast.71, bf16[256,3072]{1,0:T(8,128)(2,1)} %pad_maximum_fusion.g_ref, bf16[3072,3072]{1,0:T(8,128)(2,1)} %shard_map.75._), custom_call_target="tpu_custom_call", output_to_operand_aliasing={{}: (2, {})} | custom-call | flops 2415919104 | bytes 11796480 | tf_op jit(solution)/shard_map/pallas_call | solution.py:49
  112.7 3.7 %collective-permute-done.11 = bf16[32,3072]{1,0:T(8,128)(2,1)S(1)} collective-permute-done((bf16[32,3072]{1,0:T(8,128)(2,1)S(1)}, bf16[32,3072]{1,0:T(8,128)(2,1)S(1)}, u32[]{:S(2)}, u32[]{:S(2)}) %collective-permute-start.11) | collective-permute-done | bytes 196640 | tf_op jit(solution)/shard_map/ppermute | solution.py:64
  (41 shorter events, 13.1 us)
Async XLA Ops:
  22.1 2.3 %collective-permute-start = (bf16[4,32,3072]{2,1,0:T(8,128)(2,1)S(1)}, bf16[4,32,3072]{2,1,0:T(8,128)(2,1)S(1)}, u32[]{:S(2)}, u32[]{:S(2)}) collective-permute-start(bf16[4,32,3072]{2,1,0:T(8,128)(2,1)S(1)} %bitcast.88), channel_id=1, source_target_pairs={{0,1},{1,0},{2,3},{3,2},{4,5},{5,4},{6,7},{7,6},{8,9},{9,8},{10,11... | collective-permute-start | bytes 2359304 | tf_op jit(solution)/shard_map/ppermute | solution.py:64
  34.1 1.1 copy-start
  36.0 11.4 %collective-permute-start.1 = (bf16[2,64,1536]{2,1,0:T(8,128)(2,1)}, bf16[2,64,1536]{2,1,0:T(8,128)(2,1)S(1)}, u32[]{:S(2)}, u32[]{:S(2)}) collective-permute-start(bf16[2,64,1536]{2,1,0:T(8,128)(2,1)} %fusion.8), channel_id=1, source_target_pairs={{0,8},{8,0},{16,24},{24,16},{1,9},{9,1},{17,25},{25,17},{2,10},{10... | collective-permute-start | bytes 1179656 | tf_op jit(solution)/shard_map/ppermute | solution.py:64
  37.5 12.7 %collective-permute-start.3 = (bf16[2,64,1536]{2,1,0:T(8,128)(2,1)S(1)}, bf16[2,64,1536]{2,1,0:T(8,128)(2,1)S(1)}, u32[]{:S(2)}, u32[]{:S(2)}) collective-permute-start(bf16[2,64,1536]{2,1,0:T(8,128)(2,1)S(1)} %fusion.6), channel_id=1, source_target_pairs={{0,16},{8,24},{16,0},{24,8},{1,17},{9,25},{17,1},{25,9},{2,18},{10... | collective-permute-start | bytes 1179656 | tf_op jit(solution)/shard_map/ppermute | solution.py:64
  48.6 6.2 %collective-permute-start.2 = (bf16[64,1536]{1,0:T(8,128)(2,1)S(1)}, bf16[64,1536]{1,0:T(8,128)(2,1)S(1)}, u32[]{:S(2)}, u32[]{:S(2)}) collective-permute-start(bf16[64,1536]{1,0:T(8,128)(2,1)S(1)} %fusion.10), channel_id=1, source_target_pairs={{0,16},{8,24},{16,0},{24,8},{1,17},{9,25},{17,1},{25,9},{2,18},{10... | collective-permute-start | bytes 589832 | tf_op jit(solution)/shard_map/ppermute | solution.py:64
  50.3 6.0 %copy-start.2 = (f32[3072]{0:T(1024)S(1)}, f32[3072]{0:T(1024)}, u32[]{:S(2)}) copy-start(f32[3072]{0:T(1024)} %param.6) | copy-start | bytes 36868
  50.3 5.9 %collective-permute-start.4 = (bf16[64,1536]{1,0:T(8,128)(2,1)S(1)}, bf16[64,1536]{1,0:T(8,128)(2,1)S(1)}, u32[]{:S(2)}, u32[]{:S(2)}) collective-permute-start(bf16[64,1536]{1,0:T(8,128)(2,1)S(1)} %fusion.11), channel_id=1, source_target_pairs={{0,8},{8,0},{16,24},{24,16},{1,9},{9,1},{17,25},{25,17},{2,10},{10... | collective-permute-start | bytes 589832 | tf_op jit(solution)/shard_map/ppermute | solution.py:64
  58.5 5.7 %collective-permute-start.5 = (bf16[64,1536]{1,0:T(8,128)(2,1)S(1)}, bf16[64,1536]{1,0:T(8,128)(2,1)S(1)}, u32[]{:S(2)}, u32[]{:S(2)}) collective-permute-start(bf16[64,1536]{1,0:T(8,128)(2,1)S(1)} %get-tuple-element.24), channel_id=1, source_target_pairs={{0,8},{8,0},{16,24},{24,16},{1,9},{9,1},{17,25},{25,17},{2,10},{10... | collective-permute-start | bytes 589832 | tf_op jit(solution)/shard_map/ppermute | solution.py:64
  60.0 5.7 %collective-permute-start.7 = (bf16[64,1536]{1,0:T(8,128)(2,1)S(1)}, bf16[64,1536]{1,0:T(8,128)(2,1)S(1)}, u32[]{:S(2)}, u32[]{:S(2)}) collective-permute-start(bf16[64,1536]{1,0:T(8,128)(2,1)S(1)} %get-tuple-element.25), channel_id=1, source_target_pairs={{0,16},{8,24},{16,0},{24,8},{1,17},{9,25},{17,1},{25,9},{2,18},{10... | collective-permute-start | bytes 589832 | tf_op jit(solution)/shard_map/ppermute | solution.py:64
  65.9 8.0 %collective-permute-start.8 = (bf16[2,64,1536]{2,1,0:T(8,128)(2,1)S(1)}, bf16[2,64,1536]{2,1,0:T(8,128)(2,1)S(1)}, u32[]{:S(2)}, u32[]{:S(2)}) collective-permute-start(bf16[2,64,1536]{2,1,0:T(8,128)(2,1)S(1)} %pad_maximum_fusion.3), channel_id=1, source_target_pairs={{0,8},{8,0},{16,24},{24,16},{1,9},{9,1},{17,25},{25,17},{2,10},{10... | collective-permute-start | bytes 1179656 | tf_op jit(solution)/shard_map/ppermute | solution.py:64
  66.4 7.9 %collective-permute-start.6 = (bf16[2,64,1536]{2,1,0:T(8,128)(2,1)S(1)}, bf16[2,64,1536]{2,1,0:T(8,128)(2,1)}, u32[]{:S(2)}, u32[]{:S(2)}) collective-permute-start(bf16[2,64,1536]{2,1,0:T(8,128)(2,1)S(1)} %pad_maximum_fusion.2), channel_id=1, source_target_pairs={{0,16},{8,24},{16,0},{24,8},{1,17},{9,25},{17,1},{25,9},{2,18},{10... | collective-permute-start | bytes 1179656 | tf_op jit(solution)/shard_map/ppermute | solution.py:64
  84.8 2.2 %copy-start.1 = (f32[256,3072]{1,0:T(8,128)}, f32[256,3072]{1,0:T(8,128)S(1)}, u32[]{:S(2)}) copy-start(f32[256,3072]{1,0:T(8,128)S(1)} %fusion.13) | copy-start | bytes 9437188
  87.0 3.8 %collective-permute-start.9 = (f32[4,32,3072]{2,1,0:T(8,128)}, f32[4,32,3072]{2,1,0:T(8,128)}, u32[]{:S(2)}, u32[]{:S(2)}) collective-permute-start(f32[4,32,3072]{2,1,0:T(8,128)} %dynamic-slice_bitcast_fusion), channel_id=1, source_target_pairs={{0,1},{1,0},{2,3},{3,2},{4,5},{5,4},{6,7},{7,6},{8,9},{9,8},{10,11... | collective-permute-start | bytes 4718600 | tf_op jit(solution)/shard_map/ppermute | solution.py:64
  93.6 11.4 %collective-permute-start.10 = (bf16[2,32,3072]{2,1,0:T(8,128)(2,1)}, bf16[2,32,3072]{2,1,0:T(8,128)(2,1)S(1)}, u32[]{:S(2)}, u32[]{:S(2)}) collective-permute-start(bf16[2,32,3072]{2,1,0:T(8,128)(2,1)} %fusion.7), channel_id=1, source_target_pairs={{0,2},{1,3},{2,0},{3,1},{4,6},{5,7},{6,4},{7,5},{8,10},{9,11},{10,... | collective-permute-start | bytes 1179656 | tf_op jit(solution)/shard_map/ppermute | solution.py:64
  105.1 11.3 %collective-permute-start.11 = (bf16[32,3072]{1,0:T(8,128)(2,1)S(1)}, bf16[32,3072]{1,0:T(8,128)(2,1)S(1)}, u32[]{:S(2)}, u32[]{:S(2)}) collective-permute-start(bf16[32,3072]{1,0:T(8,128)(2,1)S(1)} %fusion.12), channel_id=1, source_target_pairs={{0,4},{1,5},{2,6},{3,7},{4,0},{5,1},{6,2},{7,3},{8,12},{9,13},{10,... | collective-permute-start | bytes 589832 | tf_op jit(solution)/shard_map/ppermute | solution.py:64

commit v15 on v14

--- a/solution.py
+++ b/solution.py
@@ -144,7 +144,8 @@
     m = partial.shape[0] // n
     k = lax.axis_index(axis) % 2
     by_core = jnp.swapaxes(partial.reshape(n // 2, 2, m, partial.shape[1]), 0, 1)
-    chip = _pick(k, by_core) + _swap(_pick(1 - k, by_core), axis, 1)
+    moved = _swap(_pick(1 - k, by_core).astype(jnp.bfloat16), axis, 1)
+    chip = _pick(k, by_core) + moved.astype(jnp.float32)
     chips = n // 2
     z = lax.axis_index(axis) // 2
     if chips & (chips - 1):

time: 117 us -> 117 us (level)
    squeeze x1 -> x0, local copies, waits for them, and re-layouts: 1.42 us -> none  [_pick(): return lax.dynamic_index_in_dim(blocks, index, axis=0, keepdims=False)]
  transfers between devices with their start and end apart: 12 -> 12, of which waited for: 11 -> 11; matrix products, arithmetic and copies ran while one was open for 4% -> 5% of each run, Pallas kernels for 11% -> 11%
where the time goes in v15:
time: 117 us; the launch traced here: 116 us
  waiting for transfers between devices  34.7 us (30%)
  blocking collectives  21.5 us (18%)
  matrix products  18 us (15%)
  Pallas kernels  13.3 us (11%)
  starting transfers between devices  10.3 us (9%)
  other arithmetic  9.94 us (8%)
  local copies, waits for them, and re-layouts  7.55 us (6%)
    ppermute x12, waiting for transfers between devices, _swap(): return lax.ppermute(value, axis, [(i, i ^ flip) for i in range(size)])  34.7 us
    all_gather x1, blocking collectives, col_all_gather(): mine = lax.all_gather(block, axis, axis_index_groups=groups)  21.5 us
    pallas_call x2, Pallas kernels, outer_product_sum(): pl.pallas_call(kernel, grid=(n // block_n, count), in_specs=in_specs, out...  13.3 us
    ppermute x12, starting transfers between devices, _swap(): return lax.ppermute(value, axis, [(i, i ^ flip) for i in range(size)])  10.3 us
    dot_general x1, matrix products, body(): lax.dot_general(full_grad, weight, (((1,), (1,)), ((), ())), preferred_el...  9.04 us
    dot_general x1, matrix products, body(): partial_value = jnp.dot(local_x, weight, preferred_element_type=jnp.float32)  8.99 us
    unnamed x6, local copies, waits for them, and re-layouts  2.8 us
  transfers between devices with their start and end apart: 12, of which 11 were waited for; matrix products, arithmetic and copies ran while one was open for 5% of the time, Pallas kernels for 11%

profile of v15, /device:TPU:0, one launch (start us, length us, event | category | flops | bytes accessed | tf_op | source)
XLA Modules:
  0.0 116.2 jit_solution(2681182316520752264)
XLA Ops:
  0.6 21.5 %all-gather = bf16[128,3072]{1,0:T(8,128)(2,1)S(1)} all-gather(bf16[32,3072]{1,0:T(8,128)(2,1)} %param.4), channel_id=2, replica_groups={{0,2,4,6},{1,3,5,7},{8,10,12,14},{9,11,13,15},{16,18,20,22},{17,19,21,2..., dimensions={0}, use_global_device_ids=true | all-gather | bytes 983040 | tf_op jit(solution)/shard_map/all_gather | solution.py:135
  22.1 2.3 %collective-permute-done = bf16[4,32,3072]{2,1,0:T(8,128)(2,1)S(1)} collective-permute-done((bf16[4,32,3072]{2,1,0:T(8,128)(2,1)S(1)}, bf16[4,32,3072]{2,1,0:T(8,128)(2,1)S(1)}, u32[]{:S(2)}, u32[]{:S(2)}) %collective-permute-start) | collective-permute-done | bytes 786464 | tf_op jit(solution)/shard_map/ppermute | solution.py:64
  24.8 9.0 %fusion.17 = f32[256,3072]{1,0:T(8,128)S(1)} fusion(bf16[256,3072]{1,0:T(8,128)(2,1)S(1)} %bitcast.82, bf16[3072,3072]{1,0:T(8,128)(2,1)} %param.5), kind=kOutput, calls=%fused_computation.52 | convolution fusion | flops 4831838208 | bytes 23592960 | tf_op jit(solution)/shard_map/dot_general | solution.py:175
  36.0 1.5 %collective-permute-start.1 = (bf16[2,64,1536]{2,1,0:T(8,128)(2,1)}, bf16[2,64,1536]{2,1,0:T(8,128)(2,1)S(1)}, u32[]{:S(2)}, u32[]{:S(2)}) collective-permute-start(bf16[2,64,1536]{2,1,0:T(8,128)(2,1)} %fusion.9), channel_id=1, source_target_pairs={{0,8},{8,0},{16,24},{24,16},{1,9},{9,1},{17,25},{25,17},{2,10},{10... | collective-permute-start | bytes 1179656 | tf_op jit(solution)/shard_map/ppermute | solution.py:64
  37.5 1.6 %collective-permute-start.3 = (bf16[2,64,1536]{2,1,0:T(8,128)(2,1)S(1)}, bf16[2,64,1536]{2,1,0:T(8,128)(2,1)S(1)}, u32[]{:S(2)}, u32[]{:S(2)}) collective-permute-start(bf16[2,64,1536]{2,1,0:T(8,128)(2,1)S(1)} %fusion.7), channel_id=1, source_target_pairs={{0,16},{8,24},{16,0},{24,8},{1,17},{9,25},{17,1},{25,9},{2,18},{10... | collective-permute-start | bytes 1179656 | tf_op jit(solution)/shard_map/ppermute | solution.py:64
  39.1 8.2 %collective-permute-done.1 = bf16[2,64,1536]{2,1,0:T(8,128)(2,1)S(1)} collective-permute-done((bf16[2,64,1536]{2,1,0:T(8,128)(2,1)}, bf16[2,64,1536]{2,1,0:T(8,128)(2,1)S(1)}, u32[]{:S(2)}, u32[]{:S(2)}) %collective-permute-start.1) | collective-permute-done | bytes 393248 | tf_op jit(solution)/shard_map/ppermute | solution.py:64
  48.6 1.6 %collective-permute-start.2 = (bf16[64,1536]{1,0:T(8,128)(2,1)S(1)}, bf16[64,1536]{1,0:T(8,128)(2,1)S(1)}, u32[]{:S(2)}, u32[]{:S(2)}) collective-permute-start(bf16[64,1536]{1,0:T(8,128)(2,1)S(1)} %fusion.11), channel_id=1, source_target_pairs={{0,16},{8,24},{16,0},{24,8},{1,17},{9,25},{17,1},{25,9},{2,18},{10... | collective-permute-start | bytes 589832 | tf_op jit(solution)/shard_map/ppermute | solution.py:64
  50.3 1.6 %collective-permute-start.4 = (bf16[64,1536]{1,0:T(8,128)(2,1)S(1)}, bf16[64,1536]{1,0:T(8,128)(2,1)S(1)}, u32[]{:S(2)}, u32[]{:S(2)}) collective-permute-start(bf16[64,1536]{1,0:T(8,128)(2,1)S(1)} %fusion.12), channel_id=1, source_target_pairs={{0,8},{8,0},{16,24},{24,16},{1,9},{9,1},{17,25},{25,17},{2,10},{10... | collective-permute-start | bytes 589832 | tf_op jit(solution)/shard_map/ppermute | solution.py:64
  51.9 2.9 %collective-permute-done.2 = bf16[64,1536]{1,0:T(8,128)(2,1)S(1)} collective-permute-done((bf16[64,1536]{1,0:T(8,128)(2,1)S(1)}, bf16[64,1536]{1,0:T(8,128)(2,1)S(1)}, u32[]{:S(2)}, u32[]{:S(2)}) %collective-permute-start.2) | collective-permute-done | bytes 196640 | tf_op jit(solution)/shard_map/ppermute | solution.py:64
  54.8 1.4 %collective-permute-done.4 = bf16[64,1536]{1,0:T(8,128)(2,1)S(1)} collective-permute-done((bf16[64,1536]{1,0:T(8,128)(2,1)S(1)}, bf16[64,1536]{1,0:T(8,128)(2,1)S(1)}, u32[]{:S(2)}, u32[]{:S(2)}) %collective-permute-start.4) | collective-permute-done | bytes 196640 | tf_op jit(solution)/shard_map/ppermute | solution.py:64
  56.3 2.2 %fusion.5 = (bf16[64,3072]{1,0:T(8,128)(2,1)S(1)}, bf16[64,3072]{1,0:T(8,128)(2,1)}) fusion(f32[64,1536]{1,0:T(8,128)S(1)} %bitcast_add_fusion.5, f32[64,1536]{1,0:T(8,128)S(1)} %bitcast_add_fusion.6, bf16[256,3072]{1,0:T(8,128)(2,1)} %param.7, s32[]{:T(128)S(6)} %select_n.121, f32[3072]{0:T(1024)S(1)} %copy-done.2), kind=kLoop, calls=%fused_computation.11 | loop fusion | flops 2949120 | bytes 1978372 | tf_op jit(solution)/shard_map/convert_element_type | solution.py:15
  58.5 1.6 %collective-permute-start.5 = (bf16[64,1536]{1,0:T(8,128)(2,1)S(1)}, bf16[64,1536]{1,0:T(8,128)(2,1)S(1)}, u32[]{:S(2)}, u32[]{:S(2)}) collective-permute-start(bf16[64,1536]{1,0:T(8,128)(2,1)S(1)} %get-tuple-element.24), channel_id=1, source_target_pairs={{0,8},{8,0},{16,24},{24,16},{1,9},{9,1},{17,25},{25,17},{2,10},{10... | collective-permute-start | bytes 589832 | tf_op jit(solution)/shard_map/ppermute | solution.py:64
  60.5 3.7 %collective-permute-done.5 = bf16[64,1536]{1,0:T(8,128)(2,1)S(1)} collective-permute-done((bf16[64,1536]{1,0:T(8,128)(2,1)S(1)}, bf16[64,1536]{1,0:T(8,128)(2,1)S(1)}, u32[]{:S(2)}, u32[]{:S(2)}) %collective-permute-start.5) | collective-permute-done | bytes 196640 | tf_op jit(solution)/shard_map/ppermute | solution.py:64
  64.2 1.6 %collective-permute-done.7 = bf16[64,1536]{1,0:T(8,128)(2,1)S(1)} collective-permute-done((bf16[64,1536]{1,0:T(8,128)(2,1)S(1)}, bf16[64,1536]{1,0:T(8,128)(2,1)S(1)}, u32[]{:S(2)}, u32[]{:S(2)}) %collective-permute-start.7) | collective-permute-done | bytes 196640 | tf_op jit(solution)/shard_map/ppermute | solution.py:64
  67.0 6.8 %collective-permute-done.8 = bf16[2,64,1536]{2,1,0:T(8,128)(2,1)S(1)} collective-permute-done((bf16[2,64,1536]{2,1,0:T(8,128)(2,1)S(1)}, bf16[2,64,1536]{2,1,0:T(8,128)(2,1)S(1)}, u32[]{:S(2)}, u32[]{:S(2)}) %collective-permute-start.8) | collective-permute-done | bytes 393248 | tf_op jit(solution)/shard_map/ppermute | solution.py:64
  75.7 9.0 %fusion.14 = f32[256,3072]{1,0:T(8,128)S(1)} fusion(bf16[3072,3072]{1,0:T(8,128)(2,1)} %param.5, bf16[256,1536]{1,0:T(8,128)(2,1)S(1)} %bitcast.76, bf16[256,1536]{1,0:T(8,128)(2,1)S(1)} %bitcast.79), kind=kOutput, calls=%fused_computation.49 | convolution fusion | flops 4834983936 | bytes 23592960 | tf_op jit(solution)/shard_map/dot_general | solution.py:184
  84.8 1.7 %copy-done.1 = f32[256,3072]{1,0:T(8,128)} copy-done((f32[256,3072]{1,0:T(8,128)}, f32[256,3072]{1,0:T(8,128)S(1)}, u32[]{:S(2)}) %copy-start.1) | copy-done | bytes 3145752
  87.4 1.6 %copy.19 = bf16[256,3072]{0,1:T(8,128)(2,1)} copy(bf16[256,3072]{1,0:T(8,128)(2,1)S(1)} %bitcast.83) | data formatting | bytes 3145728 | tf_op jit(solution)/shard_map/reshape | solution.py:137
  90.0 1.8 %bitcast_add_fusion = f32[4,32,3072]{2,1,0:T(8,128)S(1)} fusion(bf16[4,32,3072]{2,1,0:T(8,128)(2,1)} %collective-permute-done.9, f32[4,2,32,3072]{3,2,1,0:T(8,128)} %bitcast.93, s32[]{:T(128)S(6)} %select_n.132), kind=kLoop, calls=%fused_computation.4 | loop fusion | flops 786432 | bytes 3932164 | tf_op jit(solution)/shard_map/add | solution.py:148
  92.7 1.3 %pad_maximum_fusion.g_ref = bf16[256,3072]{1,0:T(8,128)(2,1)} fusion(bf16[256,1536]{1,0:T(8,128)(2,1)S(1)} %bitcast.77, bf16[256,1536]{1,0:T(8,128)(2,1)S(1)} %bitcast.80), kind=kLoop, calls=%fused_computation.2 | loop fusion | flops 3145728 | bytes 3145728 | tf_op jit(solution)/shard_map/concatenate | solution.py:127
  94.9 6.7 %shard_map.75._ = bf16[3072,3072]{1,0:T(8,128)(2,1)} custom-call(bf16[3072,256]{1,0:T(8,128)(2,1)} %bitcast.74, bf16[256,3072]{1,0:T(8,128)(2,1)} %pad_maximum_fusion.g_ref), custom_call_target="tpu_custom_call" | custom-call | flops 2415919104 | bytes 11796480 | tf_op jit(solution)/shard_map/pallas_call | solution.py:49
  101.6 2.5 %collective-permute-done.10 = bf16[2,32,3072]{2,1,0:T(8,128)(2,1)S(1)} collective-permute-done((bf16[2,32,3072]{2,1,0:T(8,128)(2,1)}, bf16[2,32,3072]{2,1,0:T(8,128)(2,1)S(1)}, u32[]{:S(2)}, u32[]{:S(2)}) %collective-permute-start.10) | collective-permute-done | bytes 393248 | tf_op jit(solution)/shard_map/ppermute | solution.py:64
  105.1 6.7 %shard_map.76 = bf16[3072,3072]{1,0:T(8,128)(2,1)} custom-call(bf16[3072,256]{1,0:T(8,128)(2,1)} %bitcast.75, bf16[256,3072]{1,0:T(8,128)(2,1)} %pad_maximum_fusion.g_ref, bf16[3072,3072]{1,0:T(8,128)(2,1)} %shard_map.75._), custom_call_target="tpu_custom_call", output_to_operand_aliasing={{}: (2, {})} | custom-call | flops 2415919104 | bytes 11796480 | tf_op jit(solution)/shard_map/pallas_call | solution.py:49
  111.7 3.7 %collective-permute-done.11 = bf16[32,3072]{1,0:T(8,128)(2,1)S(1)} collective-permute-done((bf16[32,3072]{1,0:T(8,128)(2,1)S(1)}, bf16[32,3072]{1,0:T(8,128)(2,1)S(1)}, u32[]{:S(2)}, u32[]{:S(2)}) %collective-permute-start.11) | collective-permute-done | bytes 196640 | tf_op jit(solution)/shard_map/ppermute | solution.py:64
  (41 shorter events, 13.0 us)
Async XLA Ops:
  22.1 2.3 %collective-permute-start = (bf16[4,32,3072]{2,1,0:T(8,128)(2,1)S(1)}, bf16[4,32,3072]{2,1,0:T(8,128)(2,1)S(1)}, u32[]{:S(2)}, u32[]{:S(2)}) collective-permute-start(bf16[4,32,3072]{2,1,0:T(8,128)(2,1)S(1)} %bitcast.90), channel_id=1, source_target_pairs={{0,1},{1,0},{2,3},{3,2},{4,5},{5,4},{6,7},{7,6},{8,9},{9,8},{10,11... | collective-permute-start | bytes 2359304 | tf_op jit(solution)/shard_map/ppermute | solution.py:64
  34.1 1.1 copy-start
  36.0 11.4 %collective-permute-start.1 = (bf16[2,64,1536]{2,1,0:T(8,128)(2,1)}, bf16[2,64,1536]{2,1,0:T(8,128)(2,1)S(1)}, u32[]{:S(2)}, u32[]{:S(2)}) collective-permute-start(bf16[2,64,1536]{2,1,0:T(8,128)(2,1)} %fusion.9), channel_id=1, source_target_pairs={{0,8},{8,0},{16,24},{24,16},{1,9},{9,1},{17,25},{25,17},{2,10},{10... | collective-permute-start | bytes 1179656 | tf_op jit(solution)/shard_map/ppermute | solution.py:64
  37.5 12.7 %collective-permute-start.3 = (bf16[2,64,1536]{2,1,0:T(8,128)(2,1)S(1)}, bf16[2,64,1536]{2,1,0:T(8,128)(2,1)S(1)}, u32[]{:S(2)}, u32[]{:S(2)}) collective-permute-start(bf16[2,64,1536]{2,1,0:T(8,128)(2,1)S(1)} %fusion.7), channel_id=1, source_target_pairs={{0,16},{8,24},{16,0},{24,8},{1,17},{9,25},{17,1},{25,9},{2,18},{10... | collective-permute-start | bytes 1179656 | tf_op jit(solution)/shard_map/ppermute | solution.py:64
  48.6 6.2 %collective-permute-start.2 = (bf16[64,1536]{1,0:T(8,128)(2,1)S(1)}, bf16[64,1536]{1,0:T(8,128)(2,1)S(1)}, u32[]{:S(2)}, u32[]{:S(2)}) collective-permute-start(bf16[64,1536]{1,0:T(8,128)(2,1)S(1)} %fusion.11), channel_id=1, source_target_pairs={{0,16},{8,24},{16,0},{24,8},{1,17},{9,25},{17,1},{25,9},{2,18},{10... | collective-permute-start | bytes 589832 | tf_op jit(solution)/shard_map/ppermute | solution.py:64
  50.3 6.0 %copy-start.2 = (f32[3072]{0:T(1024)S(1)}, f32[3072]{0:T(1024)}, u32[]{:S(2)}) copy-start(f32[3072]{0:T(1024)} %param.6) | copy-start | bytes 36868
  50.3 5.9 %collective-permute-start.4 = (bf16[64,1536]{1,0:T(8,128)(2,1)S(1)}, bf16[64,1536]{1,0:T(8,128)(2,1)S(1)}, u32[]{:S(2)}, u32[]{:S(2)}) collective-permute-start(bf16[64,1536]{1,0:T(8,128)(2,1)S(1)} %fusion.12), channel_id=1, source_target_pairs={{0,8},{8,0},{16,24},{24,16},{1,9},{9,1},{17,25},{25,17},{2,10},{10... | collective-permute-start | bytes 589832 | tf_op jit(solution)/shard_map/ppermute | solution.py:64
  58.5 5.7 %collective-permute-start.5 = (bf16[64,1536]{1,0:T(8,128)(2,1)S(1)}, bf16[64,1536]{1,0:T(8,128)(2,1)S(1)}, u32[]{:S(2)}, u32[]{:S(2)}) collective-permute-start(bf16[64,1536]{1,0:T(8,128)(2,1)S(1)} %get-tuple-element.24), channel_id=1, source_target_pairs={{0,8},{8,0},{16,24},{24,16},{1,9},{9,1},{17,25},{25,17},{2,10},{10... | collective-permute-start | bytes 589832 | tf_op jit(solution)/shard_map/ppermute | solution.py:64
  60.0 5.7 %collective-permute-start.7 = (bf16[64,1536]{1,0:T(8,128)(2,1)S(1)}, bf16[64,1536]{1,0:T(8,128)(2,1)S(1)}, u32[]{:S(2)}, u32[]{:S(2)}) collective-permute-start(bf16[64,1536]{1,0:T(8,128)(2,1)S(1)} %get-tuple-element.25), channel_id=1, source_target_pairs={{0,16},{8,24},{16,0},{24,8},{1,17},{9,25},{17,1},{25,9},{2,18},{10... | collective-permute-start | bytes 589832 | tf_op jit(solution)/shard_map/ppermute | solution.py:64
  65.9 8.0 %collective-permute-start.8 = (bf16[2,64,1536]{2,1,0:T(8,128)(2,1)S(1)}, bf16[2,64,1536]{2,1,0:T(8,128)(2,1)S(1)}, u32[]{:S(2)}, u32[]{:S(2)}) collective-permute-start(bf16[2,64,1536]{2,1,0:T(8,128)(2,1)S(1)} %pad_maximum_fusion.3), channel_id=1, source_target_pairs={{0,8},{8,0},{16,24},{24,16},{1,9},{9,1},{17,25},{25,17},{2,10},{10... | collective-permute-start | bytes 1179656 | tf_op jit(solution)/shard_map/ppermute | solution.py:64
  66.4 7.9 %collective-permute-start.6 = (bf16[2,64,1536]{2,1,0:T(8,128)(2,1)S(1)}, bf16[2,64,1536]{2,1,0:T(8,128)(2,1)}, u32[]{:S(2)}, u32[]{:S(2)}) collective-permute-start(bf16[2,64,1536]{2,1,0:T(8,128)(2,1)S(1)} %pad_maximum_fusion.2), channel_id=1, source_target_pairs={{0,16},{8,24},{16,0},{24,8},{1,17},{9,25},{17,1},{25,9},{2,18},{10... | collective-permute-start | bytes 1179656 | tf_op jit(solution)/shard_map/ppermute | solution.py:64
  84.8 1.7 %copy-start.1 = (f32[256,3072]{1,0:T(8,128)}, f32[256,3072]{1,0:T(8,128)S(1)}, u32[]{:S(2)}) copy-start(f32[256,3072]{1,0:T(8,128)S(1)} %fusion.14) | copy-start | bytes 9437188
  87.4 2.6 %collective-permute-start.9 = (bf16[4,32,3072]{2,1,0:T(8,128)(2,1)}, bf16[4,32,3072]{2,1,0:T(8,128)(2,1)}, u32[]{:S(2)}, u32[]{:S(2)}) collective-permute-start(bf16[4,32,3072]{2,1,0:T(8,128)(2,1)} %fusion.6), channel_id=1, source_target_pairs={{0,1},{1,0},{2,3},{3,2},{4,5},{5,4},{6,7},{7,6},{8,9},{9,8},{10,11... | collective-permute-start | bytes 2359304 | tf_op jit(solution)/shard_map/ppermute | solution.py:64
  92.7 11.4 %collective-permute-start.10 = (bf16[2,32,3072]{2,1,0:T(8,128)(2,1)}, bf16[2,32,3072]{2,1,0:T(8,128)(2,1)S(1)}, u32[]{:S(2)}, u32[]{:S(2)}) collective-permute-start(bf16[2,32,3072]{2,1,0:T(8,128)(2,1)} %fusion.8), channel_id=1, source_target_pairs={{0,2},{1,3},{2,0},{3,1},{4,6},{5,7},{6,4},{7,5},{8,10},{9,11},{10,... | collective-permute-start | bytes 1179656 | tf_op jit(solution)/shard_map/ppermute | solution.py:64
  104.2 11.3 %collective-permute-start.11 = (bf16[32,3072]{1,0:T(8,128)(2,1)S(1)}, bf16[32,3072]{1,0:T(8,128)(2,1)S(1)}, u32[]{:S(2)}, u32[]{:S(2)}) collective-permute-start(bf16[32,3072]{1,0:T(8,128)(2,1)S(1)} %fusion.13), channel_id=1, source_target_pairs={{0,4},{1,5},{2,6},{3,7},{4,0},{5,1},{6,2},{7,3},{8,12},{9,13},{10,... | collective-permute-start | bytes 589832 | tf_op jit(solution)/shard_map/ppermute | solution.py:64

commit v16 on v15

--- a/solution.py
+++ b/solution.py
@@ -155,17 +155,22 @@
             total = total + lax.ppermute(_pick((z + d) % chips, chip), axis, pairs)
         return total, hold
     levels = chips.bit_length() - 1
-    cur = chip.reshape([2] * levels + [m, partial.shape[1]])
-    bits = list(range(levels))[::-1]
-    for bit in range(levels):
-        mine = (z >> bit) & 1
-        t = jnp.moveaxis(cur, bits.index(bit), 0)
-        sent = _swap(_pick(1 - mine, t).astype(jnp.bfloat16), axis, 2 << bit)
-        cur = _pick(mine, t) + sent.astype(jnp.float32)
-        bits.remove(bit)
-        if bit == 0:
-            cur, hold = lax.optimization_barrier((cur, hold))
-    return cur.reshape(m, partial.shape[1]), hold
+    halves = _halves(chip.reshape(chips * m, -1))
+    orders = _bit_orders(chips)
+    outs = []
+    for half, order in zip(halves, orders):
+        cur = half.reshape([2] * levels + [m, half.shape[1]])
+        bits = list(range(levels))[::-1]
+        for bit in order:
+            mine = (z >> bit) & 1
+            t = jnp.moveaxis(cur, bits.index(bit), 0)
+            sent = _swap(_pick(1 - mine, t).astype(jnp.bfloat16), axis, 2 << bit)
+            cur = _pick(mine, t) + sent.astype(jnp.float32)
+            bits.remove(bit)
+            if len(bits) == levels - 1:
+                cur, hold = lax.optimization_barrier((cur, hold))
+        outs.append(cur.reshape(m, half.shape[1]))
+    return jnp.concatenate(outs, axis=1), hold
 
 
 def body(tokens, weight, bias, cotangent):

time: 117 us -> 126 us (1.077)
  waiting for transfers between devices: 34.7 us -> 40.2 us
  starting transfers between devices: 10.3 us -> 14.3 us
    ppermute x12 -> x14, waiting for transfers between devices: 34.7 us -> 40.2 us  [_swap(): return lax.ppermute(value, axis, [(i, i ^ flip) for i in range(size)])]
    ppermute x12 -> x14, starting transfers between devices: 10.3 us -> 14.3 us  [_swap(): return lax.ppermute(value, axis, [(i, i ^ flip) for i in range(size)])]
  transfers between devices with their start and end apart: 12 -> 14, of which waited for: 11 -> 11; matrix products, arithmetic and copies ran while one was open for 5% -> 4% of each run, Pallas kernels for 11% -> 11%
where the time goes in v16:
time: 126 us; the launch traced here: 125 us
  waiting for transfers between devices  40.2 us (32%)
  blocking collectives  21.5 us (17%)
  matrix products  18 us (14%)
  starting transfers between devices  14.3 us (11%)
  Pallas kernels  13.4 us (11%)
  other arithmetic  10 us (8%)
  local copies, waits for them, and re-layouts  6.88 us (5%)
    ppermute x14, waiting for transfers between devices, _swap(): return lax.ppermute(value, axis, [(i, i ^ flip) for i in range(size)])  40.2 us
    all_gather x1, blocking collectives, col_all_gather(): mine = lax.all_gather(block, axis, axis_index_groups=groups)  21.5 us
    ppermute x14, starting transfers between devices, _swap(): return lax.ppermute(value, axis, [(i, i ^ flip) for i in range(size)])  14.3 us
    pallas_call x2, Pallas kernels, outer_product_sum(): pl.pallas_call(kernel, grid=(n // block_n, count), in_specs=in_specs, out...  13.4 us
    dot_general x1, matrix products, body(): lax.dot_general(full_grad, weight, (((1,), (1,)), ((), ())), preferred_el...  9.04 us
    dot_general x1, matrix products, body(): partial_value = jnp.dot(local_x, weight, preferred_element_type=jnp.float32)  8.99 us
    unnamed x6, local copies, waits for them, and re-layouts  2.79 us
  transfers between devices with their start and end apart: 14, of which 11 were waited for; matrix products, arithmetic and copies ran while one was open for 4% of the time, Pallas kernels for 11%

profile of v16, /device:TPU:0, one launch (start us, length us, event | category | flops | bytes accessed | tf_op | source)
XLA Modules:
  0.0 125.2 jit_solution(508233102395886927)
XLA Ops:
  0.6 21.5 %all-gather = bf16[128,3072]{1,0:T(8,128)(2,1)S(1)} all-gather(bf16[32,3072]{1,0:T(8,128)(2,1)} %param.4), channel_id=2, replica_groups={{0,2,4,6},{1,3,5,7},{8,10,12,14},{9,11,13,15},{16,18,20,22},{17,19,21,2..., dimensions={0}, use_global_device_ids=true | all-gather | bytes 983040 | tf_op jit(solution)/shard_map/all_gather | solution.py:135
  22.1 2.3 %collective-permute-done = bf16[4,32,3072]{2,1,0:T(8,128)(2,1)S(1)} collective-permute-done((bf16[4,32,3072]{2,1,0:T(8,128)(2,1)S(1)}, bf16[4,32,3072]{2,1,0:T(8,128)(2,1)S(1)}, u32[]{:S(2)}, u32[]{:S(2)}) %collective-permute-start) | collective-permute-done | bytes 786464 | tf_op jit(solution)/shard_map/ppermute | solution.py:64
  24.8 9.0 %fusion.21 = f32[256,3072]{1,0:T(8,128)S(1)} fusion(bf16[256,3072]{1,0:T(8,128)(2,1)S(1)} %bitcast.90, bf16[3072,3072]{1,0:T(8,128)(2,1)} %param.5), kind=kOutput, calls=%fused_computation.61 | convolution fusion | flops 4831838208 | bytes 23592960 | tf_op jit(solution)/shard_map/dot_general | solution.py:180
  37.5 1.6 %collective-permute-start.3 = (bf16[2,64,1536]{2,1,0:T(8,128)(2,1)S(1)}, bf16[2,64,1536]{2,1,0:T(8,128)(2,1)S(1)}, u32[]{:S(2)}, u32[]{:S(2)}) collective-permute-start(bf16[2,64,1536]{2,1,0:T(8,128)(2,1)S(1)} %fusion.7), channel_id=1, source_target_pairs={{0,16},{8,24},{16,0},{24,8},{1,17},{9,25},{17,1},{25,9},{2,18},{10... | collective-permute-start | bytes 1179656 | tf_op jit(solution)/shard_map/ppermute | solution.py:64
  39.1 8.2 %collective-permute-done.1 = bf16[2,64,1536]{2,1,0:T(8,128)(2,1)S(1)} collective-permute-done((bf16[2,64,1536]{2,1,0:T(8,128)(2,1)}, bf16[2,64,1536]{2,1,0:T(8,128)(2,1)S(1)}, u32[]{:S(2)}, u32[]{:S(2)}) %collective-permute-start.1) | collective-permute-done | bytes 393248 | tf_op jit(solution)/shard_map/ppermute | solution.py:64
  48.6 1.6 %collective-permute-start.2 = (bf16[64,1536]{1,0:T(8,128)(2,1)S(1)}, bf16[64,1536]{1,0:T(8,128)(2,1)S(1)}, u32[]{:S(2)}, u32[]{:S(2)}) collective-permute-start(bf16[64,1536]{1,0:T(8,128)(2,1)S(1)} %fusion.9), channel_id=1, source_target_pairs={{0,16},{8,24},{16,0},{24,8},{1,17},{9,25},{17,1},{25,9},{2,18},{10... | collective-permute-start | bytes 589832 | tf_op jit(solution)/shard_map/ppermute | solution.py:64
  50.3 1.6 %collective-permute-start.4 = (bf16[64,1536]{1,0:T(8,128)(2,1)S(1)}, bf16[64,1536]{1,0:T(8,128)(2,1)S(1)}, u32[]{:S(2)}, u32[]{:S(2)}) collective-permute-start(bf16[64,1536]{1,0:T(8,128)(2,1)S(1)} %fusion.10), channel_id=1, source_target_pairs={{0,8},{8,0},{16,24},{24,16},{1,9},{9,1},{17,25},{25,17},{2,10},{10... | collective-permute-start | bytes 589832 | tf_op jit(solution)/shard_map/ppermute | solution.py:64
  51.9 2.9 %collective-permute-done.2 = bf16[64,1536]{1,0:T(8,128)(2,1)S(1)} collective-permute-done((bf16[64,1536]{1,0:T(8,128)(2,1)S(1)}, bf16[64,1536]{1,0:T(8,128)(2,1)S(1)}, u32[]{:S(2)}, u32[]{:S(2)}) %collective-permute-start.2) | collective-permute-done | bytes 196640 | tf_op jit(solution)/shard_map/ppermute | solution.py:64
  56.3 2.2 %fusion.5 = (bf16[64,3072]{1,0:T(8,128)(2,1)S(1)}, bf16[64,3072]{1,0:T(8,128)(2,1)}) fusion(f32[64,1536]{1,0:T(8,128)S(1)} %bitcast_add_fusion.5, f32[64,1536]{1,0:T(8,128)S(1)} %bitcast_add_fusion.6, bf16[256,3072]{1,0:T(8,128)(2,1)} %param.7, s32[]{:T(128)S(6)} %select_n.125, f32[3072]{0:T(1024)S(1)} %copy-done.2), kind=kLoop, calls=%fused_computation.11 | loop fusion | flops 2949120 | bytes 1978372 | tf_op jit(solution)/shard_map/convert_element_type | solution.py:15
  58.5 1.6 %collective-permute-start.5 = (bf16[64,1536]{1,0:T(8,128)(2,1)S(1)}, bf16[64,1536]{1,0:T(8,128)(2,1)S(1)}, u32[]{:S(2)}, u32[]{:S(2)}) collective-permute-start(bf16[64,1536]{1,0:T(8,128)(2,1)S(1)} %get-tuple-element.30), channel_id=1, source_target_pairs={{0,8},{8,0},{16,24},{24,16},{1,9},{9,1},{17,25},{25,17},{2,10},{10... | collective-permute-start | bytes 589832 | tf_op jit(solution)/shard_map/ppermute | solution.py:64
  60.5 3.7 %collective-permute-done.5 = bf16[64,1536]{1,0:T(8,128)(2,1)S(1)} collective-permute-done((bf16[64,1536]{1,0:T(8,128)(2,1)S(1)}, bf16[64,1536]{1,0:T(8,128)(2,1)S(1)}, u32[]{:S(2)}, u32[]{:S(2)}) %collective-permute-start.5) | collective-permute-done | bytes 196640 | tf_op jit(solution)/shard_map/ppermute | solution.py:64
  64.2 1.6 %collective-permute-done.7 = bf16[64,1536]{1,0:T(8,128)(2,1)S(1)} collective-permute-done((bf16[64,1536]{1,0:T(8,128)(2,1)S(1)}, bf16[64,1536]{1,0:T(8,128)(2,1)S(1)}, u32[]{:S(2)}, u32[]{:S(2)}) %collective-permute-start.7) | collective-permute-done | bytes 196640 | tf_op jit(solution)/shard_map/ppermute | solution.py:64
  67.0 6.8 %collective-permute-done.8 = bf16[2,64,1536]{2,1,0:T(8,128)(2,1)S(1)} collective-permute-done((bf16[2,64,1536]{2,1,0:T(8,128)(2,1)S(1)}, bf16[2,64,1536]{2,1,0:T(8,128)(2,1)S(1)}, u32[]{:S(2)}, u32[]{:S(2)}) %collective-permute-start.8) | collective-permute-done | bytes 393248 | tf_op jit(solution)/shard_map/ppermute | solution.py:64
  75.7 9.0 %fusion.17 = f32[256,3072]{1,0:T(8,128)S(1)} fusion(bf16[3072,3072]{1,0:T(8,128)(2,1)} %param.5, bf16[256,1536]{1,0:T(8,128)(2,1)S(1)} %bitcast.84, bf16[256,1536]{1,0:T(8,128)(2,1)S(1)} %bitcast.87), kind=kOutput, calls=%fused_computation.57 | convolution fusion | flops 4834983936 | bytes 23592960 | tf_op jit(solution)/shard_map/dot_general | solution.py:189
  84.8 1.6 %copy-done.1 = f32[256,3072]{1,0:T(8,128)} copy-done((f32[256,3072]{1,0:T(8,128)}, f32[256,3072]{1,0:T(8,128)S(1)}, u32[]{:S(2)}) %copy-start.1) | copy-done | bytes 3145752
  87.4 1.6 %copy.18 = bf16[256,3072]{0,1:T(8,128)(2,1)} copy(bf16[256,3072]{1,0:T(8,128)(2,1)S(1)} %bitcast.91) | data formatting | bytes 3145728 | tf_op jit(solution)/shard_map/reshape | solution.py:137
  91.2 6.7 %shard_map.75._ = bf16[3072,3072]{1,0:T(8,128)(2,1)} custom-call(bf16[3072,256]{1,0:T(8,128)(2,1)} %bitcast.82, bf16[256,3072]{1,0:T(8,128)(2,1)} %pad_maximum_fusion.g_ref), custom_call_target="tpu_custom_call" | custom-call | flops 2415919104 | bytes 11796480 | tf_op jit(solution)/shard_map/pallas_call | solution.py:49
  97.9 1.8 %bitcast_add_fusion = f32[4,32,3072]{2,1,0:T(8,128)S(1)} fusion(bf16[4,32,3072]{2,1,0:T(8,128)(2,1)} %collective-permute-done.9, f32[4,2,32,3072]{3,2,1,0:T(8,128)} %bitcast.104, s32[]{:T(128)S(6)} %select_n.136), kind=kLoop, calls=%fused_computation.3 | loop fusion | flops 786432 | bytes 3932164 | tf_op jit(solution)/shard_map/add | solution.py:148
  100.0 2.3 %collective-permute-start.12 = (bf16[2,32,1536]{2,1,0:T(8,128)(2,1)S(1)}, bf16[2,32,1536]{2,1,0:T(8,128)(2,1)S(1)}, u32[]{:S(2)}, u32[]{:S(2)}) collective-permute-start(bf16[2,32,1536]{2,1,0:T(8,128)(2,1)S(1)} %fusion.12), channel_id=1, source_target_pairs={{0,4},{1,5},{2,6},{3,7},{4,0},{5,1},{6,2},{7,3},{8,12},{9,13},{10,... | collective-permute-start | bytes 589832 | tf_op jit(solution)/shard_map/ppermute | solution.py:64
  102.3 8.5 %collective-permute-done.10 = bf16[2,32,1536]{2,1,0:T(8,128)(2,1)S(1)} collective-permute-done((bf16[2,32,1536]{2,1,0:T(8,128)(2,1)S(1)}, bf16[2,32,1536]{2,1,0:T(8,128)(2,1)S(1)}, u32[]{:S(2)}, u32[]{:S(2)}) %collective-permute-start.10) | collective-permute-done | bytes 196640 | tf_op jit(solution)/shard_map/ppermute | solution.py:64
  110.8 1.7 %collective-permute-done.12 = bf16[2,32,1536]{2,1,0:T(8,128)(2,1)S(1)} collective-permute-done((bf16[2,32,1536]{2,1,0:T(8,128)(2,1)S(1)}, bf16[2,32,1536]{2,1,0:T(8,128)(2,1)S(1)}, u32[]{:S(2)}, u32[]{:S(2)}) %collective-permute-start.12) | collective-permute-done | bytes 196640 | tf_op jit(solution)/shard_map/ppermute | solution.py:64
  112.9 6.7 %shard_map.76 = bf16[3072,3072]{1,0:T(8,128)(2,1)} custom-call(bf16[3072,256]{1,0:T(8,128)(2,1)} %bitcast.83, bf16[256,3072]{1,0:T(8,128)(2,1)} %pad_maximum_fusion.g_ref, bf16[3072,3072]{1,0:T(8,128)(2,1)} %shard_map.75._), custom_call_target="tpu_custom_call", output_to_operand_aliasing={{}: (2, {})} | custom-call | flops 2415919104 | bytes 11796480 | tf_op jit(solution)/shard_map/pallas_call | solution.py:49
  119.6 2.3 %collective-permute-start.13 = (bf16[32,1536]{1,0:T(8,128)(2,1)S(1)}, bf16[32,1536]{1,0:T(8,128)(2,1)S(1)}, u32[]{:S(2)}, u32[]{:S(2)}) collective-permute-start(bf16[32,1536]{1,0:T(8,128)(2,1)S(1)} %fusion.16), channel_id=1, source_target_pairs={{0,2},{1,3},{2,0},{3,1},{4,6},{5,7},{6,4},{7,5},{8,10},{9,11},{10,... | collective-permute-start | bytes 294920 | tf_op jit(solution)/shard_map/ppermute | solution.py:64
  121.9 2.6 %collective-permute-done.13 = bf16[32,1536]{1,0:T(8,128)(2,1)S(1)} collective-permute-done((bf16[32,1536]{1,0:T(8,128)(2,1)S(1)}, bf16[32,1536]{1,0:T(8,128)(2,1)S(1)}, u32[]{:S(2)}, u32[]{:S(2)}) %collective-permute-start.13) | collective-permute-done | bytes 98336 | tf_op jit(solution)/shard_map/ppermute | solution.py:64
  (51 shorter events, 15.1 us)
Async XLA Ops:
  22.1 2.3 %collective-permute-start = (bf16[4,32,3072]{2,1,0:T(8,128)(2,1)S(1)}, bf16[4,32,3072]{2,1,0:T(8,128)(2,1)S(1)}, u32[]{:S(2)}, u32[]{:S(2)}) collective-permute-start(bf16[4,32,3072]{2,1,0:T(8,128)(2,1)S(1)} %bitcast.97), channel_id=1, source_target_pairs={{0,1},{1,0},{2,3},{3,2},{4,5},{5,4},{6,7},{7,6},{8,9},{9,8},{10,11... | collective-permute-start | bytes 2359304 | tf_op jit(solution)/shard_map/ppermute | solution.py:64
  34.1 1.1 copy-start
  36.0 11.4 %collective-permute-start.1 = (bf16[2,64,1536]{2,1,0:T(8,128)(2,1)}, bf16[2,64,1536]{2,1,0:T(8,128)(2,1)S(1)}, u32[]{:S(2)}, u32[]{:S(2)}) collective-permute-start(bf16[2,64,1536]{2,1,0:T(8,128)(2,1)} %fusion.8), channel_id=1, source_target_pairs={{0,8},{8,0},{16,24},{24,16},{1,9},{9,1},{17,25},{25,17},{2,10},{10... | collective-permute-start | bytes 1179656 | tf_op jit(solution)/shard_map/ppermute | solution.py:64
  37.5 12.7 %collective-permute-start.3 = (bf16[2,64,1536]{2,1,0:T(8,128)(2,1)S(1)}, bf16[2,64,1536]{2,1,0:T(8,128)(2,1)S(1)}, u32[]{:S(2)}, u32[]{:S(2)}) collective-permute-start(bf16[2,64,1536]{2,1,0:T(8,128)(2,1)S(1)} %fusion.7), channel_id=1, source_target_pairs={{0,16},{8,24},{16,0},{24,8},{1,17},{9,25},{17,1},{25,9},{2,18},{10... | collective-permute-start | bytes 1179656 | tf_op jit(solution)/shard_map/ppermute | solution.py:64
  48.6 6.2 %collective-permute-start.2 = (bf16[64,1536]{1,0:T(8,128)(2,1)S(1)}, bf16[64,1536]{1,0:T(8,128)(2,1)S(1)}, u32[]{:S(2)}, u32[]{:S(2)}) collective-permute-start(bf16[64,1536]{1,0:T(8,128)(2,1)S(1)} %fusion.9), channel_id=1, source_target_pairs={{0,16},{8,24},{16,0},{24,8},{1,17},{9,25},{17,1},{25,9},{2,18},{10... | collective-permute-start | bytes 589832 | tf_op jit(solution)/shard_map/ppermute | solution.py:64
  50.3 6.0 %copy-start.2 = (f32[3072]{0:T(1024)S(1)}, f32[3072]{0:T(1024)}, u32[]{:S(2)}) copy-start(f32[3072]{0:T(1024)} %param.6) | copy-start | bytes 36868
  50.3 5.9 %collective-permute-start.4 = (bf16[64,1536]{1,0:T(8,128)(2,1)S(1)}, bf16[64,1536]{1,0:T(8,128)(2,1)S(1)}, u32[]{:S(2)}, u32[]{:S(2)}) collective-permute-start(bf16[64,1536]{1,0:T(8,128)(2,1)S(1)} %fusion.10), channel_id=1, source_target_pairs={{0,8},{8,0},{16,24},{24,16},{1,9},{9,1},{17,25},{25,17},{2,10},{10... | collective-permute-start | bytes 589832 | tf_op jit(solution)/shard_map/ppermute | solution.py:64
  58.5 5.7 %collective-permute-start.5 = (bf16[64,1536]{1,0:T(8,128)(2,1)S(1)}, bf16[64,1536]{1,0:T(8,128)(2,1)S(1)}, u32[]{:S(2)}, u32[]{:S(2)}) collective-permute-start(bf16[64,1536]{1,0:T(8,128)(2,1)S(1)} %get-tuple-element.30), channel_id=1, source_target_pairs={{0,8},{8,0},{16,24},{24,16},{1,9},{9,1},{17,25},{25,17},{2,10},{10... | collective-permute-start | bytes 589832 | tf_op jit(solution)/shard_map/ppermute | solution.py:64
  60.0 5.7 %collective-permute-start.7 = (bf16[64,1536]{1,0:T(8,128)(2,1)S(1)}, bf16[64,1536]{1,0:T(8,128)(2,1)S(1)}, u32[]{:S(2)}, u32[]{:S(2)}) collective-permute-start(bf16[64,1536]{1,0:T(8,128)(2,1)S(1)} %get-tuple-element.31), channel_id=1, source_target_pairs={{0,16},{8,24},{16,0},{24,8},{1,17},{9,25},{17,1},{25,9},{2,18},{10... | collective-permute-start | bytes 589832 | tf_op jit(solution)/shard_map/ppermute | solution.py:64
  65.9 8.0 %collective-permute-start.8 = (bf16[2,64,1536]{2,1,0:T(8,128)(2,1)S(1)}, bf16[2,64,1536]{2,1,0:T(8,128)(2,1)S(1)}, u32[]{:S(2)}, u32[]{:S(2)}) collective-permute-start(bf16[2,64,1536]{2,1,0:T(8,128)(2,1)S(1)} %pad_maximum_fusion.3), channel_id=1, source_target_pairs={{0,8},{8,0},{16,24},{24,16},{1,9},{9,1},{17,25},{25,17},{2,10},{10... | collective-permute-start | bytes 1179656 | tf_op jit(solution)/shard_map/ppermute | solution.py:64
  66.4 7.9 %collective-permute-start.6 = (bf16[2,64,1536]{2,1,0:T(8,128)(2,1)S(1)}, bf16[2,64,1536]{2,1,0:T(8,128)(2,1)}, u32[]{:S(2)}, u32[]{:S(2)}) collective-permute-start(bf16[2,64,1536]{2,1,0:T(8,128)(2,1)S(1)} %pad_maximum_fusion.2), channel_id=1, source_target_pairs={{0,16},{8,24},{16,0},{24,8},{1,17},{9,25},{17,1},{25,9},{2,18},{10... | collective-permute-start | bytes 1179656 | tf_op jit(solution)/shard_map/ppermute | solution.py:64
  84.8 1.7 %copy-start.1 = (f32[256,3072]{1,0:T(8,128)}, f32[256,3072]{1,0:T(8,128)S(1)}, u32[]{:S(2)}) copy-start(f32[256,3072]{1,0:T(8,128)S(1)} %fusion.17) | copy-start | bytes 9437188
  87.4 10.5 %collective-permute-start.9 = (bf16[4,32,3072]{2,1,0:T(8,128)(2,1)}, bf16[4,32,3072]{2,1,0:T(8,128)(2,1)}, u32[]{:S(2)}, u32[]{:S(2)}) collective-permute-start(bf16[4,32,3072]{2,1,0:T(8,128)(2,1)} %fusion.6), channel_id=1, source_target_pairs={{0,1},{1,0},{2,3},{3,2},{4,5},{5,4},{6,7},{7,6},{8,9},{9,8},{10,11... | collective-permute-start | bytes 2359304 | tf_op jit(solution)/shard_map/ppermute | solution.py:64
  99.9 10.9 %collective-permute-start.10 = (bf16[2,32,1536]{2,1,0:T(8,128)(2,1)S(1)}, bf16[2,32,1536]{2,1,0:T(8,128)(2,1)S(1)}, u32[]{:S(2)}, u32[]{:S(2)}) collective-permute-start(bf16[2,32,1536]{2,1,0:T(8,128)(2,1)S(1)} %fusion.11), channel_id=1, source_target_pairs={{0,2},{1,3},{2,0},{3,1},{4,6},{5,7},{6,4},{7,5},{8,10},{9,11},{10,... | collective-permute-start | bytes 589832 | tf_op jit(solution)/shard_map/ppermute | solution.py:64
  100.0 12.5 %collective-permute-start.12 = (bf16[2,32,1536]{2,1,0:T(8,128)(2,1)S(1)}, bf16[2,32,1536]{2,1,0:T(8,128)(2,1)S(1)}, u32[]{:S(2)}, u32[]{:S(2)}) collective-permute-start(bf16[2,32,1536]{2,1,0:T(8,128)(2,1)S(1)} %fusion.12), channel_id=1, source_target_pairs={{0,4},{1,5},{2,6},{3,7},{4,0},{5,1},{6,2},{7,3},{8,12},{9,13},{10,... | collective-permute-start | bytes 589832 | tf_op jit(solution)/shard_map/ppermute | solution.py:64
  112.6 9.3 %collective-permute-start.11 = (bf16[32,1536]{1,0:T(8,128)(2,1)S(1)}, bf16[32,1536]{1,0:T(8,128)(2,1)S(1)}, u32[]{:S(2)}, u32[]{:S(2)}) collective-permute-start(bf16[32,1536]{1,0:T(8,128)(2,1)S(1)} %fusion.15), channel_id=1, source_target_pairs={{0,4},{1,5},{2,6},{3,7},{4,0},{5,1},{6,2},{7,3},{8,12},{9,13},{10,... | collective-permute-start | bytes 294920 | tf_op jit(solution)/shard_map/ppermute | solution.py:64
  119.6 4.9 %collective-permute-start.13 = (bf16[32,1536]{1,0:T(8,128)(2,1)S(1)}, bf16[32,1536]{1,0:T(8,128)(2,1)S(1)}, u32[]{:S(2)}, u32[]{:S(2)}) collective-permute-start(bf16[32,1536]{1,0:T(8,128)(2,1)S(1)} %fusion.16), channel_id=1, source_target_pairs={{0,2},{1,3},{2,0},{3,1},{4,6},{5,7},{6,4},{7,5},{8,10},{9,11},{10,... | collective-permute-start | bytes 294920 | tf_op jit(solution)/shard_map/ppermute | solution.py:64

commit v17 on v15

--- a/solution.py
+++ b/solution.py
@@ -107,7 +107,7 @@
     return jnp.stack([first, second], axis=0)
 
 
-def row_all_gather(block, axis="row"):
+def row_all_gather(block, axis="row", order=None):
     n = lax.axis_size(axis)
     if n & (n - 1):
         return lax.all_gather(block, axis, axis=0, tiled=True)
@@ -115,7 +115,8 @@
     r = lax.axis_index(axis)
     m = block.shape[0]
     outs = []
-    for half, order in zip(_halves(block), _bit_orders(n)):
+    pieces = [(block, order)] if order is not None else zip(_halves(block), _bit_orders(n))
+    for half, order in pieces:
         cur = half
         bits = []
         for bit in order:
@@ -173,10 +174,18 @@
     my_rows = local_x.shape[0] // lax.axis_size("row")
     first_row = lax.axis_index("row") * my_rows
     partial_value = jnp.dot(local_x, weight, preferred_element_type=jnp.float32)
-    preact = row_reduce_scatter(partial_value) + bias
     my_cot = lax.dynamic_slice_in_dim(cotangent, first_row, my_rows, 0)
-    hidden, my_grad = activate(preact, my_cot)
-    full_grad = row_all_gather(my_grad)
+    preact = row_reduce_scatter(partial_value)
+    hidden, full_grad, start = [], [], 0
+    orders = _bit_orders(lax.axis_size("row"))
+    for number, part in enumerate(_halves(preact)):
+        cols = slice(start, start + part.shape[1])
+        h, g = activate(part + bias[cols], my_cot[:, cols])
+        hidden.append(h)
+        full_grad.append(row_all_gather(g, order=orders[number % 2]))
+        start += part.shape[1]
+    hidden = jnp.concatenate(hidden, axis=1)
+    full_grad = jnp.concatenate(full_grad, axis=1)
     local_xt = local_x.T
     blocks = local_xt.shape[0] // min(768, local_xt.shape[0])
     first_half = outer_product_sum(local_xt, full_grad, 0, blocks // 2)

time: 117 us -> 114 us (0.974)
  waiting for transfers between devices: 34.7 us -> 30.8 us
  starting transfers between devices: 10.3 us -> 13 us
    ppermute x12, waiting for transfers between devices: 34.7 us -> 30.8 us  [_swap(): return lax.ppermute(value, axis, [(i, i ^ flip) for i in range(size)])]
    ppermute x12, starting transfers between devices: 10.3 us -> 13 us  [_swap(): return lax.ppermute(value, axis, [(i, i ^ flip) for i in range(size)])]
  transfers between devices with their start and end apart: 12 -> 12, of which waited for: 11 -> 10; matrix products, arithmetic and copies ran while one was open for 5% -> 6% of each run, Pallas kernels for 11% -> 12%
where the time goes in v17:
time: 114 us
  waiting for transfers between devices  30.8 us (27%)
  blocking collectives  21.5 us (19%)
  matrix products  18 us (16%)
  Pallas kernels  13.3 us (12%)
  starting transfers between devices  13 us (11%)
  other arithmetic  8.98 us (8%)
  local copies, waits for them, and re-layouts  7.53 us (7%)
    ppermute x12, waiting for transfers between devices, _swap(): return lax.ppermute(value, axis, [(i, i ^ flip) for i in range(size)])  30.8 us
    all_gather x1, blocking collectives, col_all_gather(): mine = lax.all_gather(block, axis, axis_index_groups=groups)  21.5 us
    pallas_call x2, Pallas kernels, outer_product_sum(): pl.pallas_call(kernel, grid=(n // block_n, count), in_specs=in_specs, out...  13.3 us
    ppermute x12, starting transfers between devices, _swap(): return lax.ppermute(value, axis, [(i, i ^ flip) for i in range(size)])  13 us
    dot_general x1, matrix products, body(): lax.dot_general(full_grad, weight, (((1,), (1,)), ((), ())), preferred_el...  9.03 us
    dot_general x1, matrix products, body(): partial_value = jnp.dot(local_x, weight, preferred_element_type=jnp.float32)  8.99 us
    unnamed x6, local copies, waits for them, and re-layouts  2.8 us
  transfers between devices with their start and end apart: 12, of which 10 were waited for; matrix products, arithmetic and copies ran while one was open for 6% of the time, Pallas kernels for 12%

profile of v17, /device:TPU:0, one launch (start us, length us, event | category | flops | bytes accessed | tf_op | source)
XLA Modules:
  0.0 114.0 jit_solution(7922670094656480775)
XLA Ops:
  0.6 21.5 %all-gather = bf16[128,3072]{1,0:T(8,128)(2,1)S(1)} all-gather(bf16[32,3072]{1,0:T(8,128)(2,1)} %param.4), channel_id=2, replica_groups={{0,2,4,6},{1,3,5,7},{8,10,12,14},{9,11,13,15},{16,18,20,22},{17,19,21,2..., dimensions={0}, use_global_device_ids=true | all-gather | bytes 983040 | tf_op jit(solution)/shard_map/all_gather | solution.py:136
  22.1 2.3 %collective-permute-done = bf16[4,32,3072]{2,1,0:T(8,128)(2,1)S(1)} collective-permute-done((bf16[4,32,3072]{2,1,0:T(8,128)(2,1)S(1)}, bf16[4,32,3072]{2,1,0:T(8,128)(2,1)S(1)}, u32[]{:S(2)}, u32[]{:S(2)}) %collective-permute-start) | collective-permute-done | bytes 786464 | tf_op jit(solution)/shard_map/ppermute | solution.py:64
  24.8 9.0 %fusion.25 = f32[256,3072]{1,0:T(8,128)S(1)} fusion(bf16[256,3072]{1,0:T(8,128)(2,1)S(1)} %bitcast.106, bf16[3072,3072]{1,0:T(8,128)(2,1)} %param.5), kind=kOutput, calls=%fused_computation.63 | convolution fusion | flops 4831838208 | bytes 23592960 | tf_op jit(solution)/shard_map/dot_general | solution.py:176
  36.0 1.5 %collective-permute-start.1 = (bf16[2,64,1536]{2,1,0:T(8,128)(2,1)}, bf16[2,64,1536]{2,1,0:T(8,128)(2,1)S(1)}, u32[]{:S(2)}, u32[]{:S(2)}) collective-permute-start(bf16[2,64,1536]{2,1,0:T(8,128)(2,1)} %fusion.15), channel_id=1, source_target_pairs={{0,8},{8,0},{16,24},{24,16},{1,9},{9,1},{17,25},{25,17},{2,10},{10... | collective-permute-start | bytes 1179656 | tf_op jit(solution)/shard_map/ppermute | solution.py:64
  37.5 1.6 %collective-permute-start.3 = (bf16[2,64,1536]{2,1,0:T(8,128)(2,1)S(1)}, bf16[2,64,1536]{2,1,0:T(8,128)(2,1)S(1)}, u32[]{:S(2)}, u32[]{:S(2)}) collective-permute-start(bf16[2,64,1536]{2,1,0:T(8,128)(2,1)S(1)} %fusion.13), channel_id=1, source_target_pairs={{0,16},{8,24},{16,0},{24,8},{1,17},{9,25},{17,1},{25,9},{2,18},{10... | collective-permute-start | bytes 1179656 | tf_op jit(solution)/shard_map/ppermute | solution.py:64
  39.1 8.2 %collective-permute-done.1 = bf16[2,64,1536]{2,1,0:T(8,128)(2,1)S(1)} collective-permute-done((bf16[2,64,1536]{2,1,0:T(8,128)(2,1)}, bf16[2,64,1536]{2,1,0:T(8,128)(2,1)S(1)}, u32[]{:S(2)}, u32[]{:S(2)}) %collective-permute-start.1) | collective-permute-done | bytes 393248 | tf_op jit(solution)/shard_map/ppermute | solution.py:64
  48.6 1.6 %collective-permute-start.2 = (bf16[64,1536]{1,0:T(8,128)(2,1)S(1)}, bf16[64,1536]{1,0:T(8,128)(2,1)S(1)}, u32[]{:S(2)}, u32[]{:S(2)}) collective-permute-start(bf16[64,1536]{1,0:T(8,128)(2,1)S(1)} %fusion.19), channel_id=1, source_target_pairs={{0,16},{8,24},{16,0},{24,8},{1,17},{9,25},{17,1},{25,9},{2,18},{10... | collective-permute-start | bytes 589832 | tf_op jit(solution)/shard_map/ppermute | solution.py:64
  50.3 1.6 %collective-permute-start.4 = (bf16[64,1536]{1,0:T(8,128)(2,1)S(1)}, bf16[64,1536]{1,0:T(8,128)(2,1)S(1)}, u32[]{:S(2)}, u32[]{:S(2)}) collective-permute-start(bf16[64,1536]{1,0:T(8,128)(2,1)S(1)} %fusion.20), channel_id=1, source_target_pairs={{0,8},{8,0},{16,24},{24,16},{1,9},{9,1},{17,25},{25,17},{2,10},{10... | collective-permute-start | bytes 589832 | tf_op jit(solution)/shard_map/ppermute | solution.py:64
  51.9 2.9 %collective-permute-done.2 = bf16[64,1536]{1,0:T(8,128)(2,1)S(1)} collective-permute-done((bf16[64,1536]{1,0:T(8,128)(2,1)S(1)}, bf16[64,1536]{1,0:T(8,128)(2,1)S(1)}, u32[]{:S(2)}, u32[]{:S(2)}) %collective-permute-start.2) | collective-permute-done | bytes 196640 | tf_op jit(solution)/shard_map/ppermute | solution.py:64
  54.8 1.4 %collective-permute-done.4 = bf16[64,1536]{1,0:T(8,128)(2,1)S(1)} collective-permute-done((bf16[64,1536]{1,0:T(8,128)(2,1)S(1)}, bf16[64,1536]{1,0:T(8,128)(2,1)S(1)}, u32[]{:S(2)}, u32[]{:S(2)}) %collective-permute-start.4) | collective-permute-done | bytes 196640 | tf_op jit(solution)/shard_map/ppermute | solution.py:64
  56.2 1.5 %fusion.6 = (bf16[64,1536]{1,0:T(8,128)(2,1)S(1)}, bf16[64,1536]{1,0:T(8,128)(2,1)S(1)}, bf16[64,1536]{1,0:T(8,128)(2,1)S(1)}, bf16[64,1536]{1,0:T(8,128)(2,1)S(1)}) fusion(bf16[256,3072]{1,0:T(8,128)(2,1)} %param.7, s32[]{:T(128)S(6)} %select_n.121, f32[1536]{0:T(1024)S(1)} %get-tuple-element.24, bf16[64,1536]{1,0:T(8,128)(2,1)S(1)} %collective-permute-done.2, ...), kind=kLoop, calls=%fused_computation.23 | loop fusion | flops 3145728 | bytes 2371600 | tf_op jit(solution)/shard_map/convert_element_type | solution.py:15
  58.3 1.5 %collective-permute-start.5 = (bf16[64,1536]{1,0:T(8,128)(2,1)S(1)}, bf16[64,1536]{1,0:T(8,128)(2,1)S(1)}, u32[]{:S(2)}, u32[]{:S(2)}) collective-permute-start(bf16[64,1536]{1,0:T(8,128)(2,1)S(1)} %get-tuple-element.10), channel_id=1, source_target_pairs={{0,8},{8,0},{16,24},{24,16},{1,9},{9,1},{17,25},{25,17},{2,10},{10... | collective-permute-start | bytes 589832 | tf_op jit(solution)/shard_map/ppermute | solution.py:64
  59.8 3.7 %collective-permute-done.7 = bf16[64,1536]{1,0:T(8,128)(2,1)S(1)} collective-permute-done((bf16[64,1536]{1,0:T(8,128)(2,1)S(1)}, bf16[64,1536]{1,0:T(8,128)(2,1)S(1)}, u32[]{:S(2)}, u32[]{:S(2)}) %collective-permute-start.7) | collective-permute-done | bytes 196640 | tf_op jit(solution)/shard_map/ppermute | solution.py:64
  63.5 1.6 %collective-permute-start.8 = (bf16[2,64,1536]{2,1,0:T(8,128)(2,1)S(1)}, bf16[2,64,1536]{2,1,0:T(8,128)(2,1)S(1)}, u32[]{:S(2)}, u32[]{:S(2)}) collective-permute-start(bf16[2,64,1536]{2,1,0:T(8,128)(2,1)S(1)} %pad_maximum_fusion.4), channel_id=1, source_target_pairs={{0,8},{8,0},{16,24},{24,16},{1,9},{9,1},{17,25},{25,17},{2,10},{10... | collective-permute-start | bytes 1179656 | tf_op jit(solution)/shard_map/ppermute | solution.py:64
  65.2 2.3 %collective-permute-start.6 = (bf16[2,64,1536]{2,1,0:T(8,128)(2,1)S(1)}, bf16[2,64,1536]{2,1,0:T(8,128)(2,1)S(1)}, u32[]{:S(2)}, u32[]{:S(2)}) collective-permute-start(bf16[2,64,1536]{2,1,0:T(8,128)(2,1)S(1)} %pad_maximum_fusion.3), channel_id=1, source_target_pairs={{0,16},{8,24},{16,0},{24,8},{1,17},{9,25},{17,1},{25,9},{2,18},{10... | collective-permute-start | bytes 1179656 | tf_op jit(solution)/shard_map/ppermute | solution.py:64
  67.4 4.9 %collective-permute-done.8 = bf16[2,64,1536]{2,1,0:T(8,128)(2,1)S(1)} collective-permute-done((bf16[2,64,1536]{2,1,0:T(8,128)(2,1)S(1)}, bf16[2,64,1536]{2,1,0:T(8,128)(2,1)S(1)}, u32[]{:S(2)}, u32[]{:S(2)}) %collective-permute-start.8) | collective-permute-done | bytes 393248 | tf_op jit(solution)/shard_map/ppermute | solution.py:64
  73.3 9.0 %fusion.22 = f32[256,3072]{1,0:T(8,128)S(1)} fusion(bf16[3072,3072]{1,0:T(8,128)(2,1)} %param.5, bf16[256,1536]{1,0:T(8,128)(2,1)S(1)} %bitcast.100, bf16[256,1536]{1,0:T(8,128)(2,1)S(1)} %bitcast.103), kind=kOutput, calls=%fused_computation.60 | convolution fusion | flops 4834983936 | bytes 23592960 | tf_op jit(solution)/shard_map/dot_general | solution.py:193
  82.4 1.7 %copy-done.1 = f32[256,3072]{1,0:T(8,128)} copy-done((f32[256,3072]{1,0:T(8,128)}, f32[256,3072]{1,0:T(8,128)S(1)}, u32[]{:S(2)}) %copy-start.1) | copy-done | bytes 3145752
  85.0 1.6 %copy.19 = bf16[256,3072]{0,1:T(8,128)(2,1)} copy(bf16[256,3072]{1,0:T(8,128)(2,1)S(1)} %bitcast.107) | data formatting | bytes 3145728 | tf_op jit(solution)/shard_map/reshape | solution.py:138
  87.6 1.8 %bitcast_add_fusion = f32[4,32,3072]{2,1,0:T(8,128)S(1)} fusion(bf16[4,32,3072]{2,1,0:T(8,128)(2,1)} %collective-permute-done.9, f32[4,2,32,3072]{3,2,1,0:T(8,128)} %bitcast.117, s32[]{:T(128)S(6)} %select_n.132), kind=kLoop, calls=%fused_computation.4 | loop fusion | flops 786432 | bytes 3932164 | tf_op jit(solution)/shard_map/add | solution.py:149
  92.5 6.7 %shard_map.75._ = bf16[3072,3072]{1,0:T(8,128)(2,1)} custom-call(bf16[3072,256]{1,0:T(8,128)(2,1)} %bitcast.98, bf16[256,3072]{1,0:T(8,128)(2,1)} %pad_maximum_fusion.g_ref), custom_call_target="tpu_custom_call" | custom-call | flops 2415919104 | bytes 11796480 | tf_op jit(solution)/shard_map/pallas_call | solution.py:49
  99.2 2.6 %collective-permute-done.10 = bf16[2,32,3072]{2,1,0:T(8,128)(2,1)S(1)} collective-permute-done((bf16[2,32,3072]{2,1,0:T(8,128)(2,1)}, bf16[2,32,3072]{2,1,0:T(8,128)(2,1)S(1)}, u32[]{:S(2)}, u32[]{:S(2)}) %collective-permute-start.10) | collective-permute-done | bytes 393248 | tf_op jit(solution)/shard_map/ppermute | solution.py:64
  102.8 6.7 %shard_map.76 = bf16[3072,3072]{1,0:T(8,128)(2,1)} custom-call(bf16[3072,256]{1,0:T(8,128)(2,1)} %bitcast.99, bf16[256,3072]{1,0:T(8,128)(2,1)} %pad_maximum_fusion.g_ref, bf16[3072,3072]{1,0:T(8,128)(2,1)} %shard_map.75._), custom_call_target="tpu_custom_call", output_to_operand_aliasing={{}: (2, {})} | custom-call | flops 2415919104 | bytes 11796480 | tf_op jit(solution)/shard_map/pallas_call | solution.py:49
  109.5 3.9 %collective-permute-done.11 = bf16[32,3072]{1,0:T(8,128)(2,1)S(1)} collective-permute-done((bf16[32,3072]{1,0:T(8,128)(2,1)S(1)}, bf16[32,3072]{1,0:T(8,128)(2,1)S(1)}, u32[]{:S(2)}, u32[]{:S(2)}) %collective-permute-start.11) | collective-permute-done | bytes 196640 | tf_op jit(solution)/shard_map/ppermute | solution.py:64
  (42 shorter events, 12.3 us)
Async XLA Ops:
  22.1 2.3 %collective-permute-start = (bf16[4,32,3072]{2,1,0:T(8,128)(2,1)S(1)}, bf16[4,32,3072]{2,1,0:T(8,128)(2,1)S(1)}, u32[]{:S(2)}, u32[]{:S(2)}) collective-permute-start(bf16[4,32,3072]{2,1,0:T(8,128)(2,1)S(1)} %bitcast.114), channel_id=1, source_target_pairs={{0,1},{1,0},{2,3},{3,2},{4,5},{5,4},{6,7},{7,6},{8,9},{9,8},{10,11... | collective-permute-start | bytes 2359304 | tf_op jit(solution)/shard_map/ppermute | solution.py:64
  34.1 1.1 %copy-start = (f32[256,1536]{1,0:T(8,128)}, f32[256,1536]{1,0:T(8,128)S(1)}, u32[]{:S(2)}) copy-start(f32[256,1536]{1,0:T(8,128)S(1)} %get-tuple-element.8) | copy-start | bytes 4718596
  36.0 11.4 %collective-permute-start.1 = (bf16[2,64,1536]{2,1,0:T(8,128)(2,1)}, bf16[2,64,1536]{2,1,0:T(8,128)(2,1)S(1)}, u32[]{:S(2)}, u32[]{:S(2)}) collective-permute-start(bf16[2,64,1536]{2,1,0:T(8,128)(2,1)} %fusion.15), channel_id=1, source_target_pairs={{0,8},{8,0},{16,24},{24,16},{1,9},{9,1},{17,25},{25,17},{2,10},{10... | collective-permute-start | bytes 1179656 | tf_op jit(solution)/shard_map/ppermute | solution.py:64
  37.5 12.7 %collective-permute-start.3 = (bf16[2,64,1536]{2,1,0:T(8,128)(2,1)S(1)}, bf16[2,64,1536]{2,1,0:T(8,128)(2,1)S(1)}, u32[]{:S(2)}, u32[]{:S(2)}) collective-permute-start(bf16[2,64,1536]{2,1,0:T(8,128)(2,1)S(1)} %fusion.13), channel_id=1, source_target_pairs={{0,16},{8,24},{16,0},{24,8},{1,17},{9,25},{17,1},{25,9},{2,18},{10... | collective-permute-start | bytes 1179656 | tf_op jit(solution)/shard_map/ppermute | solution.py:64
  48.6 3.3 %copy-start.2 = (f32[3072]{0:T(1024)S(1)}, f32[3072]{0:T(1024)}, u32[]{:S(2)}) copy-start(f32[3072]{0:T(1024)} %param.6) | copy-start | bytes 36868
  48.6 6.2 %collective-permute-start.2 = (bf16[64,1536]{1,0:T(8,128)(2,1)S(1)}, bf16[64,1536]{1,0:T(8,128)(2,1)S(1)}, u32[]{:S(2)}, u32[]{:S(2)}) collective-permute-start(bf16[64,1536]{1,0:T(8,128)(2,1)S(1)} %fusion.19), channel_id=1, source_target_pairs={{0,16},{8,24},{16,0},{24,8},{1,17},{9,25},{17,1},{25,9},{2,18},{10... | collective-permute-start | bytes 589832 | tf_op jit(solution)/shard_map/ppermute | solution.py:64
  50.3 5.9 %collective-permute-start.4 = (bf16[64,1536]{1,0:T(8,128)(2,1)S(1)}, bf16[64,1536]{1,0:T(8,128)(2,1)S(1)}, u32[]{:S(2)}, u32[]{:S(2)}) collective-permute-start(bf16[64,1536]{1,0:T(8,128)(2,1)S(1)} %fusion.20), channel_id=1, source_target_pairs={{0,8},{8,0},{16,24},{24,16},{1,9},{9,1},{17,25},{25,17},{2,10},{10... | collective-permute-start | bytes 589832 | tf_op jit(solution)/shard_map/ppermute | solution.py:64
  57.7 5.7 %collective-permute-start.7 = (bf16[64,1536]{1,0:T(8,128)(2,1)S(1)}, bf16[64,1536]{1,0:T(8,128)(2,1)S(1)}, u32[]{:S(2)}, u32[]{:S(2)}) collective-permute-start(bf16[64,1536]{1,0:T(8,128)(2,1)S(1)} %get-tuple-element.11), channel_id=1, source_target_pairs={{0,16},{8,24},{16,0},{24,8},{1,17},{9,25},{17,1},{25,9},{2,18},{10... | collective-permute-start | bytes 589832 | tf_op jit(solution)/shard_map/ppermute | solution.py:64
  58.3 6.8 %collective-permute-start.5 = (bf16[64,1536]{1,0:T(8,128)(2,1)S(1)}, bf16[64,1536]{1,0:T(8,128)(2,1)S(1)}, u32[]{:S(2)}, u32[]{:S(2)}) collective-permute-start(bf16[64,1536]{1,0:T(8,128)(2,1)S(1)} %get-tuple-element.10), channel_id=1, source_target_pairs={{0,8},{8,0},{16,24},{24,16},{1,9},{9,1},{17,25},{25,17},{2,10},{10... | collective-permute-start | bytes 589832 | tf_op jit(solution)/shard_map/ppermute | solution.py:64
  63.5 8.9 %collective-permute-start.8 = (bf16[2,64,1536]{2,1,0:T(8,128)(2,1)S(1)}, bf16[2,64,1536]{2,1,0:T(8,128)(2,1)S(1)}, u32[]{:S(2)}, u32[]{:S(2)}) collective-permute-start(bf16[2,64,1536]{2,1,0:T(8,128)(2,1)S(1)} %pad_maximum_fusion.4), channel_id=1, source_target_pairs={{0,8},{8,0},{16,24},{24,16},{1,9},{9,1},{17,25},{25,17},{2,10},{10... | collective-permute-start | bytes 1179656 | tf_op jit(solution)/shard_map/ppermute | solution.py:64
  65.2 8.0 %collective-permute-start.6 = (bf16[2,64,1536]{2,1,0:T(8,128)(2,1)S(1)}, bf16[2,64,1536]{2,1,0:T(8,128)(2,1)S(1)}, u32[]{:S(2)}, u32[]{:S(2)}) collective-permute-start(bf16[2,64,1536]{2,1,0:T(8,128)(2,1)S(1)} %pad_maximum_fusion.3), channel_id=1, source_target_pairs={{0,16},{8,24},{16,0},{24,8},{1,17},{9,25},{17,1},{25,9},{2,18},{10... | collective-permute-start | bytes 1179656 | tf_op jit(solution)/shard_map/ppermute | solution.py:64
  82.4 1.7 %copy-start.1 = (f32[256,3072]{1,0:T(8,128)}, f32[256,3072]{1,0:T(8,128)S(1)}, u32[]{:S(2)}) copy-start(f32[256,3072]{1,0:T(8,128)S(1)} %fusion.22) | copy-start | bytes 9437188
  85.0 2.6 %collective-permute-start.9 = (bf16[4,32,3072]{2,1,0:T(8,128)(2,1)}, bf16[4,32,3072]{2,1,0:T(8,128)(2,1)}, u32[]{:S(2)}, u32[]{:S(2)}) collective-permute-start(bf16[4,32,3072]{2,1,0:T(8,128)(2,1)} %fusion), channel_id=1, source_target_pairs={{0,1},{1,0},{2,3},{3,2},{4,5},{5,4},{6,7},{7,6},{8,9},{9,8},{10,11... | collective-permute-start | bytes 2359304 | tf_op jit(solution)/shard_map/ppermute | solution.py:64
  90.3 11.5 %collective-permute-start.10 = (bf16[2,32,3072]{2,1,0:T(8,128)(2,1)}, bf16[2,32,3072]{2,1,0:T(8,128)(2,1)S(1)}, u32[]{:S(2)}, u32[]{:S(2)}) collective-permute-start(bf16[2,32,3072]{2,1,0:T(8,128)(2,1)} %fusion.14), channel_id=1, source_target_pairs={{0,2},{1,3},{2,0},{3,1},{4,6},{5,7},{6,4},{7,5},{8,10},{9,11},{10,... | collective-permute-start | bytes 1179656 | tf_op jit(solution)/shard_map/ppermute | solution.py:64
  101.9 11.4 %collective-permute-start.11 = (bf16[32,3072]{1,0:T(8,128)(2,1)S(1)}, bf16[32,3072]{1,0:T(8,128)(2,1)S(1)}, u32[]{:S(2)}, u32[]{:S(2)}) collective-permute-start(bf16[32,3072]{1,0:T(8,128)(2,1)S(1)} %fusion.21), channel_id=1, source_target_pairs={{0,4},{1,5},{2,6},{3,7},{4,0},{5,1},{6,2},{7,3},{8,12},{9,13},{10,... | collective-permute-start | bytes 589832 | tf_op jit(solution)/shard_map/ppermute | solution.py:64

commit v18 on v17

--- a/solution.py
+++ b/solution.py
@@ -169,6 +169,18 @@
     return cur.reshape(m, partial.shape[1]), hold
 
 
+def _grad_tokens_partial(grad_parts, weight):
+    total, start = None, 0
+    for part in grad_parts:
+        cols = slice(start, start + part.shape[1])
+        term = lax.dot_general(
+            part, weight[:, cols], (((1,), (1,)), ((), ())), preferred_element_type=jnp.float32
+        )
+        total = term if total is None else total + term
+        start += part.shape[1]
+    return total
+
+
 def body(tokens, weight, bias, cotangent):
     local_x = col_all_gather(tokens)
     my_rows = local_x.shape[0] // lax.axis_size("row")
@@ -185,14 +197,13 @@
         full_grad.append(row_all_gather(g, order=orders[number % 2]))
         start += part.shape[1]
     hidden = jnp.concatenate(hidden, axis=1)
-    full_grad = jnp.concatenate(full_grad, axis=1)
+    grad_parts = full_grad
+    full_grad = jnp.concatenate(grad_parts, axis=1)
     local_xt = local_x.T
     blocks = local_xt.shape[0] // min(768, local_xt.shape[0])
     first_half = outer_product_sum(local_xt, full_grad, 0, blocks // 2)
     grad_tokens, first_half = col_reduce_scatter(
-        lax.dot_general(
-            full_grad, weight, (((1,), (1,)), ((), ())), preferred_element_type=jnp.float32
-        ),
+        _grad_tokens_partial(grad_parts, weight),
         first_half,
     )
     grad_tokens = grad_tokens.astype(jnp.bfloat16)

time: 114 us -> 115 us (level)
  matrix products: 18 us -> 19.4 us
    dot_general x1 -> x2, matrix products: 9.03 us -> 10.4 us  [_grad_tokens_partial(): lax.dot_general(part, weight[:, cols], (((1,), (1,)), ((), ())), preferre...]
  transfers between devices with their start and end apart: 12 -> 12, of which waited for: 10 -> 9; matrix products, arithmetic and copies ran while one was open for 6% -> 10% of each run, Pallas kernels for 12% -> 12%
where the time goes in v18:
time: 115 us
  waiting for transfers between devices  30.2 us (26%)
  blocking collectives  21.5 us (19%)
  matrix products  19.4 us (17%)
  Pallas kernels  13.3 us (12%)
  starting transfers between devices  13 us (11%)
  other arithmetic  8.98 us (8%)
  local copies, waits for them, and re-layouts  7.53 us (7%)
    ppermute x12, waiting for transfers between devices, _swap(): return lax.ppermute(value, axis, [(i, i ^ flip) for i in range(size)])  30.2 us
    all_gather x1, blocking collectives, col_all_gather(): mine = lax.all_gather(block, axis, axis_index_groups=groups)  21.5 us
    pallas_call x2, Pallas kernels, outer_product_sum(): pl.pallas_call(kernel, grid=(n // block_n, count), in_specs=in_specs, out...  13.3 us
    ppermute x12, starting transfers between devices, _swap(): return lax.ppermute(value, axis, [(i, i ^ flip) for i in range(size)])  13 us
    dot_general x2, matrix products, _grad_tokens_partial(): lax.dot_general(part, weight[:, cols], (((1,), (1,)), ((), ())), preferre...  10.4 us
    dot_general x1, matrix products, body(): partial_value = jnp.dot(local_x, weight, preferred_element_type=jnp.float32)  8.99 us
    unnamed x6, local copies, waits for them, and re-layouts  2.8 us
  transfers between devices with their start and end apart: 12, of which 9 were waited for; matrix products, arithmetic and copies ran while one was open for 10% of the time, Pallas kernels for 12%

profile of v18, /device:TPU:0, one launch (start us, length us, event | category | flops | bytes accessed | tf_op | source)
XLA Modules:
  0.0 114.8 jit_solution(15316643522645800376)
XLA Ops:
  0.6 21.5 %all-gather = bf16[128,3072]{1,0:T(8,128)(2,1)S(1)} all-gather(bf16[32,3072]{1,0:T(8,128)(2,1)} %param.4), channel_id=2, replica_groups={{0,2,4,6},{1,3,5,7},{8,10,12,14},{9,11,13,15},{16,18,20,22},{17,19,21,2..., dimensions={0}, use_global_device_ids=true | all-gather | bytes 983040 | tf_op jit(solution)/shard_map/all_gather | solution.py:136
  22.1 2.3 %collective-permute-done = bf16[4,32,3072]{2,1,0:T(8,128)(2,1)S(1)} collective-permute-done((bf16[4,32,3072]{2,1,0:T(8,128)(2,1)S(1)}, bf16[4,32,3072]{2,1,0:T(8,128)(2,1)S(1)}, u32[]{:S(2)}, u32[]{:S(2)}) %collective-permute-start) | collective-permute-done | bytes 786464 | tf_op jit(solution)/shard_map/ppermute | solution.py:64
  24.8 9.0 %fusion.31 = f32[256,3072]{1,0:T(8,128)S(1)} fusion(bf16[256,3072]{1,0:T(8,128)(2,1)S(1)} %bitcast.107, bf16[3072,3072]{1,0:T(8,128)(2,1)} %param.5), kind=kOutput, calls=%fused_computation.67 | convolution fusion | flops 4831838208 | bytes 23592960 | tf_op jit(solution)/shard_map/dot_general | solution.py:188
  36.0 1.5 %collective-permute-start.1 = (bf16[2,64,1536]{2,1,0:T(8,128)(2,1)}, bf16[2,64,1536]{2,1,0:T(8,128)(2,1)S(1)}, u32[]{:S(2)}, u32[]{:S(2)}) collective-permute-start(bf16[2,64,1536]{2,1,0:T(8,128)(2,1)} %fusion.22), channel_id=1, source_target_pairs={{0,8},{8,0},{16,24},{24,16},{1,9},{9,1},{17,25},{25,17},{2,10},{10... | collective-permute-start | bytes 1179656 | tf_op jit(solution)/shard_map/ppermute | solution.py:64
  37.5 1.6 %collective-permute-start.3 = (bf16[2,64,1536]{2,1,0:T(8,128)(2,1)S(1)}, bf16[2,64,1536]{2,1,0:T(8,128)(2,1)S(1)}, u32[]{:S(2)}, u32[]{:S(2)}) collective-permute-start(bf16[2,64,1536]{2,1,0:T(8,128)(2,1)S(1)} %fusion.20), channel_id=1, source_target_pairs={{0,16},{8,24},{16,0},{24,8},{1,17},{9,25},{17,1},{25,9},{2,18},{10... | collective-permute-start | bytes 1179656 | tf_op jit(solution)/shard_map/ppermute | solution.py:64
  39.1 8.2 %collective-permute-done.1 = bf16[2,64,1536]{2,1,0:T(8,128)(2,1)S(1)} collective-permute-done((bf16[2,64,1536]{2,1,0:T(8,128)(2,1)}, bf16[2,64,1536]{2,1,0:T(8,128)(2,1)S(1)}, u32[]{:S(2)}, u32[]{:S(2)}) %collective-permute-start.1) | collective-permute-done | bytes 393248 | tf_op jit(solution)/shard_map/ppermute | solution.py:64
  48.6 1.6 %collective-permute-start.2 = (bf16[64,1536]{1,0:T(8,128)(2,1)S(1)}, bf16[64,1536]{1,0:T(8,128)(2,1)S(1)}, u32[]{:S(2)}, u32[]{:S(2)}) collective-permute-start(bf16[64,1536]{1,0:T(8,128)(2,1)S(1)} %fusion.26), channel_id=1, source_target_pairs={{0,16},{8,24},{16,0},{24,8},{1,17},{9,25},{17,1},{25,9},{2,18},{10... | collective-permute-start | bytes 589832 | tf_op jit(solution)/shard_map/ppermute | solution.py:64
  50.3 1.6 %collective-permute-start.4 = (bf16[64,1536]{1,0:T(8,128)(2,1)S(1)}, bf16[64,1536]{1,0:T(8,128)(2,1)S(1)}, u32[]{:S(2)}, u32[]{:S(2)}) collective-permute-start(bf16[64,1536]{1,0:T(8,128)(2,1)S(1)} %fusion.27), channel_id=1, source_target_pairs={{0,8},{8,0},{16,24},{24,16},{1,9},{9,1},{17,25},{25,17},{2,10},{10... | collective-permute-start | bytes 589832 | tf_op jit(solution)/shard_map/ppermute | solution.py:64
  51.9 2.9 %collective-permute-done.2 = bf16[64,1536]{1,0:T(8,128)(2,1)S(1)} collective-permute-done((bf16[64,1536]{1,0:T(8,128)(2,1)S(1)}, bf16[64,1536]{1,0:T(8,128)(2,1)S(1)}, u32[]{:S(2)}, u32[]{:S(2)}) %collective-permute-start.2) | collective-permute-done | bytes 196640 | tf_op jit(solution)/shard_map/ppermute | solution.py:64
  56.2 1.5 %fusion.13 = (bf16[64,1536]{1,0:T(8,128)(2,1)S(1)}, bf16[64,1536]{1,0:T(8,128)(2,1)S(1)}, bf16[64,1536]{1,0:T(8,128)(2,1)S(1)}, bf16[64,1536]{1,0:T(8,128)(2,1)S(1)}) fusion(bf16[256,3072]{1,0:T(8,128)(2,1)} %param.7, s32[]{:T(128)S(6)} %select_n.121, f32[1536]{0:T(1024)S(1)} %get-tuple-element.24, bf16[64,1536]{1,0:T(8,128)(2,1)S(1)} %collective-permute-done.2, ...), kind=kLoop, calls=%fused_computation.28 | loop fusion | flops 3145728 | bytes 2371600 | tf_op jit(solution)/shard_map/convert_element_type | solution.py:15
  58.3 1.5 %collective-permute-start.5 = (bf16[64,1536]{1,0:T(8,128)(2,1)S(1)}, bf16[64,1536]{1,0:T(8,128)(2,1)S(1)}, u32[]{:S(2)}, u32[]{:S(2)}) collective-permute-start(bf16[64,1536]{1,0:T(8,128)(2,1)S(1)} %get-tuple-element.10), channel_id=1, source_target_pairs={{0,8},{8,0},{16,24},{24,16},{1,9},{9,1},{17,25},{25,17},{2,10},{10... | collective-permute-start | bytes 589832 | tf_op jit(solution)/shard_map/ppermute | solution.py:64
  59.8 3.7 %collective-permute-done.7 = bf16[64,1536]{1,0:T(8,128)(2,1)S(1)} collective-permute-done((bf16[64,1536]{1,0:T(8,128)(2,1)S(1)}, bf16[64,1536]{1,0:T(8,128)(2,1)S(1)}, u32[]{:S(2)}, u32[]{:S(2)}) %collective-permute-start.7) | collective-permute-done | bytes 196640 | tf_op jit(solution)/shard_map/ppermute | solution.py:64
  63.5 1.6 %collective-permute-start.8 = (bf16[2,64,1536]{2,1,0:T(8,128)(2,1)S(1)}, bf16[2,64,1536]{2,1,0:T(8,128)(2,1)S(1)}, u32[]{:S(2)}, u32[]{:S(2)}) collective-permute-start(bf16[2,64,1536]{2,1,0:T(8,128)(2,1)S(1)} %pad_maximum_fusion.4), channel_id=1, source_target_pairs={{0,8},{8,0},{16,24},{24,16},{1,9},{9,1},{17,25},{25,17},{2,10},{10... | collective-permute-start | bytes 1179656 | tf_op jit(solution)/shard_map/ppermute | solution.py:64
  65.2 2.3 %collective-permute-start.6 = (bf16[2,64,1536]{2,1,0:T(8,128)(2,1)S(1)}, bf16[2,64,1536]{2,1,0:T(8,128)(2,1)S(1)}, u32[]{:S(2)}, u32[]{:S(2)}) collective-permute-start(bf16[2,64,1536]{2,1,0:T(8,128)(2,1)S(1)} %pad_maximum_fusion.3), channel_id=1, source_target_pairs={{0,16},{8,24},{16,0},{24,8},{1,17},{9,25},{17,1},{25,9},{2,18},{10... | collective-permute-start | bytes 1179656 | tf_op jit(solution)/shard_map/ppermute | solution.py:64
  67.4 4.9 %collective-permute-done.8 = bf16[2,64,1536]{2,1,0:T(8,128)(2,1)S(1)} collective-permute-done((bf16[2,64,1536]{2,1,0:T(8,128)(2,1)S(1)}, bf16[2,64,1536]{2,1,0:T(8,128)(2,1)S(1)}, u32[]{:S(2)}, u32[]{:S(2)}) %collective-permute-start.8) | collective-permute-done | bytes 393248 | tf_op jit(solution)/shard_map/ppermute | solution.py:64
  72.6 5.2 %fusion = f32[256,3072]{1,0:T(8,128)S(1)} fusion(bf16[256,1536]{1,0:T(8,128)(2,1)S(1)} %bitcast.101, bf16[3072,3072]{1,0:T(8,128)(2,1)} %param.5), kind=kOutput, calls=%fused_computation | convolution fusion | flops 2415919104 | bytes 13369344 | tf_op jit(solution)/shard_map/dot_general | solution.py:176
  78.0 5.2 %fusion.4 = f32[256,3072]{1,0:T(8,128)S(1)} fusion(f32[256,3072]{1,0:T(8,128)S(1)} %fusion, bf16[256,1536]{1,0:T(8,128)(2,1)S(1)} %bitcast.104, bf16[3072,3072]{1,0:T(8,128)(2,1)} %param.5), kind=kOutput, calls=%fused_computation.4 | convolution fusion | flops 2416705536 | bytes 16515072 | tf_op jit(solution)/shard_map/dot_general | solution.py:176
  83.2 1.7 %copy-done.1 = f32[256,3072]{1,0:T(8,128)} copy-done((f32[256,3072]{1,0:T(8,128)}, f32[256,3072]{1,0:T(8,128)S(1)}, u32[]{:S(2)}) %copy-start.1) | copy-done | bytes 3145752
  85.8 1.6 %copy.19 = bf16[256,3072]{0,1:T(8,128)(2,1)} copy(bf16[256,3072]{1,0:T(8,128)(2,1)S(1)} %bitcast.108) | data formatting | bytes 3145728 | tf_op jit(solution)/shard_map/reshape | solution.py:138
  88.5 1.8 %bitcast_add_fusion = f32[4,32,3072]{2,1,0:T(8,128)S(1)} fusion(bf16[4,32,3072]{2,1,0:T(8,128)(2,1)} %collective-permute-done.9, f32[4,2,32,3072]{3,2,1,0:T(8,128)} %bitcast.118, s32[]{:T(128)S(6)} %select_n.132), kind=kLoop, calls=%fused_computation.9 | loop fusion | flops 786432 | bytes 3932164 | tf_op jit(solution)/shard_map/add | solution.py:149
  93.3 6.7 %shard_map.75._ = bf16[3072,3072]{1,0:T(8,128)(2,1)} custom-call(bf16[3072,256]{1,0:T(8,128)(2,1)} %bitcast.99, bf16[256,3072]{1,0:T(8,128)(2,1)} %pad_maximum_fusion.g_ref), custom_call_target="tpu_custom_call" | custom-call | flops 2415919104 | bytes 11796480 | tf_op jit(solution)/shard_map/pallas_call | solution.py:49
  100.0 2.6 %collective-permute-done.10 = bf16[2,32,3072]{2,1,0:T(8,128)(2,1)S(1)} collective-permute-done((bf16[2,32,3072]{2,1,0:T(8,128)(2,1)}, bf16[2,32,3072]{2,1,0:T(8,128)(2,1)S(1)}, u32[]{:S(2)}, u32[]{:S(2)}) %collective-permute-start.10) | collective-permute-done | bytes 393248 | tf_op jit(solution)/shard_map/ppermute | solution.py:64
  103.6 6.7 %shard_map.76 = bf16[3072,3072]{1,0:T(8,128)(2,1)} custom-call(bf16[3072,256]{1,0:T(8,128)(2,1)} %bitcast.100, bf16[256,3072]{1,0:T(8,128)(2,1)} %pad_maximum_fusion.g_ref, bf16[3072,3072]{1,0:T(8,128)(2,1)} %shard_map.75._), custom_call_target="tpu_custom_call", output_to_operand_aliasing={{}: (2, {})} | custom-call | flops 2415919104 | bytes 11796480 | tf_op jit(solution)/shard_map/pallas_call | solution.py:49
  110.3 3.9 %collective-permute-done.11 = bf16[32,3072]{1,0:T(8,128)(2,1)S(1)} collective-permute-done((bf16[32,3072]{1,0:T(8,128)(2,1)S(1)}, bf16[32,3072]{1,0:T(8,128)(2,1)S(1)}, u32[]{:S(2)}, u32[]{:S(2)}) %collective-permute-start.11) | collective-permute-done | bytes 196640 | tf_op jit(solution)/shard_map/ppermute | solution.py:64
  (43 shorter events, 13.1 us)
Async XLA Ops:
  22.1 2.3 %collective-permute-start = (bf16[4,32,3072]{2,1,0:T(8,128)(2,1)S(1)}, bf16[4,32,3072]{2,1,0:T(8,128)(2,1)S(1)}, u32[]{:S(2)}, u32[]{:S(2)}) collective-permute-start(bf16[4,32,3072]{2,1,0:T(8,128)(2,1)S(1)} %bitcast.115), channel_id=1, source_target_pairs={{0,1},{1,0},{2,3},{3,2},{4,5},{5,4},{6,7},{7,6},{8,9},{9,8},{10,11... | collective-permute-start | bytes 2359304 | tf_op jit(solution)/shard_map/ppermute | solution.py:64
  34.1 1.1 copy-start
  35.2 16.7 %copy-start.2 = (f32[3072]{0:T(1024)S(1)}, f32[3072]{0:T(1024)}, u32[]{:S(2)}) copy-start(f32[3072]{0:T(1024)} %param.6) | copy-start | bytes 36868
  36.0 11.4 %collective-permute-start.1 = (bf16[2,64,1536]{2,1,0:T(8,128)(2,1)}, bf16[2,64,1536]{2,1,0:T(8,128)(2,1)S(1)}, u32[]{:S(2)}, u32[]{:S(2)}) collective-permute-start(bf16[2,64,1536]{2,1,0:T(8,128)(2,1)} %fusion.22), channel_id=1, source_target_pairs={{0,8},{8,0},{16,24},{24,16},{1,9},{9,1},{17,25},{25,17},{2,10},{10... | collective-permute-start | bytes 1179656 | tf_op jit(solution)/shard_map/ppermute | solution.py:64
  37.5 12.7 %collective-permute-start.3 = (bf16[2,64,1536]{2,1,0:T(8,128)(2,1)S(1)}, bf16[2,64,1536]{2,1,0:T(8,128)(2,1)S(1)}, u32[]{:S(2)}, u32[]{:S(2)}) collective-permute-start(bf16[2,64,1536]{2,1,0:T(8,128)(2,1)S(1)} %fusion.20), channel_id=1, source_target_pairs={{0,16},{8,24},{16,0},{24,8},{1,17},{9,25},{17,1},{25,9},{2,18},{10... | collective-permute-start | bytes 1179656 | tf_op jit(solution)/shard_map/ppermute | solution.py:64
  48.6 6.2 %collective-permute-start.2 = (bf16[64,1536]{1,0:T(8,128)(2,1)S(1)}, bf16[64,1536]{1,0:T(8,128)(2,1)S(1)}, u32[]{:S(2)}, u32[]{:S(2)}) collective-permute-start(bf16[64,1536]{1,0:T(8,128)(2,1)S(1)} %fusion.26), channel_id=1, source_target_pairs={{0,16},{8,24},{16,0},{24,8},{1,17},{9,25},{17,1},{25,9},{2,18},{10... | collective-permute-start | bytes 589832 | tf_op jit(solution)/shard_map/ppermute | solution.py:64
  50.3 5.9 %collective-permute-start.4 = (bf16[64,1536]{1,0:T(8,128)(2,1)S(1)}, bf16[64,1536]{1,0:T(8,128)(2,1)S(1)}, u32[]{:S(2)}, u32[]{:S(2)}) collective-permute-start(bf16[64,1536]{1,0:T(8,128)(2,1)S(1)} %fusion.27), channel_id=1, source_target_pairs={{0,8},{8,0},{16,24},{24,16},{1,9},{9,1},{17,25},{25,17},{2,10},{10... | collective-permute-start | bytes 589832 | tf_op jit(solution)/shard_map/ppermute | solution.py:64
  57.7 5.7 %collective-permute-start.7 = (bf16[64,1536]{1,0:T(8,128)(2,1)S(1)}, bf16[64,1536]{1,0:T(8,128)(2,1)S(1)}, u32[]{:S(2)}, u32[]{:S(2)}) collective-permute-start(bf16[64,1536]{1,0:T(8,128)(2,1)S(1)} %get-tuple-element.11), channel_id=1, source_target_pairs={{0,16},{8,24},{16,0},{24,8},{1,17},{9,25},{17,1},{25,9},{2,18},{10... | collective-permute-start | bytes 589832 | tf_op jit(solution)/shard_map/ppermute | solution.py:64
  58.3 6.8 %collective-permute-start.5 = (bf16[64,1536]{1,0:T(8,128)(2,1)S(1)}, bf16[64,1536]{1,0:T(8,128)(2,1)S(1)}, u32[]{:S(2)}, u32[]{:S(2)}) collective-permute-start(bf16[64,1536]{1,0:T(8,128)(2,1)S(1)} %get-tuple-element.10), channel_id=1, source_target_pairs={{0,8},{8,0},{16,24},{24,16},{1,9},{9,1},{17,25},{25,17},{2,10},{10... | collective-permute-start | bytes 589832 | tf_op jit(solution)/shard_map/ppermute | solution.py:64
  63.5 8.9 %collective-permute-start.8 = (bf16[2,64,1536]{2,1,0:T(8,128)(2,1)S(1)}, bf16[2,64,1536]{2,1,0:T(8,128)(2,1)S(1)}, u32[]{:S(2)}, u32[]{:S(2)}) collective-permute-start(bf16[2,64,1536]{2,1,0:T(8,128)(2,1)S(1)} %pad_maximum_fusion.4), channel_id=1, source_target_pairs={{0,8},{8,0},{16,24},{24,16},{1,9},{9,1},{17,25},{25,17},{2,10},{10... | collective-permute-start | bytes 1179656 | tf_op jit(solution)/shard_map/ppermute | solution.py:64
  65.2 12.7 %collective-permute-start.6 = (bf16[2,64,1536]{2,1,0:T(8,128)(2,1)S(1)}, bf16[2,64,1536]{2,1,0:T(8,128)(2,1)S(1)}, u32[]{:S(2)}, u32[]{:S(2)}) collective-permute-start(bf16[2,64,1536]{2,1,0:T(8,128)(2,1)S(1)} %pad_maximum_fusion.3), channel_id=1, source_target_pairs={{0,16},{8,24},{16,0},{24,8},{1,17},{9,25},{17,1},{25,9},{2,18},{10... | collective-permute-start | bytes 1179656 | tf_op jit(solution)/shard_map/ppermute | solution.py:64
  83.2 1.7 %copy-start.1 = (f32[256,3072]{1,0:T(8,128)}, f32[256,3072]{1,0:T(8,128)S(1)}, u32[]{:S(2)}) copy-start(f32[256,3072]{1,0:T(8,128)S(1)} %fusion.4) | copy-start | bytes 9437188
  85.8 2.6 %collective-permute-start.9 = (bf16[4,32,3072]{2,1,0:T(8,128)(2,1)}, bf16[4,32,3072]{2,1,0:T(8,128)(2,1)}, u32[]{:S(2)}, u32[]{:S(2)}) collective-permute-start(bf16[4,32,3072]{2,1,0:T(8,128)(2,1)} %fusion.7), channel_id=1, source_target_pairs={{0,1},{1,0},{2,3},{3,2},{4,5},{5,4},{6,7},{7,6},{8,9},{9,8},{10,11... | collective-permute-start | bytes 2359304 | tf_op jit(solution)/shard_map/ppermute | solution.py:64
  91.1 11.5 %collective-permute-start.10 = (bf16[2,32,3072]{2,1,0:T(8,128)(2,1)}, bf16[2,32,3072]{2,1,0:T(8,128)(2,1)S(1)}, u32[]{:S(2)}, u32[]{:S(2)}) collective-permute-start(bf16[2,32,3072]{2,1,0:T(8,128)(2,1)} %fusion.21), channel_id=1, source_target_pairs={{0,2},{1,3},{2,0},{3,1},{4,6},{5,7},{6,4},{7,5},{8,10},{9,11},{10,... | collective-permute-start | bytes 1179656 | tf_op jit(solution)/shard_map/ppermute | solution.py:64
  102.7 11.4 %collective-permute-start.11 = (bf16[32,3072]{1,0:T(8,128)(2,1)S(1)}, bf16[32,3072]{1,0:T(8,128)(2,1)S(1)}, u32[]{:S(2)}, u32[]{:S(2)}) collective-permute-start(bf16[32,3072]{1,0:T(8,128)(2,1)S(1)} %fusion.28), channel_id=1, source_target_pairs={{0,4},{1,5},{2,6},{3,7},{4,0},{5,1},{6,2},{7,3},{8,12},{9,13},{10,... | collective-permute-start | bytes 589832 | tf_op jit(solution)/shard_map/ppermute | solution.py:64

commit v19 on v17

--- a/solution.py
+++ b/solution.py
@@ -132,9 +132,26 @@
     n = lax.axis_size(axis)
     if n % 2:
         return lax.all_gather(block, axis, axis=0, tiled=True)
-    groups = [list(range(k, n, 2)) for k in range(2)]
-    mine = lax.all_gather(block, axis, axis_index_groups=groups)
-    both = _pair(mine, _swap(mine, axis, 1), lax.axis_index(axis) % 2)
+    chips = n // 2
+    c = lax.axis_index(axis)
+    z, k = c // 2, c % 2
+    held = [block]
+    for d in range(1, chips):
+        for step in (d, -d):
+            pairs = [
+                (2 * i + j, 2 * (i + step) + j)
+                for i in range(chips)
+                if 0 <= i + step < chips
+                for j in range(2)
+            ]
+            held.append(lax.ppermute(block, axis, pairs))
+    held = jnp.stack(held)
+    mine = []
+    for j in range(chips):
+        at = jnp.where(j == z, 0, jnp.where(j < z, 2 * (z - j) - 1, 2 * (j - z)))
+        mine.append(_pick(at, held))
+    mine = jnp.stack(mine)
+    both = _pair(mine, _swap(mine, axis, 1), k)
     return jnp.swapaxes(both, 0, 1).reshape(n * block.shape[0], block.shape[1])
 
 

time: 114 us -> 125 us (1.096)
  starting transfers between devices: 13 us -> 39.3 us
  blocking collectives: 21.5 us -> 0 us
  waiting for transfers between devices: 30.8 us -> 35.3 us
    ppermute x0 -> x6, starting transfers between devices: none -> 23.6 us  [col_all_gather(): held.append(lax.ppermute(block, axis, pairs))]
    all_gather x1 -> x0, blocking collectives: 21.5 us -> none  [col_all_gather(): mine = lax.all_gather(block, axis, axis_index_groups=groups)]
    ppermute x0 -> x6, waiting for transfers between devices: none -> 6.08 us  [col_all_gather(): held.append(lax.ppermute(block, axis, pairs))]
    ppermute x12, starting transfers between devices: 13 us -> 15.7 us  [_swap(): return lax.ppermute(value, axis, [(i, i ^ flip) for i in range(size)])]
    ppermute x12, waiting for transfers between devices: 30.8 us -> 29.2 us  [_swap(): return lax.ppermute(value, axis, [(i, i ^ flip) for i in range(size)])]
    unnamed x6 -> x12, local copies, waits for them, and re-layouts: 2.8 us -> 3.82 us
  transfers between devices with their start and end apart: 12 -> 18, of which waited for: 10 -> 12; matrix products, arithmetic and copies ran while one was open for 6% -> 6% of each run, Pallas kernels for 12% -> 11%
where the time goes in v19:
time: 125 us
  starting transfers between devices  39.3 us (31%)
  waiting for transfers between devices  35.3 us (28%)
  matrix products  18 us (14%)
  Pallas kernels  13.3 us (11%)
  other arithmetic  9.13 us (7%)
  local copies, waits for them, and re-layouts  8.47 us (7%)
    ppermute x12, waiting for transfers between devices, _swap(): return lax.ppermute(value, axis, [(i, i ^ flip) for i in range(size)])  29.2 us
    ppermute x6, starting transfers between devices, col_all_gather(): held.append(lax.ppermute(block, axis, pairs))  23.6 us
    ppermute x12, starting transfers between devices, _swap(): return lax.ppermute(value, axis, [(i, i ^ flip) for i in range(size)])  15.7 us
    pallas_call x2, Pallas kernels, outer_product_sum(): pl.pallas_call(kernel, grid=(n // block_n, count), in_specs=in_specs, out...  13.3 us
    dot_general x1, matrix products, body(): lax.dot_general(full_grad, weight, (((1,), (1,)), ((), ())), preferred_el...  9.04 us
    dot_general x1, matrix products, body(): partial_value = jnp.dot(local_x, weight, preferred_element_type=jnp.float32)  8.99 us
    ppermute x6, waiting for transfers between devices, col_all_gather(): held.append(lax.ppermute(block, axis, pairs))  6.08 us
    unnamed x12, local copies, waits for them, and re-layouts  3.82 us
  transfers between devices with their start and end apart: 18, of which 12 were waited for; matrix products, arithmetic and copies ran while one was open for 6% of the time, Pallas kernels for 11%

profile of v19, /device:TPU:0, one launch (start us, length us, event | category | flops | bytes accessed | tf_op | source)
XLA Modules:
  0.0 124.6 jit_solution(2318244438805952265)
XLA Ops:
  1.9 6.0 %collective-permute-start.2 = (bf16[32,3072]{1,0:T(8,128)(2,1)}, bf16[32,3072]{1,0:T(8,128)(2,1)S(1)}, u32[]{:S(2)}, u32[]{:S(2)}) collective-permute-start(bf16[32,3072]{1,0:T(8,128)(2,1)} %param.4), channel_id=1, source_target_pairs={{0,4},{1,5},{2,6},{3,7},{8,12},{9,13},{10,14},{11,15},{16,20},{17,... | collective-permute-start | bytes 589832 | tf_op jit(solution)/shard_map/ppermute | solution.py:147
  9.2 5.1 %collective-permute-start = (bf16[32,3072]{1,0:T(8,128)(2,1)}, bf16[32,3072]{1,0:T(8,128)(2,1)S(1)}, u32[]{:S(2)}, u32[]{:S(2)}) collective-permute-start(bf16[32,3072]{1,0:T(8,128)(2,1)} %param.4), channel_id=1, source_target_pairs={{0,2},{1,3},{2,4},{3,5},{4,6},{5,7},{8,10},{9,11},{10,12},{11,13},... | collective-permute-start | bytes 589832 | tf_op jit(solution)/shard_map/ppermute | solution.py:147
  16.6 1.6 %collective-permute-done = bf16[32,3072]{1,0:T(8,128)(2,1)S(1)} collective-permute-done((bf16[32,3072]{1,0:T(8,128)(2,1)}, bf16[32,3072]{1,0:T(8,128)(2,1)S(1)}, u32[]{:S(2)}, u32[]{:S(2)}) %collective-permute-start) | collective-permute-done | bytes 196640 | tf_op jit(solution)/shard_map/ppermute | solution.py:147
  18.2 8.7 %collective-permute-start.4 = (bf16[32,3072]{1,0:T(8,128)(2,1)}, bf16[32,3072]{1,0:T(8,128)(2,1)S(1)}, u32[]{:S(2)}, u32[]{:S(2)}) collective-permute-start(bf16[32,3072]{1,0:T(8,128)(2,1)} %param.4), channel_id=1, source_target_pairs={{0,6},{1,7},{8,14},{9,15},{16,22},{17,23},{24,30},{25,31}} | collective-permute-start | bytes 589832 | tf_op jit(solution)/shard_map/ppermute | solution.py:147
  27.0 4.5 %collective-permute-done.4 = bf16[32,3072]{1,0:T(8,128)(2,1)S(1)} collective-permute-done((bf16[32,3072]{1,0:T(8,128)(2,1)}, bf16[32,3072]{1,0:T(8,128)(2,1)S(1)}, u32[]{:S(2)}, u32[]{:S(2)}) %collective-permute-start.4) | collective-permute-done | bytes 196640 | tf_op jit(solution)/shard_map/ppermute | solution.py:147
  31.8 2.3 %collective-permute-done.6 = bf16[4,32,3072]{2,1,0:T(8,128)(2,1)S(1)} collective-permute-done((bf16[4,32,3072]{2,1,0:T(8,128)(2,1)S(1)}, bf16[4,32,3072]{2,1,0:T(8,128)(2,1)S(1)}, u32[]{:S(2)}, u32[]{:S(2)}) %collective-permute-start.6) | collective-permute-done | bytes 786464 | tf_op jit(solution)/shard_map/ppermute | solution.py:64
  34.4 9.0 %fusion.25 = f32[256,3072]{1,0:T(8,128)S(1)} fusion(bf16[256,3072]{1,0:T(8,128)(2,1)S(1)} %bitcast.121, bf16[3072,3072]{1,0:T(8,128)(2,1)} %param.5), kind=kOutput, calls=%fused_computation.75 | convolution fusion | flops 4831838208 | bytes 23592960 | tf_op jit(solution)/shard_map/dot_general | solution.py:193
  45.5 2.0 %collective-permute-start.7 = (bf16[2,64,1536]{2,1,0:T(8,128)(2,1)}, bf16[2,64,1536]{2,1,0:T(8,128)(2,1)S(1)}, u32[]{:S(2)}, u32[]{:S(2)}) collective-permute-start(bf16[2,64,1536]{2,1,0:T(8,128)(2,1)} %fusion.15), channel_id=1, source_target_pairs={{0,8},{8,0},{16,24},{24,16},{1,9},{9,1},{17,25},{25,17},{2,10},{10... | collective-permute-start | bytes 1179656 | tf_op jit(solution)/shard_map/ppermute | solution.py:64
  47.6 1.6 %collective-permute-start.9 = (bf16[2,64,1536]{2,1,0:T(8,128)(2,1)S(1)}, bf16[2,64,1536]{2,1,0:T(8,128)(2,1)S(1)}, u32[]{:S(2)}, u32[]{:S(2)}) collective-permute-start(bf16[2,64,1536]{2,1,0:T(8,128)(2,1)S(1)} %fusion.13), channel_id=1, source_target_pairs={{0,16},{8,24},{16,0},{24,8},{1,17},{9,25},{17,1},{25,9},{2,18},{10... | collective-permute-start | bytes 1179656 | tf_op jit(solution)/shard_map/ppermute | solution.py:64
  49.2 8.0 %collective-permute-done.7 = bf16[2,64,1536]{2,1,0:T(8,128)(2,1)S(1)} collective-permute-done((bf16[2,64,1536]{2,1,0:T(8,128)(2,1)}, bf16[2,64,1536]{2,1,0:T(8,128)(2,1)S(1)}, u32[]{:S(2)}, u32[]{:S(2)}) %collective-permute-start.7) | collective-permute-done | bytes 393248 | tf_op jit(solution)/shard_map/ppermute | solution.py:64
  58.5 1.8 %collective-permute-start.8 = (bf16[64,1536]{1,0:T(8,128)(2,1)S(1)}, bf16[64,1536]{1,0:T(8,128)(2,1)S(1)}, u32[]{:S(2)}, u32[]{:S(2)}) collective-permute-start(bf16[64,1536]{1,0:T(8,128)(2,1)S(1)} %fusion.19), channel_id=1, source_target_pairs={{0,16},{8,24},{16,0},{24,8},{1,17},{9,25},{17,1},{25,9},{2,18},{10... | collective-permute-start | bytes 589832 | tf_op jit(solution)/shard_map/ppermute | solution.py:64
  62.0 3.0 %collective-permute-done.8 = bf16[64,1536]{1,0:T(8,128)(2,1)S(1)} collective-permute-done((bf16[64,1536]{1,0:T(8,128)(2,1)S(1)}, bf16[64,1536]{1,0:T(8,128)(2,1)S(1)}, u32[]{:S(2)}, u32[]{:S(2)}) %collective-permute-start.8) | collective-permute-done | bytes 196640 | tf_op jit(solution)/shard_map/ppermute | solution.py:64
  69.9 3.7 %collective-permute-done.13 = bf16[64,1536]{1,0:T(8,128)(2,1)S(1)} collective-permute-done((bf16[64,1536]{1,0:T(8,128)(2,1)S(1)}, bf16[64,1536]{1,0:T(8,128)(2,1)S(1)}, u32[]{:S(2)}, u32[]{:S(2)}) %collective-permute-start.13) | collective-permute-done | bytes 196640 | tf_op jit(solution)/shard_map/ppermute | solution.py:64
  75.3 1.9 %collective-permute-start.12 = (bf16[2,64,1536]{2,1,0:T(8,128)(2,1)S(1)}, bf16[2,64,1536]{2,1,0:T(8,128)(2,1)S(1)}, u32[]{:S(2)}, u32[]{:S(2)}) collective-permute-start(bf16[2,64,1536]{2,1,0:T(8,128)(2,1)S(1)} %pad_maximum_fusion.5), channel_id=1, source_target_pairs={{0,16},{8,24},{16,0},{24,8},{1,17},{9,25},{17,1},{25,9},{2,18},{10... | collective-permute-start | bytes 1179656 | tf_op jit(solution)/shard_map/ppermute | solution.py:64
  77.2 5.3 %collective-permute-done.14 = bf16[2,64,1536]{2,1,0:T(8,128)(2,1)S(1)} collective-permute-done((bf16[2,64,1536]{2,1,0:T(8,128)(2,1)S(1)}, bf16[2,64,1536]{2,1,0:T(8,128)(2,1)S(1)}, u32[]{:S(2)}, u32[]{:S(2)}) %collective-permute-start.14) | collective-permute-done | bytes 393248 | tf_op jit(solution)/shard_map/ppermute | solution.py:64
  83.2 9.0 %fusion.22 = f32[256,3072]{1,0:T(8,128)S(1)} fusion(bf16[3072,3072]{1,0:T(8,128)(2,1)} %param.5, bf16[256,1536]{1,0:T(8,128)(2,1)S(1)} %bitcast.115, bf16[256,1536]{1,0:T(8,128)(2,1)S(1)} %bitcast.118), kind=kOutput, calls=%fused_computation.72 | convolution fusion | flops 4834983936 | bytes 23592960 | tf_op jit(solution)/shard_map/dot_general | solution.py:210
  92.3 1.7 %copy-done.1 = f32[256,3072]{1,0:T(8,128)} copy-done((f32[256,3072]{1,0:T(8,128)}, f32[256,3072]{1,0:T(8,128)S(1)}, u32[]{:S(2)}) %copy-start.1) | copy-done | bytes 3145752
  94.9 1.6 %copy.16 = bf16[256,3072]{0,1:T(8,128)(2,1)} copy(bf16[256,3072]{1,0:T(8,128)(2,1)S(1)} %bitcast.122) | data formatting | bytes 3145728 | tf_op jit(solution)/shard_map/reshape | solution.py:155
  97.6 1.8 %bitcast_add_fusion = f32[4,32,3072]{2,1,0:T(8,128)S(1)} fusion(bf16[4,32,3072]{2,1,0:T(8,128)(2,1)} %collective-permute-done.15, f32[4,2,32,3072]{3,2,1,0:T(8,128)} %bitcast.130, s32[]{:T(128)S(6)} %select_n.184), kind=kLoop, calls=%fused_computation.4 | loop fusion | flops 786432 | bytes 3932164 | tf_op jit(solution)/shard_map/add | solution.py:166
  102.4 6.7 %shard_map.75._ = bf16[3072,3072]{1,0:T(8,128)(2,1)} custom-call(bf16[3072,256]{1,0:T(8,128)(2,1)} %bitcast.113, bf16[256,3072]{1,0:T(8,128)(2,1)} %pad_maximum_fusion.1.g_ref), custom_call_target="tpu_custom_call" | custom-call | flops 2415919104 | bytes 11796480 | tf_op jit(solution)/shard_map/pallas_call | solution.py:49
  109.1 2.6 %collective-permute-done.16 = bf16[2,32,3072]{2,1,0:T(8,128)(2,1)S(1)} collective-permute-done((bf16[2,32,3072]{2,1,0:T(8,128)(2,1)}, bf16[2,32,3072]{2,1,0:T(8,128)(2,1)S(1)}, u32[]{:S(2)}, u32[]{:S(2)}) %collective-permute-start.16) | collective-permute-done | bytes 393248 | tf_op jit(solution)/shard_map/ppermute | solution.py:64
  111.8 3.1 %collective-permute-start.17 = (bf16[32,3072]{1,0:T(8,128)(2,1)S(1)}, bf16[32,3072]{1,0:T(8,128)(2,1)S(1)}, u32[]{:S(2)}, u32[]{:S(2)}) collective-permute-start(bf16[32,3072]{1,0:T(8,128)(2,1)S(1)} %fusion.21), channel_id=1, source_target_pairs={{0,4},{1,5},{2,6},{3,7},{4,0},{5,1},{6,2},{7,3},{8,12},{9,13},{10,... | collective-permute-start | bytes 589832 | tf_op jit(solution)/shard_map/ppermute | solution.py:64
  114.8 6.7 %shard_map.76 = bf16[3072,3072]{1,0:T(8,128)(2,1)} custom-call(bf16[3072,256]{1,0:T(8,128)(2,1)} %bitcast.114, bf16[256,3072]{1,0:T(8,128)(2,1)} %pad_maximum_fusion.1.g_ref, bf16[3072,3072]{1,0:T(8,128)(2,1)} %shard_map.75._), custom_call_target="tpu_custom_call", output_to_operand_aliasing={{}: (2, {})} | custom-call | flops 2415919104 | bytes 11796480 | tf_op jit(solution)/shard_map/pallas_call | solution.py:49
  121.5 2.4 %collective-permute-done.17 = bf16[32,3072]{1,0:T(8,128)(2,1)S(1)} collective-permute-done((bf16[32,3072]{1,0:T(8,128)(2,1)S(1)}, bf16[32,3072]{1,0:T(8,128)(2,1)S(1)}, u32[]{:S(2)}, u32[]{:S(2)}) %collective-permute-start.17) | collective-permute-done | bytes 196640 | tf_op jit(solution)/shard_map/ppermute | solution.py:64
  (61 shorter events, 23.6 us)
Async XLA Ops:
  0.6 26.3 %collective-permute-start.3 = (bf16[32,3072]{1,0:T(8,128)(2,1)}, bf16[32,3072]{1,0:T(8,128)(2,1)S(1)}, u32[]{:S(2)}, u32[]{:S(2)}) collective-permute-start(bf16[32,3072]{1,0:T(8,128)(2,1)} %param.4), channel_id=1, source_target_pairs={{4,0},{5,1},{6,2},{7,3},{12,8},{13,9},{14,10},{15,11},{20,16},{21,... | collective-permute-start | bytes 589832 | tf_op jit(solution)/shard_map/ppermute | solution.py:147
  1.9 25.0 %collective-permute-start.2 = (bf16[32,3072]{1,0:T(8,128)(2,1)}, bf16[32,3072]{1,0:T(8,128)(2,1)S(1)}, u32[]{:S(2)}, u32[]{:S(2)}) collective-permute-start(bf16[32,3072]{1,0:T(8,128)(2,1)} %param.4), channel_id=1, source_target_pairs={{0,4},{1,5},{2,6},{3,7},{8,12},{9,13},{10,14},{11,15},{16,20},{17,... | collective-permute-start | bytes 589832 | tf_op jit(solution)/shard_map/ppermute | solution.py:147
  7.9 19.0 %collective-permute-start.1 = (bf16[32,3072]{1,0:T(8,128)(2,1)}, bf16[32,3072]{1,0:T(8,128)(2,1)S(1)}, u32[]{:S(2)}, u32[]{:S(2)}) collective-permute-start(bf16[32,3072]{1,0:T(8,128)(2,1)} %param.4), channel_id=1, source_target_pairs={{2,0},{3,1},{4,2},{5,3},{6,4},{7,5},{10,8},{11,9},{12,10},{13,11},... | collective-permute-start | bytes 589832 | tf_op jit(solution)/shard_map/ppermute | solution.py:147
  9.2 9.0 %collective-permute-start = (bf16[32,3072]{1,0:T(8,128)(2,1)}, bf16[32,3072]{1,0:T(8,128)(2,1)S(1)}, u32[]{:S(2)}, u32[]{:S(2)}) collective-permute-start(bf16[32,3072]{1,0:T(8,128)(2,1)} %param.4), channel_id=1, source_target_pairs={{0,2},{1,3},{2,4},{3,5},{4,6},{5,7},{8,10},{9,11},{10,12},{11,13},... | collective-permute-start | bytes 589832 | tf_op jit(solution)/shard_map/ppermute | solution.py:147
  14.3 17.2 %collective-permute-start.5 = (bf16[32,3072]{1,0:T(8,128)(2,1)}, bf16[32,3072]{1,0:T(8,128)(2,1)S(1)}, u32[]{:S(2)}, u32[]{:S(2)}) collective-permute-start(bf16[32,3072]{1,0:T(8,128)(2,1)} %param.4), channel_id=1, source_target_pairs={{6,0},{7,1},{14,8},{15,9},{22,16},{23,17},{30,24},{31,25}} | collective-permute-start | bytes 589832 | tf_op jit(solution)/shard_map/ppermute | solution.py:147
  18.2 13.3 %collective-permute-start.4 = (bf16[32,3072]{1,0:T(8,128)(2,1)}, bf16[32,3072]{1,0:T(8,128)(2,1)S(1)}, u32[]{:S(2)}, u32[]{:S(2)}) collective-permute-start(bf16[32,3072]{1,0:T(8,128)(2,1)} %param.4), channel_id=1, source_target_pairs={{0,6},{1,7},{8,14},{9,15},{16,22},{17,23},{24,30},{25,31}} | collective-permute-start | bytes 589832 | tf_op jit(solution)/shard_map/ppermute | solution.py:147
  31.7 2.4 %collective-permute-start.6 = (bf16[4,32,3072]{2,1,0:T(8,128)(2,1)S(1)}, bf16[4,32,3072]{2,1,0:T(8,128)(2,1)S(1)}, u32[]{:S(2)}, u32[]{:S(2)}) collective-permute-start(bf16[4,32,3072]{2,1,0:T(8,128)(2,1)S(1)} %pad_maximum_fusion.2), channel_id=1, source_target_pairs={{0,1},{1,0},{2,3},{3,2},{4,5},{5,4},{6,7},{7,6},{8,9},{9,8},{10,11... | collective-permute-start | bytes 2359304 | tf_op jit(solution)/shard_map/ppermute | solution.py:64
  43.6 1.1 copy-start
  45.5 11.7 %collective-permute-start.7 = (bf16[2,64,1536]{2,1,0:T(8,128)(2,1)}, bf16[2,64,1536]{2,1,0:T(8,128)(2,1)S(1)}, u32[]{:S(2)}, u32[]{:S(2)}) collective-permute-start(bf16[2,64,1536]{2,1,0:T(8,128)(2,1)} %fusion.15), channel_id=1, source_target_pairs={{0,8},{8,0},{16,24},{24,16},{1,9},{9,1},{17,25},{25,17},{2,10},{10... | collective-permute-start | bytes 1179656 | tf_op jit(solution)/shard_map/ppermute | solution.py:64
  47.6 12.7 %collective-permute-start.9 = (bf16[2,64,1536]{2,1,0:T(8,128)(2,1)S(1)}, bf16[2,64,1536]{2,1,0:T(8,128)(2,1)S(1)}, u32[]{:S(2)}, u32[]{:S(2)}) collective-permute-start(bf16[2,64,1536]{2,1,0:T(8,128)(2,1)S(1)} %fusion.13), channel_id=1, source_target_pairs={{0,16},{8,24},{16,0},{24,8},{1,17},{9,25},{17,1},{25,9},{2,18},{10... | collective-permute-start | bytes 1179656 | tf_op jit(solution)/shard_map/ppermute | solution.py:64
  58.4 3.6 %copy-start.2 = (f32[3072]{0:T(1024)S(1)}, f32[3072]{0:T(1024)}, u32[]{:S(2)}) copy-start(f32[3072]{0:T(1024)} %param.6) | copy-start | bytes 36868
  58.5 6.5 %collective-permute-start.8 = (bf16[64,1536]{1,0:T(8,128)(2,1)S(1)}, bf16[64,1536]{1,0:T(8,128)(2,1)S(1)}, u32[]{:S(2)}, u32[]{:S(2)}) collective-permute-start(bf16[64,1536]{1,0:T(8,128)(2,1)S(1)} %fusion.19), channel_id=1, source_target_pairs={{0,16},{8,24},{16,0},{24,8},{1,17},{9,25},{17,1},{25,9},{2,18},{10... | collective-permute-start | bytes 589832 | tf_op jit(solution)/shard_map/ppermute | solution.py:64
  60.4 5.9 %collective-permute-start.10 = (bf16[64,1536]{1,0:T(8,128)(2,1)S(1)}, bf16[64,1536]{1,0:T(8,128)(2,1)S(1)}, u32[]{:S(2)}, u32[]{:S(2)}) collective-permute-start(bf16[64,1536]{1,0:T(8,128)(2,1)S(1)} %fusion.20), channel_id=1, source_target_pairs={{0,8},{8,0},{16,24},{24,16},{1,9},{9,1},{17,25},{25,17},{2,10},{10... | collective-permute-start | bytes 589832 | tf_op jit(solution)/shard_map/ppermute | solution.py:64
  67.8 5.7 %collective-permute-start.13 = (bf16[64,1536]{1,0:T(8,128)(2,1)S(1)}, bf16[64,1536]{1,0:T(8,128)(2,1)S(1)}, u32[]{:S(2)}, u32[]{:S(2)}) collective-permute-start(bf16[64,1536]{1,0:T(8,128)(2,1)S(1)} %get-tuple-element.11), channel_id=1, source_target_pairs={{0,16},{8,24},{16,0},{24,8},{1,17},{9,25},{17,1},{25,9},{2,18},{10... | collective-permute-start | bytes 589832 | tf_op jit(solution)/shard_map/ppermute | solution.py:64
  68.4 6.7 %collective-permute-start.11 = (bf16[64,1536]{1,0:T(8,128)(2,1)S(1)}, bf16[64,1536]{1,0:T(8,128)(2,1)S(1)}, u32[]{:S(2)}, u32[]{:S(2)}) collective-permute-start(bf16[64,1536]{1,0:T(8,128)(2,1)S(1)} %get-tuple-element.10), channel_id=1, source_target_pairs={{0,8},{8,0},{16,24},{24,16},{1,9},{9,1},{17,25},{25,17},{2,10},{10... | collective-permute-start | bytes 589832 | tf_op jit(solution)/shard_map/ppermute | solution.py:64
  73.6 8.9 %collective-permute-start.14 = (bf16[2,64,1536]{2,1,0:T(8,128)(2,1)S(1)}, bf16[2,64,1536]{2,1,0:T(8,128)(2,1)S(1)}, u32[]{:S(2)}, u32[]{:S(2)}) collective-permute-start(bf16[2,64,1536]{2,1,0:T(8,128)(2,1)S(1)} %pad_maximum_fusion.6), channel_id=1, source_target_pairs={{0,8},{8,0},{16,24},{24,16},{1,9},{9,1},{17,25},{25,17},{2,10},{10... | collective-permute-start | bytes 1179656 | tf_op jit(solution)/shard_map/ppermute | solution.py:64
  75.3 7.8 %collective-permute-start.12 = (bf16[2,64,1536]{2,1,0:T(8,128)(2,1)S(1)}, bf16[2,64,1536]{2,1,0:T(8,128)(2,1)S(1)}, u32[]{:S(2)}, u32[]{:S(2)}) collective-permute-start(bf16[2,64,1536]{2,1,0:T(8,128)(2,1)S(1)} %pad_maximum_fusion.5), channel_id=1, source_target_pairs={{0,16},{8,24},{16,0},{24,8},{1,17},{9,25},{17,1},{25,9},{2,18},{10... | collective-permute-start | bytes 1179656 | tf_op jit(solution)/shard_map/ppermute | solution.py:64
  92.3 1.7 %copy-start.1 = (f32[256,3072]{1,0:T(8,128)}, f32[256,3072]{1,0:T(8,128)S(1)}, u32[]{:S(2)}) copy-start(f32[256,3072]{1,0:T(8,128)S(1)} %fusion.22) | copy-start | bytes 9437188
  94.9 2.6 %collective-permute-start.15 = (bf16[4,32,3072]{2,1,0:T(8,128)(2,1)}, bf16[4,32,3072]{2,1,0:T(8,128)(2,1)}, u32[]{:S(2)}, u32[]{:S(2)}) collective-permute-start(bf16[4,32,3072]{2,1,0:T(8,128)(2,1)} %fusion), channel_id=1, source_target_pairs={{0,1},{1,0},{2,3},{3,2},{4,5},{5,4},{6,7},{7,6},{8,9},{9,8},{10,11... | collective-permute-start | bytes 2359304 | tf_op jit(solution)/shard_map/ppermute | solution.py:64
  100.2 11.5 %collective-permute-start.16 = (bf16[2,32,3072]{2,1,0:T(8,128)(2,1)}, bf16[2,32,3072]{2,1,0:T(8,128)(2,1)S(1)}, u32[]{:S(2)}, u32[]{:S(2)}) collective-permute-start(bf16[2,32,3072]{2,1,0:T(8,128)(2,1)} %fusion.14), channel_id=1, source_target_pairs={{0,2},{1,3},{2,0},{3,1},{4,6},{5,7},{6,4},{7,5},{8,10},{9,11},{10,... | collective-permute-start | bytes 1179656 | tf_op jit(solution)/shard_map/ppermute | solution.py:64
  111.8 12.1 %collective-permute-start.17 = (bf16[32,3072]{1,0:T(8,128)(2,1)S(1)}, bf16[32,3072]{1,0:T(8,128)(2,1)S(1)}, u32[]{:S(2)}, u32[]{:S(2)}) collective-permute-start(bf16[32,3072]{1,0:T(8,128)(2,1)S(1)} %fusion.21), channel_id=1, source_target_pairs={{0,4},{1,5},{2,6},{3,7},{4,0},{5,1},{6,2},{7,3},{8,12},{9,13},{10,... | collective-permute-start | bytes 589832 | tf_op jit(solution)/shard_map/ppermute | solution.py:64

commit v20 on v17

--- a/solution.py
+++ b/solution.py
@@ -80,7 +80,7 @@
     return [order, order[::-1]]
 
 
-def row_reduce_scatter(partial, axis="row"):
+def row_reduce_scatter(partial, axis="row", order=None):
     n = lax.axis_size(axis)
     if n & (n - 1):
         return lax.psum_scatter(partial, axis, scatter_dimension=0, tiled=True)
@@ -88,7 +88,8 @@
     r = lax.axis_index(axis)
     m = partial.shape[0] // n
     outs = []
-    for half, order in zip(_halves(partial), _bit_orders(n)):
+    pieces = [(partial, order)] if order is not None else zip(_halves(partial), _bit_orders(n))
+    for half, order in pieces:
         cur = half.reshape([2] * levels + [m, half.shape[1]])
         bits = list(range(levels))[::-1]
         for bit in order:
@@ -173,12 +174,18 @@
     local_x = col_all_gather(tokens)
     my_rows = local_x.shape[0] // lax.axis_size("row")
     first_row = lax.axis_index("row") * my_rows
-    partial_value = jnp.dot(local_x, weight, preferred_element_type=jnp.float32)
+    width = weight.shape[1]
+    split = width // 2 if width % 256 == 0 else width
     my_cot = lax.dynamic_slice_in_dim(cotangent, first_row, my_rows, 0)
-    preact = row_reduce_scatter(partial_value)
     hidden, full_grad, start = [], [], 0
     orders = _bit_orders(lax.axis_size("row"))
-    for number, part in enumerate(_halves(preact)):
+    row_size = lax.axis_size("row")
+    for number, lo in enumerate(range(0, width, split)):
+        part = jnp.dot(local_x, weight[:, lo : lo + split], preferred_element_type=jnp.float32)
+        if row_size & (row_size - 1):
+            part = row_reduce_scatter(part)
+        else:
+            part = row_reduce_scatter(part, order=orders[number % 2])
         cols = slice(start, start + part.shape[1])
         h, g = activate(part + bias[cols], my_cot[:, cols])
         hidden.append(h)

time: 114 us -> 114 us (level)
  waiting for transfers between devices: 30.8 us -> 34.1 us
    ppermute x12, waiting for transfers between devices: 30.8 us -> 34.1 us  [_swap(): return lax.ppermute(value, axis, [(i, i ^ flip) for i in range(size)])]
    dot_general x1 -> x2, matrix products: 8.99 us -> 8.02 us  [body(): jnp.dot(local_x, weight[:, lo:lo + split], preferred_element_type=jnp.flo...]
  transfers between devices with their start and end apart: 12 -> 12, of which waited for: 10 -> 12; matrix products, arithmetic and copies ran while one was open for 6% -> 7% of each run, Pallas kernels for 12% -> 12%
where the time goes in v20:
time: 114 us
  waiting for transfers between devices  34.1 us (30%)
  blocking collectives  21.5 us (19%)
  matrix products  17.1 us (15%)
  Pallas kernels  13.4 us (12%)
  starting transfers between devices  11.9 us (10%)
  other arithmetic  7.86 us (7%)
  local copies, waits for them, and re-layouts  7.63 us (7%)
    ppermute x12, waiting for transfers between devices, _swap(): return lax.ppermute(value, axis, [(i, i ^ flip) for i in range(size)])  34.1 us
    all_gather x1, blocking collectives, col_all_gather(): mine = lax.all_gather(block, axis, axis_index_groups=groups)  21.5 us
    pallas_call x2, Pallas kernels, outer_product_sum(): pl.pallas_call(kernel, grid=(n // block_n, count), in_specs=in_specs, out...  13.4 us
    ppermute x12, starting transfers between devices, _swap(): return lax.ppermute(value, axis, [(i, i ^ flip) for i in range(size)])  11.9 us
    dot_general x1, matrix products, body(): lax.dot_general(full_grad, weight, (((1,), (1,)), ((), ())), preferred_el...  9.03 us
    dot_general x2, matrix products, body(): jnp.dot(local_x, weight[:, lo:lo + split], preferred_element_type=jnp.flo...  8.02 us
    unnamed x6, local copies, waits for them, and re-layouts  3.84 us
  transfers between devices with their start and end apart: 12, of which 12 were waited for; matrix products, arithmetic and copies ran while one was open for 7% of the time, Pallas kernels for 12%

profile of v20, /device:TPU:0, one launch (start us, length us, event | category | flops | bytes accessed | tf_op | source)
XLA Modules:
  0.0 114.2 jit_solution(4782909843667648054)
XLA Ops:
  0.6 21.5 %all-gather = bf16[128,3072]{1,0:T(8,128)(2,1)S(1)} all-gather(bf16[32,3072]{1,0:T(8,128)(2,1)} %param.4), channel_id=2, replica_groups={{0,2,4,6},{1,3,5,7},{8,10,12,14},{9,11,13,15},{16,18,20,22},{17,19,21,2..., dimensions={0}, use_global_device_ids=true | all-gather | bytes 983040 | tf_op jit(solution)/shard_map/all_gather | solution.py:137
  22.1 2.3 %collective-permute-done = bf16[4,32,3072]{2,1,0:T(8,128)(2,1)S(1)} collective-permute-done((bf16[4,32,3072]{2,1,0:T(8,128)(2,1)S(1)}, bf16[4,32,3072]{2,1,0:T(8,128)(2,1)S(1)}, u32[]{:S(2)}, u32[]{:S(2)}) %collective-permute-start) | collective-permute-done | bytes 786464 | tf_op jit(solution)/shard_map/ppermute | solution.py:64
  24.9 5.3 %fusion = f32[2,2,64,1536]{3,2,1,0:T(8,128)S(1)} fusion(bf16[2,2,64,3072]{3,2,1,0:T(8,128)(2,1)S(1)} %bitcast.111, bf16[3072,3072]{1,0:T(8,128)(2,1)} %param.5), kind=kOutput, calls=%fused_computation | convolution fusion | flops 2415919104 | bytes 12582912 | tf_op jit(solution)/shard_map/dot_general | solution.py:184
  30.3 1.6 %collective-permute-start.3 = (bf16[2,64,1536]{2,1,0:T(8,128)(2,1)S(1)}, bf16[2,64,1536]{2,1,0:T(8,128)(2,1)S(1)}, u32[]{:S(2)}, u32[]{:S(2)}) collective-permute-start(bf16[2,64,1536]{2,1,0:T(8,128)(2,1)S(1)} %fusion.20), channel_id=1, source_target_pairs={{0,16},{8,24},{16,0},{24,8},{1,17},{9,25},{17,1},{25,9},{2,18},{10... | collective-permute-start | bytes 1179656 | tf_op jit(solution)/shard_map/ppermute | solution.py:64
  31.8 2.2 %copy-done.2 = bf16[3072,3072]{1,0:T(8,128)(2,1)S(1)} copy-done((bf16[3072,3072]{1,0:T(8,128)(2,1)S(1)}, bf16[3072,3072]{1,0:T(8,128)(2,1)}, u32[]{:S(2)}) %copy-start.2) | copy-done | bytes 18874392
  34.0 2.7 %fusion.2 = f32[2,2,64,1536]{3,2,1,0:T(8,128)S(1)} fusion(bf16[2,2,64,3072]{3,2,1,0:T(8,128)(2,1)S(1)} %bitcast.112, bf16[3072,3072]{1,0:T(8,128)(2,1)S(1)} %copy-done.2), kind=kOutput, calls=%fused_computation.2 | convolution fusion | flops 2415919104 | bytes 12582912 | tf_op jit(solution)/shard_map/dot_general | solution.py:184
  38.3 3.2 %collective-permute-done.3 = bf16[2,64,1536]{2,1,0:T(8,128)(2,1)S(1)} collective-permute-done((bf16[2,64,1536]{2,1,0:T(8,128)(2,1)S(1)}, bf16[2,64,1536]{2,1,0:T(8,128)(2,1)S(1)}, u32[]{:S(2)}, u32[]{:S(2)}) %collective-permute-start.3) | collective-permute-done | bytes 393248 | tf_op jit(solution)/shard_map/ppermute | solution.py:64
  43.2 5.6 %collective-permute-done.1 = bf16[2,64,1536]{2,1,0:T(8,128)(2,1)S(1)} collective-permute-done((bf16[2,64,1536]{2,1,0:T(8,128)(2,1)S(1)}, bf16[2,64,1536]{2,1,0:T(8,128)(2,1)S(1)}, u32[]{:S(2)}, u32[]{:S(2)}) %collective-permute-start.1) | collective-permute-done | bytes 393248 | tf_op jit(solution)/shard_map/ppermute | solution.py:64
  48.9 1.6 %collective-permute-start.2 = (bf16[64,1536]{1,0:T(8,128)(2,1)S(1)}, bf16[64,1536]{1,0:T(8,128)(2,1)S(1)}, u32[]{:S(2)}, u32[]{:S(2)}) collective-permute-start(bf16[64,1536]{1,0:T(8,128)(2,1)S(1)} %fusion.25), channel_id=1, source_target_pairs={{0,16},{8,24},{16,0},{24,8},{1,17},{9,25},{17,1},{25,9},{2,18},{10... | collective-permute-start | bytes 589832 | tf_op jit(solution)/shard_map/ppermute | solution.py:64
  50.5 1.7 %collective-permute-done.4 = bf16[64,1536]{1,0:T(8,128)(2,1)S(1)} collective-permute-done((bf16[64,1536]{1,0:T(8,128)(2,1)S(1)}, bf16[64,1536]{1,0:T(8,128)(2,1)S(1)}, u32[]{:S(2)}, u32[]{:S(2)}) %collective-permute-start.4) | collective-permute-done | bytes 196640 | tf_op jit(solution)/shard_map/ppermute | solution.py:64
  52.2 2.5 %collective-permute-done.2 = bf16[64,1536]{1,0:T(8,128)(2,1)S(1)} collective-permute-done((bf16[64,1536]{1,0:T(8,128)(2,1)S(1)}, bf16[64,1536]{1,0:T(8,128)(2,1)S(1)}, u32[]{:S(2)}, u32[]{:S(2)}) %collective-permute-start.2) | collective-permute-done | bytes 196640 | tf_op jit(solution)/shard_map/ppermute | solution.py:64
  56.1 1.6 %collective-permute-start.7 = (bf16[64,1536]{1,0:T(8,128)(2,1)S(1)}, bf16[64,1536]{1,0:T(8,128)(2,1)S(1)}, u32[]{:S(2)}, u32[]{:S(2)}) collective-permute-start(bf16[64,1536]{1,0:T(8,128)(2,1)S(1)} %get-tuple-element.9), channel_id=1, source_target_pairs={{0,16},{8,24},{16,0},{24,8},{1,17},{9,25},{17,1},{25,9},{2,18},{10... | collective-permute-start | bytes 589832 | tf_op jit(solution)/shard_map/ppermute | solution.py:64
  59.2 2.7 %collective-permute-done.7 = bf16[64,1536]{1,0:T(8,128)(2,1)S(1)} collective-permute-done((bf16[64,1536]{1,0:T(8,128)(2,1)S(1)}, bf16[64,1536]{1,0:T(8,128)(2,1)S(1)}, u32[]{:S(2)}, u32[]{:S(2)}) %collective-permute-start.7) | collective-permute-done | bytes 196640 | tf_op jit(solution)/shard_map/ppermute | solution.py:64
  63.5 2.0 %collective-permute-done.5 = bf16[64,1536]{1,0:T(8,128)(2,1)S(1)} collective-permute-done((bf16[64,1536]{1,0:T(8,128)(2,1)S(1)}, bf16[64,1536]{1,0:T(8,128)(2,1)S(1)}, u32[]{:S(2)}, u32[]{:S(2)}) %collective-permute-start.5) | collective-permute-done | bytes 196640 | tf_op jit(solution)/shard_map/ppermute | solution.py:64
  65.7 6.0 %collective-permute-done.8 = bf16[2,64,1536]{2,1,0:T(8,128)(2,1)S(1)} collective-permute-done((bf16[2,64,1536]{2,1,0:T(8,128)(2,1)S(1)}, bf16[2,64,1536]{2,1,0:T(8,128)(2,1)S(1)}, u32[]{:S(2)}, u32[]{:S(2)}) %collective-permute-start.8) | collective-permute-done | bytes 393248 | tf_op jit(solution)/shard_map/ppermute | solution.py:64
  71.9 1.6 %collective-permute-done.6 = bf16[2,64,1536]{2,1,0:T(8,128)(2,1)S(1)} collective-permute-done((bf16[2,64,1536]{2,1,0:T(8,128)(2,1)S(1)}, bf16[2,64,1536]{2,1,0:T(8,128)(2,1)S(1)}, u32[]{:S(2)}, u32[]{:S(2)}) %collective-permute-start.6) | collective-permute-done | bytes 393248 | tf_op jit(solution)/shard_map/ppermute | solution.py:64
  73.6 9.0 %fusion.28 = f32[256,3072]{1,0:T(8,128)S(1)} fusion(bf16[3072,3072]{1,0:T(8,128)(2,1)} %param.5, bf16[256,1536]{1,0:T(8,128)(2,1)S(1)} %bitcast.105, bf16[256,1536]{1,0:T(8,128)(2,1)S(1)} %bitcast.108), kind=kOutput, calls=%fused_computation.66 | convolution fusion | flops 4834983936 | bytes 23592960 | tf_op jit(solution)/shard_map/dot_general | solution.py:200
  82.6 1.7 %copy-done = f32[256,3072]{1,0:T(8,128)} copy-done((f32[256,3072]{1,0:T(8,128)}, f32[256,3072]{1,0:T(8,128)S(1)}, u32[]{:S(2)}) %copy-start) | copy-done | bytes 3145752
  85.3 1.6 %copy.19 = bf16[256,3072]{0,1:T(8,128)(2,1)} copy(bf16[256,3072]{1,0:T(8,128)(2,1)S(1)} %bitcast.113) | data formatting | bytes 3145728 | tf_op jit(solution)/shard_map/reshape | solution.py:139
  87.9 1.8 %bitcast_add_fusion = f32[4,32,3072]{2,1,0:T(8,128)S(1)} fusion(bf16[4,32,3072]{2,1,0:T(8,128)(2,1)} %collective-permute-done.9, f32[4,2,32,3072]{3,2,1,0:T(8,128)} %bitcast.119, s32[]{:T(128)S(6)} %select_n.132), kind=kLoop, calls=%fused_computation.10 | loop fusion | flops 786432 | bytes 3932164 | tf_op jit(solution)/shard_map/add | solution.py:150
  92.7 6.7 %shard_map.75._ = bf16[3072,3072]{1,0:T(8,128)(2,1)} custom-call(bf16[3072,256]{1,0:T(8,128)(2,1)} %bitcast.103, bf16[256,3072]{1,0:T(8,128)(2,1)} %pad_maximum_fusion.g_ref), custom_call_target="tpu_custom_call" | custom-call | flops 2415919104 | bytes 11796480 | tf_op jit(solution)/shard_map/pallas_call | solution.py:49
  99.4 2.6 %collective-permute-done.10 = bf16[2,32,3072]{2,1,0:T(8,128)(2,1)S(1)} collective-permute-done((bf16[2,32,3072]{2,1,0:T(8,128)(2,1)}, bf16[2,32,3072]{2,1,0:T(8,128)(2,1)S(1)}, u32[]{:S(2)}, u32[]{:S(2)}) %collective-permute-start.10) | collective-permute-done | bytes 393248 | tf_op jit(solution)/shard_map/ppermute | solution.py:64
  103.0 6.7 %shard_map.76 = bf16[3072,3072]{1,0:T(8,128)(2,1)} custom-call(bf16[3072,256]{1,0:T(8,128)(2,1)} %bitcast.104, bf16[256,3072]{1,0:T(8,128)(2,1)} %pad_maximum_fusion.g_ref, bf16[3072,3072]{1,0:T(8,128)(2,1)} %shard_map.75._), custom_call_target="tpu_custom_call", output_to_operand_aliasing={{}: (2, {})} | custom-call | flops 2415919104 | bytes 11796480 | tf_op jit(solution)/shard_map/pallas_call | solution.py:49
  109.7 3.8 %collective-permute-done.11 = bf16[32,3072]{1,0:T(8,128)(2,1)S(1)} collective-permute-done((bf16[32,3072]{1,0:T(8,128)(2,1)S(1)}, bf16[32,3072]{1,0:T(8,128)(2,1)S(1)}, u32[]{:S(2)}, u32[]{:S(2)}) %collective-permute-start.11) | collective-permute-done | bytes 196640 | tf_op jit(solution)/shard_map/ppermute | solution.py:64
  (42 shorter events, 15.7 us)
Async XLA Ops:
  22.1 2.3 %collective-permute-start = (bf16[4,32,3072]{2,1,0:T(8,128)(2,1)S(1)}, bf16[4,32,3072]{2,1,0:T(8,128)(2,1)S(1)}, u32[]{:S(2)}, u32[]{:S(2)}) collective-permute-start(bf16[4,32,3072]{2,1,0:T(8,128)(2,1)S(1)} %bitcast.116), channel_id=1, source_target_pairs={{0,1},{1,0},{2,3},{3,2},{4,5},{5,4},{6,7},{7,6},{8,9},{9,8},{10,11... | collective-permute-start | bytes 2359304 | tf_op jit(solution)/shard_map/ppermute | solution.py:64
  24.8 9.2 %copy-start.2 = (bf16[3072,3072]{1,0:T(8,128)(2,1)S(1)}, bf16[3072,3072]{1,0:T(8,128)(2,1)}, u32[]{:S(2)}) copy-start(bf16[3072,3072]{1,0:T(8,128)(2,1)} %param.5) | copy-start | bytes 56623108
  30.3 11.2 %collective-permute-start.3 = (bf16[2,64,1536]{2,1,0:T(8,128)(2,1)S(1)}, bf16[2,64,1536]{2,1,0:T(8,128)(2,1)S(1)}, u32[]{:S(2)}, u32[]{:S(2)}) collective-permute-start(bf16[2,64,1536]{2,1,0:T(8,128)(2,1)S(1)} %fusion.20), channel_id=1, source_target_pairs={{0,16},{8,24},{16,0},{24,8},{1,17},{9,25},{17,1},{25,9},{2,18},{10... | collective-permute-start | bytes 1179656 | tf_op jit(solution)/shard_map/ppermute | solution.py:64
  36.8 12.0 %collective-permute-start.1 = (bf16[2,64,1536]{2,1,0:T(8,128)(2,1)S(1)}, bf16[2,64,1536]{2,1,0:T(8,128)(2,1)S(1)}, u32[]{:S(2)}, u32[]{:S(2)}) collective-permute-start(bf16[2,64,1536]{2,1,0:T(8,128)(2,1)S(1)} %fusion.19), channel_id=1, source_target_pairs={{0,8},{8,0},{16,24},{24,16},{1,9},{9,1},{17,25},{25,17},{2,10},{10... | collective-permute-start | bytes 1179656 | tf_op jit(solution)/shard_map/ppermute | solution.py:64
  41.6 9.0 %copy-start.1 = (f32[3072]{0:T(1024)S(1)}, f32[3072]{0:T(1024)}, u32[]{:S(2)}) copy-start(f32[3072]{0:T(1024)} %param.6) | copy-start | bytes 36868
  41.6 10.6 %collective-permute-start.4 = (bf16[64,1536]{1,0:T(8,128)(2,1)S(1)}, bf16[64,1536]{1,0:T(8,128)(2,1)S(1)}, u32[]{:S(2)}, u32[]{:S(2)}) collective-permute-start(bf16[64,1536]{1,0:T(8,128)(2,1)S(1)} %fusion.26), channel_id=1, source_target_pairs={{0,8},{8,0},{16,24},{24,16},{1,9},{9,1},{17,25},{25,17},{2,10},{10... | collective-permute-start | bytes 589832 | tf_op jit(solution)/shard_map/ppermute | solution.py:64
  48.9 5.7 %collective-permute-start.2 = (bf16[64,1536]{1,0:T(8,128)(2,1)S(1)}, bf16[64,1536]{1,0:T(8,128)(2,1)S(1)}, u32[]{:S(2)}, u32[]{:S(2)}) collective-permute-start(bf16[64,1536]{1,0:T(8,128)(2,1)S(1)} %fusion.25), channel_id=1, source_target_pairs={{0,16},{8,24},{16,0},{24,8},{1,17},{9,25},{17,1},{25,9},{2,18},{10... | collective-permute-start | bytes 589832 | tf_op jit(solution)/shard_map/ppermute | solution.py:64
  56.1 5.7 %collective-permute-start.7 = (bf16[64,1536]{1,0:T(8,128)(2,1)S(1)}, bf16[64,1536]{1,0:T(8,128)(2,1)S(1)}, u32[]{:S(2)}, u32[]{:S(2)}) collective-permute-start(bf16[64,1536]{1,0:T(8,128)(2,1)S(1)} %get-tuple-element.9), channel_id=1, source_target_pairs={{0,16},{8,24},{16,0},{24,8},{1,17},{9,25},{17,1},{25,9},{2,18},{10... | collective-permute-start | bytes 589832 | tf_op jit(solution)/shard_map/ppermute | solution.py:64
  57.7 7.8 %collective-permute-start.5 = (bf16[64,1536]{1,0:T(8,128)(2,1)S(1)}, bf16[64,1536]{1,0:T(8,128)(2,1)S(1)}, u32[]{:S(2)}, u32[]{:S(2)}) collective-permute-start(bf16[64,1536]{1,0:T(8,128)(2,1)S(1)} %get-tuple-element.8), channel_id=1, source_target_pairs={{0,8},{8,0},{16,24},{24,16},{1,9},{9,1},{17,25},{25,17},{2,10},{10... | collective-permute-start | bytes 589832 | tf_op jit(solution)/shard_map/ppermute | solution.py:64
  62.0 9.7 %collective-permute-start.8 = (bf16[2,64,1536]{2,1,0:T(8,128)(2,1)S(1)}, bf16[2,64,1536]{2,1,0:T(8,128)(2,1)S(1)}, u32[]{:S(2)}, u32[]{:S(2)}) collective-permute-start(bf16[2,64,1536]{2,1,0:T(8,128)(2,1)S(1)} %pad_maximum_fusion.4), channel_id=1, source_target_pairs={{0,8},{8,0},{16,24},{24,16},{1,9},{9,1},{17,25},{25,17},{2,10},{10... | collective-permute-start | bytes 1179656 | tf_op jit(solution)/shard_map/ppermute | solution.py:64
  65.6 7.8 %collective-permute-start.6 = (bf16[2,64,1536]{2,1,0:T(8,128)(2,1)S(1)}, bf16[2,64,1536]{2,1,0:T(8,128)(2,1)S(1)}, u32[]{:S(2)}, u32[]{:S(2)}) collective-permute-start(bf16[2,64,1536]{2,1,0:T(8,128)(2,1)S(1)} %pad_maximum_fusion.3), channel_id=1, source_target_pairs={{0,16},{8,24},{16,0},{24,8},{1,17},{9,25},{17,1},{25,9},{2,18},{10... | collective-permute-start | bytes 1179656 | tf_op jit(solution)/shard_map/ppermute | solution.py:64
  82.6 1.7 %copy-start = (f32[256,3072]{1,0:T(8,128)}, f32[256,3072]{1,0:T(8,128)S(1)}, u32[]{:S(2)}) copy-start(f32[256,3072]{1,0:T(8,128)S(1)} %fusion.28) | copy-start | bytes 9437188
  85.3 2.6 %collective-permute-start.9 = (bf16[4,32,3072]{2,1,0:T(8,128)(2,1)}, bf16[4,32,3072]{2,1,0:T(8,128)(2,1)}, u32[]{:S(2)}, u32[]{:S(2)}) collective-permute-start(bf16[4,32,3072]{2,1,0:T(8,128)(2,1)} %fusion.6), channel_id=1, source_target_pairs={{0,1},{1,0},{2,3},{3,2},{4,5},{5,4},{6,7},{7,6},{8,9},{9,8},{10,11... | collective-permute-start | bytes 2359304 | tf_op jit(solution)/shard_map/ppermute | solution.py:64
  90.5 11.5 %collective-permute-start.10 = (bf16[2,32,3072]{2,1,0:T(8,128)(2,1)}, bf16[2,32,3072]{2,1,0:T(8,128)(2,1)S(1)}, u32[]{:S(2)}, u32[]{:S(2)}) collective-permute-start(bf16[2,32,3072]{2,1,0:T(8,128)(2,1)} %fusion.21), channel_id=1, source_target_pairs={{0,2},{1,3},{2,0},{3,1},{4,6},{5,7},{6,4},{7,5},{8,10},{9,11},{10,... | collective-permute-start | bytes 1179656 | tf_op jit(solution)/shard_map/ppermute | solution.py:64
  102.1 11.4 %collective-permute-start.11 = (bf16[32,3072]{1,0:T(8,128)(2,1)S(1)}, bf16[32,3072]{1,0:T(8,128)(2,1)S(1)}, u32[]{:S(2)}, u32[]{:S(2)}) collective-permute-start(bf16[32,3072]{1,0:T(8,128)(2,1)S(1)} %fusion.27), channel_id=1, source_target_pairs={{0,4},{1,5},{2,6},{3,7},{4,0},{5,1},{6,2},{7,3},{8,12},{9,13},{10,... | collective-permute-start | bytes 589832 | tf_op jit(solution)/shard_map/ppermute | solution.py:64
